TPU v7x, 32 devices: a whole 2x2x4 slice. The times are simulated.
32 devices in a mesh: req: 4 (over y, x), cand: 8 (over z, core).
Axes of the slice: x: 2, y: 2, z: 4, core: 2. Of those that a mesh axis runs over, the one named last changes fastest.
Arguments:
- table: bfloat16 [32768, 256], P('req'), may hold values from -6 to 6
- history_shard: int32 [4, 1024, 1], P('req', 'cand'), may hold values from 0 to 3; in each aligned block of 128 rows (0 to 127, 128 to 255, ..., all dimensions but the last counted through in order) at most 128 rows name the same one
- history_row: int32 [4, 1024], P('req', 'cand'), may hold values from 0 to 8191
- candidate_shard: int32 [4, 2048, 1], P('req', 'cand'), may hold values from 0 to 3; in each aligned block of 256 rows (0 to 255, 256 to 511, ..., all dimensions but the last counted through in order) at most 192 rows name the same one
- candidate_row: int32 [4, 2048], P('req', 'cand'), may hold values from 0 to 8191
- history_length: int32 [4], P('req'), may hold values from 128 to 1024, as said below
- w_query: bfloat16 [256, 256], replicated, may hold values from -0.375 to 0.375
- w_key: bfloat16 [256, 256], replicated, may hold values from -0.375 to 0.375
- w_value: bfloat16 [256, 256], replicated, may hold values from -0.375 to 0.375
- tower_in: bfloat16 [512, 1024], replicated, may hold values from -0.25 to 0.25
- tower_out: bfloat16 [1024], replicated, may hold values from -0.1875 to 0.1875
Outputs:
- logits: float32 [4, 2048], P('req', 'cand')
Inputs may be any that keep to these rules, and one draw needn't show every extreme that they name: `history_shard`: among the 128 events of one request that one device holds, at most 128 name the same table shard, a bound that some block reaches. `candidate_shard`: among the 256 candidates of one request that one device holds, at most 192 name the same table shard, a bound that some block reaches. `history_length`: some request has all 1024 events live.
All inputs are finite; a program needn't handle non-finite values.
Results may differ from a plain program's by a relative error of at most 0.004.
Values may be sent and summed in bfloat16 or wider, within the bound.
No kernel may reach another device: no remote copies, remote signals or barrier semaphores. Data moves between devices by JAX's collectives and lax.ppermute only.
A program may use at most 64 MiB of HBM per device.

v0:
```python
import math

import jax
import jax.numpy as jnp
from jax import lax
from jax.sharding import PartitionSpec as P

HEADS = 4


def slot_index(shard_ids, n_dest, slot_count, first_slot):
    onehot = (shard_ids[:, None] == jnp.arange(n_dest, dtype=jnp.int32)[None, :]).astype(jnp.int32)
    before = jnp.cumsum(onehot, axis=0) - onehot
    rank = jnp.sum(before * onehot, axis=1)
    return shard_ids * slot_count + first_slot + rank


def body(
    table,
    history_shard,
    history_row,
    candidate_shard,
    candidate_row,
    history_length,
    w_query,
    w_key,
    w_value,
    tower_in,
    tower_out,
):
    n_dest = lax.axis_size("req")
    d_model = table.shape[1]
    hist_shards = history_shard[0, :, 0]
    cand_shards = candidate_shard[0, :, 0]
    hist_dev = hist_shards.shape[0]
    cand_dev = cand_shards.shape[0]
    hist_cap = 4 * hist_dev // n_dest
    cand_cap = 3 * cand_dev // n_dest
    slot_count = hist_cap + cand_cap
    hist_slot = slot_index(hist_shards, n_dest, slot_count, 0)
    cand_slot = slot_index(cand_shards, n_dest, slot_count, hist_cap)
    wanted = jnp.zeros((n_dest * slot_count,), jnp.int32)
    wanted = wanted.at[hist_slot].set(history_row[0]).at[cand_slot].set(candidate_row[0])
    wanted = wanted.reshape(n_dest, slot_count)
    fetched = jnp.take(
        table, lax.all_to_all(wanted, "req", split_axis=0, concat_axis=0, tiled=True), axis=0
    )
    replies = lax.all_to_all(fetched, "req", split_axis=0, concat_axis=0, tiled=True)
    flat_rows = replies.reshape(n_dest * slot_count, d_model)
    hist_emb = jnp.take(flat_rows, hist_slot, axis=0)
    cand_emb = jnp.take(flat_rows, cand_slot, axis=0)
    head_size = d_model // HEADS
    scale_factor = 1.0 / math.sqrt(head_size)
    length = history_length[0]
    w_pair = jnp.concatenate([w_key, w_value], axis=1)
    query_row_matrix = jnp.dot(cand_emb, w_query, preferred_element_type=jnp.float32).astype(
        jnp.bfloat16
    )
    query_row_matrix = query_row_matrix.reshape(cand_dev, HEADS, head_size)
    pair_local = jnp.dot(hist_emb, w_pair, preferred_element_type=jnp.float32).astype(jnp.bfloat16)
    pair_rows = lax.all_gather(pair_local, "cand", axis=0, tiled=True)
    count = pair_rows.shape[0]
    key_portion_slice = pair_rows[:, :d_model].reshape(count, HEADS, head_size)
    value_portion_slice = pair_rows[:, d_model:].reshape(count, HEADS, head_size)
    score_matrix = (
        jnp.einsum(
            "zun,aun->zua", query_row_matrix, key_portion_slice, preferred_element_type=jnp.float32
        )
        * scale_factor
    )
    live_mask = jnp.arange(count, dtype=jnp.int32) < length
    gate_weights = jnp.where(
        live_mask[None, None, :], jax.nn.sigmoid(score_matrix), jnp.float32(0.0)
    ).astype(jnp.bfloat16)
    weighted_sum = jnp.einsum(
        "bgo,ogl->bgl", gate_weights, value_portion_slice, preferred_element_type=jnp.float32
    )
    attended = (
        (weighted_sum / jnp.sqrt(length.astype(jnp.float32)))
        .reshape(cand_dev, d_model)
        .astype(jnp.bfloat16)
    )
    pre_act = jnp.dot(cand_emb, tower_in[:d_model], preferred_element_type=jnp.float32) + jnp.dot(
        attended, tower_in[d_model:], preferred_element_type=jnp.float32
    )
    hidden = jax.nn.silu(pre_act).astype(jnp.bfloat16)
    return jnp.dot(hidden, tower_out, preferred_element_type=jnp.float32)[None, :]


def solution(mesh):
    placed = (
        P("req", None),
        P("req", "cand", None),
        P("req", "cand"),
        P("req", "cand", None),
        P("req", "cand"),
        P("req"),
        P(),
        P(),
        P(),
        P(),
        P(),
    )
    return jax.shard_map(
        body, mesh=mesh, in_specs=placed, out_specs=P("req", "cand"), check_vma=False
    )
```

profile of v0, /device:TPU:0, one launch (start us, length us, event | category | flops | bytes accessed | tf_op | source)
XLA Modules:
  0.0 80.8 jit_solution(6493712422928214452)
XLA Ops:
  6.5 0.7 compare_convert_fusion
  7.3 1.2 %reduce-window.6 = s32[4,2,128]{2,1,0:T(2,128)S(1)} reduce-window(s32[4,2,128]{2,1,0:T(2,128)S(1)} %compare_convert_fusion, s32[]{:T(128)} %constant.41.clone.1), window={size=1x1x128 pad=0_0x0_0x127_0}, to_apply=%region_0.0 | reduce-window | flops 130048 | bytes 8196 | tf_op jit(solution)/shard_map/reduce-window
  8.5 0.1 slice.30
  8.5 0.1 copy.19
  8.7 0.1 copy.20
  8.8 0.1 add_bitcast_fusion
  8.9 0.7 fusion.24
  9.6 0.7 compare_select_fusion.2
  10.2 0.7 fusion.18
  11.0 0.2 reduce_window_sum.28
  11.2 0.8 %select_reduce_fusion = s32[128]{0:T(128)S(1)} fusion(s32[128,4]{1,0:T(8,128)S(1)} %reduce_window_sum.28, s32[128]{0:T(128)} %bitcast.86), kind=kLoop, calls=%fused_computation.25 | loop fusion | flops 2432 | bytes 3072 | tf_op jit(solution)/shard_map/reduce_sum | solution.py:14
  12.0 0.7 fusion.27
  12.7 1.1 %scatter_custom_fusion = s32[1280]{0:T(1024)S(1)} fusion(s32[128]{0:T(128)S(1)} %fusion.27, s32[128]{0:T(128)} %bitcast.88, s32[]{:T(128)} %constant.41.clone.1), kind=kCustom, calls=%fused_computation.44 | custom fusion | bytes 5632 | tf_op jit(solution)/shard_map/scatter | solution.py:43
  13.8 1.6 %scatter_fusion = s32[1280]{0:T(1024)S(1)} fusion(s32[1280]{0:T(1024)S(1)} %scatter_custom_fusion, s32[256]{0:T(256)S(1)} %bitcast.81, s32[256]{0:T(256)} %bitcast.87), kind=kCustom, calls=%fused_computation.4 | custom fusion | bytes 4096 | tf_op jit(solution)/shard_map/scatter | solution.py:43
  15.4 0.1 all_to_all.13
  15.4 9.6 %all_to_all.20 = s32[4,1,320]{2,1,0:T(1,128)S(1)} all-to-all(s32[4,1,320]{2,1,0:T(1,128)S(1)} %all_to_all.13), channel_id=1, replica_groups=mesh['req'=4,'cand'=8] {'req'}, dimensions={0} | all-to-all | bytes 10240 | tf_op jit(solution)/shard_map/all_to_all | solution.py:46
  25.1 0.1 reshape.156
  25.3 5.9 %gather_fusion = bf16[1280,256]{1,0:T(8,128)(2,1)S(1)} fusion(bf16[8192,256]{1,0:T(8,128)(2,1)} %param.11, s32[2048]{0:T(1024)S(1)} %pad_clamp_fusion), kind=kCustom, calls=%fused_computation | custom fusion | bytes 1315840 | tf_op jit(solution)/shard_map/jit(_take)/gather | solution.py:45
  31.2 1.1 %broadcast_select_fusion = bf16[4,320,256]{2,1,0:T(8,128)(2,1)} fusion(bf16[4,320,256]{2,1,0:T(8,128)(2,1)S(1)} %bitcast.74, pred[4,320]{1,0:T(4,128)(4,1)S(1)} %compare_and_fusion), kind=kLoop, calls=%fused_computation.15 | loop fusion | flops 327680 | bytes 1312000 | tf_op jit(solution)/shard_map/jit(_take)/select_n | solution.py:45
  32.3 3.5 %all-to-all-start.1 = ((bf16[4,320,256]{2,1,0:T(8,128)(2,1)}), bf16[4,320,256]{2,1,0:T(8,128)(2,1)S(1)}, u32[]{:S(2)}, u32[]{:S(2)}) async-start(bf16[4,320,256]{2,1,0:T(8,128)(2,1)} %broadcast_select_fusion), calls=%async_computation.1 | async-start | bytes 1310720 | tf_op jit(solution)/shard_map/all_to_all | solution.py:48
  35.9 8.1 %all-to-all-done.1 = bf16[4,320,256]{2,1,0:T(8,128)(2,1)S(1)} async-done(((bf16[4,320,256]{2,1,0:T(8,128)(2,1)}), bf16[4,320,256]{2,1,0:T(8,128)(2,1)S(1)}, u32[]{:S(2)}, u32[]{:S(2)}) %all-to-all-start.1) | async-done | bytes 655392 | tf_op jit(solution)/shard_map/all_to_all | solution.py:48
  44.0 0.8 %gather_fusion.2 = bf16[128,256]{1,0:T(8,128)(2,1)S(1)} fusion(bf16[1280,256]{1,0:T(8,128)(2,1)S(1)} %bitcast.72, s32[1024]{0:T(1024)S(1)} %pad_clamp_fusion.1), kind=kCustom, calls=%fused_computation.2 | custom fusion | bytes 131584 | tf_op jit(solution)/shard_map/jit(_take)/gather | solution.py:50
  44.9 0.9 %convolution_convert_fusion.1 = bf16[128,512]{1,0:T(8,128)(2,1)} fusion(bf16[256,256]{1,0:T(8,128)(2,1)S(1)} %copy-done.5, bf16[256,256]{1,0:T(8,128)(2,1)S(1)} %copy-done.6, bf16[128,256]{1,0:T(8,128)(2,1)S(1)} %gather_fusion.2, pred[128]{0:T(512)(128)(4,1)S(1)} %compare_and_fusion.1), kind=kOutput, calls=%fused_computation.10 | convolution fusion | flops 34177024 | bytes 458880 | tf_op jit(solution)/shard_map/dot_general | solution.py:60
  46.6 1.2 %gather_fusion.1 = bf16[256,256]{1,0:T(8,128)(2,1)S(1)} fusion(bf16[1280,256]{1,0:T(8,128)(2,1)S(1)} %bitcast.73, s32[1024]{0:T(1024)S(1)} %pad_clamp_fusion.2), kind=kCustom, calls=%fused_computation.1 | custom fusion | bytes 263168 | tf_op jit(solution)/shard_map/jit(_take)/gather | solution.py:51
  47.7 0.3 convolution_convert_fusion
  48.1 0.3 fusion.12
  48.4 19.9 %all-gather.2.cloned.1.call-done = bf16[1024,512]{1,0:T(8,128)(2,1)} async-done(((bf16[128,512]{1,0:T(8,128)(2,1)}), bf16[1024,512]{1,0:T(8,128)(2,1)}) %all-gather.2.cloned.1.call-update) | async-done | bytes 1048592 | tf_op jit(solution)/shard_map/all_gather | solution.py:61
  68.3 1.3 %fusion.36 = (bf16[1024,256]{1,0:T(8,128)(2,1)S(1)}, bf16[1024,256]{1,0:T(8,128)(2,1)S(1)}) fusion(bf16[1024,512]{1,0:T(8,128)(2,1)} %all-gather.2.cloned.1.call-done), kind=kLoop, calls=%fused_computation.64 | loop fusion | bytes 2097152 | tf_op jit(solution)/shard_map/slice | solution.py:63
  69.6 0.2 copy.22
  69.8 0.2 copy.21
  70.0 1.6 %fusion.5 = bf16[4,64,256]{2,1,0:T(8,128)(2,1)S(1)} fusion(bf16[1024,4,64]{0,2,1:T(8,128)(2,1)S(1)} %bitcast.76, bf16[1024,4,64]{0,2,1:T(8,128)(2,1)S(1)} %bitcast.75, bf16[256,4,64]{0,2,1:T(8,128)(2,1)S(1)} %bitcast.77, pred[1024]{0:T(1024)(128)(4,1)S(1)} %iota_compare_fusion.1, f32[]{:T(128)S(6)} %sqrt.3), kind=kOutput, calls=%fused_computation.12 | convolution fusion | flops 274857984 | bytes 1311748 | tf_op jit(solution)/shard_map/bgo,ogl->bgl/dot_general | solution.py:75
  71.6 2.3 %fusion.8 = f32[1,256]{1,0:T(1,128)} fusion(bf16[1024,1]{0,1:T(2,128)(2,1)S(1)} %reshape.195, f32[256,1024]{1,0:T(8,128)S(1)} %fusion.12, bf16[256,256]{0,1:T(8,128)(2,1)S(1)} %bitcast.89, bf16[512,1024]{1,0:T(8,128)(2,1)} %param.20), kind=kOutput, calls=%fused_computation.14 | convolution fusion | flops 136314880 | bytes 1707008 | tf_op jit(solution)/shard_map/dot_general | solution.py:87
  (27 shorter events, 0.2 us)
Async XLA Ops:
  6.5 41.2 %copy-start = (bf16[256,256]{1,0:T(8,128)(2,1)S(1)}, bf16[256,256]{1,0:T(8,128)(2,1)}, u32[]{:S(2)}) copy-start(bf16[256,256]{1,0:T(8,128)(2,1)} %param.17) | copy-start | bytes 393220
  25.2 10.7 %copy-start.3 = (s32[1,128,1]{1,2,0:T(1,128)S(1)}, s32[1,128,1]{1,2,0:T(1,128)}, u32[]{:S(2)}) copy-start(s32[1,128,1]{1,2,0:T(1,128)} %param.12) | copy-start | bytes 1540
  25.2 19.7 %copy-start.5 = (bf16[256,256]{1,0:T(8,128)(2,1)S(1)}, bf16[256,256]{1,0:T(8,128)(2,1)}, u32[]{:S(2)}) copy-start(bf16[256,256]{1,0:T(8,128)(2,1)} %param.19) | copy-start | bytes 393220
  25.2 19.7 %copy-start.6 = (bf16[256,256]{1,0:T(8,128)(2,1)S(1)}, bf16[256,256]{1,0:T(8,128)(2,1)}, u32[]{:S(2)}) copy-start(bf16[256,256]{1,0:T(8,128)(2,1)} %param.18) | copy-start | bytes 393220
  25.2 21.3 %copy-start.4 = (bf16[1024]{0:T(1024)(128)(2,1)S(1)}, bf16[1024]{0:T(1024)(128)(2,1)}, u32[]{:S(2)}) copy-start(bf16[1024]{0:T(1024)(128)(2,1)} %param.21) | copy-start | bytes 6148
  25.2 21.3 %copy-start.2 = (s32[1,256,1]{1,2,0:T(1,128)S(1)}, s32[1,256,1]{1,2,0:T(1,128)}, u32[]{:S(2)}) copy-start(s32[1,256,1]{1,2,0:T(1,128)} %param.14) | copy-start | bytes 3076
  31.2 16.8 %copy-start.1 = (bf16[512,1024]{1,0:T(8,128)(2,1)S(1)}, bf16[512,1024]{1,0:T(8,128)(2,1)}, u32[]{:S(2)}) copy-start(bf16[512,1024]{1,0:T(8,128)(2,1)} %param.20) | copy-start | bytes 3145732
  32.3 11.7 %all-to-all-start.1 = ((bf16[4,320,256]{2,1,0:T(8,128)(2,1)}), bf16[4,320,256]{2,1,0:T(8,128)(2,1)S(1)}, u32[]{:S(2)}, u32[]{:S(2)}) async-start(bf16[4,320,256]{2,1,0:T(8,128)(2,1)} %broadcast_select_fusion), calls=%async_computation.1 | async-start | bytes 1310720 | tf_op jit(solution)/shard_map/all_to_all | solution.py:48
  35.8 32.5 %all-gather.2.cloned.1.call-start = ((), (), s32[]{:S(2)}) async-start(), calls=%async_computation.2 | async-start | bytes 1179648 | tf_op jit(solution)/shard_map/all_gather | solution.py:61
Sparse Core Ops, SparseCore 0:
  45.9 22.3 all-gather.1
where the time goes:
time: 81.1 us; the launch traced here: 80.8 us
  waiting for transfers between devices  28.1 us (35%)
  between operations  14.3 us (18%)
  local copies, waits for them, and re-layouts  12.8 us (16%)
  blocking collectives  9.64 us (12%)
  other arithmetic  6.98 us (9%)
  matrix products  5.39 us (7%)
  starting transfers between devices  3.52 us (4%)
    all_gather x1, waiting for transfers between devices, body(): pair_rows = lax.all_gather(pair_local, 'cand', axis=0, tiled=True)  19.9 us
    all_to_all x1, blocking collectives, body(): lax.all_to_all(wanted, 'req', split_axis=0, concat_axis=0, tiled=True)  9.64 us
    all_to_all x1, waiting for transfers between devices, body(): lax.all_to_all(fetched, 'req', split_axis=0, concat_axis=0, tiled=True)  8.15 us
    gather x1, local copies, waits for them, and re-layouts, body(): jnp.take(table, lax.all_to_all(wanted, 'req', split_axis=0, concat_axis=0...  5.95 us
    all_to_all x1, starting transfers between devices, body(): lax.all_to_all(fetched, 'req', split_axis=0, concat_axis=0, tiled=True)  3.48 us
    scatter x2, local copies, waits for them, and re-layouts, body(): wanted.at[hist_slot].set(history_row[0]).at[cand_slot].set(candidate_row[0])  2.7 us
    dot_general x1, matrix products, body(): jnp.dot(hidden, tower_out, preferred_element_type=jnp.float32)[None, :]  2.27 us
  transfers between devices with their start and end apart: 2, of which 2 were waited for; matrix products, arithmetic and copies ran while one was open for 2% of the time, Pallas kernels for 0%

commit v1 on v0

--- a/solution.py
+++ b/solution.py
@@ -57,8 +57,8 @@
         jnp.bfloat16
     )
     query_row_matrix = query_row_matrix.reshape(cand_dev, HEADS, head_size)
-    pair_local = jnp.dot(hist_emb, w_pair, preferred_element_type=jnp.float32).astype(jnp.bfloat16)
-    pair_rows = lax.all_gather(pair_local, "cand", axis=0, tiled=True)
+    hist_all = lax.all_gather(hist_emb, "cand", axis=0, tiled=True)
+    pair_rows = jnp.dot(hist_all, w_pair, preferred_element_type=jnp.float32).astype(jnp.bfloat16)
     count = pair_rows.shape[0]
     key_portion_slice = pair_rows[:, :d_model].reshape(count, HEADS, head_size)
     value_portion_slice = pair_rows[:, d_model:].reshape(count, HEADS, head_size)

time: 81.1 us -> 60.3 us (0.74)
  waiting for transfers between devices: 28.1 us -> 12.1 us
  between operations: 14.3 us -> 0.9 us
  blocking collectives: 9.64 us -> 15.4 us
  starting transfers between devices: 3.52 us -> 8.78 us
  matrix products: 5.39 us -> 3.94 us
  local copies, waits for them, and re-layouts: 12.8 us -> 11.8 us
    all_gather x1 -> x0, waiting for transfers between devices: 19.9 us -> none  [body(): pair_rows = lax.all_gather(pair_local, 'cand', axis=0, tiled=True)]
    all_gather x0 -> x1, blocking collectives: none -> 15.4 us  [body(): hist_all = lax.all_gather(hist_emb, 'cand', axis=0, tiled=True)]
    all_to_all x1 -> x0, blocking collectives: 9.64 us -> none  [body(): lax.all_to_all(wanted, 'req', split_axis=0, concat_axis=0, tiled=True)]
    all_to_all x0 -> x1, starting transfers between devices: none -> 5.16 us  [body(): lax.all_to_all(wanted, 'req', split_axis=0, concat_axis=0, tiled=True)]
    all_to_all x0 -> x1, waiting for transfers between devices: none -> 4.02 us  [body(): lax.all_to_all(wanted, 'req', split_axis=0, concat_axis=0, tiled=True)]
    slice x2 -> x1, local copies, waits for them, and re-layouts: 1.47 us -> 0.07 us  [body(): key_portion_slice = pair_rows[:, :d_model].reshape(count, HEADS, head_size)]
    dot_general x1, matrix products: 2.27 us -> 1.23 us  [body(): jnp.dot(hidden, tower_out, preferred_element_type=jnp.float32)[None, :]]
  transfers between devices with their start and end apart: 2 -> 2, of which waited for: 2 -> 2; matrix products, arithmetic and copies ran while one was open for 2% -> 0% of each run, Pallas kernels for 0% -> 0%
where the time goes in v1:
time: 60.3 us; the launch traced here: 60 us
  blocking collectives  15.4 us (26%)
  waiting for transfers between devices  12.1 us (20%)
  local copies, waits for them, and re-layouts  11.8 us (20%)
  starting transfers between devices  8.78 us (15%)
  other arithmetic  7.07 us (12%)
  matrix products  3.94 us (7%)
  between operations  0.9 us (1%)
    all_gather x1, blocking collectives, body(): hist_all = lax.all_gather(hist_emb, 'cand', axis=0, tiled=True)  15.4 us
    all_to_all x1, waiting for transfers between devices, body(): lax.all_to_all(fetched, 'req', split_axis=0, concat_axis=0, tiled=True)  8.1 us
    gather x1, local copies, waits for them, and re-layouts, body(): jnp.take(table, lax.all_to_all(wanted, 'req', split_axis=0, concat_axis=0...  5.92 us
    all_to_all x1, starting transfers between devices, body(): lax.all_to_all(wanted, 'req', split_axis=0, concat_axis=0, tiled=True)  5.16 us
    all_to_all x1, waiting for transfers between devices, body(): lax.all_to_all(wanted, 'req', split_axis=0, concat_axis=0, tiled=True)  4.02 us
    all_to_all x1, starting transfers between devices, body(): lax.all_to_all(fetched, 'req', split_axis=0, concat_axis=0, tiled=True)  3.61 us
    scatter x2, local copies, waits for them, and re-layouts, body(): wanted.at[hist_slot].set(history_row[0]).at[cand_slot].set(candidate_row[0])  2.7 us
    dot_general x1, matrix products, body(): jnp.einsum('bgo,ogl->bgl', gate_weights, value_portion_slice, preferred_e...  1.6 us
  transfers between devices with their start and end apart: 2, of which 2 were waited for; matrix products, arithmetic and copies ran while one was open for 0% of the time, Pallas kernels for 0%

profile of v1, /device:TPU:0, one launch (start us, length us, event | category | flops | bytes accessed | tf_op | source)
XLA Modules:
  0.0 60.0 jit_solution(1121352162373728478)
XLA Ops:
  0.0 0.7 %compare_convert_fusion = s32[4,2,128]{2,1,0:T(2,128)S(1)} fusion(s32[2,128]{1,0:T(2,128)} %bitcast.77), kind=kLoop, calls=%fused_computation.31 | loop fusion | flops 2048 | bytes 5120 | tf_op jit(solution)/shard_map/convert_element_type | solution.py:12
  0.7 1.2 %reduce-window.6 = s32[4,2,128]{2,1,0:T(2,128)S(1)} reduce-window(s32[4,2,128]{2,1,0:T(2,128)S(1)} %compare_convert_fusion, s32[]{:T(128)} %constant.41.clone.1), window={size=1x1x128 pad=0_0x0_0x127_0}, to_apply=%region_0.0 | reduce-window | flops 130048 | bytes 8196 | tf_op jit(solution)/shard_map/reduce-window
  1.9 0.1 slice.30
  2.0 0.1 copy.16
  2.1 0.1 copy.17
  2.2 0.1 add_bitcast_fusion
  2.3 0.7 %fusion.21 = s32[256]{0:T(256)S(1)} fusion(s32[1,4,2,128]{3,2,1,0:T(2,128)S(1)} %add_bitcast_fusion, s32[256]{0:T(256)} %bitcast.78), kind=kLoop, calls=%fused_computation.38 | loop fusion | flops 4864 | bytes 6144 | tf_op jit(solution)/shard_map/reduce_sum | solution.py:14
  3.0 0.7 %compare_select_fusion.2 = s32[256,1]{0,1:T(1,128)S(1)} fusion(s32[256,1]{0,1:T(1,128)S(1)} %bitcast.82, s32[1,256,1]{1,2,0:T(1,128)} %param.14), kind=kLoop, calls=%fused_computation.34 | loop fusion | flops 1536 | bytes 3072 | tf_op jit(solution)/shard_map/jit(_take)/jit(_where)/select_n | solution.py:51
  3.7 0.7 %fusion.17 = s32[128,4]{1,0:T(8,128)S(1)} fusion(s32[128]{0:T(128)} %bitcast.84), kind=kLoop, calls=%fused_computation.26 | loop fusion | flops 1024 | bytes 2560 | tf_op jit(solution)/shard_map/convert_element_type | solution.py:12
  4.4 0.2 reduce_window_sum.28
  4.6 0.8 %select_reduce_fusion = s32[128]{0:T(128)S(1)} fusion(s32[128,4]{1,0:T(8,128)S(1)} %reduce_window_sum.28, s32[128]{0:T(128)} %bitcast.85), kind=kLoop, calls=%fused_computation.24 | loop fusion | flops 2432 | bytes 3072 | tf_op jit(solution)/shard_map/reduce_sum | solution.py:14
  5.5 0.7 %fusion.24 = s32[128]{0:T(128)S(1)} fusion(s32[128]{0:T(128)S(1)} %select_reduce_fusion, s32[1,128,1]{1,2,0:T(1,128)} %param.12), kind=kLoop, calls=%fused_computation.52 | loop fusion | flops 640 | bytes 1536 | tf_op jit(solution)/shard_map/select_n | solution.py:43
  6.1 1.1 %scatter_custom_fusion = s32[1280]{0:T(1024)S(1)} fusion(s32[128]{0:T(128)S(1)} %fusion.24, s32[128]{0:T(128)} %bitcast.87, s32[]{:T(128)} %constant.41.clone.1), kind=kCustom, calls=%fused_computation.42 | custom fusion | bytes 5632 | tf_op jit(solution)/shard_map/scatter | solution.py:43
  7.2 1.6 %scatter_fusion = s32[1280]{0:T(1024)S(1)} fusion(s32[1280]{0:T(1024)S(1)} %scatter_custom_fusion, s32[256]{0:T(256)S(1)} %bitcast.80, s32[256]{0:T(256)} %bitcast.86), kind=kCustom, calls=%fused_computation.4 | custom fusion | bytes 4096 | tf_op jit(solution)/shard_map/scatter | solution.py:43
  8.8 0.7 %all_to_all.13 = s32[4,1,320]{2,1,0:T(1,128)} reshape(s32[1280]{0:T(1024)S(1)} %scatter_fusion) | data formatting | bytes 10240 | tf_op jit(solution)/shard_map/all_to_all | solution.py:46
  9.5 5.2 %all-to-all-start = ((s32[4,1,320]{2,1,0:T(1,128)}), s32[4,1,320]{2,1,0:T(1,128)S(1)}, u32[]{:S(2)}, u32[]{:S(2)}) async-start(s32[4,1,320]{2,1,0:T(1,128)} %all_to_all.13), calls=%async_computation | async-start | bytes 12288 | tf_op jit(solution)/shard_map/all_to_all | solution.py:46
  15.3 4.0 %all-to-all-done = s32[4,1,320]{2,1,0:T(1,128)S(1)} async-done(((s32[4,1,320]{2,1,0:T(1,128)}), s32[4,1,320]{2,1,0:T(1,128)S(1)}, u32[]{:S(2)}, u32[]{:S(2)}) %all-to-all-start) | async-done | bytes 5152 | tf_op jit(solution)/shard_map/all_to_all | solution.py:46
  19.4 0.1 reshape.156
  19.5 5.9 %gather_fusion = bf16[1280,256]{1,0:T(8,128)(2,1)S(1)} fusion(bf16[8192,256]{1,0:T(8,128)(2,1)} %param.11, s32[2048]{0:T(1024)S(1)} %pad_clamp_fusion), kind=kCustom, calls=%fused_computation | custom fusion | bytes 1315840 | tf_op jit(solution)/shard_map/jit(_take)/gather | solution.py:45
  25.5 1.1 %broadcast_select_fusion = bf16[4,320,256]{2,1,0:T(8,128)(2,1)} fusion(bf16[4,320,256]{2,1,0:T(8,128)(2,1)S(1)} %bitcast.73, pred[4,320]{1,0:T(4,128)(4,1)S(1)} %compare_and_fusion), kind=kLoop, calls=%fused_computation.15 | loop fusion | flops 327680 | bytes 1312000 | tf_op jit(solution)/shard_map/jit(_take)/select_n | solution.py:45
  26.6 3.6 %all-to-all-start.1 = ((bf16[4,320,256]{2,1,0:T(8,128)(2,1)}), bf16[4,320,256]{2,1,0:T(8,128)(2,1)S(1)}, u32[]{:S(2)}, u32[]{:S(2)}) async-start(bf16[4,320,256]{2,1,0:T(8,128)(2,1)} %broadcast_select_fusion), calls=%async_computation.1 | async-start | bytes 1310720 | tf_op jit(solution)/shard_map/all_to_all | solution.py:48
  30.3 8.1 %all-to-all-done.1 = bf16[4,320,256]{2,1,0:T(8,128)(2,1)S(1)} async-done(((bf16[4,320,256]{2,1,0:T(8,128)(2,1)}), bf16[4,320,256]{2,1,0:T(8,128)(2,1)S(1)}, u32[]{:S(2)}, u32[]{:S(2)}) %all-to-all-start.1) | async-done | bytes 655392 | tf_op jit(solution)/shard_map/all_to_all | solution.py:48
  38.4 1.2 %gather_fusion.1 = bf16[256,256]{1,0:T(8,128)(2,1)S(1)} fusion(bf16[1280,256]{1,0:T(8,128)(2,1)S(1)} %bitcast.71, s32[1024]{0:T(1024)S(1)} %pad_clamp_fusion.2), kind=kCustom, calls=%fused_computation.1 | custom fusion | bytes 263168 | tf_op jit(solution)/shard_map/jit(_take)/gather | solution.py:51
  39.6 0.8 %gather_fusion.2 = bf16[128,256]{1,0:T(8,128)(2,1)S(1)} fusion(bf16[1280,256]{1,0:T(8,128)(2,1)S(1)} %bitcast.72, s32[1024]{0:T(1024)S(1)} %pad_clamp_fusion.1), kind=kCustom, calls=%fused_computation.2 | custom fusion | bytes 131584 | tf_op jit(solution)/shard_map/jit(_take)/gather | solution.py:50
  40.4 0.1 broadcast_select_fusion.2
  40.5 15.4 %all_gather.3 = bf16[1024,256]{1,0:T(8,128)(2,1)S(1)} all-gather(bf16[128,256]{1,0:T(8,128)(2,1)S(1)} %broadcast_select_fusion.2), channel_id=1, replica_groups=mesh['req'=4,'cand'=8] {'cand'}, dimensions={0}, use_global_device_ids=true | all-gather | bytes 589824 | tf_op jit(solution)/shard_map/all_gather | solution.py:60
  55.9 0.5 convolution_convert_fusion
  56.4 0.1 fusion.32
  56.5 0.3 convolution_convert_fusion.1
  56.8 0.3 fusion.12
  57.2 1.6 %fusion.5 = bf16[4,64,256]{2,1,0:T(8,128)(2,1)S(1)} fusion(bf16[1024,4,64]{0,2,1:T(8,128)(2,1)S(1)} %bitcast.75, bf16[1024,4,64]{0,2,1:T(8,128)(2,1)S(1)} %bitcast.74, bf16[256,4,64]{0,2,1:T(8,128)(2,1)S(1)} %bitcast.76, pred[1024]{0:T(1024)(128)(4,1)S(1)} %iota_compare_fusion.1, f32[]{:T(128)S(6)} %sqrt.3), kind=kOutput, calls=%fused_computation.12 | convolution fusion | flops 274857984 | bytes 1311748 | tf_op jit(solution)/shard_map/bgo,ogl->bgl/dot_general | solution.py:75
  58.8 1.2 %fusion.8 = f32[1,256]{1,0:T(1,128)} fusion(bf16[1024,1]{0,1:T(2,128)(2,1)S(1)} %reshape.195, f32[256,1024]{1,0:T(8,128)S(1)} %fusion.12, bf16[256,256]{0,1:T(8,128)(2,1)S(1)} %bitcast.88, bf16[512,1024]{1,0:T(8,128)(2,1)S(1)} %copy-done.1), kind=kOutput, calls=%fused_computation.14 | convolution fusion | flops 136314880 | bytes 1709056 | tf_op jit(solution)/shard_map/dot_general | solution.py:87
  (25 shorter events, 0.2 us)
Async XLA Ops:
  0.0 56.5 %copy-start = (bf16[256,256]{1,0:T(8,128)(2,1)S(1)}, bf16[256,256]{1,0:T(8,128)(2,1)}, u32[]{:S(2)}) copy-start(bf16[256,256]{1,0:T(8,128)(2,1)} %param.17) | copy-start | bytes 393220
  9.5 9.8 %all-to-all-start = ((s32[4,1,320]{2,1,0:T(1,128)}), s32[4,1,320]{2,1,0:T(1,128)S(1)}, u32[]{:S(2)}, u32[]{:S(2)}) async-start(s32[4,1,320]{2,1,0:T(1,128)} %all_to_all.13), calls=%async_computation | async-start | bytes 12288 | tf_op jit(solution)/shard_map/all_to_all | solution.py:46
  19.5 10.8 %copy-start.6 = (bf16[1024]{0:T(1024)(128)(2,1)S(1)}, bf16[1024]{0:T(1024)(128)(2,1)}, u32[]{:S(2)}) copy-start(bf16[1024]{0:T(1024)(128)(2,1)} %param.21) | copy-start | bytes 6148
  19.5 10.8 %copy-start.5 = (s32[1,128,1]{1,2,0:T(1,128)S(1)}, s32[1,128,1]{1,2,0:T(1,128)}, u32[]{:S(2)}) copy-start(s32[1,128,1]{1,2,0:T(1,128)} %param.12) | copy-start | bytes 1540
  19.5 10.8 %copy-start.4 = (s32[1,256,1]{1,2,0:T(1,128)S(1)}, s32[1,256,1]{1,2,0:T(1,128)}, u32[]{:S(2)}) copy-start(s32[1,256,1]{1,2,0:T(1,128)} %param.14) | copy-start | bytes 3076
  19.5 36.4 %copy-start.2 = (bf16[256,256]{1,0:T(8,128)(2,1)S(1)}, bf16[256,256]{1,0:T(8,128)(2,1)}, u32[]{:S(2)}) copy-start(bf16[256,256]{1,0:T(8,128)(2,1)} %param.19) | copy-start | bytes 393220
  19.5 36.4 %copy-start.3 = (bf16[256,256]{1,0:T(8,128)(2,1)S(1)}, bf16[256,256]{1,0:T(8,128)(2,1)}, u32[]{:S(2)}) copy-start(bf16[256,256]{1,0:T(8,128)(2,1)} %param.18) | copy-start | bytes 393220
  26.5 30.3 %copy-start.1 = (bf16[512,1024]{1,0:T(8,128)(2,1)S(1)}, bf16[512,1024]{1,0:T(8,128)(2,1)}, u32[]{:S(2)}) copy-start(bf16[512,1024]{1,0:T(8,128)(2,1)} %param.20) | copy-start | bytes 3145732
  26.6 11.9 %all-to-all-start.1 = ((bf16[4,320,256]{2,1,0:T(8,128)(2,1)}), bf16[4,320,256]{2,1,0:T(8,128)(2,1)S(1)}, u32[]{:S(2)}, u32[]{:S(2)}) async-start(bf16[4,320,256]{2,1,0:T(8,128)(2,1)} %broadcast_select_fusion), calls=%async_computation.1 | async-start | bytes 1310720 | tf_op jit(solution)/shard_map/all_to_all | solution.py:48

commit v2 on v1

--- a/solution.py
+++ b/solution.py
@@ -9,10 +9,20 @@
 
 
 def slot_index(shard_ids, n_dest, slot_count, first_slot):
-    onehot = (shard_ids[:, None] == jnp.arange(n_dest, dtype=jnp.int32)[None, :]).astype(jnp.int32)
-    before = jnp.cumsum(onehot, axis=0) - onehot
-    rank = jnp.sum(before * onehot, axis=1)
+    count = shard_ids.shape[0]
+    onehot = (shard_ids[:, None] == jnp.arange(n_dest, dtype=jnp.int32)[None, :]).astype(jnp.bfloat16)
+    earlier = lax.broadcasted_iota(jnp.int32, (count, count), 1) < lax.broadcasted_iota(
+        jnp.int32, (count, count), 0
+    )
+    before = jnp.dot(earlier.astype(jnp.bfloat16), onehot, preferred_element_type=jnp.float32)
+    rank = jnp.sum(before * onehot.astype(jnp.float32), axis=1).astype(jnp.int32)
     return shard_ids * slot_count + first_slot + rank
+
+
+def select_rows(slots, n_slots):
+    return (slots[:, None] == lax.broadcasted_iota(jnp.int32, (slots.shape[0], n_slots), 1)).astype(
+        jnp.bfloat16
+    )
 
 
 def body(
@@ -37,18 +47,26 @@
     hist_cap = 4 * hist_dev // n_dest
     cand_cap = 3 * cand_dev // n_dest
     slot_count = hist_cap + cand_cap
+    n_slots = n_dest * slot_count
     hist_slot = slot_index(hist_shards, n_dest, slot_count, 0)
     cand_slot = slot_index(cand_shards, n_dest, slot_count, hist_cap)
-    wanted = jnp.zeros((n_dest * slot_count,), jnp.int32)
-    wanted = wanted.at[hist_slot].set(history_row[0]).at[cand_slot].set(candidate_row[0])
-    wanted = wanted.reshape(n_dest, slot_count)
-    fetched = jnp.take(
-        table, lax.all_to_all(wanted, "req", split_axis=0, concat_axis=0, tiled=True), axis=0
+    hist_pick = select_rows(hist_slot, n_slots)
+    cand_pick = select_rows(cand_slot, n_slots)
+    all_pick = jnp.concatenate([hist_pick, cand_pick], axis=0)
+    all_rows = jnp.concatenate([history_row[0], candidate_row[0]], axis=0)
+    row_parts = jnp.stack([all_rows // 128, all_rows % 128], axis=1).astype(jnp.bfloat16)
+    wanted_parts = lax.dot_general(
+        all_pick, row_parts, (((0,), (0,)), ((), ())), preferred_element_type=jnp.float32
+    ).astype(jnp.int32)
+    wanted = (wanted_parts[:, 0] * 128 + wanted_parts[:, 1]).reshape(n_dest, slot_count)
+    asked = lax.all_to_all(wanted, "req", split_axis=0, concat_axis=0, tiled=True)
+    fetched = jnp.take(table, asked.reshape(-1), axis=0, mode="clip").reshape(
+        n_dest, slot_count, d_model
     )
     replies = lax.all_to_all(fetched, "req", split_axis=0, concat_axis=0, tiled=True)
-    flat_rows = replies.reshape(n_dest * slot_count, d_model)
-    hist_emb = jnp.take(flat_rows, hist_slot, axis=0)
-    cand_emb = jnp.take(flat_rows, cand_slot, axis=0)
+    flat_rows = replies.reshape(n_slots, d_model)
+    hist_emb = jnp.dot(hist_pick, flat_rows, preferred_element_type=jnp.float32).astype(jnp.bfloat16)
+    cand_emb = jnp.dot(cand_pick, flat_rows, preferred_element_type=jnp.float32).astype(jnp.bfloat16)
     head_size = d_model // HEADS
     scale_factor = 1.0 / math.sqrt(head_size)
     length = history_length[0]

time: 60.3 us -> 53.6 us (0.89)
  blocking collectives: 15.4 us -> 25.1 us
  starting transfers between devices: 8.78 us -> 3.61 us
  local copies, waits for them, and re-layouts: 11.8 us -> 7 us
  waiting for transfers between devices: 12.1 us -> 7.51 us
  other arithmetic: 7.07 us -> 2.55 us
  matrix products: 3.94 us -> 6.7 us
    all_to_all x0 -> x1, blocking collectives: none -> 9.64 us  [body(): lax.all_to_all(wanted, 'req', split_axis=0, concat_axis=0, tiled=True)]
    all_to_all x1 -> x0, starting transfers between devices: 5.16 us -> none  [body(): lax.all_to_all(wanted, 'req', split_axis=0, concat_axis=0, tiled=True)]
    all_to_all x1 -> x0, waiting for transfers between devices: 4.02 us -> none  [body(): lax.all_to_all(wanted, 'req', split_axis=0, concat_axis=0, tiled=True)]
    dot_general x0 -> x5, matrix products: none -> 2.86 us  [the longest x2 1.83 us: slot_index(): jnp.dot(earlier.astype(jnp.bfloat16), onehot, preferred_element_type=jnp....]
    scatter x2 -> x0, local copies, waits for them, and re-layouts: 2.7 us -> none  [body(): wanted.at[hist_slot].set(history_row[0]).at[cand_slot].set(candidate_row[0])]
    select_n x5 -> x0, other arithmetic: 2.54 us -> none  [the longest x2 1.1 us: body(): jnp.take(table, lax.all_to_all(wanted, 'req', split_axis=0, concat_axis=0...]
    reduce_sum x2 -> x0, other arithmetic: 1.53 us -> none  [slot_index(): rank = jnp.sum(before * onehot, axis=1)]
    convert_element_type x2 -> x0, other arithmetic: 1.45 us -> none  [slot_index(): (shard_ids[:, None] == jnp.arange(n_dest, dtype=jnp.int32)[None, :]).asty...]
  transfers between devices with their start and end apart: 2 -> 1, of which waited for: 2 -> 1; matrix products, arithmetic and copies ran while one was open for 0% -> 0% of each run, Pallas kernels for 0% -> 0%
where the time goes in v2:
time: 53.6 us; the launch traced here: 53.3 us
  blocking collectives  25.1 us (47%)
  waiting for transfers between devices  7.51 us (14%)
  local copies, waits for them, and re-layouts  7 us (13%)
  matrix products  6.7 us (12%)
  starting transfers between devices  3.61 us (7%)
  other arithmetic  2.55 us (5%)
  between operations  0.84 us (2%)
    all_gather x1, blocking collectives, body(): hist_all = lax.all_gather(hist_emb, 'cand', axis=0, tiled=True)  15.4 us
    all_to_all x1, blocking collectives, body(): lax.all_to_all(wanted, 'req', split_axis=0, concat_axis=0, tiled=True)  9.64 us
    all_to_all x1, waiting for transfers between devices, body(): lax.all_to_all(fetched, 'req', split_axis=0, concat_axis=0, tiled=True)  7.51 us
    gather x1, local copies, waits for them, and re-layouts, body(): jnp.take(table, asked.reshape(-1), axis=0, mode='clip')  6.74 us
    all_to_all x1, starting transfers between devices, body(): lax.all_to_all(fetched, 'req', split_axis=0, concat_axis=0, tiled=True)  3.61 us
    dot_general x2, matrix products, slot_index(): jnp.dot(earlier.astype(jnp.bfloat16), onehot, preferred_element_type=jnp....  1.83 us
    dot_general x1, matrix products, body(): jnp.einsum('bgo,ogl->bgl', gate_weights, value_portion_slice, preferred_e...  1.59 us
    add x2, other arithmetic, slot_index(): return shard_ids * slot_count + first_slot + rank  1.37 us
  transfers between devices with their start and end apart: 1, of which 1 were waited for; matrix products, arithmetic and copies ran while one was open for 0% of the time, Pallas kernels for 0%

profile of v2, /device:TPU:0, one launch (start us, length us, event | category | flops | bytes accessed | tf_op | source)
XLA Modules:
  0.0 53.3 jit_solution(2658929312946107102)
XLA Ops:
  0.0 0.0 copy-start
  0.0 0.9 %fusion.3 = f32[256]{0:T(256)S(1)} fusion(s32[256]{0:T(256)} %bitcast.40), kind=kOutput, calls=%fused_computation.14 | convolution fusion | flops 595712 | bytes 2048 | tf_op jit(solution)/shard_map/dot_general | solution.py:17
  1.0 0.7 %convert_add_fusion = s32[256]{0:T(256)S(1)} fusion(f32[256]{0:T(256)S(1)} %fusion.3, s32[256]{0:T(256)} %bitcast.41), kind=kLoop, calls=%fused_computation.53 | loop fusion | flops 1024 | bytes 3072 | tf_op jit(solution)/shard_map/add | solution.py:19
  1.6 0.3 iota_compare_fusion
  1.9 0.9 %fusion.4 = f32[128]{0:T(128)S(1)} fusion(s32[128]{0:T(128)} %bitcast.44), kind=kOutput, calls=%fused_computation.16 | convolution fusion | flops 150400 | bytes 1024 | tf_op jit(solution)/shard_map/dot_general | solution.py:17
  2.8 0.7 %convert_add_fusion.1 = s32[128]{0:T(128)S(1)} fusion(f32[128]{0:T(128)S(1)} %fusion.4, s32[1,128,1]{1,2,0:T(1,128)} %param.12), kind=kLoop, calls=%fused_computation.54 | loop fusion | flops 384 | bytes 1536 | tf_op jit(solution)/shard_map/add | solution.py:19
  3.5 0.2 iota_compare_fusion.1
  3.6 0.7 %fusion.28 = (bf16[384,1]{0,1:T(2,128)(2,1)S(1)}, s32[384,1]{0,1:T(1,128)S(1)}) fusion(s32[256,1]{0,1:T(1,128)} %bitcast.42, s32[128,1]{0,1:T(1,128)} %bitcast.43), kind=kLoop, calls=%fused_computation.51 | loop fusion | flops 6528 | bytes 3840 | tf_op jit(solution)/shard_map/convert.1
  4.3 0.0 copy-start.4
  4.4 0.3 convolution_convert_fusion
  4.7 0.1 add.83
  4.8 9.6 %all_to_all.11 = s32[4,1,320]{2,1,0:T(1,128)S(1)} all-to-all(s32[4,1,320]{2,1,0:T(1,128)S(1)} %add.83), channel_id=1, replica_groups=mesh['req'=4,'cand'=8] {'req'}, dimensions={0} | all-to-all | bytes 10240 | tf_op jit(solution)/shard_map/all_to_all | solution.py:62
  14.5 0.1 reshape.296
  14.6 0.0 copy-start.2
  14.6 0.0 copy-start.3
  14.6 6.7 %gather_fusion = bf16[1280,256]{1,0:T(8,128)(2,1)} fusion(bf16[8192,256]{1,0:T(8,128)(2,1)} %param.11, s32[2048]{0:T(1024)S(1)} %pad_clamp_fusion), kind=kCustom, calls=%fused_computation | custom fusion | bytes 1315840 | tf_op jit(solution)/shard_map/jit(_take)/gather | solution.py:63
  21.3 3.6 %all-to-all-start.1 = ((bf16[4,320,256]{2,1,0:T(8,128)(2,1)}), bf16[4,320,256]{2,1,0:T(8,128)(2,1)S(1)}, u32[]{:S(2)}, u32[]{:S(2)}) async-start(bf16[4,320,256]{2,1,0:T(8,128)(2,1)} %bitcast.4), calls=%async_computation.1 | async-start | bytes 1310720 | tf_op jit(solution)/shard_map/all_to_all | solution.py:66
  25.6 0.0 copy-done.4
  25.7 7.5 %all-to-all-done.1 = bf16[4,320,256]{2,1,0:T(8,128)(2,1)S(1)} async-done(((bf16[4,320,256]{2,1,0:T(8,128)(2,1)}), bf16[4,320,256]{2,1,0:T(8,128)(2,1)S(1)}, u32[]{:S(2)}, u32[]{:S(2)}) %all-to-all-start.1) | async-done | bytes 655392 | tf_op jit(solution)/shard_map/all_to_all | solution.py:66
  33.2 0.4 convolution_convert_fusion.2
  33.6 0.3 convolution_convert_fusion.4
  33.9 15.4 %all_gather.3 = bf16[1024,256]{1,0:T(8,128)(2,1)S(1)} all-gather(bf16[128,256]{1,0:T(8,128)(2,1)S(1)} %convolution_convert_fusion.4), channel_id=1, replica_groups=mesh['req'=4,'cand'=8] {'cand'}, dimensions={0}, use_global_device_ids=true | all-gather | bytes 589824 | tf_op jit(solution)/shard_map/all_gather | solution.py:78
  49.3 0.0 copy-done.2
  49.3 0.0 copy-done.3
  49.3 0.5 convolution_convert_fusion.1
  49.8 0.1 fusion.37
  49.9 0.0 copy-done
  49.9 0.2 convolution_convert_fusion.3
  50.1 0.0 copy-done.1
  50.1 0.3 fusion.15
  50.4 1.6 %fusion.8 = bf16[4,64,256]{2,1,0:T(8,128)(2,1)S(1)} fusion(bf16[1024,4,64]{0,2,1:T(8,128)(2,1)S(1)} %bitcast.38, bf16[1024,4,64]{0,2,1:T(8,128)(2,1)S(1)} %bitcast.37, bf16[256,4,64]{0,2,1:T(8,128)(2,1)S(1)} %bitcast.39, pred[1024]{0:T(1024)(128)(4,1)S(1)} %iota_compare_fusion.8, f32[]{:T(128)S(6)} %sqrt.3), kind=kOutput, calls=%fused_computation.18 | convolution fusion | flops 274857984 | bytes 1311748 | tf_op jit(solution)/shard_map/bgo,ogl->bgl/dot_general | solution.py:93
  52.0 1.2 %fusion.11 = f32[1,256]{1,0:T(1,128)} fusion(bf16[1024,1]{0,1:T(2,128)(2,1)S(1)} %reshape.303, f32[256,1024]{1,0:T(8,128)S(1)} %fusion.15, bf16[256,256]{0,1:T(8,128)(2,1)S(1)} %bitcast.45, bf16[512,1024]{1,0:T(8,128)(2,1)S(1)} %copy-done.1), kind=kOutput, calls=%fused_computation.20 | convolution fusion | flops 136314880 | bytes 1709056 | tf_op jit(solution)/shard_map/dot_general | solution.py:105
  (7 shorter events, 0.1 us)
Async XLA Ops:
  0.0 49.9 %copy-start = (bf16[256,256]{1,0:T(8,128)(2,1)S(1)}, bf16[256,256]{1,0:T(8,128)(2,1)}, u32[]{:S(2)}) copy-start(bf16[256,256]{1,0:T(8,128)(2,1)} %param.17) | copy-start | bytes 393220
  4.3 21.3 %copy-start.4 = (bf16[1024]{0:T(1024)(128)(2,1)S(1)}, bf16[1024]{0:T(1024)(128)(2,1)}, u32[]{:S(2)}) copy-start(bf16[1024]{0:T(1024)(128)(2,1)} %param.21) | copy-start | bytes 6148
  14.6 34.7 %copy-start.2 = (bf16[256,256]{1,0:T(8,128)(2,1)S(1)}, bf16[256,256]{1,0:T(8,128)(2,1)}, u32[]{:S(2)}) copy-start(bf16[256,256]{1,0:T(8,128)(2,1)} %param.19) | copy-start | bytes 393220
  14.6 34.7 %copy-start.3 = (bf16[256,256]{1,0:T(8,128)(2,1)S(1)}, bf16[256,256]{1,0:T(8,128)(2,1)}, u32[]{:S(2)}) copy-start(bf16[256,256]{1,0:T(8,128)(2,1)} %param.18) | copy-start | bytes 393220
  21.3 28.8 %copy-start.1 = (bf16[512,1024]{1,0:T(8,128)(2,1)S(1)}, bf16[512,1024]{1,0:T(8,128)(2,1)}, u32[]{:S(2)}) copy-start(bf16[512,1024]{1,0:T(8,128)(2,1)} %param.20) | copy-start | bytes 3145732
  21.3 11.9 %all-to-all-start.1 = ((bf16[4,320,256]{2,1,0:T(8,128)(2,1)}), bf16[4,320,256]{2,1,0:T(8,128)(2,1)S(1)}, u32[]{:S(2)}, u32[]{:S(2)}) async-start(bf16[4,320,256]{2,1,0:T(8,128)(2,1)} %bitcast.4), calls=%async_computation.1 | async-start | bytes 1310720 | tf_op jit(solution)/shard_map/all_to_all | solution.py:66

commit v3 on v2

--- a/solution.py
+++ b/solution.py
@@ -25,6 +25,14 @@
     )
 
 
+def wanted_rows(pick, rows):
+    row_parts = jnp.stack([rows // 128, rows % 128], axis=1).astype(jnp.bfloat16)
+    parts = lax.dot_general(
+        pick, row_parts, (((0,), (0,)), ((), ())), preferred_element_type=jnp.float32
+    ).astype(jnp.int32)
+    return parts[:, 0] * 128 + parts[:, 1]
+
+
 def body(
     table,
     history_shard,
@@ -46,27 +54,29 @@
     cand_dev = cand_shards.shape[0]
     hist_cap = 4 * hist_dev // n_dest
     cand_cap = 3 * cand_dev // n_dest
-    slot_count = hist_cap + cand_cap
-    n_slots = n_dest * slot_count
-    hist_slot = slot_index(hist_shards, n_dest, slot_count, 0)
-    cand_slot = slot_index(cand_shards, n_dest, slot_count, hist_cap)
-    hist_pick = select_rows(hist_slot, n_slots)
-    cand_pick = select_rows(cand_slot, n_slots)
-    all_pick = jnp.concatenate([hist_pick, cand_pick], axis=0)
-    all_rows = jnp.concatenate([history_row[0], candidate_row[0]], axis=0)
-    row_parts = jnp.stack([all_rows // 128, all_rows % 128], axis=1).astype(jnp.bfloat16)
-    wanted_parts = lax.dot_general(
-        all_pick, row_parts, (((0,), (0,)), ((), ())), preferred_element_type=jnp.float32
-    ).astype(jnp.int32)
-    wanted = (wanted_parts[:, 0] * 128 + wanted_parts[:, 1]).reshape(n_dest, slot_count)
-    asked = lax.all_to_all(wanted, "req", split_axis=0, concat_axis=0, tiled=True)
-    fetched = jnp.take(table, asked.reshape(-1), axis=0, mode="clip").reshape(
-        n_dest, slot_count, d_model
+    hist_slot = slot_index(hist_shards, n_dest, hist_cap, 0)
+    cand_slot = slot_index(cand_shards, n_dest, cand_cap, 0)
+    hist_pick = select_rows(hist_slot, n_dest * hist_cap)
+    cand_pick = select_rows(cand_slot, n_dest * cand_cap)
+    hist_wanted = wanted_rows(hist_pick, history_row[0]).reshape(n_dest, hist_cap)
+    cand_wanted = wanted_rows(cand_pick, candidate_row[0]).reshape(n_dest, cand_cap)
+    asked = lax.all_to_all(
+        jnp.concatenate([hist_wanted, cand_wanted], axis=1),
+        "req",
+        split_axis=0,
+        concat_axis=0,
+        tiled=True,
     )
-    replies = lax.all_to_all(fetched, "req", split_axis=0, concat_axis=0, tiled=True)
-    flat_rows = replies.reshape(n_slots, d_model)
-    hist_emb = jnp.dot(hist_pick, flat_rows, preferred_element_type=jnp.float32).astype(jnp.bfloat16)
-    cand_emb = jnp.dot(cand_pick, flat_rows, preferred_element_type=jnp.float32).astype(jnp.bfloat16)
+    hist_fetched = jnp.take(table, asked[:, :hist_cap].reshape(-1), axis=0, mode="clip")
+    hist_replies = lax.all_to_all(
+        hist_fetched.reshape(n_dest, hist_cap, d_model), "req", split_axis=0, concat_axis=0, tiled=True
+    ).reshape(n_dest * hist_cap, d_model)
+    cand_fetched = jnp.take(table, asked[:, hist_cap:].reshape(-1), axis=0, mode="clip")
+    cand_replies = lax.all_to_all(
+        cand_fetched.reshape(n_dest, cand_cap, d_model), "req", split_axis=0, concat_axis=0, tiled=True
+    ).reshape(n_dest * cand_cap, d_model)
+    hist_emb = jnp.dot(hist_pick, hist_replies, preferred_element_type=jnp.float32).astype(jnp.bfloat16)
+    cand_emb = jnp.dot(cand_pick, cand_replies, preferred_element_type=jnp.float32).astype(jnp.bfloat16)
     head_size = d_model // HEADS
     scale_factor = 1.0 / math.sqrt(head_size)
     length = history_length[0]

time: 53.6 us -> 54.5 us (1.017)
  blocking collectives: 25.1 us -> 15.4 us
  starting transfers between devices: 3.61 us -> 12.8 us
  local copies, waits for them, and re-layouts: 7 us -> 12 us
  waiting for transfers between devices: 7.51 us -> 3.31 us
    all_to_all x1 -> x0, blocking collectives: 9.64 us -> none  [body(): lax.all_to_all(wanted, 'req', split_axis=0, concat_axis=0, tiled=True)]
    all_to_all x1 -> x3, starting transfers between devices: 3.61 us -> 12.8 us  [the longest x1 5.16 us: body(): lax.all_to_all(jnp.concatenate([hist_wanted, cand_wanted], axis=1), 'req'...]
    all_to_all x1 -> x3, waiting for transfers between devices: 7.51 us -> 3.31 us  [the longest x1 3.3 us: body(): lax.all_to_all(jnp.concatenate([hist_wanted, cand_wanted], axis=1), 'req'...]
    gather x1 -> x2, local copies, waits for them, and re-layouts: 6.74 us -> 10.5 us  [the longest x1 5.55 us: body(): jnp.take(table, asked[:, hist_cap:].reshape(-1), axis=0, mode='clip')]
    another operation x2 -> x3, other arithmetic: 0.7 us -> 1.39 us
    unnamed x11 -> x10, local copies, waits for them, and re-layouts: 0.03 us -> 0.71 us
    all_to_all x0 -> x1, local copies, waits for them, and re-layouts: none -> 0.6 us  [body(): lax.all_to_all(jnp.concatenate([hist_wanted, cand_wanted], axis=1), 'req'...]
  transfers between devices with their start and end apart: 1 -> 3, of which waited for: 1 -> 1; matrix products, arithmetic and copies ran while one was open for 0% -> 13% of each run, Pallas kernels for 0% -> 0%
where the time goes in v3:
time: 54.5 us; the launch traced here: 54 us
  blocking collectives  15.4 us (28%)
  starting transfers between devices  12.8 us (23%)
  local copies, waits for them, and re-layouts  12 us (22%)
  matrix products  6.73 us (12%)
  waiting for transfers between devices  3.31 us (6%)
  other arithmetic  2.81 us (5%)
  between operations  0.83 us (2%)
    all_gather x1, blocking collectives, body(): hist_all = lax.all_gather(hist_emb, 'cand', axis=0, tiled=True)  15.4 us
    gather x1, local copies, waits for them, and re-layouts, body(): jnp.take(table, asked[:, hist_cap:].reshape(-1), axis=0, mode='clip')  5.55 us
    all_to_all x1, starting transfers between devices, body(): lax.all_to_all(jnp.concatenate([hist_wanted, cand_wanted], axis=1), 'req'...  5.16 us
    gather x1, local copies, waits for them, and re-layouts, body(): jnp.take(table, asked[:, :hist_cap].reshape(-1), axis=0, mode='clip')  4.92 us
    all_to_all x1, starting transfers between devices, body(): lax.all_to_all(cand_fetched.reshape(n_dest, cand_cap, d_model), 'req', sp...  4.28 us
    all_to_all x1, starting transfers between devices, body(): lax.all_to_all(hist_fetched.reshape(n_dest, hist_cap, d_model), 'req', sp...  3.4 us
    all_to_all x1, waiting for transfers between devices, body(): lax.all_to_all(jnp.concatenate([hist_wanted, cand_wanted], axis=1), 'req'...  3.3 us
    dot_general x2, matrix products, slot_index(): jnp.dot(earlier.astype(jnp.bfloat16), onehot, preferred_element_type=jnp....  1.83 us
  transfers between devices with their start and end apart: 3, of which 1 were waited for; matrix products, arithmetic and copies ran while one was open for 13% of the time, Pallas kernels for 0%

profile of v3, /device:TPU:0, one launch (start us, length us, event | category | flops | bytes accessed | tf_op | source)
XLA Modules:
  0.0 54.0 jit_solution(1714159575479499430)
XLA Ops:
  0.0 0.0 copy-start
  0.0 0.9 %fusion.2 = f32[256]{0:T(256)S(1)} fusion(s32[256]{0:T(256)} %bitcast.80), kind=kOutput, calls=%fused_computation.13 | convolution fusion | flops 595712 | bytes 2048 | tf_op jit(solution)/shard_map/dot_general | solution.py:17
  1.0 0.7 %convert_add_fusion = s32[256]{0:T(256)S(1)} fusion(f32[256]{0:T(256)S(1)} %fusion.2, s32[256]{0:T(256)} %bitcast.81), kind=kLoop, calls=%fused_computation.67 | loop fusion | flops 768 | bytes 3072 | tf_op jit(solution)/shard_map/add | solution.py:19
  1.6 0.7 %fusion.32 = (bf16[256,1]{0,1:T(2,128)(2,1)S(1)}, s32[256,1]{0,1:T(1,128)S(1)}) fusion(s32[1,256]{1,0:T(1,128)} %param.15), kind=kLoop, calls=%fused_computation.68 | loop fusion | flops 4096 | bytes 2560 | tf_op jit(solution)/shard_map/convert
  2.3 0.3 convolution_convert_fusion.4
  2.7 0.1 add.90
  2.8 0.7 %fusion.37 = (bf16[128,1]{0,1:T(2,128)(2,1)S(1)}, bf16[128,1]{0,1:T(2,128)(2,1)S(1)}) fusion(s32[1,128]{1,0:T(1,128)} %param.13), kind=kLoop, calls=%fused_computation.75 | loop fusion | flops 2688 | bytes 1024 | tf_op jit(solution)/shard_map/convert.2
  3.5 0.9 %fusion.3 = f32[128]{0:T(128)S(1)} fusion(s32[128]{0:T(128)} %bitcast.82), kind=kOutput, calls=%fused_computation.15 | convolution fusion | flops 150400 | bytes 1024 | tf_op jit(solution)/shard_map/dot_general | solution.py:17
  4.3 0.7 %convert_add_fusion.1 = s32[128]{0:T(128)S(1)} fusion(f32[128]{0:T(128)S(1)} %fusion.3, s32[1,128,1]{1,2,0:T(1,128)} %param.12), kind=kLoop, calls=%fused_computation.74 | loop fusion | flops 384 | bytes 1536 | tf_op jit(solution)/shard_map/add | solution.py:19
  5.0 0.2 convolution_convert_fusion.5
  5.3 0.6 %all_to_all.14 = s32[4,1,320]{2,1,0:T(1,128)} reshape(s32[4,320]{1,0:T(4,128)S(1)} %pad_add_fusion) | data formatting | bytes 10240 | tf_op jit(solution)/shard_map/all_to_all | solution.py:63
  5.9 5.2 %all-to-all-start = ((s32[4,1,320]{2,1,0:T(1,128)}), s32[4,1,320]{2,1,0:T(1,128)S(1)}, u32[]{:S(2)}, u32[]{:S(2)}) async-start(s32[4,1,320]{2,1,0:T(1,128)} %all_to_all.14), calls=%async_computation | async-start | bytes 12288 | tf_op jit(solution)/shard_map/all_to_all | solution.py:63
  11.7 0.7 %reshape.294 = bf16[1024,1]{0,1:T(2,128)(2,1)S(1)} reshape(bf16[1024]{0:T(1024)(128)(2,1)} %param.21) | data formatting | bytes 4096 | tf_op args[10]
  12.4 3.3 %all-to-all-done = s32[4,1,320]{2,1,0:T(1,128)S(1)} async-done(((s32[4,1,320]{2,1,0:T(1,128)}), s32[4,1,320]{2,1,0:T(1,128)S(1)}, u32[]{:S(2)}, u32[]{:S(2)}) %all-to-all-start) | async-done | bytes 5152 | tf_op jit(solution)/shard_map/all_to_all | solution.py:63
  15.7 4.9 %gather_fusion.1 = bf16[512,256]{1,0:T(8,128)(2,1)} fusion(bf16[8192,256]{1,0:T(8,128)(2,1)} %param.11, s32[1024]{0:T(1024)S(1)} %pad_clamp_fusion), kind=kCustom, calls=%fused_computation.1 | custom fusion | bytes 526336 | tf_op jit(solution)/shard_map/jit(_take)/gather | solution.py:70
  20.6 3.4 %all-to-all-start.2 = ((bf16[4,128,256]{2,1,0:T(8,128)(2,1)}), bf16[4,128,256]{2,1,0:T(8,128)(2,1)S(1)}, u32[]{:S(2)}, u32[]{:S(2)}) async-start(bf16[4,128,256]{2,1,0:T(8,128)(2,1)} %bitcast.8), calls=%async_computation.2 | async-start | bytes 524288 | tf_op jit(solution)/shard_map/all_to_all | solution.py:71
  24.1 0.1 reshape.278
  24.2 5.6 %gather_fusion = bf16[768,256]{1,0:T(8,128)(2,1)} fusion(bf16[8192,256]{1,0:T(8,128)(2,1)} %param.11, s32[1024]{0:T(1024)S(1)} %pad_clamp_fusion.1), kind=kCustom, calls=%fused_computation | custom fusion | bytes 789504 | tf_op jit(solution)/shard_map/jit(_take)/gather | solution.py:74
  29.7 0.0 all-to-all-done.2
  29.7 4.3 %all-to-all-start.1 = ((bf16[4,192,256]{2,1,0:T(8,128)(2,1)}), bf16[4,192,256]{2,1,0:T(8,128)(2,1)S(1)}, u32[]{:S(2)}, u32[]{:S(2)}) async-start(bf16[4,192,256]{2,1,0:T(8,128)(2,1)} %bitcast.5), calls=%async_computation.1 | async-start | bytes 786432 | tf_op jit(solution)/shard_map/all_to_all | solution.py:75
  34.0 0.2 convolution_convert_fusion.3
  34.2 15.4 %all_gather.3 = bf16[1024,256]{1,0:T(8,128)(2,1)S(1)} all-gather(bf16[128,256]{1,0:T(8,128)(2,1)S(1)} %convolution_convert_fusion.3), channel_id=1, replica_groups=mesh['req'=4,'cand'=8] {'cand'}, dimensions={0}, use_global_device_ids=true | all-gather | bytes 589824 | tf_op jit(solution)/shard_map/all_gather | solution.py:88
  49.7 0.0 copy-done.2
  49.7 0.0 copy-done.3
  49.7 0.5 convolution_convert_fusion
  50.1 0.1 fusion.45
  50.2 0.0 all-to-all-done.1
  50.2 0.3 convolution_convert_fusion.1
  50.6 0.2 convolution_convert_fusion.2
  50.8 0.3 fusion.14
  51.1 1.6 %fusion.7 = bf16[4,64,256]{2,1,0:T(8,128)(2,1)S(1)} fusion(bf16[1024,4,64]{0,2,1:T(8,128)(2,1)S(1)} %bitcast.74, bf16[1024,4,64]{0,2,1:T(8,128)(2,1)S(1)} %bitcast.73, bf16[256,4,64]{0,2,1:T(8,128)(2,1)S(1)} %bitcast.76, pred[1024]{0:T(1024)(128)(4,1)S(1)} %iota_compare_fusion.10, f32[]{:T(128)S(6)} %sqrt.3), kind=kOutput, calls=%fused_computation.17 | convolution fusion | flops 274857984 | bytes 1311748 | tf_op jit(solution)/shard_map/bgo,ogl->bgl/dot_general | solution.py:103
  52.7 1.2 %fusion.10 = f32[1,256]{1,0:T(1,128)} fusion(bf16[1024,1]{0,1:T(2,128)(2,1)S(1)} %reshape.294, f32[256,1024]{1,0:T(8,128)S(1)} %fusion.14, bf16[256,256]{0,1:T(8,128)(2,1)S(1)} %bitcast.83, bf16[512,1024]{1,0:T(8,128)(2,1)S(1)} %copy-done.1), kind=kOutput, calls=%fused_computation.19 | convolution fusion | flops 136314880 | bytes 1709056 | tf_op jit(solution)/shard_map/dot_general | solution.py:115
  (15 shorter events, 0.1 us)
Async XLA Ops:
  0.0 50.6 %copy-start = (bf16[256,256]{1,0:T(8,128)(2,1)S(1)}, bf16[256,256]{1,0:T(8,128)(2,1)}, u32[]{:S(2)}) copy-start(bf16[256,256]{1,0:T(8,128)(2,1)} %param.17) | copy-start | bytes 393220
  2.6 47.0 %copy-start.2 = (bf16[256,256]{1,0:T(8,128)(2,1)S(1)}, bf16[256,256]{1,0:T(8,128)(2,1)}, u32[]{:S(2)}) copy-start(bf16[256,256]{1,0:T(8,128)(2,1)} %param.19) | copy-start | bytes 393220
  2.6 47.0 %copy-start.3 = (bf16[256,256]{1,0:T(8,128)(2,1)S(1)}, bf16[256,256]{1,0:T(8,128)(2,1)}, u32[]{:S(2)}) copy-start(bf16[256,256]{1,0:T(8,128)(2,1)} %param.18) | copy-start | bytes 393220
  5.9 9.8 %all-to-all-start = ((s32[4,1,320]{2,1,0:T(1,128)}), s32[4,1,320]{2,1,0:T(1,128)S(1)}, u32[]{:S(2)}, u32[]{:S(2)}) async-start(s32[4,1,320]{2,1,0:T(1,128)} %all_to_all.14), calls=%async_computation | async-start | bytes 12288 | tf_op jit(solution)/shard_map/all_to_all | solution.py:63
  20.6 9.1 %all-to-all-start.2 = ((bf16[4,128,256]{2,1,0:T(8,128)(2,1)}), bf16[4,128,256]{2,1,0:T(8,128)(2,1)S(1)}, u32[]{:S(2)}, u32[]{:S(2)}) async-start(bf16[4,128,256]{2,1,0:T(8,128)(2,1)} %bitcast.8), calls=%async_computation.2 | async-start | bytes 524288 | tf_op jit(solution)/shard_map/all_to_all | solution.py:71
  29.7 21.1 %copy-start.1 = (bf16[512,1024]{1,0:T(8,128)(2,1)S(1)}, bf16[512,1024]{1,0:T(8,128)(2,1)}, u32[]{:S(2)}) copy-start(bf16[512,1024]{1,0:T(8,128)(2,1)} %param.20) | copy-start | bytes 3145732
  29.7 20.5 %all-to-all-start.1 = ((bf16[4,192,256]{2,1,0:T(8,128)(2,1)}), bf16[4,192,256]{2,1,0:T(8,128)(2,1)S(1)}, u32[]{:S(2)}, u32[]{:S(2)}) async-start(bf16[4,192,256]{2,1,0:T(8,128)(2,1)} %bitcast.5), calls=%async_computation.1 | async-start | bytes 786432 | tf_op jit(solution)/shard_map/all_to_all | solution.py:75

commit v4 on v2

--- a/solution.py
+++ b/solution.py
@@ -3,6 +3,8 @@
 import jax
 import jax.numpy as jnp
 from jax import lax
+from jax.experimental import pallas as pl
+from jax.experimental.pallas import tpu as pltpu
 from jax.sharding import PartitionSpec as P
 
 HEADS = 4
@@ -23,6 +25,39 @@
     return (slots[:, None] == lax.broadcasted_iota(jnp.int32, (slots.shape[0], n_slots), 1)).astype(
         jnp.bfloat16
     )
+
+
+def gather_kernel(idx_ref, table_ref, out_ref, sem):
+    count = out_ref.shape[0] // 2
+
+    def issue(i, carry):
+        first = pl.multiple_of(idx_ref[i] // 2 * 2, 2)
+        pltpu.make_async_copy(
+            table_ref.at[pl.ds(first, 2)], out_ref.at[pl.ds(pl.multiple_of(2 * i, 2), 2)], sem
+        ).start()
+        return carry
+
+    lax.fori_loop(0, count, issue, 0, unroll=8)
+    pltpu.make_async_copy(table_ref.at[pl.ds(0, 2 * count)], out_ref, sem).wait()
+
+
+def gather_rows(table, idx):
+    count, width = idx.shape[0], table.shape[1]
+    pairs = pl.pallas_call(
+        gather_kernel,
+        out_shape=jax.ShapeDtypeStruct((2 * count, width), table.dtype),
+        grid_spec=pltpu.PrefetchScalarGridSpec(
+            num_scalar_prefetch=1,
+            grid=(1,),
+            in_specs=[pl.BlockSpec(memory_space=pl.ANY)],
+            out_specs=pl.BlockSpec((2 * count, width), lambda i, idx_ref: (0, 0)),
+            scratch_shapes=[pltpu.SemaphoreType.DMA(())],
+        ),
+        cost_estimate=pl.CostEstimate(
+            flops=0, transcendentals=0, bytes_accessed=4 * count * width * table.dtype.itemsize
+        ),
+    )(idx, table).reshape(count, 2, width)
+    return jnp.where((idx % 2 == 1)[:, None], pairs[:, 1], pairs[:, 0])
 
 
 def body(
@@ -60,7 +95,7 @@
     ).astype(jnp.int32)
     wanted = (wanted_parts[:, 0] * 128 + wanted_parts[:, 1]).reshape(n_dest, slot_count)
     asked = lax.all_to_all(wanted, "req", split_axis=0, concat_axis=0, tiled=True)
-    fetched = jnp.take(table, asked.reshape(-1), axis=0, mode="clip").reshape(
+    fetched = gather_rows(table, jnp.clip(asked.reshape(-1), 0, table.shape[0] - 1)).reshape(
         n_dest, slot_count, d_model
     )
     replies = lax.all_to_all(fetched, "req", split_axis=0, concat_axis=0, tiled=True)

time: 53.6 us -> 95.8 us (1.79)
  Pallas kernels: 0 us -> 26.8 us
  starting transfers between devices: 3.61 us -> 18.1 us
  other arithmetic: 2.55 us -> 3.63 us
    pallas_call x0 -> x1, Pallas kernels: none -> 26.8 us  [gather_rows(): pl.pallas_call(gather_kernel, out_shape=jax.ShapeDtypeStruct((2 * count,...]
    all_to_all x1, starting transfers between devices: 3.61 us -> 18.1 us  [body(): lax.all_to_all(fetched, 'req', split_axis=0, concat_axis=0, tiled=True)]
    gather x1 -> x0, local copies, waits for them, and re-layouts: 6.74 us -> none  [body(): jnp.take(table, asked.reshape(-1), axis=0, mode='clip')]
    reshape x0 -> x1, local copies, waits for them, and re-layouts: none -> 3.09 us  [gather_rows(): pairs = pl.pallas_call(gather_kernel, out_shape=jax.ShapeDtypeStruct((2 *...]
    slice x0 -> x1, local copies, waits for them, and re-layouts: none -> 1.88 us  [gather_rows(): return jnp.where((idx % 2 == 1)[:, None], pairs[:, 1], pairs[:, 0])]
    select_n x0 -> x1, other arithmetic: none -> 1.07 us  [gather_rows(): return jnp.where((idx % 2 == 1)[:, None], pairs[:, 1], pairs[:, 0])]
where the time goes in v4:
time: 95.8 us; the launch traced here: 95.2 us
  Pallas kernels  26.8 us (28%)
  blocking collectives  24.3 us (25%)
  starting transfers between devices  18.1 us (19%)
  waiting for transfers between devices  8.37 us (9%)
  matrix products  6.71 us (7%)
  local copies, waits for them, and re-layouts  6.49 us (7%)
  other arithmetic  3.63 us (4%)
    pallas_call x1, Pallas kernels, gather_rows(): pl.pallas_call(gather_kernel, out_shape=jax.ShapeDtypeStruct((2 * count,...  26.8 us
    all_to_all x1, starting transfers between devices, body(): lax.all_to_all(fetched, 'req', split_axis=0, concat_axis=0, tiled=True)  18.1 us
    all_gather x1, blocking collectives, body(): hist_all = lax.all_gather(hist_emb, 'cand', axis=0, tiled=True)  14.7 us
    all_to_all x1, blocking collectives, body(): lax.all_to_all(wanted, 'req', split_axis=0, concat_axis=0, tiled=True)  9.64 us
    all_to_all x1, waiting for transfers between devices, body(): lax.all_to_all(fetched, 'req', split_axis=0, concat_axis=0, tiled=True)  8.37 us
    reshape x1, local copies, waits for them, and re-layouts, gather_rows(): pairs = pl.pallas_call(gather_kernel, out_shape=jax.ShapeDtypeStruct((2 *...  3.09 us
  transfers between devices with their start and end apart: 1, of which 1 were waited for; matrix products, arithmetic and copies ran while one was open for 0% of the time, Pallas kernels for 0%

profile of v4, /device:TPU:0, one launch (start us, length us, event | category | flops | bytes accessed | tf_op | source)
XLA Modules:
  0.0 95.2 jit_solution(4080410760485833726)
XLA Ops:
  0.0 0.0 copy-start
  0.0 0.9 fusion.3
  1.0 0.7 convert_add_fusion
  1.6 0.3 iota_compare_fusion
  1.9 0.9 fusion.4
  2.8 0.7 convert_add_fusion.1
  3.5 0.2 iota_compare_fusion.1
  3.6 0.7 fusion.30
  4.3 0.3 convolution_convert_fusion
  4.7 0.1 add.94
  4.8 9.6 %all_to_all.11 = s32[4,1,320]{2,1,0:T(1,128)S(1)} all-to-all(s32[4,1,320]{2,1,0:T(1,128)S(1)} %add.94), channel_id=1, replica_groups=mesh['req'=4,'cand'=8] {'req'}, dimensions={0} | all-to-all | bytes 10240 | tf_op jit(solution)/shard_map/all_to_all | solution.py:97
  14.5 0.7 min.15.idx_ref
  15.2 26.8 %shard_map.109 = bf16[2560,256]{1,0:T(8,128)(2,1)} custom-call(s32[1280]{0:T(1024)} %min.15.idx_ref, bf16[8192,256]{1,0:T(8,128)(2,1)} %table_ref.1), custom_call_target="tpu_custom_call" | custom-call | bytes 2621440 | tf_op jit(solution)/shard_map/pallas_call | solution.py:46
  41.9 3.1 %reshape.320 = bf16[1280,2,256]{2,1,0:T(2,128)(2,1)S(1)} reshape(bf16[2560,256]{1,0:T(8,128)(2,1)} %shard_map.109) | data formatting | bytes 2621440 | tf_op jit(solution)/shard_map/reshape | solution.py:59
  45.0 1.9 %fusion.40 = (bf16[1280,1,256]{2,1,0:T(2,128)(2,1)S(1)}, bf16[1280,1,256]{2,1,0:T(2,128)(2,1)S(1)}) fusion(bf16[1280,2,256]{2,1,0:T(2,128)(2,1)S(1)} %reshape.320), kind=kLoop, calls=%fused_computation.68 | loop fusion | bytes 2621440 | tf_op jit(solution)/shard_map/slice | solution.py:60
  46.9 0.1 copy.21
  47.1 0.1 copy.22
  47.2 0.0 copy-start.4
  47.2 1.1 %broadcast_select_fusion = bf16[4,320,256]{2,1,0:T(8,128)(2,1)} fusion(bf16[4,320,256]{2,1,0:T(8,128)(2,1)S(1)} %bitcast.40, bf16[4,320,256]{2,1,0:T(8,128)(2,1)S(1)} %bitcast.41, pred[4,320]{1,0:T(4,128)(4,1)S(1)} %fusion.21), kind=kLoop, calls=%fused_computation.21 | loop fusion | flops 327680 | bytes 1967360 | tf_op jit(solution)/shard_map/jit(_where)/select_n | solution.py:60
  48.3 18.1 %all-to-all-start.1 = ((bf16[4,320,256]{2,1,0:T(8,128)(2,1)}), bf16[4,320,256]{2,1,0:T(8,128)(2,1)S(1)}, u32[]{:S(2)}, u32[]{:S(2)}) async-start(bf16[4,320,256]{2,1,0:T(8,128)(2,1)} %broadcast_select_fusion), calls=%async_computation.1 | async-start | bytes 1310720 | tf_op jit(solution)/shard_map/all_to_all | solution.py:101
  67.1 8.4 %all-to-all-done.1 = bf16[4,320,256]{2,1,0:T(8,128)(2,1)S(1)} async-done(((bf16[4,320,256]{2,1,0:T(8,128)(2,1)}), bf16[4,320,256]{2,1,0:T(8,128)(2,1)S(1)}, u32[]{:S(2)}, u32[]{:S(2)}) %all-to-all-start.1) | async-done | bytes 655392 | tf_op jit(solution)/shard_map/all_to_all | solution.py:101
  75.5 0.4 convolution_convert_fusion.2
  75.9 0.3 convolution_convert_fusion.4
  76.2 14.7 %all_gather.3 = bf16[1024,256]{1,0:T(8,128)(2,1)S(1)} all-gather(bf16[128,256]{1,0:T(8,128)(2,1)S(1)} %convolution_convert_fusion.4), channel_id=1, replica_groups=mesh['req'=4,'cand'=8] {'cand'}, dimensions={0}, use_global_device_ids=true | all-gather | bytes 589824 | tf_op jit(solution)/shard_map/all_gather | solution.py:113
  90.9 0.0 copy-done.2
  90.9 0.5 convolution_convert_fusion.1
  91.4 0.1 fusion.41
  91.5 0.2 convolution_convert_fusion.3
  91.7 0.4 copy-done.1
  92.1 0.3 fusion.15
  92.4 1.6 %fusion.8 = bf16[4,64,256]{2,1,0:T(8,128)(2,1)S(1)} fusion(bf16[1024,4,64]{0,2,1:T(8,128)(2,1)S(1)} %bitcast.45, bf16[1024,4,64]{0,2,1:T(8,128)(2,1)S(1)} %bitcast.44, bf16[256,4,64]{0,2,1:T(8,128)(2,1)S(1)} %bitcast.46, pred[1024]{0:T(1024)(128)(4,1)S(1)} %iota_compare_fusion.8, f32[]{:T(128)S(6)} %sqrt.3), kind=kOutput, calls=%fused_computation.17 | convolution fusion | flops 274857984 | bytes 1311748 | tf_op jit(solution)/shard_map/bgo,ogl->bgl/dot_general | solution.py:128
  94.0 1.2 %fusion.11 = f32[1,256]{1,0:T(1,128)} fusion(bf16[1024,1]{0,1:T(2,128)(2,1)S(1)} %reshape.325, f32[256,1024]{1,0:T(8,128)S(1)} %fusion.15, bf16[256,256]{0,1:T(8,128)(2,1)S(1)} %bitcast.52, bf16[512,1024]{1,0:T(8,128)(2,1)S(1)} %copy-done.1), kind=kOutput, calls=%fused_computation.19 | convolution fusion | flops 136314880 | bytes 1709056 | tf_op jit(solution)/shard_map/dot_general | solution.py:140
  (12 shorter events, 0.1 us)
Async XLA Ops:
  0.0 91.4 %copy-start = (bf16[256,256]{1,0:T(8,128)(2,1)S(1)}, bf16[256,256]{1,0:T(8,128)(2,1)}, u32[]{:S(2)}) copy-start(bf16[256,256]{1,0:T(8,128)(2,1)} %param.17) | copy-start | bytes 393220
  47.2 19.9 %copy-start.4 = (bf16[1024]{0:T(1024)(128)(2,1)S(1)}, bf16[1024]{0:T(1024)(128)(2,1)}, u32[]{:S(2)}) copy-start(bf16[1024]{0:T(1024)(128)(2,1)} %param.21) | copy-start | bytes 6148
  48.3 42.6 %copy-start.2 = (bf16[256,256]{1,0:T(8,128)(2,1)S(1)}, bf16[256,256]{1,0:T(8,128)(2,1)}, u32[]{:S(2)}) copy-start(bf16[256,256]{1,0:T(8,128)(2,1)} %param.19) | copy-start | bytes 393220
  48.3 42.6 %copy-start.3 = (bf16[256,256]{1,0:T(8,128)(2,1)S(1)}, bf16[256,256]{1,0:T(8,128)(2,1)}, u32[]{:S(2)}) copy-start(bf16[256,256]{1,0:T(8,128)(2,1)} %param.18) | copy-start | bytes 393220
  48.3 27.2 %all-to-all-start.1 = ((bf16[4,320,256]{2,1,0:T(8,128)(2,1)}), bf16[4,320,256]{2,1,0:T(8,128)(2,1)S(1)}, u32[]{:S(2)}, u32[]{:S(2)}) async-start(bf16[4,320,256]{2,1,0:T(8,128)(2,1)} %broadcast_select_fusion), calls=%async_computation.1 | async-start | bytes 1310720 | tf_op jit(solution)/shard_map/all_to_all | solution.py:101
  90.9 1.2 %copy-start.1 = (bf16[512,1024]{1,0:T(8,128)(2,1)S(1)}, bf16[512,1024]{1,0:T(8,128)(2,1)}, u32[]{:S(2)}) copy-start(bf16[512,1024]{1,0:T(8,128)(2,1)} %param.20) | copy-start | bytes 3145732

commit v5 on v2

--- a/solution.py
+++ b/solution.py
@@ -23,6 +23,22 @@
     return (slots[:, None] == lax.broadcasted_iota(jnp.int32, (slots.shape[0], n_slots), 1)).astype(
         jnp.bfloat16
     )
+
+
+def gather_over_cand(rows):
+    n_cand = lax.axis_size("cand")
+    me = lax.axis_index("cand")
+    blocks, sources = [rows], [me]
+    for hop in range(2, n_cand, 2):
+        blocks.append(lax.ppermute(rows, "cand", [(i, (i + hop) % n_cand) for i in range(n_cand)]))
+        sources.append((me - hop) % n_cand)
+    mine = jnp.stack(blocks, axis=0)
+    partner = lax.ppermute(mine, "cand", [(i, i ^ 1) for i in range(n_cand)])
+    held = jnp.concatenate([mine, partner], axis=0)
+    source = jnp.stack(sources)
+    source = jnp.concatenate([source, source ^ 1])
+    order = jnp.argmax(source[None, :] == jnp.arange(n_cand)[:, None], axis=1)
+    return jnp.take(held, order, axis=0).reshape(-1, rows.shape[1])
 
 
 def body(
@@ -75,7 +91,7 @@
         jnp.bfloat16
     )
     query_row_matrix = query_row_matrix.reshape(cand_dev, HEADS, head_size)
-    hist_all = lax.all_gather(hist_emb, "cand", axis=0, tiled=True)
+    hist_all = gather_over_cand(hist_emb)
     pair_rows = jnp.dot(hist_all, w_pair, preferred_element_type=jnp.float32).astype(jnp.bfloat16)
     count = pair_rows.shape[0]
     key_portion_slice = pair_rows[:, :d_model].reshape(count, HEADS, head_size)

time: 53.6 us -> 51.4 us (0.959)
  blocking collectives: 25.1 us -> 0 us
  starting transfers between devices: 3.61 us -> 13.4 us
  waiting for transfers between devices: 7.51 us -> 16.6 us
  matrix products: 6.7 us -> 8.25 us
  local copies, waits for them, and re-layouts: 7 us -> 8.42 us
  other arithmetic: 2.55 us -> 3.51 us
    all_gather x1 -> x0, blocking collectives: 15.4 us -> none  [body(): hist_all = lax.all_gather(hist_emb, 'cand', axis=0, tiled=True)]
    all_to_all x1 -> x0, blocking collectives: 9.64 us -> none  [body(): lax.all_to_all(wanted, 'req', split_axis=0, concat_axis=0, tiled=True)]
    ppermute x0 -> x4, waiting for transfers between devices: none -> 5.34 us  [the longest x3 3.86 us: gather_over_cand(): lax.ppermute(rows, 'cand', [(i, (i + hop) % n_cand) for i in range(n_cand)])]
    all_to_all x0 -> x1, starting transfers between devices: none -> 5.16 us  [body(): lax.all_to_all(wanted, 'req', split_axis=0, concat_axis=0, tiled=True)]
    ppermute x0 -> x4, starting transfers between devices: none -> 4.74 us  [the longest x3 4.67 us: gather_over_cand(): lax.ppermute(rows, 'cand', [(i, (i + hop) % n_cand) for i in range(n_cand)])]
    all_to_all x0 -> x1, waiting for transfers between devices: none -> 3.22 us  [body(): lax.all_to_all(wanted, 'req', split_axis=0, concat_axis=0, tiled=True)]
    dot_general x1, matrix products: 1.59 us -> 2.5 us  [body(): jnp.einsum('bgo,ogl->bgl', gate_weights, value_portion_slice, preferred_e...]
    another operation x2 -> x4, other arithmetic: 0.7 us -> 1.37 us
  transfers between devices with their start and end apart: 1 -> 6, of which waited for: 1 -> 5; matrix products, arithmetic and copies ran while one was open for 0% -> 4% of each run, Pallas kernels for 0% -> 0%
where the time goes in v5:
time: 51.4 us; the launch traced here: 51.1 us
  waiting for transfers between devices  16.6 us (32%)
  starting transfers between devices  13.4 us (26%)
  local copies, waits for them, and re-layouts  8.42 us (16%)
  matrix products  8.25 us (16%)
  other arithmetic  3.51 us (7%)
  between operations  0.92 us (2%)
    all_to_all x1, waiting for transfers between devices, body(): lax.all_to_all(fetched, 'req', split_axis=0, concat_axis=0, tiled=True)  8.04 us
    gather x1, local copies, waits for them, and re-layouts, body(): jnp.take(table, asked.reshape(-1), axis=0, mode='clip')  6.78 us
    all_to_all x1, starting transfers between devices, body(): lax.all_to_all(wanted, 'req', split_axis=0, concat_axis=0, tiled=True)  5.16 us
    ppermute x3, starting transfers between devices, gather_over_cand(): lax.ppermute(rows, 'cand', [(i, (i + hop) % n_cand) for i in range(n_cand)])  4.67 us
    ppermute x3, waiting for transfers between devices, gather_over_cand(): lax.ppermute(rows, 'cand', [(i, (i + hop) % n_cand) for i in range(n_cand)])  3.86 us
    all_to_all x1, starting transfers between devices, body(): lax.all_to_all(fetched, 'req', split_axis=0, concat_axis=0, tiled=True)  3.48 us
    all_to_all x1, waiting for transfers between devices, body(): lax.all_to_all(wanted, 'req', split_axis=0, concat_axis=0, tiled=True)  3.22 us
    dot_general x1, matrix products, body(): jnp.einsum('bgo,ogl->bgl', gate_weights, value_portion_slice, preferred_e...  2.5 us
  transfers between devices with their start and end apart: 6, of which 5 were waited for; matrix products, arithmetic and copies ran while one was open for 4% of the time, Pallas kernels for 0%

profile of v5, /device:TPU:0, one launch (start us, length us, event | category | flops | bytes accessed | tf_op | source)
XLA Modules:
  0.0 51.1 jit_solution(15508773135307948019)
XLA Ops:
  0.0 0.9 %fusion.4 = f32[128]{0:T(128)S(1)} fusion(s32[128]{0:T(128)} %bitcast.64), kind=kOutput, calls=%fused_computation.17 | convolution fusion | flops 150400 | bytes 1024 | tf_op jit(solution)/shard_map/dot_general | solution.py:17
  0.9 0.7 %convert_add_fusion.1 = s32[128]{0:T(128)S(1)} fusion(f32[128]{0:T(128)S(1)} %fusion.4, s32[1,128,1]{1,2,0:T(1,128)} %param.12), kind=kLoop, calls=%fused_computation.69 | loop fusion | flops 384 | bytes 1536 | tf_op jit(solution)/shard_map/add | solution.py:19
  1.6 0.9 %fusion.3 = f32[256]{0:T(256)S(1)} fusion(s32[256]{0:T(256)} %bitcast.60), kind=kOutput, calls=%fused_computation.15 | convolution fusion | flops 595712 | bytes 2048 | tf_op jit(solution)/shard_map/dot_general | solution.py:17
  2.5 0.7 %convert_add_fusion = s32[256]{0:T(256)S(1)} fusion(f32[256]{0:T(256)S(1)} %fusion.3, s32[256]{0:T(256)} %bitcast.61), kind=kLoop, calls=%fused_computation.67 | loop fusion | flops 1024 | bytes 3072 | tf_op jit(solution)/shard_map/add | solution.py:19
  3.2 0.7 %fusion.28 = (bf16[384,1]{0,1:T(2,128)(2,1)S(1)}, s32[384,1]{0,1:T(1,128)S(1)}) fusion(s32[256,1]{0,1:T(1,128)} %bitcast.62, s32[128,1]{0,1:T(1,128)} %bitcast.63), kind=kLoop, calls=%fused_computation.65 | loop fusion | flops 6528 | bytes 3840 | tf_op jit(solution)/shard_map/convert.1
  3.9 0.2 iota_compare_fusion.1
  4.1 0.2 iota_compare_fusion
  4.3 0.3 convolution_convert_fusion
  4.7 0.7 %add.104 = s32[4,1,320]{2,1,0:T(1,128)} reshape(s32[1280]{0:T(1024)S(1)} %fusion.20) | data formatting | bytes 10240 | tf_op jit(solution)/shard_map/add | solution.py:77
  5.4 5.2 %all-to-all-start = ((s32[4,1,320]{2,1,0:T(1,128)}), s32[4,1,320]{2,1,0:T(1,128)S(1)}, u32[]{:S(2)}, u32[]{:S(2)}) async-start(s32[4,1,320]{2,1,0:T(1,128)} %add.104), calls=%async_computation | async-start | bytes 12288 | tf_op jit(solution)/shard_map/all_to_all | solution.py:78
  10.6 0.1 add_xor_fusion
  10.6 0.1 concatenate.67
  10.7 0.6 %iota_reduce_fusion = (pred[8]{0:T(512)(128)(4,1)}, s32[8]{0:T(128)S(1)}) fusion(s32[8]{0:T(128)S(1)} %concatenate.67), kind=kLoop, calls=%fused_computation.47 | loop fusion | flops 456 | bytes 72 | tf_op jit(solution)/shard_map/gather_over_cand/reduce | solution.py:40
  12.0 3.2 %all-to-all-done = s32[4,1,320]{2,1,0:T(1,128)S(1)} async-done(((s32[4,1,320]{2,1,0:T(1,128)}), s32[4,1,320]{2,1,0:T(1,128)S(1)}, u32[]{:S(2)}, u32[]{:S(2)}) %all-to-all-start) | async-done | bytes 5152 | tf_op jit(solution)/shard_map/all_to_all | solution.py:78
  15.3 0.1 reshape.305
  15.4 6.8 %gather_fusion = bf16[1280,256]{1,0:T(8,128)(2,1)} fusion(bf16[8192,256]{1,0:T(8,128)(2,1)} %param.11, s32[2048]{0:T(1024)S(1)} %pad_clamp_fusion), kind=kCustom, calls=%fused_computation | custom fusion | bytes 1315840 | tf_op jit(solution)/shard_map/jit(_take)/gather | solution.py:79
  22.2 3.5 %all-to-all-start.1 = ((bf16[4,320,256]{2,1,0:T(8,128)(2,1)}), bf16[4,320,256]{2,1,0:T(8,128)(2,1)S(1)}, u32[]{:S(2)}, u32[]{:S(2)}) async-start(bf16[4,320,256]{2,1,0:T(8,128)(2,1)} %bitcast.4), calls=%async_computation.1 | async-start | bytes 1310720 | tf_op jit(solution)/shard_map/all_to_all | solution.py:82
  25.8 8.0 %all-to-all-done.1 = bf16[4,320,256]{2,1,0:T(8,128)(2,1)S(1)} async-done(((bf16[4,320,256]{2,1,0:T(8,128)(2,1)}), bf16[4,320,256]{2,1,0:T(8,128)(2,1)S(1)}, u32[]{:S(2)}, u32[]{:S(2)}) %all-to-all-start.1) | async-done | bytes 655392 | tf_op jit(solution)/shard_map/all_to_all | solution.py:82
  33.9 0.4 convolution_convert_fusion.2
  34.3 0.3 constant_dynamic-update-slice_fusion.4
  34.6 3.7 %collective-permute-start.2 = (bf16[128,256]{1,0:T(8,128)(2,1)S(1)}, bf16[128,256]{1,0:T(8,128)(2,1)S(1)}, u32[]{:S(2)}, u32[]{:S(2)}) collective-permute-start(bf16[128,256]{1,0:T(8,128)(2,1)S(1)} %get-tuple-element.12), channel_id=1, source_target_pairs={{0,6},{1,7},{2,0},{3,1},{4,2},{5,3},{6,4},{7,5},{8,14},{9,15},{10,... | collective-permute-start | bytes 196616 | tf_op jit(solution)/shard_map/ppermute | solution.py:33
  38.2 1.0 %collective-permute-start = (bf16[128,256]{1,0:T(8,128)(2,1)S(1)}, bf16[128,256]{1,0:T(8,128)(2,1)S(1)}, u32[]{:S(2)}, u32[]{:S(2)}) collective-permute-start(bf16[128,256]{1,0:T(8,128)(2,1)S(1)} %get-tuple-element.12), channel_id=1, source_target_pairs={{0,2},{1,3},{2,4},{3,5},{4,6},{5,7},{6,0},{7,1},{8,10},{9,11},{10,... | collective-permute-start | bytes 196616 | tf_op jit(solution)/shard_map/ppermute | solution.py:33
  39.3 0.3 fusion.15
  39.6 0.9 %convolution_convert_fusion.3 = bf16[256,256]{0,1:T(8,128)(2,1)} fusion(bf16[256,256]{1,0:T(8,128)(2,1)S(1)} %convolution_convert_fusion.2, bf16[256,256]{1,0:T(8,128)(2,1)S(1)} %copy-done), kind=kOutput, calls=%fused_computation.12 | convolution fusion | flops 33619968 | bytes 393216 | tf_op jit(solution)/shard_map/dot_general | solution.py:90
  40.4 3.0 %collective-permute-done.1 = bf16[128,256]{1,0:T(8,128)(2,1)S(1)} collective-permute-done((bf16[128,256]{1,0:T(8,128)(2,1)S(1)}, bf16[128,256]{1,0:T(8,128)(2,1)S(1)}, u32[]{:S(2)}, u32[]{:S(2)}) %collective-permute-start.1) | collective-permute-done | bytes 65568 | tf_op jit(solution)/shard_map/ppermute | solution.py:33
  43.4 0.9 %collective-permute-done = bf16[128,256]{1,0:T(8,128)(2,1)S(1)} collective-permute-done((bf16[128,256]{1,0:T(8,128)(2,1)S(1)}, bf16[128,256]{1,0:T(8,128)(2,1)S(1)}, u32[]{:S(2)}, u32[]{:S(2)}) %collective-permute-start) | collective-permute-done | bytes 65568 | tf_op jit(solution)/shard_map/ppermute | solution.py:33
  44.5 1.5 %collective-permute-done.3 = bf16[4,128,256]{2,1,0:T(8,128)(2,1)S(1)} collective-permute-done((bf16[4,128,256]{2,1,0:T(8,128)(2,1)S(1)}, bf16[4,128,256]{2,1,0:T(8,128)(2,1)S(1)}, u32[]{:S(2)}, u32[]{:S(2)}) %collective-permute-start.3) | collective-permute-done | bytes 262176 | tf_op jit(solution)/shard_map/ppermute | solution.py:36
  46.0 0.6 %gather_fusion.1 = bf16[8,128,256]{2,1,0:T(8,128)(2,1)S(1)} fusion(bf16[8,128,256]{2,1,0:T(8,128)(2,1)S(1)} %constant_dynamic-update-slice_fusion, s32[1024]{0:T(1024)S(1)} %pad_clamp_fusion.1), kind=kCustom, calls=%fused_computation.1 | custom fusion | bytes 1048608 | tf_op jit(solution)/shard_map/jit(_take)/gather | solution.py:41
  46.6 0.2 bitcast_select_fusion
  46.8 0.5 convolution_convert_fusion.1
  47.4 2.5 %fusion.8 = bf16[4,64,256]{2,1,0:T(8,128)(2,1)S(1)} fusion(bf16[1024,4,64]{0,2,1:T(8,128)(2,1)S(1)} %bitcast.54, bf16[1024,4,64]{0,2,1:T(8,128)(2,1)S(1)} %bitcast.53, bf16[256,4,64]{0,2,1:T(8,128)(2,1)} %bitcast.58, pred[1024]{0:T(1024)(128)(4,1)S(1)} %iota_compare_fusion.8, f32[]{:T(128)S(6)} %sqrt.3), kind=kOutput, calls=%fused_computation.19 | convolution fusion | flops 274857984 | bytes 1311748 | tf_op jit(solution)/shard_map/bgo,ogl->bgl/dot_general | solution.py:109
  49.9 1.2 %fusion.11 = f32[1,256]{1,0:T(1,128)} fusion(bf16[1024,1]{0,1:T(2,128)(2,1)S(1)} %reshape.321, f32[256,1024]{1,0:T(8,128)S(1)} %fusion.15, bf16[256,256]{0,1:T(8,128)(2,1)S(1)} %bitcast.65, bf16[512,1024]{1,0:T(8,128)(2,1)S(1)} %copy-done.1), kind=kOutput, calls=%fused_computation.21 | convolution fusion | flops 136314880 | bytes 1709056 | tf_op jit(solution)/shard_map/dot_general | solution.py:121
  (29 shorter events, 0.4 us)
Async XLA Ops:
  0.0 39.6 %copy-start = (bf16[256,256]{1,0:T(8,128)(2,1)S(1)}, bf16[256,256]{1,0:T(8,128)(2,1)}, u32[]{:S(2)}) copy-start(bf16[256,256]{1,0:T(8,128)(2,1)} %param.17) | copy-start | bytes 393220
  4.3 21.4 %copy-start.4 = (bf16[1024]{0:T(1024)(128)(2,1)S(1)}, bf16[1024]{0:T(1024)(128)(2,1)}, u32[]{:S(2)}) copy-start(bf16[1024]{0:T(1024)(128)(2,1)} %param.21) | copy-start | bytes 6148
  5.4 9.8 %all-to-all-start = ((s32[4,1,320]{2,1,0:T(1,128)}), s32[4,1,320]{2,1,0:T(1,128)S(1)}, u32[]{:S(2)}, u32[]{:S(2)}) async-start(s32[4,1,320]{2,1,0:T(1,128)} %add.104), calls=%async_computation | async-start | bytes 12288 | tf_op jit(solution)/shard_map/all_to_all | solution.py:78
  15.4 23.9 %copy-start.1 = (bf16[512,1024]{1,0:T(8,128)(2,1)S(1)}, bf16[512,1024]{1,0:T(8,128)(2,1)}, u32[]{:S(2)}) copy-start(bf16[512,1024]{1,0:T(8,128)(2,1)} %param.20) | copy-start | bytes 3145732
  22.2 11.7 %all-to-all-start.1 = ((bf16[4,320,256]{2,1,0:T(8,128)(2,1)}), bf16[4,320,256]{2,1,0:T(8,128)(2,1)S(1)}, u32[]{:S(2)}, u32[]{:S(2)}) async-start(bf16[4,320,256]{2,1,0:T(8,128)(2,1)} %bitcast.4), calls=%async_computation.1 | async-start | bytes 1310720 | tf_op jit(solution)/shard_map/all_to_all | solution.py:82
  25.6 21.1 %copy-start.2 = (bf16[256,256]{1,0:T(8,128)(2,1)S(1)}, bf16[256,256]{1,0:T(8,128)(2,1)}, u32[]{:S(2)}) copy-start(bf16[256,256]{1,0:T(8,128)(2,1)} %param.19) | copy-start | bytes 393220
  25.7 21.1 %copy-start.3 = (bf16[256,256]{1,0:T(8,128)(2,1)S(1)}, bf16[256,256]{1,0:T(8,128)(2,1)}, u32[]{:S(2)}) copy-start(bf16[256,256]{1,0:T(8,128)(2,1)} %param.18) | copy-start | bytes 393220
  34.6 5.9 %collective-permute-start.2 = (bf16[128,256]{1,0:T(8,128)(2,1)S(1)}, bf16[128,256]{1,0:T(8,128)(2,1)S(1)}, u32[]{:S(2)}, u32[]{:S(2)}) collective-permute-start(bf16[128,256]{1,0:T(8,128)(2,1)S(1)} %get-tuple-element.12), channel_id=1, source_target_pairs={{0,6},{1,7},{2,0},{3,1},{4,2},{5,3},{6,4},{7,5},{8,14},{9,15},{10,... | collective-permute-start | bytes 196616 | tf_op jit(solution)/shard_map/ppermute | solution.py:33
  38.2 5.2 %collective-permute-start.1 = (bf16[128,256]{1,0:T(8,128)(2,1)S(1)}, bf16[128,256]{1,0:T(8,128)(2,1)S(1)}, u32[]{:S(2)}, u32[]{:S(2)}) collective-permute-start(bf16[128,256]{1,0:T(8,128)(2,1)S(1)} %get-tuple-element.12), channel_id=1, source_target_pairs={{0,4},{1,5},{2,6},{3,7},{4,0},{5,1},{6,2},{7,3},{8,12},{9,13},{10,... | collective-permute-start | bytes 196616 | tf_op jit(solution)/shard_map/ppermute | solution.py:33
  38.2 6.1 %collective-permute-start = (bf16[128,256]{1,0:T(8,128)(2,1)S(1)}, bf16[128,256]{1,0:T(8,128)(2,1)S(1)}, u32[]{:S(2)}, u32[]{:S(2)}) collective-permute-start(bf16[128,256]{1,0:T(8,128)(2,1)S(1)} %get-tuple-element.12), channel_id=1, source_target_pairs={{0,2},{1,3},{2,4},{3,5},{4,6},{5,7},{6,0},{7,1},{8,10},{9,11},{10,... | collective-permute-start | bytes 196616 | tf_op jit(solution)/shard_map/ppermute | solution.py:33
  44.3 1.6 %collective-permute-start.3 = (bf16[4,128,256]{2,1,0:T(8,128)(2,1)S(1)}, bf16[4,128,256]{2,1,0:T(8,128)(2,1)S(1)}, u32[]{:S(2)}, u32[]{:S(2)}) collective-permute-start(bf16[4,128,256]{2,1,0:T(8,128)(2,1)S(1)} %pad_maximum_fusion), channel_id=1, source_target_pairs={{0,1},{1,0},{2,3},{3,2},{4,5},{5,4},{6,7},{7,6},{8,9},{9,8},{10,11... | collective-permute-start | bytes 786440 | tf_op jit(solution)/shard_map/ppermute | solution.py:36

commit v6 on v5

--- a/solution.py
+++ b/solution.py
@@ -41,6 +41,14 @@
     return jnp.take(held, order, axis=0).reshape(-1, rows.shape[1])
 
 
+def swap_over_req(blocks):
+    n_req = blocks.shape[0]
+    swapped = [blocks[0]]
+    for hop in range(1, n_req):
+        swapped.append(lax.ppermute(blocks[hop], "req", [(i, i ^ hop) for i in range(n_req)]))
+    return jnp.stack(swapped, axis=0)
+
+
 def body(
     table,
     history_shard,
@@ -64,8 +72,10 @@
     cand_cap = 3 * cand_dev // n_dest
     slot_count = hist_cap + cand_cap
     n_slots = n_dest * slot_count
-    hist_slot = slot_index(hist_shards, n_dest, slot_count, 0)
-    cand_slot = slot_index(cand_shards, n_dest, slot_count, hist_cap)
+    assert n_dest & (n_dest - 1) == 0
+    me = lax.axis_index("req")
+    hist_slot = slot_index(hist_shards ^ me, n_dest, slot_count, 0)
+    cand_slot = slot_index(cand_shards ^ me, n_dest, slot_count, hist_cap)
     hist_pick = select_rows(hist_slot, n_slots)
     cand_pick = select_rows(cand_slot, n_slots)
     all_pick = jnp.concatenate([hist_pick, cand_pick], axis=0)
@@ -75,11 +85,11 @@
         all_pick, row_parts, (((0,), (0,)), ((), ())), preferred_element_type=jnp.float32
     ).astype(jnp.int32)
     wanted = (wanted_parts[:, 0] * 128 + wanted_parts[:, 1]).reshape(n_dest, slot_count)
-    asked = lax.all_to_all(wanted, "req", split_axis=0, concat_axis=0, tiled=True)
+    asked = swap_over_req(wanted)
     fetched = jnp.take(table, asked.reshape(-1), axis=0, mode="clip").reshape(
         n_dest, slot_count, d_model
     )
-    replies = lax.all_to_all(fetched, "req", split_axis=0, concat_axis=0, tiled=True)
+    replies = swap_over_req(fetched)
     flat_rows = replies.reshape(n_slots, d_model)
     hist_emb = jnp.dot(hist_pick, flat_rows, preferred_element_type=jnp.float32).astype(jnp.bfloat16)
     cand_emb = jnp.dot(cand_pick, flat_rows, preferred_element_type=jnp.float32).astype(jnp.bfloat16)

time: 51.4 us -> 44.8 us (0.87)
  waiting for transfers between devices: 16.6 us -> 12.7 us
  matrix products: 8.25 us -> 6.77 us
  local copies, waits for them, and re-layouts: 8.42 us -> 7.06 us
  other arithmetic: 3.51 us -> 4.26 us
    all_to_all x2 -> x0, waiting for transfers between devices: 11.3 us -> none  [the longest x1 8.04 us: body(): lax.all_to_all(fetched, 'req', split_axis=0, concat_axis=0, tiled=True)]
    all_to_all x2 -> x0, starting transfers between devices: 8.64 us -> none  [the longest x1 5.16 us: body(): lax.all_to_all(wanted, 'req', split_axis=0, concat_axis=0, tiled=True)]
    ppermute x0 -> x6, starting transfers between devices: none -> 8.1 us  [swap_over_req(): lax.ppermute(blocks[hop], 'req', [(i, i ^ hop) for i in range(n_req)])]
    ppermute x0 -> x6, waiting for transfers between devices: none -> 7.36 us  [swap_over_req(): lax.ppermute(blocks[hop], 'req', [(i, i ^ hop) for i in range(n_req)])]
    dot_general x2, matrix products: 1.83 us -> 0.35 us  [slot_index(): jnp.dot(earlier.astype(jnp.bfloat16), onehot, preferred_element_type=jnp....]
    xor x0 -> x2, other arithmetic: none -> 1.37 us  [the longest x1 0.69 us: body(): hist_slot = slot_index(hist_shards ^ me, n_dest, slot_count, 0)]
    gather x1, local copies, waits for them, and re-layouts: 6.78 us -> 5.96 us  [body(): jnp.take(table, asked.reshape(-1), axis=0, mode='clip')]
    add x2, other arithmetic: 1.37 us -> 0.69 us  [slot_index(): return shard_ids * slot_count + first_slot + rank]
  transfers between devices with their start and end apart: 6 -> 10, of which waited for: 5 -> 7; matrix products, arithmetic and copies ran while one was open for 4% -> 5% of each run, Pallas kernels for 0% -> 0%
where the time goes in v6:
time: 44.8 us; the launch traced here: 44.6 us
  starting transfers between devices  12.9 us (29%)
  waiting for transfers between devices  12.7 us (28%)
  local copies, waits for them, and re-layouts  7.06 us (16%)
  matrix products  6.77 us (15%)
  other arithmetic  4.26 us (10%)
  between operations  0.95 us (2%)
    ppermute x6, starting transfers between devices, swap_over_req(): lax.ppermute(blocks[hop], 'req', [(i, i ^ hop) for i in range(n_req)])  8.1 us
    ppermute x6, waiting for transfers between devices, swap_over_req(): lax.ppermute(blocks[hop], 'req', [(i, i ^ hop) for i in range(n_req)])  7.36 us
    gather x1, local copies, waits for them, and re-layouts, body(): jnp.take(table, asked.reshape(-1), axis=0, mode='clip')  5.96 us
    ppermute x3, starting transfers between devices, gather_over_cand(): lax.ppermute(rows, 'cand', [(i, (i + hop) % n_cand) for i in range(n_cand)])  4.71 us
    ppermute x3, waiting for transfers between devices, gather_over_cand(): lax.ppermute(rows, 'cand', [(i, (i + hop) % n_cand) for i in range(n_cand)])  3.86 us
    dot_general x1, matrix products, body(): jnp.einsum('bgo,ogl->bgl', gate_weights, value_portion_slice, preferred_e...  2.5 us
    ppermute x1, waiting for transfers between devices, gather_over_cand(): partner = lax.ppermute(mine, 'cand', [(i, i ^ 1) for i in range(n_cand)])  1.48 us
    dot_general x1, matrix products, body(): jnp.dot(hidden, tower_out, preferred_element_type=jnp.float32)[None, :]  1.23 us
  transfers between devices with their start and end apart: 10, of which 7 were waited for; matrix products, arithmetic and copies ran while one was open for 5% of the time, Pallas kernels for 0%

profile of v6, /device:TPU:0, one launch (start us, length us, event | category | flops | bytes accessed | tf_op | source)
XLA Modules:
  0.0 44.6 jit_solution(11842293627342462205)
XLA Ops:
  0.0 0.7 %xor_bitcast_fusion = s32[128]{0:T(128)S(1)} fusion(s32[1,128,1]{1,2,0:T(1,128)} %param.12, s32[]{:T(128)S(6)} %axis_index.23), kind=kLoop, calls=%fused_computation.76 | loop fusion | flops 128 | bytes 1028 | tf_op jit(solution)/shard_map/xor | solution.py:77
  0.8 0.7 %convert_add_fusion.1 = s32[128]{0:T(128)S(1)} fusion(f32[128]{0:T(128)S(1)} %fusion.4, s32[1,128,1]{1,2,0:T(1,128)} %param.12, s32[]{:T(128)S(6)} %axis_index.23), kind=kLoop, calls=%fused_computation.75 | loop fusion | flops 512 | bytes 1540 | tf_op jit(solution)/shard_map/add | solution.py:19
  1.5 0.7 %broadcast_xor_fusion = s32[1,256,1]{1,2,0:T(1,128)S(1)} fusion(s32[1,256,1]{1,2,0:T(1,128)} %param.14, s32[]{:T(128)S(6)} %axis_index.23), kind=kLoop, calls=%fused_computation.77 | loop fusion | flops 256 | bytes 2052 | tf_op jit(solution)/shard_map/xor | solution.py:78
  2.2 0.2 fusion.3
  2.4 0.7 %fusion.27 = (bf16[384,1]{0,1:T(2,128)(2,1)S(1)}, s32[384,1]{0,1:T(1,128)S(1)}) fusion(s32[256,1]{0,1:T(1,128)} %bitcast.73, s32[128,1]{0,1:T(1,128)} %bitcast.74), kind=kLoop, calls=%fused_computation.71 | loop fusion | flops 6528 | bytes 3840 | tf_op jit(solution)/shard_map/convert.1
  3.3 0.2 iota_compare_fusion
  3.6 0.3 convolution_convert_fusion
  4.0 3.0 %collective-permute-start = (s32[320]{0:T(512)S(1)}, s32[320]{0:T(512)S(1)}, u32[]{:S(2)}, u32[]{:S(2)}) collective-permute-start(s32[320]{0:T(512)S(1)} %get-tuple-element.7), channel_id=1, source_target_pairs={{0,8},{8,0},{16,24},{24,16},{1,9},{9,1},{17,25},{25,17},{2,10},{10... | collective-permute-start | bytes 3848 | tf_op jit(solution)/shard_map/ppermute | solution.py:48
  7.0 1.5 %collective-permute-start.2 = (s32[320]{0:T(512)S(1)}, s32[320]{0:T(512)S(1)}, u32[]{:S(2)}, u32[]{:S(2)}) collective-permute-start(s32[320]{0:T(512)S(1)} %get-tuple-element.8), channel_id=1, source_target_pairs={{0,24},{8,16},{16,8},{24,0},{1,25},{9,17},{17,9},{25,1},{2,26},{10... | collective-permute-start | bytes 3848 | tf_op jit(solution)/shard_map/ppermute | solution.py:48
  8.7 0.6 %iota_reduce_fusion = (pred[8]{0:T(512)(128)(4,1)}, s32[8]{0:T(128)S(1)}) fusion(s32[8]{0:T(128)S(1)} %concatenate.67), kind=kLoop, calls=%fused_computation.49 | loop fusion | flops 456 | bytes 72 | tf_op jit(solution)/shard_map/gather_over_cand/reduce | solution.py:40
  10.1 1.4 %collective-permute-done.2 = s32[320]{0:T(512)S(1)} collective-permute-done((s32[320]{0:T(512)S(1)}, s32[320]{0:T(512)S(1)}, u32[]{:S(2)}, u32[]{:S(2)}) %collective-permute-start.2) | collective-permute-done | bytes 1312 | tf_op jit(solution)/shard_map/ppermute | solution.py:48
  11.5 0.6 %collective-permute-done.1 = s32[320]{0:T(512)S(1)} collective-permute-done((s32[320]{0:T(512)S(1)}, s32[320]{0:T(512)S(1)}, u32[]{:S(2)}, u32[]{:S(2)}) %collective-permute-start.1) | collective-permute-done | bytes 1312 | tf_op jit(solution)/shard_map/ppermute | solution.py:48
  12.2 6.0 %gather_fusion = bf16[1280,256]{1,0:T(8,128)(2,1)S(1)} fusion(bf16[8192,256]{1,0:T(8,128)(2,1)} %param.11, s32[2048]{0:T(1024)S(1)} %pad_clamp_fusion), kind=kCustom, calls=%fused_computation | custom fusion | bytes 1315840 | tf_op jit(solution)/shard_map/jit(_take)/gather | solution.py:89
  18.2 1.0 %collective-permute-start.4 = (bf16[320,256]{1,0:T(8,128)(2,1)S(1)}, bf16[320,256]{1,0:T(8,128)(2,1)S(1)}, u32[]{:S(2)}, u32[]{:S(2)}) collective-permute-start(bf16[320,256]{1,0:T(8,128)(2,1)S(1)} %get-tuple-element.15), channel_id=1, source_target_pairs={{0,16},{8,24},{16,0},{24,8},{1,17},{9,25},{17,1},{25,9},{2,18},{10... | collective-permute-start | bytes 491528 | tf_op jit(solution)/shard_map/ppermute | solution.py:48
  19.2 1.1 %collective-permute-start.3 = (bf16[320,256]{1,0:T(8,128)(2,1)S(1)}, bf16[320,256]{1,0:T(8,128)(2,1)S(1)}, u32[]{:S(2)}, u32[]{:S(2)}) collective-permute-start(bf16[320,256]{1,0:T(8,128)(2,1)S(1)} %get-tuple-element.16), channel_id=1, source_target_pairs={{0,8},{8,0},{16,24},{24,16},{1,9},{9,1},{17,25},{25,17},{2,10},{10... | collective-permute-start | bytes 491528 | tf_op jit(solution)/shard_map/ppermute | solution.py:48
  20.3 1.5 %collective-permute-start.5 = (bf16[320,256]{1,0:T(8,128)(2,1)S(1)}, bf16[320,256]{1,0:T(8,128)(2,1)S(1)}, u32[]{:S(2)}, u32[]{:S(2)}) collective-permute-start(bf16[320,256]{1,0:T(8,128)(2,1)S(1)} %get-tuple-element.17), channel_id=1, source_target_pairs={{0,24},{8,16},{16,8},{24,0},{1,25},{9,17},{17,9},{25,1},{2,26},{10... | collective-permute-start | bytes 491528 | tf_op jit(solution)/shard_map/ppermute | solution.py:48
  21.9 3.5 %collective-permute-done.4 = bf16[320,256]{1,0:T(8,128)(2,1)S(1)} collective-permute-done((bf16[320,256]{1,0:T(8,128)(2,1)S(1)}, bf16[320,256]{1,0:T(8,128)(2,1)S(1)}, u32[]{:S(2)}, u32[]{:S(2)}) %collective-permute-start.4) | collective-permute-done | bytes 163872 | tf_op jit(solution)/shard_map/ppermute | solution.py:48
  25.4 1.9 %collective-permute-done.5 = bf16[320,256]{1,0:T(8,128)(2,1)S(1)} collective-permute-done((bf16[320,256]{1,0:T(8,128)(2,1)S(1)}, bf16[320,256]{1,0:T(8,128)(2,1)S(1)}, u32[]{:S(2)}, u32[]{:S(2)}) %collective-permute-start.5) | collective-permute-done | bytes 163872 | tf_op jit(solution)/shard_map/ppermute | solution.py:48
  27.4 0.4 convolution_convert_fusion.2
  27.8 0.3 constant_dynamic-update-slice_fusion.4
  28.1 3.7 %collective-permute-start.8 = (bf16[128,256]{1,0:T(8,128)(2,1)S(1)}, bf16[128,256]{1,0:T(8,128)(2,1)S(1)}, u32[]{:S(2)}, u32[]{:S(2)}) collective-permute-start(bf16[128,256]{1,0:T(8,128)(2,1)S(1)} %get-tuple-element.20), channel_id=1, source_target_pairs={{0,6},{1,7},{2,0},{3,1},{4,2},{5,3},{6,4},{7,5},{8,14},{9,15},{10,... | collective-permute-start | bytes 196616 | tf_op jit(solution)/shard_map/ppermute | solution.py:33
  31.8 1.0 %collective-permute-start.6 = (bf16[128,256]{1,0:T(8,128)(2,1)S(1)}, bf16[128,256]{1,0:T(8,128)(2,1)S(1)}, u32[]{:S(2)}, u32[]{:S(2)}) collective-permute-start(bf16[128,256]{1,0:T(8,128)(2,1)S(1)} %get-tuple-element.20), channel_id=1, source_target_pairs={{0,2},{1,3},{2,4},{3,5},{4,6},{5,7},{6,0},{7,1},{8,10},{9,11},{10,... | collective-permute-start | bytes 196616 | tf_op jit(solution)/shard_map/ppermute | solution.py:33
  32.8 0.3 fusion.15
  33.1 0.9 %convolution_convert_fusion.3 = bf16[256,256]{0,1:T(8,128)(2,1)} fusion(bf16[256,256]{1,0:T(8,128)(2,1)S(1)} %convolution_convert_fusion.2, bf16[256,256]{1,0:T(8,128)(2,1)S(1)} %copy-done), kind=kOutput, calls=%fused_computation.12 | convolution fusion | flops 33619968 | bytes 393216 | tf_op jit(solution)/shard_map/dot_general | solution.py:100
  34.0 3.0 %collective-permute-done.7 = bf16[128,256]{1,0:T(8,128)(2,1)S(1)} collective-permute-done((bf16[128,256]{1,0:T(8,128)(2,1)S(1)}, bf16[128,256]{1,0:T(8,128)(2,1)S(1)}, u32[]{:S(2)}, u32[]{:S(2)}) %collective-permute-start.7) | collective-permute-done | bytes 65568 | tf_op jit(solution)/shard_map/ppermute | solution.py:33
  36.9 0.9 %collective-permute-done.6 = bf16[128,256]{1,0:T(8,128)(2,1)S(1)} collective-permute-done((bf16[128,256]{1,0:T(8,128)(2,1)S(1)}, bf16[128,256]{1,0:T(8,128)(2,1)S(1)}, u32[]{:S(2)}, u32[]{:S(2)}) %collective-permute-start.6) | collective-permute-done | bytes 65568 | tf_op jit(solution)/shard_map/ppermute | solution.py:33
  38.0 1.5 %collective-permute-done.9 = bf16[4,128,256]{2,1,0:T(8,128)(2,1)S(1)} collective-permute-done((bf16[4,128,256]{2,1,0:T(8,128)(2,1)S(1)}, bf16[4,128,256]{2,1,0:T(8,128)(2,1)S(1)}, u32[]{:S(2)}, u32[]{:S(2)}) %collective-permute-start.9) | collective-permute-done | bytes 262176 | tf_op jit(solution)/shard_map/ppermute | solution.py:36
  39.5 0.6 %gather_fusion.1 = bf16[8,128,256]{2,1,0:T(8,128)(2,1)S(1)} fusion(bf16[8,128,256]{2,1,0:T(8,128)(2,1)S(1)} %constant_dynamic-update-slice_fusion, s32[1024]{0:T(1024)S(1)} %pad_clamp_fusion.1), kind=kCustom, calls=%fused_computation.1 | custom fusion | bytes 1048608 | tf_op jit(solution)/shard_map/jit(_take)/gather | solution.py:41
  40.1 0.2 bitcast_select_fusion
  40.3 0.5 %convolution_convert_fusion.1 = bf16[1024,512]{0,1:T(8,128)(2,1)S(1)} fusion(bf16[1024,256]{1,0:T(8,128)(2,1)S(1)} %bitcast_select_fusion, bf16[256,256]{1,0:T(8,128)(2,1)S(1)} %copy-done.2, bf16[256,256]{1,0:T(8,128)(2,1)S(1)} %copy-done.3), kind=kOutput, calls=%fused_computation.8 | convolution fusion | flops 269484032 | bytes 1835008 | tf_op jit(solution)/shard_map/dot_general | solution.py:105
  40.9 2.5 %fusion.8 = bf16[4,64,256]{2,1,0:T(8,128)(2,1)S(1)} fusion(bf16[1024,4,64]{0,2,1:T(8,128)(2,1)S(1)} %bitcast.62, bf16[1024,4,64]{0,2,1:T(8,128)(2,1)S(1)} %bitcast.61, bf16[256,4,64]{0,2,1:T(8,128)(2,1)} %bitcast.69, pred[1024]{0:T(1024)(128)(4,1)S(1)} %iota_compare_fusion.8, f32[]{:T(128)S(6)} %sqrt.3), kind=kOutput, calls=%fused_computation.19 | convolution fusion | flops 274857984 | bytes 1311748 | tf_op jit(solution)/shard_map/bgo,ogl->bgl/dot_general | solution.py:119
  43.4 1.2 %fusion.11 = f32[1,256]{1,0:T(1,128)} fusion(bf16[1024,1]{0,1:T(2,128)(2,1)S(1)} %reshape.322, f32[256,1024]{1,0:T(8,128)S(1)} %fusion.15, bf16[256,256]{0,1:T(8,128)(2,1)S(1)} %bitcast.75, bf16[512,1024]{1,0:T(8,128)(2,1)S(1)} %copy-done.1), kind=kOutput, calls=%fused_computation.21 | convolution fusion | flops 136314880 | bytes 1709056 | tf_op jit(solution)/shard_map/dot_general | solution.py:131
  (44 shorter events, 1.2 us)
Async XLA Ops:
  0.0 33.1 %copy-start = (bf16[256,256]{1,0:T(8,128)(2,1)S(1)}, bf16[256,256]{1,0:T(8,128)(2,1)}, u32[]{:S(2)}) copy-start(bf16[256,256]{1,0:T(8,128)(2,1)} %param.17) | copy-start | bytes 393220
  3.6 18.3 %copy-start.4 = (bf16[1024]{0:T(1024)(128)(2,1)S(1)}, bf16[1024]{0:T(1024)(128)(2,1)}, u32[]{:S(2)}) copy-start(bf16[1024]{0:T(1024)(128)(2,1)} %param.21) | copy-start | bytes 6148
  4.0 6.1 %collective-permute-start = (s32[320]{0:T(512)S(1)}, s32[320]{0:T(512)S(1)}, u32[]{:S(2)}, u32[]{:S(2)}) collective-permute-start(s32[320]{0:T(512)S(1)} %get-tuple-element.7), channel_id=1, source_target_pairs={{0,8},{8,0},{16,24},{24,16},{1,9},{9,1},{17,25},{25,17},{2,10},{10... | collective-permute-start | bytes 3848 | tf_op jit(solution)/shard_map/ppermute | solution.py:48
  7.0 4.5 %collective-permute-start.2 = (s32[320]{0:T(512)S(1)}, s32[320]{0:T(512)S(1)}, u32[]{:S(2)}, u32[]{:S(2)}) collective-permute-start(s32[320]{0:T(512)S(1)} %get-tuple-element.8), channel_id=1, source_target_pairs={{0,24},{8,16},{16,8},{24,0},{1,25},{9,17},{17,9},{25,1},{2,26},{10... | collective-permute-start | bytes 3848 | tf_op jit(solution)/shard_map/ppermute | solution.py:48
  8.5 3.6 %collective-permute-start.1 = (s32[320]{0:T(512)S(1)}, s32[320]{0:T(512)S(1)}, u32[]{:S(2)}, u32[]{:S(2)}) collective-permute-start(s32[320]{0:T(512)S(1)} %get-tuple-element.9), channel_id=1, source_target_pairs={{0,16},{8,24},{16,0},{24,8},{1,17},{9,25},{17,1},{25,9},{2,18},{10... | collective-permute-start | bytes 3848 | tf_op jit(solution)/shard_map/ppermute | solution.py:48
  12.2 20.6 %copy-start.1 = (bf16[512,1024]{1,0:T(8,128)(2,1)S(1)}, bf16[512,1024]{1,0:T(8,128)(2,1)}, u32[]{:S(2)}) copy-start(bf16[512,1024]{1,0:T(8,128)(2,1)} %param.20) | copy-start | bytes 3145732
  18.2 7.1 %collective-permute-start.4 = (bf16[320,256]{1,0:T(8,128)(2,1)S(1)}, bf16[320,256]{1,0:T(8,128)(2,1)S(1)}, u32[]{:S(2)}, u32[]{:S(2)}) collective-permute-start(bf16[320,256]{1,0:T(8,128)(2,1)S(1)} %get-tuple-element.15), channel_id=1, source_target_pairs={{0,16},{8,24},{16,0},{24,8},{1,17},{9,25},{17,1},{25,9},{2,18},{10... | collective-permute-start | bytes 491528 | tf_op jit(solution)/shard_map/ppermute | solution.py:48
  19.2 6.1 %collective-permute-start.3 = (bf16[320,256]{1,0:T(8,128)(2,1)S(1)}, bf16[320,256]{1,0:T(8,128)(2,1)S(1)}, u32[]{:S(2)}, u32[]{:S(2)}) collective-permute-start(bf16[320,256]{1,0:T(8,128)(2,1)S(1)} %get-tuple-element.16), channel_id=1, source_target_pairs={{0,8},{8,0},{16,24},{24,16},{1,9},{9,1},{17,25},{25,17},{2,10},{10... | collective-permute-start | bytes 491528 | tf_op jit(solution)/shard_map/ppermute | solution.py:48
  20.3 7.0 %collective-permute-start.5 = (bf16[320,256]{1,0:T(8,128)(2,1)S(1)}, bf16[320,256]{1,0:T(8,128)(2,1)S(1)}, u32[]{:S(2)}, u32[]{:S(2)}) collective-permute-start(bf16[320,256]{1,0:T(8,128)(2,1)S(1)} %get-tuple-element.17), channel_id=1, source_target_pairs={{0,24},{8,16},{16,8},{24,0},{1,25},{9,17},{17,9},{25,1},{2,26},{10... | collective-permute-start | bytes 491528 | tf_op jit(solution)/shard_map/ppermute | solution.py:48
  27.3 13.0 %copy-start.2 = (bf16[256,256]{1,0:T(8,128)(2,1)S(1)}, bf16[256,256]{1,0:T(8,128)(2,1)}, u32[]{:S(2)}) copy-start(bf16[256,256]{1,0:T(8,128)(2,1)} %param.19) | copy-start | bytes 393220
  27.3 13.0 %copy-start.3 = (bf16[256,256]{1,0:T(8,128)(2,1)S(1)}, bf16[256,256]{1,0:T(8,128)(2,1)}, u32[]{:S(2)}) copy-start(bf16[256,256]{1,0:T(8,128)(2,1)} %param.18) | copy-start | bytes 393220
  28.1 5.9 %collective-permute-start.8 = (bf16[128,256]{1,0:T(8,128)(2,1)S(1)}, bf16[128,256]{1,0:T(8,128)(2,1)S(1)}, u32[]{:S(2)}, u32[]{:S(2)}) collective-permute-start(bf16[128,256]{1,0:T(8,128)(2,1)S(1)} %get-tuple-element.20), channel_id=1, source_target_pairs={{0,6},{1,7},{2,0},{3,1},{4,2},{5,3},{6,4},{7,5},{8,14},{9,15},{10,... | collective-permute-start | bytes 196616 | tf_op jit(solution)/shard_map/ppermute | solution.py:33
  31.8 5.2 %collective-permute-start.7 = (bf16[128,256]{1,0:T(8,128)(2,1)S(1)}, bf16[128,256]{1,0:T(8,128)(2,1)S(1)}, u32[]{:S(2)}, u32[]{:S(2)}) collective-permute-start(bf16[128,256]{1,0:T(8,128)(2,1)S(1)} %get-tuple-element.20), channel_id=1, source_target_pairs={{0,4},{1,5},{2,6},{3,7},{4,0},{5,1},{6,2},{7,3},{8,12},{9,13},{10,... | collective-permute-start | bytes 196616 | tf_op jit(solution)/shard_map/ppermute | solution.py:33
  31.8 6.1 %collective-permute-start.6 = (bf16[128,256]{1,0:T(8,128)(2,1)S(1)}, bf16[128,256]{1,0:T(8,128)(2,1)S(1)}, u32[]{:S(2)}, u32[]{:S(2)}) collective-permute-start(bf16[128,256]{1,0:T(8,128)(2,1)S(1)} %get-tuple-element.20), channel_id=1, source_target_pairs={{0,2},{1,3},{2,4},{3,5},{4,6},{5,7},{6,0},{7,1},{8,10},{9,11},{10,... | collective-permute-start | bytes 196616 | tf_op jit(solution)/shard_map/ppermute | solution.py:33
  37.9 1.6 %collective-permute-start.9 = (bf16[4,128,256]{2,1,0:T(8,128)(2,1)S(1)}, bf16[4,128,256]{2,1,0:T(8,128)(2,1)S(1)}, u32[]{:S(2)}, u32[]{:S(2)}) collective-permute-start(bf16[4,128,256]{2,1,0:T(8,128)(2,1)S(1)} %pad_maximum_fusion.1), channel_id=1, source_target_pairs={{0,1},{1,0},{2,3},{3,2},{4,5},{5,4},{6,7},{7,6},{8,9},{9,8},{10,11... | collective-permute-start | bytes 786440 | tf_op jit(solution)/shard_map/ppermute | solution.py:36

commit v7 on v6

--- a/solution.py
+++ b/solution.py
@@ -41,6 +41,14 @@
     return jnp.take(held, order, axis=0).reshape(-1, rows.shape[1])
 
 
+def wanted_rows(pick, rows):
+    row_parts = jnp.stack([rows // 128, rows % 128], axis=1).astype(jnp.bfloat16)
+    parts = lax.dot_general(
+        pick, row_parts, (((0,), (0,)), ((), ())), preferred_element_type=jnp.float32
+    ).astype(jnp.int32)
+    return parts[:, 0] * 128 + parts[:, 1]
+
+
 def swap_over_req(blocks):
     n_req = blocks.shape[0]
     swapped = [blocks[0]]
@@ -70,29 +78,22 @@
     cand_dev = cand_shards.shape[0]
     hist_cap = 4 * hist_dev // n_dest
     cand_cap = 3 * cand_dev // n_dest
-    slot_count = hist_cap + cand_cap
-    n_slots = n_dest * slot_count
     assert n_dest & (n_dest - 1) == 0
     me = lax.axis_index("req")
-    hist_slot = slot_index(hist_shards ^ me, n_dest, slot_count, 0)
-    cand_slot = slot_index(cand_shards ^ me, n_dest, slot_count, hist_cap)
-    hist_pick = select_rows(hist_slot, n_slots)
-    cand_pick = select_rows(cand_slot, n_slots)
-    all_pick = jnp.concatenate([hist_pick, cand_pick], axis=0)
-    all_rows = jnp.concatenate([history_row[0], candidate_row[0]], axis=0)
-    row_parts = jnp.stack([all_rows // 128, all_rows % 128], axis=1).astype(jnp.bfloat16)
-    wanted_parts = lax.dot_general(
-        all_pick, row_parts, (((0,), (0,)), ((), ())), preferred_element_type=jnp.float32
-    ).astype(jnp.int32)
-    wanted = (wanted_parts[:, 0] * 128 + wanted_parts[:, 1]).reshape(n_dest, slot_count)
-    asked = swap_over_req(wanted)
+    hist_slot = slot_index(hist_shards ^ me, n_dest, hist_cap, 0)
+    cand_slot = slot_index(cand_shards ^ me, n_dest, cand_cap, 0)
+    hist_pick = select_rows(hist_slot, n_dest * hist_cap)
+    cand_pick = select_rows(cand_slot, n_dest * cand_cap)
+    hist_wanted = wanted_rows(hist_pick, history_row[0]).reshape(n_dest, hist_cap)
+    cand_wanted = wanted_rows(cand_pick, candidate_row[0]).reshape(n_dest, cand_cap)
+    asked = swap_over_req(jnp.concatenate([hist_wanted, cand_wanted], axis=1))
     fetched = jnp.take(table, asked.reshape(-1), axis=0, mode="clip").reshape(
-        n_dest, slot_count, d_model
+        n_dest, hist_cap + cand_cap, d_model
     )
-    replies = swap_over_req(fetched)
-    flat_rows = replies.reshape(n_slots, d_model)
-    hist_emb = jnp.dot(hist_pick, flat_rows, preferred_element_type=jnp.float32).astype(jnp.bfloat16)
-    cand_emb = jnp.dot(cand_pick, flat_rows, preferred_element_type=jnp.float32).astype(jnp.bfloat16)
+    hist_replies = swap_over_req(fetched[:, :hist_cap]).reshape(n_dest * hist_cap, d_model)
+    cand_replies = swap_over_req(fetched[:, hist_cap:]).reshape(n_dest * cand_cap, d_model)
+    hist_emb = jnp.dot(hist_pick, hist_replies, preferred_element_type=jnp.float32).astype(jnp.bfloat16)
+    cand_emb = jnp.dot(cand_pick, cand_replies, preferred_element_type=jnp.float32).astype(jnp.bfloat16)
     head_size = d_model // HEADS
     scale_factor = 1.0 / math.sqrt(head_size)
     length = history_length[0]

time: 44.8 us -> 43.6 us (0.973)
  waiting for transfers between devices: 12.7 us -> 6.69 us
  starting transfers between devices: 12.9 us -> 16.7 us
  local copies, waits for them, and re-layouts: 7.06 us -> 7.72 us
    ppermute x6 -> x9, waiting for transfers between devices: 7.36 us -> 1.75 us  [swap_over_req(): lax.ppermute(blocks[hop], 'req', [(i, i ^ hop) for i in range(n_req)])]
    ppermute x6 -> x9, starting transfers between devices: 8.1 us -> 12 us  [swap_over_req(): lax.ppermute(blocks[hop], 'req', [(i, i ^ hop) for i in range(n_req)])]
    unnamed x14 -> x12, local copies, waits for them, and re-layouts: 0.05 us -> 0.73 us
    another operation x2 -> x3, other arithmetic: 0.7 us -> 1.36 us
    dot_general x3 -> x4, matrix products: 1.03 us -> 1.07 us  [the longest x2 0.52 us: wanted_rows(): lax.dot_general(pick, row_parts, (((0,), (0,)), ((), ())), preferred_elem...]
  transfers between devices with their start and end apart: 10 -> 13, of which waited for: 7 -> 6; matrix products, arithmetic and copies ran while one was open for 5% -> 8% of each run, Pallas kernels for 0% -> 0%
where the time goes in v7:
time: 43.6 us; the launch traced here: 43.4 us
  starting transfers between devices  16.7 us (38%)
  local copies, waits for them, and re-layouts  7.72 us (18%)
  matrix products  6.8 us (16%)
  waiting for transfers between devices  6.69 us (15%)
  other arithmetic  4.56 us (10%)
  between operations  0.93 us (2%)
    ppermute x9, starting transfers between devices, swap_over_req(): lax.ppermute(blocks[hop], 'req', [(i, i ^ hop) for i in range(n_req)])  12 us
    gather x1, local copies, waits for them, and re-layouts, body(): jnp.take(table, asked.reshape(-1), axis=0, mode='clip')  5.96 us
    ppermute x3, starting transfers between devices, gather_over_cand(): lax.ppermute(rows, 'cand', [(i, (i + hop) % n_cand) for i in range(n_cand)])  4.69 us
    ppermute x3, waiting for transfers between devices, gather_over_cand(): lax.ppermute(rows, 'cand', [(i, (i + hop) % n_cand) for i in range(n_cand)])  3.47 us
    dot_general x1, matrix products, body(): jnp.einsum('bgo,ogl->bgl', gate_weights, value_portion_slice, preferred_e...  2.49 us
    ppermute x9, waiting for transfers between devices, swap_over_req(): lax.ppermute(blocks[hop], 'req', [(i, i ^ hop) for i in range(n_req)])  1.75 us
    ppermute x1, waiting for transfers between devices, gather_over_cand(): partner = lax.ppermute(mine, 'cand', [(i, i ^ 1) for i in range(n_cand)])  1.48 us
    another operation x3, other arithmetic  1.36 us
  transfers between devices with their start and end apart: 13, of which 6 were waited for; matrix products, arithmetic and copies ran while one was open for 8% of the time, Pallas kernels for 0%

profile of v7, /device:TPU:0, one launch (start us, length us, event | category | flops | bytes accessed | tf_op | source)
XLA Modules:
  0.0 43.4 jit_solution(15522668107941587674)
XLA Ops:
  0.0 0.7 %xor_bitcast_fusion = s32[128]{0:T(128)S(1)} fusion(s32[1,128,1]{1,2,0:T(1,128)} %param.12, s32[]{:T(128)S(6)} %axis_index.23), kind=kLoop, calls=%fused_computation.107 | loop fusion | flops 128 | bytes 1028 | tf_op jit(solution)/shard_map/xor | solution.py:83
  0.8 0.7 %convert_add_fusion.1 = s32[128]{0:T(128)S(1)} fusion(f32[128]{0:T(128)S(1)} %fusion.3, s32[1,128,1]{1,2,0:T(1,128)} %param.12, s32[]{:T(128)S(6)} %axis_index.23), kind=kLoop, calls=%fused_computation.106 | loop fusion | flops 512 | bytes 1540 | tf_op jit(solution)/shard_map/add | solution.py:19
  1.5 0.7 %broadcast_xor_fusion = s32[1,256,1]{1,2,0:T(1,128)S(1)} fusion(s32[1,256,1]{1,2,0:T(1,128)} %param.14, s32[]{:T(128)S(6)} %axis_index.23), kind=kLoop, calls=%fused_computation.108 | loop fusion | flops 256 | bytes 2052 | tf_op jit(solution)/shard_map/xor | solution.py:84
  2.4 0.7 %fusion.43 = (bf16[128,1]{0,1:T(2,128)(2,1)S(1)}, bf16[128,1]{0,1:T(2,128)(2,1)S(1)}) fusion(s32[1,128]{1,0:T(1,128)} %param.13), kind=kLoop, calls=%fused_computation.109 | loop fusion | flops 2688 | bytes 1024 | tf_op jit(solution)/shard_map/convert.2
  3.1 0.7 %fusion.38 = (bf16[256,1]{0,1:T(2,128)(2,1)S(1)}, s32[256,1]{0,1:T(1,128)S(1)}) fusion(s32[1,256]{1,0:T(1,128)} %param.15), kind=kLoop, calls=%fused_computation.99 | loop fusion | flops 4096 | bytes 2560 | tf_op jit(solution)/shard_map/convert
  4.0 0.3 convolution_convert_fusion.4
  4.5 3.0 %collective-permute-start = (s32[320]{0:T(512)S(1)}, s32[320]{0:T(512)S(1)}, u32[]{:S(2)}, u32[]{:S(2)}) collective-permute-start(s32[320]{0:T(512)S(1)} %get-tuple-element.7), channel_id=1, source_target_pairs={{0,8},{8,0},{16,24},{24,16},{1,9},{9,1},{17,25},{25,17},{2,10},{10... | collective-permute-start | bytes 3848 | tf_op jit(solution)/shard_map/ppermute | solution.py:56
  7.5 1.5 %collective-permute-start.2 = (s32[320]{0:T(512)S(1)}, s32[320]{0:T(512)S(1)}, u32[]{:S(2)}, u32[]{:S(2)}) collective-permute-start(s32[320]{0:T(512)S(1)} %get-tuple-element.8), channel_id=1, source_target_pairs={{0,24},{8,16},{16,8},{24,0},{1,25},{9,17},{17,9},{25,1},{2,26},{10... | collective-permute-start | bytes 3848 | tf_op jit(solution)/shard_map/ppermute | solution.py:56
  9.2 0.6 %iota_reduce_fusion = (pred[8]{0:T(512)(128)(4,1)}, s32[8]{0:T(128)S(1)}) fusion(s32[8]{0:T(128)S(1)} %concatenate.15), kind=kLoop, calls=%fused_computation.60 | loop fusion | flops 456 | bytes 72 | tf_op jit(solution)/shard_map/gather_over_cand/reduce | solution.py:40
  10.6 0.7 %reshape.305 = bf16[1024,1]{0,1:T(2,128)(2,1)S(1)} reshape(bf16[1024]{0:T(1024)(128)(2,1)} %param.21) | data formatting | bytes 4096 | tf_op args[10]
  11.3 0.6 %collective-permute-done.2 = s32[320]{0:T(512)S(1)} collective-permute-done((s32[320]{0:T(512)S(1)}, s32[320]{0:T(512)S(1)}, u32[]{:S(2)}, u32[]{:S(2)}) %collective-permute-start.2) | collective-permute-done | bytes 1312 | tf_op jit(solution)/shard_map/ppermute | solution.py:56
  12.0 0.6 %collective-permute-done.1 = s32[320]{0:T(512)S(1)} collective-permute-done((s32[320]{0:T(512)S(1)}, s32[320]{0:T(512)S(1)}, u32[]{:S(2)}, u32[]{:S(2)}) %collective-permute-start.1) | collective-permute-done | bytes 1312 | tf_op jit(solution)/shard_map/ppermute | solution.py:56
  12.7 6.0 %gather_fusion = bf16[1280,256]{1,0:T(8,128)(2,1)S(1)} fusion(bf16[8192,256]{1,0:T(8,128)(2,1)} %param.11, s32[2048]{0:T(1024)S(1)} %pad_clamp_fusion), kind=kCustom, calls=%fused_computation | custom fusion | bytes 1315840 | tf_op jit(solution)/shard_map/jit(_take)/gather | solution.py:90
  18.7 1.8 %collective-permute-start.8 = (bf16[128,256]{1,0:T(8,128)(2,1)S(1)}, bf16[128,256]{1,0:T(8,128)(2,1)S(1)}, u32[]{:S(2)}, u32[]{:S(2)}) collective-permute-start(bf16[128,256]{1,0:T(8,128)(2,1)S(1)} %get-tuple-element.15), channel_id=1, source_target_pairs={{0,24},{8,16},{16,8},{24,0},{1,25},{9,17},{17,9},{25,1},{2,26},{10... | collective-permute-start | bytes 196616 | tf_op jit(solution)/shard_map/ppermute | solution.py:56
  20.4 1.2 %collective-permute-start.7 = (bf16[128,256]{1,0:T(8,128)(2,1)S(1)}, bf16[128,256]{1,0:T(8,128)(2,1)S(1)}, u32[]{:S(2)}, u32[]{:S(2)}) collective-permute-start(bf16[128,256]{1,0:T(8,128)(2,1)S(1)} %get-tuple-element.16), channel_id=1, source_target_pairs={{0,16},{8,24},{16,0},{24,8},{1,17},{9,25},{17,1},{25,9},{2,18},{10... | collective-permute-start | bytes 196616 | tf_op jit(solution)/shard_map/ppermute | solution.py:56
  21.7 0.5 %collective-permute-start.6 = (bf16[128,256]{1,0:T(8,128)(2,1)S(1)}, bf16[128,256]{1,0:T(8,128)(2,1)S(1)}, u32[]{:S(2)}, u32[]{:S(2)}) collective-permute-start(bf16[128,256]{1,0:T(8,128)(2,1)S(1)} %get-tuple-element.17), channel_id=1, source_target_pairs={{0,8},{8,0},{16,24},{24,16},{1,9},{9,1},{17,25},{25,17},{2,10},{10... | collective-permute-start | bytes 196616 | tf_op jit(solution)/shard_map/ppermute | solution.py:56
  22.3 1.8 %collective-permute-start.5 = (bf16[192,256]{1,0:T(8,128)(2,1)S(1)}, bf16[192,256]{1,0:T(8,128)(2,1)S(1)}, u32[]{:S(2)}, u32[]{:S(2)}) collective-permute-start(bf16[192,256]{1,0:T(8,128)(2,1)S(1)} %get-tuple-element.19), channel_id=1, source_target_pairs={{0,24},{8,16},{16,8},{24,0},{1,25},{9,17},{17,9},{25,1},{2,26},{10... | collective-permute-start | bytes 294920 | tf_op jit(solution)/shard_map/ppermute | solution.py:56
  24.0 1.2 %collective-permute-start.4 = (bf16[192,256]{1,0:T(8,128)(2,1)S(1)}, bf16[192,256]{1,0:T(8,128)(2,1)S(1)}, u32[]{:S(2)}, u32[]{:S(2)}) collective-permute-start(bf16[192,256]{1,0:T(8,128)(2,1)S(1)} %get-tuple-element.20), channel_id=1, source_target_pairs={{0,16},{8,24},{16,0},{24,8},{1,17},{9,25},{17,1},{25,9},{2,18},{10... | collective-permute-start | bytes 294920 | tf_op jit(solution)/shard_map/ppermute | solution.py:56
  25.3 0.8 %collective-permute-start.3 = (bf16[192,256]{1,0:T(8,128)(2,1)S(1)}, bf16[192,256]{1,0:T(8,128)(2,1)S(1)}, u32[]{:S(2)}, u32[]{:S(2)}) collective-permute-start(bf16[192,256]{1,0:T(8,128)(2,1)S(1)} %get-tuple-element.21), channel_id=1, source_target_pairs={{0,8},{8,0},{16,24},{24,16},{1,9},{9,1},{17,25},{25,17},{2,10},{10... | collective-permute-start | bytes 294920 | tf_op jit(solution)/shard_map/ppermute | solution.py:56
  26.1 0.5 %collective-permute-done.7 = bf16[128,256]{1,0:T(8,128)(2,1)S(1)} collective-permute-done((bf16[128,256]{1,0:T(8,128)(2,1)S(1)}, bf16[128,256]{1,0:T(8,128)(2,1)S(1)}, u32[]{:S(2)}, u32[]{:S(2)}) %collective-permute-start.7) | collective-permute-done | bytes 65568 | tf_op jit(solution)/shard_map/ppermute | solution.py:56
  26.9 3.7 %collective-permute-start.11 = (bf16[128,256]{1,0:T(8,128)(2,1)S(1)}, bf16[128,256]{1,0:T(8,128)(2,1)S(1)}, u32[]{:S(2)}, u32[]{:S(2)}) collective-permute-start(bf16[128,256]{1,0:T(8,128)(2,1)S(1)} %get-tuple-element.26), channel_id=1, source_target_pairs={{0,6},{1,7},{2,0},{3,1},{4,2},{5,3},{6,4},{7,5},{8,14},{9,15},{10,... | collective-permute-start | bytes 196616 | tf_op jit(solution)/shard_map/ppermute | solution.py:33
  30.6 1.0 %collective-permute-start.9 = (bf16[128,256]{1,0:T(8,128)(2,1)S(1)}, bf16[128,256]{1,0:T(8,128)(2,1)S(1)}, u32[]{:S(2)}, u32[]{:S(2)}) collective-permute-start(bf16[128,256]{1,0:T(8,128)(2,1)S(1)} %get-tuple-element.26), channel_id=1, source_target_pairs={{0,2},{1,3},{2,4},{3,5},{4,6},{5,7},{6,0},{7,1},{8,10},{9,11},{10,... | collective-permute-start | bytes 196616 | tf_op jit(solution)/shard_map/ppermute | solution.py:33
  31.6 0.3 convolution_convert_fusion.1
  32.0 0.3 fusion.14
  32.3 0.9 %convolution_convert_fusion.2 = bf16[256,256]{0,1:T(8,128)(2,1)} fusion(bf16[256,256]{1,0:T(8,128)(2,1)S(1)} %convolution_convert_fusion.1, bf16[256,256]{1,0:T(8,128)(2,1)S(1)} %copy-done), kind=kOutput, calls=%fused_computation.8 | convolution fusion | flops 33619968 | bytes 393216 | tf_op jit(solution)/shard_map/dot_general | solution.py:101
  33.2 2.6 %collective-permute-done.10 = bf16[128,256]{1,0:T(8,128)(2,1)S(1)} collective-permute-done((bf16[128,256]{1,0:T(8,128)(2,1)S(1)}, bf16[128,256]{1,0:T(8,128)(2,1)S(1)}, u32[]{:S(2)}, u32[]{:S(2)}) %collective-permute-start.10) | collective-permute-done | bytes 65568 | tf_op jit(solution)/shard_map/ppermute | solution.py:33
  35.7 0.9 %collective-permute-done.9 = bf16[128,256]{1,0:T(8,128)(2,1)S(1)} collective-permute-done((bf16[128,256]{1,0:T(8,128)(2,1)S(1)}, bf16[128,256]{1,0:T(8,128)(2,1)S(1)}, u32[]{:S(2)}, u32[]{:S(2)}) %collective-permute-start.9) | collective-permute-done | bytes 65568 | tf_op jit(solution)/shard_map/ppermute | solution.py:33
  36.8 1.5 %collective-permute-done.12 = bf16[4,128,256]{2,1,0:T(8,128)(2,1)S(1)} collective-permute-done((bf16[4,128,256]{2,1,0:T(8,128)(2,1)S(1)}, bf16[4,128,256]{2,1,0:T(8,128)(2,1)S(1)}, u32[]{:S(2)}, u32[]{:S(2)}) %collective-permute-start.12) | collective-permute-done | bytes 262176 | tf_op jit(solution)/shard_map/ppermute | solution.py:36
  38.3 0.6 %gather_fusion.1 = bf16[8,128,256]{2,1,0:T(8,128)(2,1)S(1)} fusion(bf16[8,128,256]{2,1,0:T(8,128)(2,1)S(1)} %constant_dynamic-update-slice_fusion, s32[1024]{0:T(1024)S(1)} %pad_clamp_fusion.1), kind=kCustom, calls=%fused_computation.1 | custom fusion | bytes 1048608 | tf_op jit(solution)/shard_map/jit(_take)/gather | solution.py:41
  39.1 0.5 %convolution_convert_fusion = bf16[1024,512]{0,1:T(8,128)(2,1)S(1)} fusion(bf16[1024,256]{1,0:T(8,128)(2,1)S(1)} %bitcast_select_fusion, bf16[256,256]{1,0:T(8,128)(2,1)S(1)} %copy-done.2, bf16[256,256]{1,0:T(8,128)(2,1)S(1)} %copy-done.3), kind=kOutput, calls=%fused_computation.5 | convolution fusion | flops 269484032 | bytes 1835008 | tf_op jit(solution)/shard_map/dot_general | solution.py:106
  39.7 2.5 %fusion.7 = bf16[4,64,256]{2,1,0:T(8,128)(2,1)S(1)} fusion(bf16[1024,4,64]{0,2,1:T(8,128)(2,1)S(1)} %bitcast.106, bf16[1024,4,64]{0,2,1:T(8,128)(2,1)S(1)} %bitcast.105, bf16[256,4,64]{0,2,1:T(8,128)(2,1)} %bitcast.112, pred[1024]{0:T(1024)(128)(4,1)S(1)} %iota_compare_fusion.10, f32[]{:T(128)S(6)} %sqrt.3), kind=kOutput, calls=%fused_computation.17 | convolution fusion | flops 274857984 | bytes 1311748 | tf_op jit(solution)/shard_map/bgo,ogl->bgl/dot_general | solution.py:120
  42.2 1.2 %fusion.10 = f32[1,256]{1,0:T(1,128)} fusion(bf16[1024,1]{0,1:T(2,128)(2,1)S(1)} %reshape.305, f32[256,1024]{1,0:T(8,128)S(1)} %fusion.14, bf16[256,256]{0,1:T(8,128)(2,1)S(1)} %bitcast.122, bf16[512,1024]{1,0:T(8,128)(2,1)S(1)} %copy-done.1), kind=kOutput, calls=%fused_computation.19 | convolution fusion | flops 136314880 | bytes 1709056 | tf_op jit(solution)/shard_map/dot_general | solution.py:132
  (52 shorter events, 2.0 us)
Async XLA Ops:
  0.0 32.3 %copy-start = (bf16[256,256]{1,0:T(8,128)(2,1)S(1)}, bf16[256,256]{1,0:T(8,128)(2,1)}, u32[]{:S(2)}) copy-start(bf16[256,256]{1,0:T(8,128)(2,1)} %param.17) | copy-start | bytes 393220
  4.5 6.8 %collective-permute-start = (s32[320]{0:T(512)S(1)}, s32[320]{0:T(512)S(1)}, u32[]{:S(2)}, u32[]{:S(2)}) collective-permute-start(s32[320]{0:T(512)S(1)} %get-tuple-element.7), channel_id=1, source_target_pairs={{0,8},{8,0},{16,24},{24,16},{1,9},{9,1},{17,25},{25,17},{2,10},{10... | collective-permute-start | bytes 3848 | tf_op jit(solution)/shard_map/ppermute | solution.py:56
  7.5 4.5 %collective-permute-start.2 = (s32[320]{0:T(512)S(1)}, s32[320]{0:T(512)S(1)}, u32[]{:S(2)}, u32[]{:S(2)}) collective-permute-start(s32[320]{0:T(512)S(1)} %get-tuple-element.8), channel_id=1, source_target_pairs={{0,24},{8,16},{16,8},{24,0},{1,25},{9,17},{17,9},{25,1},{2,26},{10... | collective-permute-start | bytes 3848 | tf_op jit(solution)/shard_map/ppermute | solution.py:56
  9.0 3.6 %collective-permute-start.1 = (s32[320]{0:T(512)S(1)}, s32[320]{0:T(512)S(1)}, u32[]{:S(2)}, u32[]{:S(2)}) collective-permute-start(s32[320]{0:T(512)S(1)} %get-tuple-element.9), channel_id=1, source_target_pairs={{0,16},{8,24},{16,0},{24,8},{1,17},{9,25},{17,1},{25,9},{2,18},{10... | collective-permute-start | bytes 3848 | tf_op jit(solution)/shard_map/ppermute | solution.py:56
  12.7 19.3 %copy-start.1 = (bf16[512,1024]{1,0:T(8,128)(2,1)S(1)}, bf16[512,1024]{1,0:T(8,128)(2,1)}, u32[]{:S(2)}) copy-start(bf16[512,1024]{1,0:T(8,128)(2,1)} %param.20) | copy-start | bytes 3145732
  18.7 6.6 %collective-permute-start.8 = (bf16[128,256]{1,0:T(8,128)(2,1)S(1)}, bf16[128,256]{1,0:T(8,128)(2,1)S(1)}, u32[]{:S(2)}, u32[]{:S(2)}) collective-permute-start(bf16[128,256]{1,0:T(8,128)(2,1)S(1)} %get-tuple-element.15), channel_id=1, source_target_pairs={{0,24},{8,16},{16,8},{24,0},{1,25},{9,17},{17,9},{25,1},{2,26},{10... | collective-permute-start | bytes 196616 | tf_op jit(solution)/shard_map/ppermute | solution.py:56
  20.4 6.2 %collective-permute-start.7 = (bf16[128,256]{1,0:T(8,128)(2,1)S(1)}, bf16[128,256]{1,0:T(8,128)(2,1)S(1)}, u32[]{:S(2)}, u32[]{:S(2)}) collective-permute-start(bf16[128,256]{1,0:T(8,128)(2,1)S(1)} %get-tuple-element.16), channel_id=1, source_target_pairs={{0,16},{8,24},{16,0},{24,8},{1,17},{9,25},{17,1},{25,9},{2,18},{10... | collective-permute-start | bytes 196616 | tf_op jit(solution)/shard_map/ppermute | solution.py:56
  21.7 4.9 %collective-permute-start.6 = (bf16[128,256]{1,0:T(8,128)(2,1)S(1)}, bf16[128,256]{1,0:T(8,128)(2,1)S(1)}, u32[]{:S(2)}, u32[]{:S(2)}) collective-permute-start(bf16[128,256]{1,0:T(8,128)(2,1)S(1)} %get-tuple-element.17), channel_id=1, source_target_pairs={{0,8},{8,0},{16,24},{24,16},{1,9},{9,1},{17,25},{25,17},{2,10},{10... | collective-permute-start | bytes 196616 | tf_op jit(solution)/shard_map/ppermute | solution.py:56
  22.2 16.9 %copy-start.2 = (bf16[256,256]{1,0:T(8,128)(2,1)S(1)}, bf16[256,256]{1,0:T(8,128)(2,1)}, u32[]{:S(2)}) copy-start(bf16[256,256]{1,0:T(8,128)(2,1)} %param.19) | copy-start | bytes 393220
  22.2 16.9 %copy-start.3 = (bf16[256,256]{1,0:T(8,128)(2,1)S(1)}, bf16[256,256]{1,0:T(8,128)(2,1)}, u32[]{:S(2)}) copy-start(bf16[256,256]{1,0:T(8,128)(2,1)} %param.18) | copy-start | bytes 393220
  22.3 8.3 %collective-permute-start.5 = (bf16[192,256]{1,0:T(8,128)(2,1)S(1)}, bf16[192,256]{1,0:T(8,128)(2,1)S(1)}, u32[]{:S(2)}, u32[]{:S(2)}) collective-permute-start(bf16[192,256]{1,0:T(8,128)(2,1)S(1)} %get-tuple-element.19), channel_id=1, source_target_pairs={{0,24},{8,16},{16,8},{24,0},{1,25},{9,17},{17,9},{25,1},{2,26},{10... | collective-permute-start | bytes 294920 | tf_op jit(solution)/shard_map/ppermute | solution.py:56
  24.0 7.6 %collective-permute-start.4 = (bf16[192,256]{1,0:T(8,128)(2,1)S(1)}, bf16[192,256]{1,0:T(8,128)(2,1)S(1)}, u32[]{:S(2)}, u32[]{:S(2)}) collective-permute-start(bf16[192,256]{1,0:T(8,128)(2,1)S(1)} %get-tuple-element.20), channel_id=1, source_target_pairs={{0,16},{8,24},{16,0},{24,8},{1,17},{9,25},{17,1},{25,9},{2,18},{10... | collective-permute-start | bytes 294920 | tf_op jit(solution)/shard_map/ppermute | solution.py:56
  25.3 6.3 %collective-permute-start.3 = (bf16[192,256]{1,0:T(8,128)(2,1)S(1)}, bf16[192,256]{1,0:T(8,128)(2,1)S(1)}, u32[]{:S(2)}, u32[]{:S(2)}) collective-permute-start(bf16[192,256]{1,0:T(8,128)(2,1)S(1)} %get-tuple-element.21), channel_id=1, source_target_pairs={{0,8},{8,0},{16,24},{24,16},{1,9},{9,1},{17,25},{25,17},{2,10},{10... | collective-permute-start | bytes 294920 | tf_op jit(solution)/shard_map/ppermute | solution.py:56
  26.9 6.3 %collective-permute-start.11 = (bf16[128,256]{1,0:T(8,128)(2,1)S(1)}, bf16[128,256]{1,0:T(8,128)(2,1)S(1)}, u32[]{:S(2)}, u32[]{:S(2)}) collective-permute-start(bf16[128,256]{1,0:T(8,128)(2,1)S(1)} %get-tuple-element.26), channel_id=1, source_target_pairs={{0,6},{1,7},{2,0},{3,1},{4,2},{5,3},{6,4},{7,5},{8,14},{9,15},{10,... | collective-permute-start | bytes 196616 | tf_op jit(solution)/shard_map/ppermute | solution.py:33
  30.6 5.2 %collective-permute-start.10 = (bf16[128,256]{1,0:T(8,128)(2,1)S(1)}, bf16[128,256]{1,0:T(8,128)(2,1)S(1)}, u32[]{:S(2)}, u32[]{:S(2)}) collective-permute-start(bf16[128,256]{1,0:T(8,128)(2,1)S(1)} %get-tuple-element.26), channel_id=1, source_target_pairs={{0,4},{1,5},{2,6},{3,7},{4,0},{5,1},{6,2},{7,3},{8,12},{9,13},{10,... | collective-permute-start | bytes 196616 | tf_op jit(solution)/shard_map/ppermute | solution.py:33
  30.6 6.1 %collective-permute-start.9 = (bf16[128,256]{1,0:T(8,128)(2,1)S(1)}, bf16[128,256]{1,0:T(8,128)(2,1)S(1)}, u32[]{:S(2)}, u32[]{:S(2)}) collective-permute-start(bf16[128,256]{1,0:T(8,128)(2,1)S(1)} %get-tuple-element.26), channel_id=1, source_target_pairs={{0,2},{1,3},{2,4},{3,5},{4,6},{5,7},{6,0},{7,1},{8,10},{9,11},{10,... | collective-permute-start | bytes 196616 | tf_op jit(solution)/shard_map/ppermute | solution.py:33
  36.7 1.6 %collective-permute-start.12 = (bf16[4,128,256]{2,1,0:T(8,128)(2,1)S(1)}, bf16[4,128,256]{2,1,0:T(8,128)(2,1)S(1)}, u32[]{:S(2)}, u32[]{:S(2)}) collective-permute-start(bf16[4,128,256]{2,1,0:T(8,128)(2,1)S(1)} %pad_maximum_fusion.2), channel_id=1, source_target_pairs={{0,1},{1,0},{2,3},{3,2},{4,5},{5,4},{6,7},{7,6},{8,9},{9,8},{10,11... | collective-permute-start | bytes 786440 | tf_op jit(solution)/shard_map/ppermute | solution.py:36

commit v8 on v7

--- a/solution.py
+++ b/solution.py
@@ -8,15 +8,14 @@
 HEADS = 4
 
 
-def slot_index(shard_ids, n_dest, slot_count, first_slot):
+def slot_index(shard_ids, slot_count):
     count = shard_ids.shape[0]
-    onehot = (shard_ids[:, None] == jnp.arange(n_dest, dtype=jnp.int32)[None, :]).astype(jnp.bfloat16)
     earlier = lax.broadcasted_iota(jnp.int32, (count, count), 1) < lax.broadcasted_iota(
         jnp.int32, (count, count), 0
     )
-    before = jnp.dot(earlier.astype(jnp.bfloat16), onehot, preferred_element_type=jnp.float32)
-    rank = jnp.sum(before * onehot.astype(jnp.float32), axis=1).astype(jnp.int32)
-    return shard_ids * slot_count + first_slot + rank
+    same = (shard_ids[:, None] == shard_ids[None, :]) & earlier
+    rank = jnp.sum(same.astype(jnp.int32), axis=1)
+    return shard_ids * slot_count + rank
 
 
 def select_rows(slots, n_slots):
@@ -41,11 +40,12 @@
     return jnp.take(held, order, axis=0).reshape(-1, rows.shape[1])
 
 
-def wanted_rows(pick, rows):
+def wanted_rows(slots, n_slots, rows):
+    pick_t = (lax.broadcasted_iota(jnp.int32, (n_slots, slots.shape[0]), 0) == slots[None, :]).astype(
+        jnp.bfloat16
+    )
     row_parts = jnp.stack([rows // 128, rows % 128], axis=1).astype(jnp.bfloat16)
-    parts = lax.dot_general(
-        pick, row_parts, (((0,), (0,)), ((), ())), preferred_element_type=jnp.float32
-    ).astype(jnp.int32)
+    parts = jnp.dot(pick_t, row_parts, preferred_element_type=jnp.float32).astype(jnp.int32)
     return parts[:, 0] * 128 + parts[:, 1]
 
 
@@ -80,12 +80,12 @@
     cand_cap = 3 * cand_dev // n_dest
     assert n_dest & (n_dest - 1) == 0
     me = lax.axis_index("req")
-    hist_slot = slot_index(hist_shards ^ me, n_dest, hist_cap, 0)
-    cand_slot = slot_index(cand_shards ^ me, n_dest, cand_cap, 0)
+    hist_slot = slot_index(hist_shards ^ me, hist_cap)
+    cand_slot = slot_index(cand_shards ^ me, cand_cap)
     hist_pick = select_rows(hist_slot, n_dest * hist_cap)
     cand_pick = select_rows(cand_slot, n_dest * cand_cap)
-    hist_wanted = wanted_rows(hist_pick, history_row[0]).reshape(n_dest, hist_cap)
-    cand_wanted = wanted_rows(cand_pick, candidate_row[0]).reshape(n_dest, cand_cap)
+    hist_wanted = wanted_rows(hist_slot, n_dest * hist_cap, history_row[0]).reshape(n_dest, hist_cap)
+    cand_wanted = wanted_rows(cand_slot, n_dest * cand_cap, candidate_row[0]).reshape(n_dest, cand_cap)
     asked = swap_over_req(jnp.concatenate([hist_wanted, cand_wanted], axis=1))
     fetched = jnp.take(table, asked.reshape(-1), axis=0, mode="clip").reshape(
         n_dest, hist_cap + cand_cap, d_model

time: 43.6 us -> 43.5 us (level)
  matrix products: 6.8 us -> 6.36 us
    dot_general x4 -> x2, matrix products: 0.87 us -> 0.42 us  [wanted_rows(): jnp.dot(pick_t, row_parts, preferred_element_type=jnp.float32)]
where the time goes in v8:
time: 43.5 us; the launch traced here: 43.3 us
  starting transfers between devices  16.7 us (38%)
  local copies, waits for them, and re-layouts  7.72 us (18%)
  waiting for transfers between devices  6.69 us (15%)
  matrix products  6.36 us (15%)
  other arithmetic  4.91 us (11%)
  between operations  0.92 us (2%)
    ppermute x9, starting transfers between devices, swap_over_req(): lax.ppermute(blocks[hop], 'req', [(i, i ^ hop) for i in range(n_req)])  12 us
    gather x1, local copies, waits for them, and re-layouts, body(): jnp.take(table, asked.reshape(-1), axis=0, mode='clip')  5.96 us
    ppermute x3, starting transfers between devices, gather_over_cand(): lax.ppermute(rows, 'cand', [(i, (i + hop) % n_cand) for i in range(n_cand)])  4.69 us
    ppermute x3, waiting for transfers between devices, gather_over_cand(): lax.ppermute(rows, 'cand', [(i, (i + hop) % n_cand) for i in range(n_cand)])  3.47 us
    dot_general x1, matrix products, body(): jnp.einsum('bgo,ogl->bgl', gate_weights, value_portion_slice, preferred_e...  2.5 us
    ppermute x9, waiting for transfers between devices, swap_over_req(): lax.ppermute(blocks[hop], 'req', [(i, i ^ hop) for i in range(n_req)])  1.75 us
    ppermute x1, waiting for transfers between devices, gather_over_cand(): partner = lax.ppermute(mine, 'cand', [(i, i ^ 1) for i in range(n_cand)])  1.48 us
    another operation x3, other arithmetic  1.37 us
  transfers between devices with their start and end apart: 13, of which 6 were waited for; matrix products, arithmetic and copies ran while one was open for 8% of the time, Pallas kernels for 0%

profile of v8, /device:TPU:0, one launch (start us, length us, event | category | flops | bytes accessed | tf_op | source)
XLA Modules:
  0.0 43.3 jit_solution(16932420387857270431)
XLA Ops:
  0.0 0.7 %xor_bitcast_fusion = s32[128]{0:T(128)S(1)} fusion(s32[1,128,1]{1,2,0:T(1,128)} %param.12, s32[]{:T(128)S(6)} %axis_index.23), kind=kLoop, calls=%fused_computation.103 | loop fusion | flops 128 | bytes 1028 | tf_op jit(solution)/shard_map/xor | solution.py:83
  0.9 0.7 %multiply_add_fusion.1 = s32[128]{0:T(128)S(1)} fusion(s32[128]{0:T(128)S(1)} %convert_reduce_fusion.1, s32[1,128,1]{1,2,0:T(1,128)} %param.12, s32[]{:T(128)S(6)} %axis_index.23), kind=kLoop, calls=%fused_computation.102 | loop fusion | flops 384 | bytes 1540 | tf_op jit(solution)/shard_map/add | solution.py:18
  1.5 0.7 %broadcast_xor_fusion = s32[1,256,1]{1,2,0:T(1,128)S(1)} fusion(s32[1,256,1]{1,2,0:T(1,128)} %param.14, s32[]{:T(128)S(6)} %axis_index.23), kind=kLoop, calls=%fused_computation.104 | loop fusion | flops 256 | bytes 2052 | tf_op jit(solution)/shard_map/xor | solution.py:84
  2.4 0.7 %fusion.39 = (bf16[128,1]{0,1:T(2,128)(2,1)S(1)}, bf16[128,1]{0,1:T(2,128)(2,1)S(1)}) fusion(s32[1,128]{1,0:T(1,128)} %param.13), kind=kLoop, calls=%fused_computation.105 | loop fusion | flops 2688 | bytes 1024 | tf_op jit(solution)/shard_map/convert.2
  3.1 0.7 %fusion.34 = (bf16[256,1]{0,1:T(2,128)(2,1)S(1)}, s32[256,1]{0,1:T(1,128)S(1)}) fusion(s32[1,256]{1,0:T(1,128)} %param.15), kind=kLoop, calls=%fused_computation.95 | loop fusion | flops 4096 | bytes 2560 | tf_op jit(solution)/shard_map/convert
  4.0 0.3 convolution_convert_fusion.4
  4.4 3.0 %collective-permute-start = (s32[320]{0:T(512)S(1)}, s32[320]{0:T(512)S(1)}, u32[]{:S(2)}, u32[]{:S(2)}) collective-permute-start(s32[320]{0:T(512)S(1)} %get-tuple-element.7), channel_id=1, source_target_pairs={{0,8},{8,0},{16,24},{24,16},{1,9},{9,1},{17,25},{25,17},{2,10},{10... | collective-permute-start | bytes 3848 | tf_op jit(solution)/shard_map/ppermute | solution.py:56
  7.4 1.5 %collective-permute-start.2 = (s32[320]{0:T(512)S(1)}, s32[320]{0:T(512)S(1)}, u32[]{:S(2)}, u32[]{:S(2)}) collective-permute-start(s32[320]{0:T(512)S(1)} %get-tuple-element.8), channel_id=1, source_target_pairs={{0,24},{8,16},{16,8},{24,0},{1,25},{9,17},{17,9},{25,1},{2,26},{10... | collective-permute-start | bytes 3848 | tf_op jit(solution)/shard_map/ppermute | solution.py:56
  9.1 0.6 %iota_reduce_fusion = (pred[8]{0:T(512)(128)(4,1)}, s32[8]{0:T(128)S(1)}) fusion(s32[8]{0:T(128)S(1)} %concatenate.15), kind=kLoop, calls=%fused_computation.62 | loop fusion | flops 456 | bytes 72 | tf_op jit(solution)/shard_map/gather_over_cand/reduce | solution.py:39
  10.5 0.7 %reshape.327 = bf16[1024,1]{0,1:T(2,128)(2,1)S(1)} reshape(bf16[1024]{0:T(1024)(128)(2,1)} %param.21) | data formatting | bytes 4096 | tf_op args[10]
  11.2 0.6 %collective-permute-done.2 = s32[320]{0:T(512)S(1)} collective-permute-done((s32[320]{0:T(512)S(1)}, s32[320]{0:T(512)S(1)}, u32[]{:S(2)}, u32[]{:S(2)}) %collective-permute-start.2) | collective-permute-done | bytes 1312 | tf_op jit(solution)/shard_map/ppermute | solution.py:56
  11.8 0.6 %collective-permute-done.1 = s32[320]{0:T(512)S(1)} collective-permute-done((s32[320]{0:T(512)S(1)}, s32[320]{0:T(512)S(1)}, u32[]{:S(2)}, u32[]{:S(2)}) %collective-permute-start.1) | collective-permute-done | bytes 1312 | tf_op jit(solution)/shard_map/ppermute | solution.py:56
  12.5 6.0 %gather_fusion = bf16[1280,256]{1,0:T(8,128)(2,1)S(1)} fusion(bf16[8192,256]{1,0:T(8,128)(2,1)} %param.11, s32[2048]{0:T(1024)S(1)} %pad_clamp_fusion), kind=kCustom, calls=%fused_computation | custom fusion | bytes 1315840 | tf_op jit(solution)/shard_map/jit(_take)/gather | solution.py:90
  18.5 1.8 %collective-permute-start.8 = (bf16[128,256]{1,0:T(8,128)(2,1)S(1)}, bf16[128,256]{1,0:T(8,128)(2,1)S(1)}, u32[]{:S(2)}, u32[]{:S(2)}) collective-permute-start(bf16[128,256]{1,0:T(8,128)(2,1)S(1)} %get-tuple-element.15), channel_id=1, source_target_pairs={{0,24},{8,16},{16,8},{24,0},{1,25},{9,17},{17,9},{25,1},{2,26},{10... | collective-permute-start | bytes 196616 | tf_op jit(solution)/shard_map/ppermute | solution.py:56
  20.3 1.2 %collective-permute-start.7 = (bf16[128,256]{1,0:T(8,128)(2,1)S(1)}, bf16[128,256]{1,0:T(8,128)(2,1)S(1)}, u32[]{:S(2)}, u32[]{:S(2)}) collective-permute-start(bf16[128,256]{1,0:T(8,128)(2,1)S(1)} %get-tuple-element.16), channel_id=1, source_target_pairs={{0,16},{8,24},{16,0},{24,8},{1,17},{9,25},{17,1},{25,9},{2,18},{10... | collective-permute-start | bytes 196616 | tf_op jit(solution)/shard_map/ppermute | solution.py:56
  21.6 0.5 %collective-permute-start.6 = (bf16[128,256]{1,0:T(8,128)(2,1)S(1)}, bf16[128,256]{1,0:T(8,128)(2,1)S(1)}, u32[]{:S(2)}, u32[]{:S(2)}) collective-permute-start(bf16[128,256]{1,0:T(8,128)(2,1)S(1)} %get-tuple-element.17), channel_id=1, source_target_pairs={{0,8},{8,0},{16,24},{24,16},{1,9},{9,1},{17,25},{25,17},{2,10},{10... | collective-permute-start | bytes 196616 | tf_op jit(solution)/shard_map/ppermute | solution.py:56
  22.1 1.8 %collective-permute-start.5 = (bf16[192,256]{1,0:T(8,128)(2,1)S(1)}, bf16[192,256]{1,0:T(8,128)(2,1)S(1)}, u32[]{:S(2)}, u32[]{:S(2)}) collective-permute-start(bf16[192,256]{1,0:T(8,128)(2,1)S(1)} %get-tuple-element.19), channel_id=1, source_target_pairs={{0,24},{8,16},{16,8},{24,0},{1,25},{9,17},{17,9},{25,1},{2,26},{10... | collective-permute-start | bytes 294920 | tf_op jit(solution)/shard_map/ppermute | solution.py:56
  23.9 1.2 %collective-permute-start.4 = (bf16[192,256]{1,0:T(8,128)(2,1)S(1)}, bf16[192,256]{1,0:T(8,128)(2,1)S(1)}, u32[]{:S(2)}, u32[]{:S(2)}) collective-permute-start(bf16[192,256]{1,0:T(8,128)(2,1)S(1)} %get-tuple-element.20), channel_id=1, source_target_pairs={{0,16},{8,24},{16,0},{24,8},{1,17},{9,25},{17,1},{25,9},{2,18},{10... | collective-permute-start | bytes 294920 | tf_op jit(solution)/shard_map/ppermute | solution.py:56
  25.2 0.8 %collective-permute-start.3 = (bf16[192,256]{1,0:T(8,128)(2,1)S(1)}, bf16[192,256]{1,0:T(8,128)(2,1)S(1)}, u32[]{:S(2)}, u32[]{:S(2)}) collective-permute-start(bf16[192,256]{1,0:T(8,128)(2,1)S(1)} %get-tuple-element.21), channel_id=1, source_target_pairs={{0,8},{8,0},{16,24},{24,16},{1,9},{9,1},{17,25},{25,17},{2,10},{10... | collective-permute-start | bytes 294920 | tf_op jit(solution)/shard_map/ppermute | solution.py:56
  26.0 0.5 %collective-permute-done.7 = bf16[128,256]{1,0:T(8,128)(2,1)S(1)} collective-permute-done((bf16[128,256]{1,0:T(8,128)(2,1)S(1)}, bf16[128,256]{1,0:T(8,128)(2,1)S(1)}, u32[]{:S(2)}, u32[]{:S(2)}) %collective-permute-start.7) | collective-permute-done | bytes 65568 | tf_op jit(solution)/shard_map/ppermute | solution.py:56
  26.8 3.7 %collective-permute-start.11 = (bf16[128,256]{1,0:T(8,128)(2,1)S(1)}, bf16[128,256]{1,0:T(8,128)(2,1)S(1)}, u32[]{:S(2)}, u32[]{:S(2)}) collective-permute-start(bf16[128,256]{1,0:T(8,128)(2,1)S(1)} %get-tuple-element.26), channel_id=1, source_target_pairs={{0,6},{1,7},{2,0},{3,1},{4,2},{5,3},{6,4},{7,5},{8,14},{9,15},{10,... | collective-permute-start | bytes 196616 | tf_op jit(solution)/shard_map/ppermute | solution.py:32
  30.5 1.0 %collective-permute-start.9 = (bf16[128,256]{1,0:T(8,128)(2,1)S(1)}, bf16[128,256]{1,0:T(8,128)(2,1)S(1)}, u32[]{:S(2)}, u32[]{:S(2)}) collective-permute-start(bf16[128,256]{1,0:T(8,128)(2,1)S(1)} %get-tuple-element.26), channel_id=1, source_target_pairs={{0,2},{1,3},{2,4},{3,5},{4,6},{5,7},{6,0},{7,1},{8,10},{9,11},{10,... | collective-permute-start | bytes 196616 | tf_op jit(solution)/shard_map/ppermute | solution.py:32
  31.5 0.3 convolution_convert_fusion.1
  31.9 0.3 fusion.12
  32.2 0.9 %convolution_convert_fusion.2 = bf16[256,256]{0,1:T(8,128)(2,1)} fusion(bf16[256,256]{1,0:T(8,128)(2,1)S(1)} %convolution_convert_fusion.1, bf16[256,256]{1,0:T(8,128)(2,1)S(1)} %copy-done), kind=kOutput, calls=%fused_computation.8 | convolution fusion | flops 33619968 | bytes 393216 | tf_op jit(solution)/shard_map/dot_general | solution.py:101
  33.1 2.6 %collective-permute-done.10 = bf16[128,256]{1,0:T(8,128)(2,1)S(1)} collective-permute-done((bf16[128,256]{1,0:T(8,128)(2,1)S(1)}, bf16[128,256]{1,0:T(8,128)(2,1)S(1)}, u32[]{:S(2)}, u32[]{:S(2)}) %collective-permute-start.10) | collective-permute-done | bytes 65568 | tf_op jit(solution)/shard_map/ppermute | solution.py:32
  35.6 0.9 %collective-permute-done.9 = bf16[128,256]{1,0:T(8,128)(2,1)S(1)} collective-permute-done((bf16[128,256]{1,0:T(8,128)(2,1)S(1)}, bf16[128,256]{1,0:T(8,128)(2,1)S(1)}, u32[]{:S(2)}, u32[]{:S(2)}) %collective-permute-start.9) | collective-permute-done | bytes 65568 | tf_op jit(solution)/shard_map/ppermute | solution.py:32
  36.7 1.5 %collective-permute-done.12 = bf16[4,128,256]{2,1,0:T(8,128)(2,1)S(1)} collective-permute-done((bf16[4,128,256]{2,1,0:T(8,128)(2,1)S(1)}, bf16[4,128,256]{2,1,0:T(8,128)(2,1)S(1)}, u32[]{:S(2)}, u32[]{:S(2)}) %collective-permute-start.12) | collective-permute-done | bytes 262176 | tf_op jit(solution)/shard_map/ppermute | solution.py:35
  38.2 0.6 %gather_fusion.1 = bf16[8,128,256]{2,1,0:T(8,128)(2,1)S(1)} fusion(bf16[8,128,256]{2,1,0:T(8,128)(2,1)S(1)} %constant_dynamic-update-slice_fusion, s32[1024]{0:T(1024)S(1)} %pad_clamp_fusion.1), kind=kCustom, calls=%fused_computation.1 | custom fusion | bytes 1048608 | tf_op jit(solution)/shard_map/jit(_take)/gather | solution.py:40
  39.0 0.5 %convolution_convert_fusion = bf16[1024,512]{0,1:T(8,128)(2,1)S(1)} fusion(bf16[1024,256]{1,0:T(8,128)(2,1)S(1)} %bitcast_select_fusion, bf16[256,256]{1,0:T(8,128)(2,1)S(1)} %copy-done.2, bf16[256,256]{1,0:T(8,128)(2,1)S(1)} %copy-done.3), kind=kOutput, calls=%fused_computation.5 | convolution fusion | flops 269484032 | bytes 1835008 | tf_op jit(solution)/shard_map/dot_general | solution.py:106
  39.6 2.5 %fusion.5 = bf16[4,64,256]{2,1,0:T(8,128)(2,1)S(1)} fusion(bf16[1024,4,64]{0,2,1:T(8,128)(2,1)S(1)} %bitcast.106, bf16[1024,4,64]{0,2,1:T(8,128)(2,1)S(1)} %bitcast.105, bf16[256,4,64]{0,2,1:T(8,128)(2,1)} %bitcast.112, pred[1024]{0:T(1024)(128)(4,1)S(1)} %iota_compare_fusion.10, f32[]{:T(128)S(6)} %sqrt.3), kind=kOutput, calls=%fused_computation.13 | convolution fusion | flops 274857984 | bytes 1311748 | tf_op jit(solution)/shard_map/bgo,ogl->bgl/dot_general | solution.py:120
  42.1 1.2 %fusion.8 = f32[1,256]{1,0:T(1,128)} fusion(bf16[1024,1]{0,1:T(2,128)(2,1)S(1)} %reshape.327, f32[256,1024]{1,0:T(8,128)S(1)} %fusion.12, bf16[256,256]{0,1:T(8,128)(2,1)S(1)} %bitcast.122, bf16[512,1024]{1,0:T(8,128)(2,1)S(1)} %copy-done.1), kind=kOutput, calls=%fused_computation.15 | convolution fusion | flops 136314880 | bytes 1709056 | tf_op jit(solution)/shard_map/dot_general | solution.py:132
  (52 shorter events, 1.9 us)
Async XLA Ops:
  0.0 32.2 %copy-start = (bf16[256,256]{1,0:T(8,128)(2,1)S(1)}, bf16[256,256]{1,0:T(8,128)(2,1)}, u32[]{:S(2)}) copy-start(bf16[256,256]{1,0:T(8,128)(2,1)} %param.17) | copy-start | bytes 393220
  4.4 6.8 %collective-permute-start = (s32[320]{0:T(512)S(1)}, s32[320]{0:T(512)S(1)}, u32[]{:S(2)}, u32[]{:S(2)}) collective-permute-start(s32[320]{0:T(512)S(1)} %get-tuple-element.7), channel_id=1, source_target_pairs={{0,8},{8,0},{16,24},{24,16},{1,9},{9,1},{17,25},{25,17},{2,10},{10... | collective-permute-start | bytes 3848 | tf_op jit(solution)/shard_map/ppermute | solution.py:56
  7.4 4.5 %collective-permute-start.2 = (s32[320]{0:T(512)S(1)}, s32[320]{0:T(512)S(1)}, u32[]{:S(2)}, u32[]{:S(2)}) collective-permute-start(s32[320]{0:T(512)S(1)} %get-tuple-element.8), channel_id=1, source_target_pairs={{0,24},{8,16},{16,8},{24,0},{1,25},{9,17},{17,9},{25,1},{2,26},{10... | collective-permute-start | bytes 3848 | tf_op jit(solution)/shard_map/ppermute | solution.py:56
  8.8 3.6 %collective-permute-start.1 = (s32[320]{0:T(512)S(1)}, s32[320]{0:T(512)S(1)}, u32[]{:S(2)}, u32[]{:S(2)}) collective-permute-start(s32[320]{0:T(512)S(1)} %get-tuple-element.9), channel_id=1, source_target_pairs={{0,16},{8,24},{16,0},{24,8},{1,17},{9,25},{17,1},{25,9},{2,18},{10... | collective-permute-start | bytes 3848 | tf_op jit(solution)/shard_map/ppermute | solution.py:56
  12.5 19.3 %copy-start.1 = (bf16[512,1024]{1,0:T(8,128)(2,1)S(1)}, bf16[512,1024]{1,0:T(8,128)(2,1)}, u32[]{:S(2)}) copy-start(bf16[512,1024]{1,0:T(8,128)(2,1)} %param.20) | copy-start | bytes 3145732
  18.5 6.6 %collective-permute-start.8 = (bf16[128,256]{1,0:T(8,128)(2,1)S(1)}, bf16[128,256]{1,0:T(8,128)(2,1)S(1)}, u32[]{:S(2)}, u32[]{:S(2)}) collective-permute-start(bf16[128,256]{1,0:T(8,128)(2,1)S(1)} %get-tuple-element.15), channel_id=1, source_target_pairs={{0,24},{8,16},{16,8},{24,0},{1,25},{9,17},{17,9},{25,1},{2,26},{10... | collective-permute-start | bytes 196616 | tf_op jit(solution)/shard_map/ppermute | solution.py:56
  20.3 6.2 %collective-permute-start.7 = (bf16[128,256]{1,0:T(8,128)(2,1)S(1)}, bf16[128,256]{1,0:T(8,128)(2,1)S(1)}, u32[]{:S(2)}, u32[]{:S(2)}) collective-permute-start(bf16[128,256]{1,0:T(8,128)(2,1)S(1)} %get-tuple-element.16), channel_id=1, source_target_pairs={{0,16},{8,24},{16,0},{24,8},{1,17},{9,25},{17,1},{25,9},{2,18},{10... | collective-permute-start | bytes 196616 | tf_op jit(solution)/shard_map/ppermute | solution.py:56
  21.6 4.9 %collective-permute-start.6 = (bf16[128,256]{1,0:T(8,128)(2,1)S(1)}, bf16[128,256]{1,0:T(8,128)(2,1)S(1)}, u32[]{:S(2)}, u32[]{:S(2)}) collective-permute-start(bf16[128,256]{1,0:T(8,128)(2,1)S(1)} %get-tuple-element.17), channel_id=1, source_target_pairs={{0,8},{8,0},{16,24},{24,16},{1,9},{9,1},{17,25},{25,17},{2,10},{10... | collective-permute-start | bytes 196616 | tf_op jit(solution)/shard_map/ppermute | solution.py:56
  22.1 16.9 %copy-start.2 = (bf16[256,256]{1,0:T(8,128)(2,1)S(1)}, bf16[256,256]{1,0:T(8,128)(2,1)}, u32[]{:S(2)}) copy-start(bf16[256,256]{1,0:T(8,128)(2,1)} %param.19) | copy-start | bytes 393220
  22.1 16.9 %copy-start.3 = (bf16[256,256]{1,0:T(8,128)(2,1)S(1)}, bf16[256,256]{1,0:T(8,128)(2,1)}, u32[]{:S(2)}) copy-start(bf16[256,256]{1,0:T(8,128)(2,1)} %param.18) | copy-start | bytes 393220
  22.1 8.3 %collective-permute-start.5 = (bf16[192,256]{1,0:T(8,128)(2,1)S(1)}, bf16[192,256]{1,0:T(8,128)(2,1)S(1)}, u32[]{:S(2)}, u32[]{:S(2)}) collective-permute-start(bf16[192,256]{1,0:T(8,128)(2,1)S(1)} %get-tuple-element.19), channel_id=1, source_target_pairs={{0,24},{8,16},{16,8},{24,0},{1,25},{9,17},{17,9},{25,1},{2,26},{10... | collective-permute-start | bytes 294920 | tf_op jit(solution)/shard_map/ppermute | solution.py:56
  23.9 7.6 %collective-permute-start.4 = (bf16[192,256]{1,0:T(8,128)(2,1)S(1)}, bf16[192,256]{1,0:T(8,128)(2,1)S(1)}, u32[]{:S(2)}, u32[]{:S(2)}) collective-permute-start(bf16[192,256]{1,0:T(8,128)(2,1)S(1)} %get-tuple-element.20), channel_id=1, source_target_pairs={{0,16},{8,24},{16,0},{24,8},{1,17},{9,25},{17,1},{25,9},{2,18},{10... | collective-permute-start | bytes 294920 | tf_op jit(solution)/shard_map/ppermute | solution.py:56
  25.2 6.3 %collective-permute-start.3 = (bf16[192,256]{1,0:T(8,128)(2,1)S(1)}, bf16[192,256]{1,0:T(8,128)(2,1)S(1)}, u32[]{:S(2)}, u32[]{:S(2)}) collective-permute-start(bf16[192,256]{1,0:T(8,128)(2,1)S(1)} %get-tuple-element.21), channel_id=1, source_target_pairs={{0,8},{8,0},{16,24},{24,16},{1,9},{9,1},{17,25},{25,17},{2,10},{10... | collective-permute-start | bytes 294920 | tf_op jit(solution)/shard_map/ppermute | solution.py:56
  26.8 6.3 %collective-permute-start.11 = (bf16[128,256]{1,0:T(8,128)(2,1)S(1)}, bf16[128,256]{1,0:T(8,128)(2,1)S(1)}, u32[]{:S(2)}, u32[]{:S(2)}) collective-permute-start(bf16[128,256]{1,0:T(8,128)(2,1)S(1)} %get-tuple-element.26), channel_id=1, source_target_pairs={{0,6},{1,7},{2,0},{3,1},{4,2},{5,3},{6,4},{7,5},{8,14},{9,15},{10,... | collective-permute-start | bytes 196616 | tf_op jit(solution)/shard_map/ppermute | solution.py:32
  30.5 5.2 %collective-permute-start.10 = (bf16[128,256]{1,0:T(8,128)(2,1)S(1)}, bf16[128,256]{1,0:T(8,128)(2,1)S(1)}, u32[]{:S(2)}, u32[]{:S(2)}) collective-permute-start(bf16[128,256]{1,0:T(8,128)(2,1)S(1)} %get-tuple-element.26), channel_id=1, source_target_pairs={{0,4},{1,5},{2,6},{3,7},{4,0},{5,1},{6,2},{7,3},{8,12},{9,13},{10,... | collective-permute-start | bytes 196616 | tf_op jit(solution)/shard_map/ppermute | solution.py:32
  30.5 6.1 %collective-permute-start.9 = (bf16[128,256]{1,0:T(8,128)(2,1)S(1)}, bf16[128,256]{1,0:T(8,128)(2,1)S(1)}, u32[]{:S(2)}, u32[]{:S(2)}) collective-permute-start(bf16[128,256]{1,0:T(8,128)(2,1)S(1)} %get-tuple-element.26), channel_id=1, source_target_pairs={{0,2},{1,3},{2,4},{3,5},{4,6},{5,7},{6,0},{7,1},{8,10},{9,11},{10,... | collective-permute-start | bytes 196616 | tf_op jit(solution)/shard_map/ppermute | solution.py:32
  36.6 1.6 %collective-permute-start.12 = (bf16[4,128,256]{2,1,0:T(8,128)(2,1)S(1)}, bf16[4,128,256]{2,1,0:T(8,128)(2,1)S(1)}, u32[]{:S(2)}, u32[]{:S(2)}) collective-permute-start(bf16[4,128,256]{2,1,0:T(8,128)(2,1)S(1)} %pad_maximum_fusion.2), channel_id=1, source_target_pairs={{0,1},{1,0},{2,3},{3,2},{4,5},{5,4},{6,7},{7,6},{8,9},{9,8},{10,11... | collective-permute-start | bytes 786440 | tf_op jit(solution)/shard_map/ppermute | solution.py:35

commit v9 on v8

--- a/solution.py
+++ b/solution.py
@@ -72,10 +72,17 @@
 ):
     n_dest = lax.axis_size("req")
     d_model = table.shape[1]
-    hist_shards = history_shard[0, :, 0]
-    cand_shards = candidate_shard[0, :, 0]
-    hist_dev = hist_shards.shape[0]
-    cand_dev = cand_shards.shape[0]
+    hist_dev = history_row.shape[1]
+    cand_dev = candidate_row.shape[1]
+    packed = lax.optimization_barrier(
+        jnp.concatenate(
+            [history_shard[0, :, 0], history_row[0], candidate_shard[0, :, 0], candidate_row[0]]
+        )
+    )
+    hist_shards = packed[:hist_dev]
+    hist_rows = packed[hist_dev : 2 * hist_dev]
+    cand_shards = packed[2 * hist_dev : 2 * hist_dev + cand_dev]
+    cand_rows = packed[2 * hist_dev + cand_dev :]
     hist_cap = 4 * hist_dev // n_dest
     cand_cap = 3 * cand_dev // n_dest
     assert n_dest & (n_dest - 1) == 0
@@ -84,8 +91,8 @@
     cand_slot = slot_index(cand_shards ^ me, cand_cap)
     hist_pick = select_rows(hist_slot, n_dest * hist_cap)
     cand_pick = select_rows(cand_slot, n_dest * cand_cap)
-    hist_wanted = wanted_rows(hist_slot, n_dest * hist_cap, history_row[0]).reshape(n_dest, hist_cap)
-    cand_wanted = wanted_rows(cand_slot, n_dest * cand_cap, candidate_row[0]).reshape(n_dest, cand_cap)
+    hist_wanted = wanted_rows(hist_slot, n_dest * hist_cap, hist_rows).reshape(n_dest, hist_cap)
+    cand_wanted = wanted_rows(cand_slot, n_dest * cand_cap, cand_rows).reshape(n_dest, cand_cap)
     asked = swap_over_req(jnp.concatenate([hist_wanted, cand_wanted], axis=1))
     fetched = jnp.take(table, asked.reshape(-1), axis=0, mode="clip").reshape(
         n_dest, hist_cap + cand_cap, d_model

time: 43.5 us -> 40.9 us (0.940)
  other arithmetic: 4.91 us -> 2.28 us
    xor x2 -> x0, other arithmetic: 1.37 us -> none  [the longest x1 0.69 us: body(): hist_slot = slot_index(hist_shards ^ me, hist_cap)]
    another operation x3, other arithmetic: 1.37 us -> 0.04 us  [the longest x2 0.02 us: wanted_rows(): jnp.stack([rows // 128, rows % 128], axis=1).astype(jnp.bfloat16)]
    concatenate x0 -> x1, other arithmetic: none -> 0.75 us  [body(): jnp.concatenate([history_shard[0, :, 0], history_row[0], candidate_shard[...]
    add x2, other arithmetic: 0.68 us -> 0.01 us  [slot_index(): return shard_ids * slot_count + rank]
where the time goes in v9:
time: 40.9 us; the launch traced here: 40.7 us
  starting transfers between devices  16.7 us (41%)
  local copies, waits for them, and re-layouts  7.73 us (19%)
  waiting for transfers between devices  6.69 us (16%)
  matrix products  6.35 us (16%)
  other arithmetic  2.28 us (6%)
  between operations  0.95 us (2%)
    ppermute x9, starting transfers between devices, swap_over_req(): lax.ppermute(blocks[hop], 'req', [(i, i ^ hop) for i in range(n_req)])  12 us
    gather x1, local copies, waits for them, and re-layouts, body(): jnp.take(table, asked.reshape(-1), axis=0, mode='clip')  5.96 us
    ppermute x3, starting transfers between devices, gather_over_cand(): lax.ppermute(rows, 'cand', [(i, (i + hop) % n_cand) for i in range(n_cand)])  4.69 us
    ppermute x3, waiting for transfers between devices, gather_over_cand(): lax.ppermute(rows, 'cand', [(i, (i + hop) % n_cand) for i in range(n_cand)])  3.47 us
    dot_general x1, matrix products, body(): jnp.einsum('bgo,ogl->bgl', gate_weights, value_portion_slice, preferred_e...  2.49 us
    ppermute x9, waiting for transfers between devices, swap_over_req(): lax.ppermute(blocks[hop], 'req', [(i, i ^ hop) for i in range(n_req)])  1.75 us
    ppermute x1, waiting for transfers between devices, gather_over_cand(): partner = lax.ppermute(mine, 'cand', [(i, i ^ 1) for i in range(n_cand)])  1.48 us
    dot_general x1, matrix products, body(): jnp.dot(hidden, tower_out, preferred_element_type=jnp.float32)[None, :]  1.23 us
  transfers between devices with their start and end apart: 13, of which 6 were waited for; matrix products, arithmetic and copies ran while one was open for 8% of the time, Pallas kernels for 0%

profile of v9, /device:TPU:0, one launch (start us, length us, event | category | flops | bytes accessed | tf_op | source)
XLA Modules:
  0.0 40.7 jit_solution(13329383769734497064)
XLA Ops:
  0.0 0.7 %pad_add_fusion.1 = s32[768]{0:T(1024)S(1)} fusion(s32[256]{0:T(256)} %bitcast.92, s32[256]{0:T(256)} %bitcast.93, s32[128]{0:T(128)} %bitcast.94, s32[128]{0:T(128)} %bitcast.95), kind=kLoop, calls=%fused_computation.61 | loop fusion | flops 2304 | bytes 6144 | tf_op jit(solution)/shard_map/concatenate | solution.py:78
  0.8 0.2 convert_reduce_fusion.1
  1.0 0.2 convert_reduce_fusion
  1.4 0.3 convolution_convert_fusion.4
  1.8 3.0 %collective-permute-start = (s32[320]{0:T(512)S(1)}, s32[320]{0:T(512)S(1)}, u32[]{:S(2)}, u32[]{:S(2)}) collective-permute-start(s32[320]{0:T(512)S(1)} %get-tuple-element.7), channel_id=1, source_target_pairs={{0,8},{8,0},{16,24},{24,16},{1,9},{9,1},{17,25},{25,17},{2,10},{10... | collective-permute-start | bytes 3848 | tf_op jit(solution)/shard_map/ppermute | solution.py:56
  4.8 1.5 %collective-permute-start.2 = (s32[320]{0:T(512)S(1)}, s32[320]{0:T(512)S(1)}, u32[]{:S(2)}, u32[]{:S(2)}) collective-permute-start(s32[320]{0:T(512)S(1)} %get-tuple-element.8), channel_id=1, source_target_pairs={{0,24},{8,16},{16,8},{24,0},{1,25},{9,17},{17,9},{25,1},{2,26},{10... | collective-permute-start | bytes 3848 | tf_op jit(solution)/shard_map/ppermute | solution.py:56
  6.5 0.6 %iota_reduce_fusion = (pred[8]{0:T(512)(128)(4,1)}, s32[8]{0:T(128)S(1)}) fusion(s32[8]{0:T(128)S(1)} %concatenate.19), kind=kLoop, calls=%fused_computation.63 | loop fusion | flops 456 | bytes 72 | tf_op jit(solution)/shard_map/gather_over_cand/reduce | solution.py:39
  7.9 0.7 %reshape.79 = bf16[1024,1]{0,1:T(2,128)(2,1)S(1)} reshape(bf16[1024]{0:T(1024)(128)(2,1)} %param.21) | data formatting | bytes 4096 | tf_op args[10]
  8.6 0.6 %collective-permute-done.2 = s32[320]{0:T(512)S(1)} collective-permute-done((s32[320]{0:T(512)S(1)}, s32[320]{0:T(512)S(1)}, u32[]{:S(2)}, u32[]{:S(2)}) %collective-permute-start.2) | collective-permute-done | bytes 1312 | tf_op jit(solution)/shard_map/ppermute | solution.py:56
  9.3 0.6 %collective-permute-done.1 = s32[320]{0:T(512)S(1)} collective-permute-done((s32[320]{0:T(512)S(1)}, s32[320]{0:T(512)S(1)}, u32[]{:S(2)}, u32[]{:S(2)}) %collective-permute-start.1) | collective-permute-done | bytes 1312 | tf_op jit(solution)/shard_map/ppermute | solution.py:56
  10.0 6.0 %gather_fusion = bf16[1280,256]{1,0:T(8,128)(2,1)S(1)} fusion(bf16[8192,256]{1,0:T(8,128)(2,1)} %param.11, s32[2048]{0:T(1024)S(1)} %pad_clamp_fusion), kind=kCustom, calls=%fused_computation | custom fusion | bytes 1315840 | tf_op jit(solution)/shard_map/jit(_take)/gather | solution.py:97
  16.0 1.8 %collective-permute-start.8 = (bf16[128,256]{1,0:T(8,128)(2,1)S(1)}, bf16[128,256]{1,0:T(8,128)(2,1)S(1)}, u32[]{:S(2)}, u32[]{:S(2)}) collective-permute-start(bf16[128,256]{1,0:T(8,128)(2,1)S(1)} %get-tuple-element.15), channel_id=1, source_target_pairs={{0,24},{8,16},{16,8},{24,0},{1,25},{9,17},{17,9},{25,1},{2,26},{10... | collective-permute-start | bytes 196616 | tf_op jit(solution)/shard_map/ppermute | solution.py:56
  17.7 1.2 %collective-permute-start.7 = (bf16[128,256]{1,0:T(8,128)(2,1)S(1)}, bf16[128,256]{1,0:T(8,128)(2,1)S(1)}, u32[]{:S(2)}, u32[]{:S(2)}) collective-permute-start(bf16[128,256]{1,0:T(8,128)(2,1)S(1)} %get-tuple-element.16), channel_id=1, source_target_pairs={{0,16},{8,24},{16,0},{24,8},{1,17},{9,25},{17,1},{25,9},{2,18},{10... | collective-permute-start | bytes 196616 | tf_op jit(solution)/shard_map/ppermute | solution.py:56
  19.0 0.5 %collective-permute-start.6 = (bf16[128,256]{1,0:T(8,128)(2,1)S(1)}, bf16[128,256]{1,0:T(8,128)(2,1)S(1)}, u32[]{:S(2)}, u32[]{:S(2)}) collective-permute-start(bf16[128,256]{1,0:T(8,128)(2,1)S(1)} %get-tuple-element.17), channel_id=1, source_target_pairs={{0,8},{8,0},{16,24},{24,16},{1,9},{9,1},{17,25},{25,17},{2,10},{10... | collective-permute-start | bytes 196616 | tf_op jit(solution)/shard_map/ppermute | solution.py:56
  19.6 1.8 %collective-permute-start.5 = (bf16[192,256]{1,0:T(8,128)(2,1)S(1)}, bf16[192,256]{1,0:T(8,128)(2,1)S(1)}, u32[]{:S(2)}, u32[]{:S(2)}) collective-permute-start(bf16[192,256]{1,0:T(8,128)(2,1)S(1)} %get-tuple-element.19), channel_id=1, source_target_pairs={{0,24},{8,16},{16,8},{24,0},{1,25},{9,17},{17,9},{25,1},{2,26},{10... | collective-permute-start | bytes 294920 | tf_op jit(solution)/shard_map/ppermute | solution.py:56
  21.3 1.2 %collective-permute-start.4 = (bf16[192,256]{1,0:T(8,128)(2,1)S(1)}, bf16[192,256]{1,0:T(8,128)(2,1)S(1)}, u32[]{:S(2)}, u32[]{:S(2)}) collective-permute-start(bf16[192,256]{1,0:T(8,128)(2,1)S(1)} %get-tuple-element.20), channel_id=1, source_target_pairs={{0,16},{8,24},{16,0},{24,8},{1,17},{9,25},{17,1},{25,9},{2,18},{10... | collective-permute-start | bytes 294920 | tf_op jit(solution)/shard_map/ppermute | solution.py:56
  22.6 0.8 %collective-permute-start.3 = (bf16[192,256]{1,0:T(8,128)(2,1)S(1)}, bf16[192,256]{1,0:T(8,128)(2,1)S(1)}, u32[]{:S(2)}, u32[]{:S(2)}) collective-permute-start(bf16[192,256]{1,0:T(8,128)(2,1)S(1)} %get-tuple-element.21), channel_id=1, source_target_pairs={{0,8},{8,0},{16,24},{24,16},{1,9},{9,1},{17,25},{25,17},{2,10},{10... | collective-permute-start | bytes 294920 | tf_op jit(solution)/shard_map/ppermute | solution.py:56
  23.4 0.5 %collective-permute-done.7 = bf16[128,256]{1,0:T(8,128)(2,1)S(1)} collective-permute-done((bf16[128,256]{1,0:T(8,128)(2,1)S(1)}, bf16[128,256]{1,0:T(8,128)(2,1)S(1)}, u32[]{:S(2)}, u32[]{:S(2)}) %collective-permute-start.7) | collective-permute-done | bytes 65568 | tf_op jit(solution)/shard_map/ppermute | solution.py:56
  24.0 0.2 constant_dynamic-update-slice_fusion.4
  24.2 3.7 %collective-permute-start.11 = (bf16[128,256]{1,0:T(8,128)(2,1)S(1)}, bf16[128,256]{1,0:T(8,128)(2,1)S(1)}, u32[]{:S(2)}, u32[]{:S(2)}) collective-permute-start(bf16[128,256]{1,0:T(8,128)(2,1)S(1)} %get-tuple-element.28), channel_id=1, source_target_pairs={{0,6},{1,7},{2,0},{3,1},{4,2},{5,3},{6,4},{7,5},{8,14},{9,15},{10,... | collective-permute-start | bytes 196616 | tf_op jit(solution)/shard_map/ppermute | solution.py:32
  27.9 1.0 %collective-permute-start.9 = (bf16[128,256]{1,0:T(8,128)(2,1)S(1)}, bf16[128,256]{1,0:T(8,128)(2,1)S(1)}, u32[]{:S(2)}, u32[]{:S(2)}) collective-permute-start(bf16[128,256]{1,0:T(8,128)(2,1)S(1)} %get-tuple-element.28), channel_id=1, source_target_pairs={{0,2},{1,3},{2,4},{3,5},{4,6},{5,7},{6,0},{7,1},{8,10},{9,11},{10,... | collective-permute-start | bytes 196616 | tf_op jit(solution)/shard_map/ppermute | solution.py:32
  29.0 0.3 convolution_convert_fusion.1
  29.3 0.3 fusion.12
  29.6 0.9 %convolution_convert_fusion.2 = bf16[256,256]{0,1:T(8,128)(2,1)} fusion(bf16[256,256]{1,0:T(8,128)(2,1)S(1)} %convolution_convert_fusion.1, bf16[256,256]{1,0:T(8,128)(2,1)S(1)} %copy-done), kind=kOutput, calls=%fused_computation.8 | convolution fusion | flops 33619968 | bytes 393216 | tf_op jit(solution)/shard_map/dot_general | solution.py:108
  30.5 2.6 %collective-permute-done.10 = bf16[128,256]{1,0:T(8,128)(2,1)S(1)} collective-permute-done((bf16[128,256]{1,0:T(8,128)(2,1)S(1)}, bf16[128,256]{1,0:T(8,128)(2,1)S(1)}, u32[]{:S(2)}, u32[]{:S(2)}) %collective-permute-start.10) | collective-permute-done | bytes 65568 | tf_op jit(solution)/shard_map/ppermute | solution.py:32
  33.0 0.9 %collective-permute-done.9 = bf16[128,256]{1,0:T(8,128)(2,1)S(1)} collective-permute-done((bf16[128,256]{1,0:T(8,128)(2,1)S(1)}, bf16[128,256]{1,0:T(8,128)(2,1)S(1)}, u32[]{:S(2)}, u32[]{:S(2)}) %collective-permute-start.9) | collective-permute-done | bytes 65568 | tf_op jit(solution)/shard_map/ppermute | solution.py:32
  34.1 1.5 %collective-permute-done.12 = bf16[4,128,256]{2,1,0:T(8,128)(2,1)S(1)} collective-permute-done((bf16[4,128,256]{2,1,0:T(8,128)(2,1)S(1)}, bf16[4,128,256]{2,1,0:T(8,128)(2,1)S(1)}, u32[]{:S(2)}, u32[]{:S(2)}) %collective-permute-start.12) | collective-permute-done | bytes 262176 | tf_op jit(solution)/shard_map/ppermute | solution.py:35
  35.6 0.6 %gather_fusion.1 = bf16[8,128,256]{2,1,0:T(8,128)(2,1)S(1)} fusion(bf16[8,128,256]{2,1,0:T(8,128)(2,1)S(1)} %constant_dynamic-update-slice_fusion, s32[1024]{0:T(1024)S(1)} %pad_clamp_fusion.1), kind=kCustom, calls=%fused_computation.1 | custom fusion | bytes 1048608 | tf_op jit(solution)/shard_map/jit(_take)/gather | solution.py:40
  36.2 0.2 bitcast_select_fusion
  36.4 0.5 %convolution_convert_fusion = bf16[1024,512]{0,1:T(8,128)(2,1)S(1)} fusion(bf16[1024,256]{1,0:T(8,128)(2,1)S(1)} %bitcast_select_fusion, bf16[256,256]{1,0:T(8,128)(2,1)S(1)} %copy-done.2, bf16[256,256]{1,0:T(8,128)(2,1)S(1)} %copy-done.3), kind=kOutput, calls=%fused_computation.5 | convolution fusion | flops 269484032 | bytes 1835008 | tf_op jit(solution)/shard_map/dot_general | solution.py:113
  37.0 2.5 %fusion.5 = bf16[4,64,256]{2,1,0:T(8,128)(2,1)S(1)} fusion(bf16[1024,4,64]{0,2,1:T(8,128)(2,1)S(1)} %bitcast.78, bf16[1024,4,64]{0,2,1:T(8,128)(2,1)S(1)} %bitcast.77, bf16[256,4,64]{0,2,1:T(8,128)(2,1)} %bitcast.84, pred[1024]{0:T(1024)(128)(4,1)S(1)} %iota_compare_fusion.10, f32[]{:T(128)S(6)} %sqrt.3), kind=kOutput, calls=%fused_computation.13 | convolution fusion | flops 274857984 | bytes 1311748 | tf_op jit(solution)/shard_map/bgo,ogl->bgl/dot_general | solution.py:127
  39.5 1.2 %fusion.8 = f32[1,256]{1,0:T(1,128)} fusion(bf16[1024,1]{0,1:T(2,128)(2,1)S(1)} %reshape.79, f32[256,1024]{1,0:T(8,128)S(1)} %fusion.12, bf16[256,256]{0,1:T(8,128)(2,1)S(1)} %bitcast.96, bf16[512,1024]{1,0:T(8,128)(2,1)S(1)} %copy-done.1), kind=kOutput, calls=%fused_computation.15 | convolution fusion | flops 136314880 | bytes 1709056 | tf_op jit(solution)/shard_map/dot_general | solution.py:139
  (53 shorter events, 1.2 us)
Async XLA Ops:
  0.0 29.6 %copy-start = (bf16[256,256]{1,0:T(8,128)(2,1)S(1)}, bf16[256,256]{1,0:T(8,128)(2,1)}, u32[]{:S(2)}) copy-start(bf16[256,256]{1,0:T(8,128)(2,1)} %param.17) | copy-start | bytes 393220
  1.8 6.8 %collective-permute-start = (s32[320]{0:T(512)S(1)}, s32[320]{0:T(512)S(1)}, u32[]{:S(2)}, u32[]{:S(2)}) collective-permute-start(s32[320]{0:T(512)S(1)} %get-tuple-element.7), channel_id=1, source_target_pairs={{0,8},{8,0},{16,24},{24,16},{1,9},{9,1},{17,25},{25,17},{2,10},{10... | collective-permute-start | bytes 3848 | tf_op jit(solution)/shard_map/ppermute | solution.py:56
  4.8 4.5 %collective-permute-start.2 = (s32[320]{0:T(512)S(1)}, s32[320]{0:T(512)S(1)}, u32[]{:S(2)}, u32[]{:S(2)}) collective-permute-start(s32[320]{0:T(512)S(1)} %get-tuple-element.8), channel_id=1, source_target_pairs={{0,24},{8,16},{16,8},{24,0},{1,25},{9,17},{17,9},{25,1},{2,26},{10... | collective-permute-start | bytes 3848 | tf_op jit(solution)/shard_map/ppermute | solution.py:56
  6.3 3.6 %collective-permute-start.1 = (s32[320]{0:T(512)S(1)}, s32[320]{0:T(512)S(1)}, u32[]{:S(2)}, u32[]{:S(2)}) collective-permute-start(s32[320]{0:T(512)S(1)} %get-tuple-element.9), channel_id=1, source_target_pairs={{0,16},{8,24},{16,0},{24,8},{1,17},{9,25},{17,1},{25,9},{2,18},{10... | collective-permute-start | bytes 3848 | tf_op jit(solution)/shard_map/ppermute | solution.py:56
  10.0 19.3 %copy-start.1 = (bf16[512,1024]{1,0:T(8,128)(2,1)S(1)}, bf16[512,1024]{1,0:T(8,128)(2,1)}, u32[]{:S(2)}) copy-start(bf16[512,1024]{1,0:T(8,128)(2,1)} %param.20) | copy-start | bytes 3145732
  16.0 6.6 %collective-permute-start.8 = (bf16[128,256]{1,0:T(8,128)(2,1)S(1)}, bf16[128,256]{1,0:T(8,128)(2,1)S(1)}, u32[]{:S(2)}, u32[]{:S(2)}) collective-permute-start(bf16[128,256]{1,0:T(8,128)(2,1)S(1)} %get-tuple-element.15), channel_id=1, source_target_pairs={{0,24},{8,16},{16,8},{24,0},{1,25},{9,17},{17,9},{25,1},{2,26},{10... | collective-permute-start | bytes 196616 | tf_op jit(solution)/shard_map/ppermute | solution.py:56
  17.7 6.2 %collective-permute-start.7 = (bf16[128,256]{1,0:T(8,128)(2,1)S(1)}, bf16[128,256]{1,0:T(8,128)(2,1)S(1)}, u32[]{:S(2)}, u32[]{:S(2)}) collective-permute-start(bf16[128,256]{1,0:T(8,128)(2,1)S(1)} %get-tuple-element.16), channel_id=1, source_target_pairs={{0,16},{8,24},{16,0},{24,8},{1,17},{9,25},{17,1},{25,9},{2,18},{10... | collective-permute-start | bytes 196616 | tf_op jit(solution)/shard_map/ppermute | solution.py:56
  19.0 4.9 %collective-permute-start.6 = (bf16[128,256]{1,0:T(8,128)(2,1)S(1)}, bf16[128,256]{1,0:T(8,128)(2,1)S(1)}, u32[]{:S(2)}, u32[]{:S(2)}) collective-permute-start(bf16[128,256]{1,0:T(8,128)(2,1)S(1)} %get-tuple-element.17), channel_id=1, source_target_pairs={{0,8},{8,0},{16,24},{24,16},{1,9},{9,1},{17,25},{25,17},{2,10},{10... | collective-permute-start | bytes 196616 | tf_op jit(solution)/shard_map/ppermute | solution.py:56
  19.5 16.9 %copy-start.2 = (bf16[256,256]{1,0:T(8,128)(2,1)S(1)}, bf16[256,256]{1,0:T(8,128)(2,1)}, u32[]{:S(2)}) copy-start(bf16[256,256]{1,0:T(8,128)(2,1)} %param.19) | copy-start | bytes 393220
  19.6 16.9 %copy-start.3 = (bf16[256,256]{1,0:T(8,128)(2,1)S(1)}, bf16[256,256]{1,0:T(8,128)(2,1)}, u32[]{:S(2)}) copy-start(bf16[256,256]{1,0:T(8,128)(2,1)} %param.18) | copy-start | bytes 393220
  19.6 8.3 %collective-permute-start.5 = (bf16[192,256]{1,0:T(8,128)(2,1)S(1)}, bf16[192,256]{1,0:T(8,128)(2,1)S(1)}, u32[]{:S(2)}, u32[]{:S(2)}) collective-permute-start(bf16[192,256]{1,0:T(8,128)(2,1)S(1)} %get-tuple-element.19), channel_id=1, source_target_pairs={{0,24},{8,16},{16,8},{24,0},{1,25},{9,17},{17,9},{25,1},{2,26},{10... | collective-permute-start | bytes 294920 | tf_op jit(solution)/shard_map/ppermute | solution.py:56
  21.3 7.6 %collective-permute-start.4 = (bf16[192,256]{1,0:T(8,128)(2,1)S(1)}, bf16[192,256]{1,0:T(8,128)(2,1)S(1)}, u32[]{:S(2)}, u32[]{:S(2)}) collective-permute-start(bf16[192,256]{1,0:T(8,128)(2,1)S(1)} %get-tuple-element.20), channel_id=1, source_target_pairs={{0,16},{8,24},{16,0},{24,8},{1,17},{9,25},{17,1},{25,9},{2,18},{10... | collective-permute-start | bytes 294920 | tf_op jit(solution)/shard_map/ppermute | solution.py:56
  22.6 6.3 %collective-permute-start.3 = (bf16[192,256]{1,0:T(8,128)(2,1)S(1)}, bf16[192,256]{1,0:T(8,128)(2,1)S(1)}, u32[]{:S(2)}, u32[]{:S(2)}) collective-permute-start(bf16[192,256]{1,0:T(8,128)(2,1)S(1)} %get-tuple-element.21), channel_id=1, source_target_pairs={{0,8},{8,0},{16,24},{24,16},{1,9},{9,1},{17,25},{25,17},{2,10},{10... | collective-permute-start | bytes 294920 | tf_op jit(solution)/shard_map/ppermute | solution.py:56
  24.2 6.3 %collective-permute-start.11 = (bf16[128,256]{1,0:T(8,128)(2,1)S(1)}, bf16[128,256]{1,0:T(8,128)(2,1)S(1)}, u32[]{:S(2)}, u32[]{:S(2)}) collective-permute-start(bf16[128,256]{1,0:T(8,128)(2,1)S(1)} %get-tuple-element.28), channel_id=1, source_target_pairs={{0,6},{1,7},{2,0},{3,1},{4,2},{5,3},{6,4},{7,5},{8,14},{9,15},{10,... | collective-permute-start | bytes 196616 | tf_op jit(solution)/shard_map/ppermute | solution.py:32
  27.9 5.2 %collective-permute-start.10 = (bf16[128,256]{1,0:T(8,128)(2,1)S(1)}, bf16[128,256]{1,0:T(8,128)(2,1)S(1)}, u32[]{:S(2)}, u32[]{:S(2)}) collective-permute-start(bf16[128,256]{1,0:T(8,128)(2,1)S(1)} %get-tuple-element.28), channel_id=1, source_target_pairs={{0,4},{1,5},{2,6},{3,7},{4,0},{5,1},{6,2},{7,3},{8,12},{9,13},{10,... | collective-permute-start | bytes 196616 | tf_op jit(solution)/shard_map/ppermute | solution.py:32
  27.9 6.1 %collective-permute-start.9 = (bf16[128,256]{1,0:T(8,128)(2,1)S(1)}, bf16[128,256]{1,0:T(8,128)(2,1)S(1)}, u32[]{:S(2)}, u32[]{:S(2)}) collective-permute-start(bf16[128,256]{1,0:T(8,128)(2,1)S(1)} %get-tuple-element.28), channel_id=1, source_target_pairs={{0,2},{1,3},{2,4},{3,5},{4,6},{5,7},{6,0},{7,1},{8,10},{9,11},{10,... | collective-permute-start | bytes 196616 | tf_op jit(solution)/shard_map/ppermute | solution.py:32
  34.0 1.6 %collective-permute-start.12 = (bf16[4,128,256]{2,1,0:T(8,128)(2,1)S(1)}, bf16[4,128,256]{2,1,0:T(8,128)(2,1)S(1)}, u32[]{:S(2)}, u32[]{:S(2)}) collective-permute-start(bf16[4,128,256]{2,1,0:T(8,128)(2,1)S(1)} %pad_maximum_fusion.2), channel_id=1, source_target_pairs={{0,1},{1,0},{2,3},{3,2},{4,5},{5,4},{6,7},{7,6},{8,9},{9,8},{10,11... | collective-permute-start | bytes 786440 | tf_op jit(solution)/shard_map/ppermute | solution.py:35

commit v10 on v9

--- a/solution.py
+++ b/solution.py
@@ -33,11 +33,27 @@
         sources.append((me - hop) % n_cand)
     mine = jnp.stack(blocks, axis=0)
     partner = lax.ppermute(mine, "cand", [(i, i ^ 1) for i in range(n_cand)])
-    held = jnp.concatenate([mine, partner], axis=0)
     source = jnp.stack(sources)
-    source = jnp.concatenate([source, source ^ 1])
-    order = jnp.argmax(source[None, :] == jnp.arange(n_cand)[:, None], axis=1)
-    return jnp.take(held, order, axis=0).reshape(-1, rows.shape[1])
+    return (mine, source), (partner, source ^ 1)
+
+
+def attend(query, blocks, sources, w_pair, length, scale_factor):
+    n_blocks, block_rows, d_model = blocks.shape
+    count = n_blocks * block_rows
+    head_size = d_model // HEADS
+    pair_rows = jnp.dot(
+        blocks.reshape(count, d_model), w_pair, preferred_element_type=jnp.float32
+    ).astype(jnp.bfloat16)
+    keys = pair_rows[:, :d_model].reshape(count, HEADS, head_size)
+    values = pair_rows[:, d_model:].reshape(count, HEADS, head_size)
+    scores = jnp.einsum("zun,aun->zua", query, keys, preferred_element_type=jnp.float32) * scale_factor
+    position = (sources[:, None] * block_rows + jnp.arange(block_rows, dtype=jnp.int32)[None, :]).reshape(
+        count
+    )
+    gates = jnp.where(
+        (position < length)[None, None, :], jax.nn.sigmoid(scores), jnp.float32(0.0)
+    ).astype(jnp.bfloat16)
+    return jnp.einsum("bgo,ogl->bgl", gates, values, preferred_element_type=jnp.float32)
 
 
 def wanted_rows(slots, n_slots, rows):
@@ -109,23 +125,10 @@
         jnp.bfloat16
     )
     query_row_matrix = query_row_matrix.reshape(cand_dev, HEADS, head_size)
-    hist_all = gather_over_cand(hist_emb)
-    pair_rows = jnp.dot(hist_all, w_pair, preferred_element_type=jnp.float32).astype(jnp.bfloat16)
-    count = pair_rows.shape[0]
-    key_portion_slice = pair_rows[:, :d_model].reshape(count, HEADS, head_size)
-    value_portion_slice = pair_rows[:, d_model:].reshape(count, HEADS, head_size)
-    score_matrix = (
-        jnp.einsum(
-            "zun,aun->zua", query_row_matrix, key_portion_slice, preferred_element_type=jnp.float32
-        )
-        * scale_factor
-    )
-    live_mask = jnp.arange(count, dtype=jnp.int32) < length
-    gate_weights = jnp.where(
-        live_mask[None, None, :], jax.nn.sigmoid(score_matrix), jnp.float32(0.0)
-    ).astype(jnp.bfloat16)
-    weighted_sum = jnp.einsum(
-        "bgo,ogl->bgl", gate_weights, value_portion_slice, preferred_element_type=jnp.float32
+    halves = gather_over_cand(hist_emb)
+    weighted_sum = sum(
+        attend(query_row_matrix, blocks, sources, w_pair, length, scale_factor)
+        for blocks, sources in halves
     )
     attended = (
         (weighted_sum / jnp.sqrt(length.astype(jnp.float32)))

time: 40.9 us -> 41.7 us (1.020)
  local copies, waits for them, and re-layouts: 7.73 us -> 8.69 us
  other arithmetic: 2.28 us -> 1.51 us
  matrix products: 6.35 us -> 6.96 us
    dot_general x2 -> x4, matrix products: 2.97 us -> 4.22 us  [the longest x2 3.56 us: attend(): jnp.einsum('bgo,ogl->bgl', gates, values, preferred_element_type=jnp.floa...]
    unnamed x12 -> x6, local copies, waits for them, and re-layouts: 0.73 us -> 1.61 us
    concatenate x2 -> x1, local copies, waits for them, and re-layouts: 0.1 us -> 0.91 us  [body(): w_pair = jnp.concatenate([w_key, w_value], axis=1)]
    ppermute x9, waiting for transfers between devices: 1.75 us -> 1.06 us  [swap_over_req(): lax.ppermute(blocks[hop], 'req', [(i, i ^ hop) for i in range(n_req)])]
    dot_general x1, matrix products: 0.87 us -> 0.23 us  [body(): jnp.dot(cand_emb, w_query, preferred_element_type=jnp.float32)]
    another operation x2 -> x1, other arithmetic: 0.65 us -> 0.01 us  [the longest x1 0.63 us: gather_over_cand(): order = jnp.argmax(source[None, :] == jnp.arange(n_cand)[:, None], axis=1)]
    ppermute x3, waiting for transfers between devices: 3.47 us -> 4.1 us  [gather_over_cand(): lax.ppermute(rows, 'cand', [(i, (i + hop) % n_cand) for i in range(n_cand)])]
    gather x1 -> x0, local copies, waits for them, and re-layouts: 0.58 us -> none  [gather_over_cand(): return jnp.take(held, order, axis=0).reshape(-1, rows.shape[1])]
  transfers between devices with their start and end apart: 13 -> 13, of which waited for: 6 -> 5; matrix products, arithmetic and copies ran while one was open for 8% -> 10% of each run, Pallas kernels for 0% -> 0%
where the time goes in v10:
time: 41.7 us; the launch traced here: 41.4 us
  starting transfers between devices  17 us (41%)
  local copies, waits for them, and re-layouts  8.69 us (21%)
  matrix products  6.96 us (17%)
  waiting for transfers between devices  6.29 us (15%)
  other arithmetic  1.51 us (4%)
  between operations  0.94 us (2%)
    ppermute x9, starting transfers between devices, swap_over_req(): lax.ppermute(blocks[hop], 'req', [(i, i ^ hop) for i in range(n_req)])  12.1 us
    gather x1, local copies, waits for them, and re-layouts, body(): jnp.take(table, asked.reshape(-1), axis=0, mode='clip')  5.86 us
    ppermute x3, starting transfers between devices, gather_over_cand(): lax.ppermute(rows, 'cand', [(i, (i + hop) % n_cand) for i in range(n_cand)])  4.89 us
    ppermute x3, waiting for transfers between devices, gather_over_cand(): lax.ppermute(rows, 'cand', [(i, (i + hop) % n_cand) for i in range(n_cand)])  4.1 us
    dot_general x2, matrix products, attend(): jnp.einsum('bgo,ogl->bgl', gates, values, preferred_element_type=jnp.floa...  3.56 us
    unnamed x6, local copies, waits for them, and re-layouts  1.61 us
    dot_general x1, matrix products, body(): jnp.dot(hidden, tower_out, preferred_element_type=jnp.float32)[None, :]  1.24 us
    ppermute x1, waiting for transfers between devices, gather_over_cand(): partner = lax.ppermute(mine, 'cand', [(i, i ^ 1) for i in range(n_cand)])  1.14 us
  transfers between devices with their start and end apart: 13, of which 5 were waited for; matrix products, arithmetic and copies ran while one was open for 10% of the time, Pallas kernels for 0%

profile of v10, /device:TPU:0, one launch (start us, length us, event | category | flops | bytes accessed | tf_op | source)
XLA Modules:
  0.0 41.4 jit_solution(14272407182655495193)
XLA Ops:
  0.0 0.7 %pad_add_fusion.1 = s32[768]{0:T(1024)S(1)} fusion(s32[256]{0:T(256)} %bitcast.110, s32[256]{0:T(256)} %bitcast.111, s32[128]{0:T(128)} %bitcast.112, s32[128]{0:T(128)} %bitcast.113), kind=kLoop, calls=%fused_computation.63 | loop fusion | flops 2304 | bytes 6144 | tf_op jit(solution)/shard_map/concatenate | solution.py:94
  0.8 0.2 convert_reduce_fusion.1
  1.0 0.2 convert_reduce_fusion
  1.2 0.2 convolution_convert_fusion.6
  1.4 0.3 convolution_convert_fusion.5
  1.8 3.0 %collective-permute-start = (s32[320]{0:T(512)S(1)}, s32[320]{0:T(512)S(1)}, u32[]{:S(2)}, u32[]{:S(2)}) collective-permute-start(s32[320]{0:T(512)S(1)} %get-tuple-element.5), channel_id=1, source_target_pairs={{0,8},{8,0},{16,24},{24,16},{1,9},{9,1},{17,25},{25,17},{2,10},{10... | collective-permute-start | bytes 3848 | tf_op jit(solution)/shard_map/ppermute | solution.py:72
  4.8 1.5 %collective-permute-start.2 = (s32[320]{0:T(512)S(1)}, s32[320]{0:T(512)S(1)}, u32[]{:S(2)}, u32[]{:S(2)}) collective-permute-start(s32[320]{0:T(512)S(1)} %get-tuple-element.6), channel_id=1, source_target_pairs={{0,24},{8,16},{16,8},{24,0},{1,25},{9,17},{17,9},{25,1},{2,26},{10... | collective-permute-start | bytes 3848 | tf_op jit(solution)/shard_map/ppermute | solution.py:72
  7.1 0.9 %constant_dynamic-update-slice_fusion.1 = bf16[256,512]{1,0:T(8,128)(2,1)S(1)} fusion(bf16[256,256]{1,0:T(8,128)(2,1)} %param.18), kind=kLoop, calls=%fused_computation.65 | loop fusion | bytes 262144
  8.1 0.9 %constant_dynamic-update-slice_fusion = bf16[256,512]{1,0:T(8,128)(2,1)S(1)} fusion(bf16[256,512]{1,0:T(8,128)(2,1)S(1)} %constant_dynamic-update-slice_fusion.1, bf16[256,256]{1,0:T(8,128)(2,1)} %param.19), kind=kLoop, calls=%fused_computation.64 | loop fusion | bytes 262144 | tf_op jit(solution)/shard_map/concatenate | solution.py:123
  9.0 0.7 %reshape.174 = bf16[1024,1]{0,1:T(2,128)(2,1)S(1)} reshape(bf16[1024]{0:T(1024)(128)(2,1)} %param.21) | data formatting | bytes 4096 | tf_op args[10]
  10.0 5.9 %gather_fusion = bf16[1280,256]{1,0:T(8,128)(2,1)S(1)} fusion(bf16[8192,256]{1,0:T(8,128)(2,1)} %param.11, s32[2048]{0:T(1024)S(1)} %pad_clamp_fusion), kind=kCustom, calls=%fused_computation | custom fusion | bytes 1315840 | tf_op jit(solution)/shard_map/jit(_take)/gather | solution.py:113
  15.9 2.9 %collective-permute-start.8 = (bf16[128,256]{1,0:T(8,128)(2,1)S(1)}, bf16[128,256]{1,0:T(8,128)(2,1)S(1)}, u32[]{:S(2)}, u32[]{:S(2)}) collective-permute-start(bf16[128,256]{1,0:T(8,128)(2,1)S(1)} %get-tuple-element.13), channel_id=1, source_target_pairs={{0,24},{8,16},{16,8},{24,0},{1,25},{9,17},{17,9},{25,1},{2,26},{10... | collective-permute-start | bytes 196616 | tf_op jit(solution)/shard_map/ppermute | solution.py:72
  18.8 0.5 %collective-permute-start.7 = (bf16[128,256]{1,0:T(8,128)(2,1)S(1)}, bf16[128,256]{1,0:T(8,128)(2,1)S(1)}, u32[]{:S(2)}, u32[]{:S(2)}) collective-permute-start(bf16[128,256]{1,0:T(8,128)(2,1)S(1)} %get-tuple-element.14), channel_id=1, source_target_pairs={{0,16},{8,24},{16,0},{24,8},{1,17},{9,25},{17,1},{25,9},{2,18},{10... | collective-permute-start | bytes 196616 | tf_op jit(solution)/shard_map/ppermute | solution.py:72
  19.3 0.2 collective-permute-start.6
  19.5 2.9 %collective-permute-start.5 = (bf16[192,256]{1,0:T(8,128)(2,1)S(1)}, bf16[192,256]{1,0:T(8,128)(2,1)S(1)}, u32[]{:S(2)}, u32[]{:S(2)}) collective-permute-start(bf16[192,256]{1,0:T(8,128)(2,1)S(1)} %get-tuple-element.17), channel_id=1, source_target_pairs={{0,24},{8,16},{16,8},{24,0},{1,25},{9,17},{17,9},{25,1},{2,26},{10... | collective-permute-start | bytes 294920 | tf_op jit(solution)/shard_map/ppermute | solution.py:72
  22.3 0.5 %collective-permute-start.4 = (bf16[192,256]{1,0:T(8,128)(2,1)S(1)}, bf16[192,256]{1,0:T(8,128)(2,1)S(1)}, u32[]{:S(2)}, u32[]{:S(2)}) collective-permute-start(bf16[192,256]{1,0:T(8,128)(2,1)S(1)} %get-tuple-element.18), channel_id=1, source_target_pairs={{0,16},{8,24},{16,0},{24,8},{1,17},{9,25},{17,1},{25,9},{2,18},{10... | collective-permute-start | bytes 294920 | tf_op jit(solution)/shard_map/ppermute | solution.py:72
  22.9 0.6 %collective-permute-start.3 = (bf16[192,256]{1,0:T(8,128)(2,1)S(1)}, bf16[192,256]{1,0:T(8,128)(2,1)S(1)}, u32[]{:S(2)}, u32[]{:S(2)}) collective-permute-start(bf16[192,256]{1,0:T(8,128)(2,1)S(1)} %get-tuple-element.19), channel_id=1, source_target_pairs={{0,8},{8,0},{16,24},{24,16},{1,9},{9,1},{17,25},{25,17},{2,10},{10... | collective-permute-start | bytes 294920 | tf_op jit(solution)/shard_map/ppermute | solution.py:72
  23.4 0.9 %collective-permute-done.7 = bf16[128,256]{1,0:T(8,128)(2,1)S(1)} collective-permute-done((bf16[128,256]{1,0:T(8,128)(2,1)S(1)}, bf16[128,256]{1,0:T(8,128)(2,1)S(1)}, u32[]{:S(2)}, u32[]{:S(2)}) %collective-permute-start.7) | collective-permute-done | bytes 65568 | tf_op jit(solution)/shard_map/ppermute | solution.py:72
  24.4 0.2 convolution_convert_fusion.4
  24.6 3.9 %collective-permute-start.11 = (bf16[128,256]{1,0:T(8,128)(2,1)S(1)}, bf16[128,256]{1,0:T(8,128)(2,1)S(1)}, u32[]{:S(2)}, u32[]{:S(2)}) collective-permute-start(bf16[128,256]{1,0:T(8,128)(2,1)S(1)} %convolution_convert_fusion.4), channel_id=1, source_target_pairs={{0,6},{1,7},{2,0},{3,1},{4,2},{5,3},{6,4},{7,5},{8,14},{9,15},{10,... | collective-permute-start | bytes 196616 | tf_op jit(solution)/shard_map/ppermute | solution.py:32
  28.5 1.0 %collective-permute-start.9 = (bf16[128,256]{1,0:T(8,128)(2,1)S(1)}, bf16[128,256]{1,0:T(8,128)(2,1)S(1)}, u32[]{:S(2)}, u32[]{:S(2)}) collective-permute-start(bf16[128,256]{1,0:T(8,128)(2,1)S(1)} %convolution_convert_fusion.4), channel_id=1, source_target_pairs={{0,2},{1,3},{2,4},{3,5},{4,6},{5,7},{6,0},{7,1},{8,10},{9,11},{10,... | collective-permute-start | bytes 196616 | tf_op jit(solution)/shard_map/ppermute | solution.py:32
  29.6 0.3 convolution_convert_fusion.2
  29.9 0.3 fusion.19
  30.3 0.2 convolution_convert_fusion.3
  30.5 3.2 %collective-permute-done.10 = bf16[128,256]{1,0:T(8,128)(2,1)S(1)} collective-permute-done((bf16[128,256]{1,0:T(8,128)(2,1)S(1)}, bf16[128,256]{1,0:T(8,128)(2,1)S(1)}, u32[]{:S(2)}, u32[]{:S(2)}) %collective-permute-start.10) | collective-permute-done | bytes 65568 | tf_op jit(solution)/shard_map/ppermute | solution.py:32
  33.7 0.9 %collective-permute-done.9 = bf16[128,256]{1,0:T(8,128)(2,1)S(1)} collective-permute-done((bf16[128,256]{1,0:T(8,128)(2,1)S(1)}, bf16[128,256]{1,0:T(8,128)(2,1)S(1)}, u32[]{:S(2)}, u32[]{:S(2)}) %collective-permute-start.9) | collective-permute-done | bytes 65568 | tf_op jit(solution)/shard_map/ppermute | solution.py:32
  34.7 0.3 convolution_convert_fusion.1
  35.1 1.1 %collective-permute-done.12 = bf16[4,128,256]{2,1,0:T(8,128)(2,1)S(1)} collective-permute-done((bf16[4,128,256]{2,1,0:T(8,128)(2,1)S(1)}, bf16[4,128,256]{2,1,0:T(8,128)(2,1)S(1)}, u32[]{:S(2)}, u32[]{:S(2)}) %collective-permute-start.12) | collective-permute-done | bytes 262176 | tf_op jit(solution)/shard_map/ppermute | solution.py:35
  36.2 0.3 convolution_convert_fusion
  36.6 1.7 %fusion.2 = f32[4,64,256]{2,1,0:T(8,128)} fusion(bf16[512,4,64]{0,2,1:T(8,128)(2,1)S(1)} %bitcast.96, bf16[512,4,64]{0,2,1:T(8,128)(2,1)S(1)} %bitcast.95, bf16[256,4,64]{0,2,1:T(8,128)(2,1)S(1)} %bitcast.98, pred[512]{0:T(512)(128)(4,1)S(1)} %get-tuple-element.30), kind=kOutput, calls=%fused_computation.8 | convolution fusion | flops 137363456 | bytes 918016 | tf_op jit(solution)/shard_map/bgo,ogl->bgl/dot_general | solution.py:56
  38.3 1.9 %fusion.6 = bf16[4,64,256]{2,1,0:T(8,128)(2,1)S(1)} fusion(f32[4,64,256]{2,1,0:T(8,128)} %fusion.2, bf16[512,4,64]{0,2,1:T(8,128)(2,1)S(1)} %bitcast.93, bf16[512,4,64]{0,2,1:T(8,128)(2,1)S(1)} %bitcast.92, bf16[256,4,64]{0,2,1:T(8,128)(2,1)S(1)} %bitcast.99, pred[512]{0:T(512)(128)(4,1)S(1)} %get-tuple-element.29, f32[]{:T(128)S(6)} %sqrt.3), kind=kOutput, calls=%fused_computation.17 | convolution fusion | flops 137560064 | bytes 1049092 | tf_op jit(solution)/shard_map/bgo,ogl->bgl/dot_general | solution.py:56
  40.2 1.2 %fusion.11 = f32[1,256]{1,0:T(1,128)} fusion(bf16[1024,1]{0,1:T(2,128)(2,1)S(1)} %reshape.174, f32[256,1024]{1,0:T(8,128)S(1)} %fusion.19, bf16[256,256]{0,1:T(8,128)(2,1)S(1)} %bitcast.114, bf16[512,1024]{1,0:T(8,128)(2,1)S(1)} %copy-done.1), kind=kOutput, calls=%fused_computation.23 | convolution fusion | flops 136314880 | bytes 1709056 | tf_op jit(solution)/shard_map/dot_general | solution.py:142
  (43 shorter events, 1.0 us)
Async XLA Ops:
  0.0 30.2 %copy-start = (bf16[256,256]{1,0:T(8,128)(2,1)S(1)}, bf16[256,256]{1,0:T(8,128)(2,1)}, u32[]{:S(2)}) copy-start(bf16[256,256]{1,0:T(8,128)(2,1)} %param.17) | copy-start | bytes 393220
  1.8 7.9 %collective-permute-start = (s32[320]{0:T(512)S(1)}, s32[320]{0:T(512)S(1)}, u32[]{:S(2)}, u32[]{:S(2)}) collective-permute-start(s32[320]{0:T(512)S(1)} %get-tuple-element.5), channel_id=1, source_target_pairs={{0,8},{8,0},{16,24},{24,16},{1,9},{9,1},{17,25},{25,17},{2,10},{10... | collective-permute-start | bytes 3848 | tf_op jit(solution)/shard_map/ppermute | solution.py:72
  4.8 4.9 %collective-permute-start.2 = (s32[320]{0:T(512)S(1)}, s32[320]{0:T(512)S(1)}, u32[]{:S(2)}, u32[]{:S(2)}) collective-permute-start(s32[320]{0:T(512)S(1)} %get-tuple-element.6), channel_id=1, source_target_pairs={{0,24},{8,16},{16,8},{24,0},{1,25},{9,17},{17,9},{25,1},{2,26},{10... | collective-permute-start | bytes 3848 | tf_op jit(solution)/shard_map/ppermute | solution.py:72
  6.3 3.6 %collective-permute-start.1 = (s32[320]{0:T(512)S(1)}, s32[320]{0:T(512)S(1)}, u32[]{:S(2)}, u32[]{:S(2)}) collective-permute-start(s32[320]{0:T(512)S(1)} %get-tuple-element.7), channel_id=1, source_target_pairs={{0,16},{8,24},{16,0},{24,8},{1,17},{9,25},{17,1},{25,9},{2,18},{10... | collective-permute-start | bytes 3848 | tf_op jit(solution)/shard_map/ppermute | solution.py:72
  15.8 14.1 %copy-start.1 = (bf16[512,1024]{1,0:T(8,128)(2,1)S(1)}, bf16[512,1024]{1,0:T(8,128)(2,1)}, u32[]{:S(2)}) copy-start(bf16[512,1024]{1,0:T(8,128)(2,1)} %param.20) | copy-start | bytes 3145732
  15.9 7.0 %collective-permute-start.8 = (bf16[128,256]{1,0:T(8,128)(2,1)S(1)}, bf16[128,256]{1,0:T(8,128)(2,1)S(1)}, u32[]{:S(2)}, u32[]{:S(2)}) collective-permute-start(bf16[128,256]{1,0:T(8,128)(2,1)S(1)} %get-tuple-element.13), channel_id=1, source_target_pairs={{0,24},{8,16},{16,8},{24,0},{1,25},{9,17},{17,9},{25,1},{2,26},{10... | collective-permute-start | bytes 196616 | tf_op jit(solution)/shard_map/ppermute | solution.py:72
  18.8 5.6 %collective-permute-start.7 = (bf16[128,256]{1,0:T(8,128)(2,1)S(1)}, bf16[128,256]{1,0:T(8,128)(2,1)S(1)}, u32[]{:S(2)}, u32[]{:S(2)}) collective-permute-start(bf16[128,256]{1,0:T(8,128)(2,1)S(1)} %get-tuple-element.14), channel_id=1, source_target_pairs={{0,16},{8,24},{16,0},{24,8},{1,17},{9,25},{17,1},{25,9},{2,18},{10... | collective-permute-start | bytes 196616 | tf_op jit(solution)/shard_map/ppermute | solution.py:72
  19.3 5.1 %collective-permute-start.6 = (bf16[128,256]{1,0:T(8,128)(2,1)S(1)}, bf16[128,256]{1,0:T(8,128)(2,1)S(1)}, u32[]{:S(2)}, u32[]{:S(2)}) collective-permute-start(bf16[128,256]{1,0:T(8,128)(2,1)S(1)} %get-tuple-element.15), channel_id=1, source_target_pairs={{0,8},{8,0},{16,24},{24,16},{1,9},{9,1},{17,25},{25,17},{2,10},{10... | collective-permute-start | bytes 196616 | tf_op jit(solution)/shard_map/ppermute | solution.py:72
  19.5 9.1 %collective-permute-start.5 = (bf16[192,256]{1,0:T(8,128)(2,1)S(1)}, bf16[192,256]{1,0:T(8,128)(2,1)S(1)}, u32[]{:S(2)}, u32[]{:S(2)}) collective-permute-start(bf16[192,256]{1,0:T(8,128)(2,1)S(1)} %get-tuple-element.17), channel_id=1, source_target_pairs={{0,24},{8,16},{16,8},{24,0},{1,25},{9,17},{17,9},{25,1},{2,26},{10... | collective-permute-start | bytes 294920 | tf_op jit(solution)/shard_map/ppermute | solution.py:72
  22.3 7.2 %collective-permute-start.4 = (bf16[192,256]{1,0:T(8,128)(2,1)S(1)}, bf16[192,256]{1,0:T(8,128)(2,1)S(1)}, u32[]{:S(2)}, u32[]{:S(2)}) collective-permute-start(bf16[192,256]{1,0:T(8,128)(2,1)S(1)} %get-tuple-element.18), channel_id=1, source_target_pairs={{0,16},{8,24},{16,0},{24,8},{1,17},{9,25},{17,1},{25,9},{2,18},{10... | collective-permute-start | bytes 294920 | tf_op jit(solution)/shard_map/ppermute | solution.py:72
  22.9 6.7 %collective-permute-start.3 = (bf16[192,256]{1,0:T(8,128)(2,1)S(1)}, bf16[192,256]{1,0:T(8,128)(2,1)S(1)}, u32[]{:S(2)}, u32[]{:S(2)}) collective-permute-start(bf16[192,256]{1,0:T(8,128)(2,1)S(1)} %get-tuple-element.19), channel_id=1, source_target_pairs={{0,8},{8,0},{16,24},{24,16},{1,9},{9,1},{17,25},{25,17},{2,10},{10... | collective-permute-start | bytes 294920 | tf_op jit(solution)/shard_map/ppermute | solution.py:72
  24.6 5.8 %collective-permute-start.11 = (bf16[128,256]{1,0:T(8,128)(2,1)S(1)}, bf16[128,256]{1,0:T(8,128)(2,1)S(1)}, u32[]{:S(2)}, u32[]{:S(2)}) collective-permute-start(bf16[128,256]{1,0:T(8,128)(2,1)S(1)} %convolution_convert_fusion.4), channel_id=1, source_target_pairs={{0,6},{1,7},{2,0},{3,1},{4,2},{5,3},{6,4},{7,5},{8,14},{9,15},{10,... | collective-permute-start | bytes 196616 | tf_op jit(solution)/shard_map/ppermute | solution.py:32
  28.5 5.2 %collective-permute-start.10 = (bf16[128,256]{1,0:T(8,128)(2,1)S(1)}, bf16[128,256]{1,0:T(8,128)(2,1)S(1)}, u32[]{:S(2)}, u32[]{:S(2)}) collective-permute-start(bf16[128,256]{1,0:T(8,128)(2,1)S(1)} %convolution_convert_fusion.4), channel_id=1, source_target_pairs={{0,4},{1,5},{2,6},{3,7},{4,0},{5,1},{6,2},{7,3},{8,12},{9,13},{10,... | collective-permute-start | bytes 196616 | tf_op jit(solution)/shard_map/ppermute | solution.py:32
  28.5 6.1 %collective-permute-start.9 = (bf16[128,256]{1,0:T(8,128)(2,1)S(1)}, bf16[128,256]{1,0:T(8,128)(2,1)S(1)}, u32[]{:S(2)}, u32[]{:S(2)}) collective-permute-start(bf16[128,256]{1,0:T(8,128)(2,1)S(1)} %convolution_convert_fusion.4), channel_id=1, source_target_pairs={{0,2},{1,3},{2,4},{3,5},{4,6},{5,7},{6,0},{7,1},{8,10},{9,11},{10,... | collective-permute-start | bytes 196616 | tf_op jit(solution)/shard_map/ppermute | solution.py:32
  34.6 1.6 %collective-permute-start.12 = (bf16[4,128,256]{2,1,0:T(8,128)(2,1)S(1)}, bf16[4,128,256]{2,1,0:T(8,128)(2,1)S(1)}, u32[]{:S(2)}, u32[]{:S(2)}) collective-permute-start(bf16[4,128,256]{2,1,0:T(8,128)(2,1)S(1)} %pad_maximum_fusion.2), channel_id=1, source_target_pairs={{0,1},{1,0},{2,3},{3,2},{4,5},{5,4},{6,7},{7,6},{8,9},{9,8},{10,11... | collective-permute-start | bytes 786440 | tf_op jit(solution)/shard_map/ppermute | solution.py:35

commit v11 on v10

--- a/solution.py
+++ b/solution.py
@@ -125,10 +125,14 @@
         jnp.bfloat16
     )
     query_row_matrix = query_row_matrix.reshape(cand_dev, HEADS, head_size)
-    halves = gather_over_cand(hist_emb)
-    weighted_sum = sum(
-        attend(query_row_matrix, blocks, sources, w_pair, length, scale_factor)
-        for blocks, sources in halves
+    (mine, mine_sources), (partner, partner_sources) = gather_over_cand(hist_emb)
+    weighted_sum = attend(
+        query_row_matrix,
+        jnp.concatenate([mine, partner], axis=0),
+        jnp.concatenate([mine_sources, partner_sources]),
+        w_pair,
+        length,
+        scale_factor,
     )
     attended = (
         (weighted_sum / jnp.sqrt(length.astype(jnp.float32)))

time: 41.7 us -> 39.1 us (0.938)
  matrix products: 6.96 us -> 4.82 us
  local copies, waits for them, and re-layouts: 8.69 us -> 7.08 us
  waiting for transfers between devices: 6.29 us -> 7.61 us
    dot_general x2 -> x1, matrix products: 3.56 us -> 1.6 us  [attend(): jnp.einsum('bgo,ogl->bgl', gates, values, preferred_element_type=jnp.floa...]
    ppermute x9, waiting for transfers between devices: 1.06 us -> 2.04 us  [swap_over_req(): lax.ppermute(blocks[hop], 'req', [(i, i ^ hop) for i in range(n_req)])]
    unnamed x6 -> x12, local copies, waits for them, and re-layouts: 1.61 us -> 0.73 us
    concatenate x1 -> x2, local copies, waits for them, and re-layouts: 0.91 us -> 0.1 us  [the longest x1 0.09 us: body(): jnp.concatenate([mine_sources, partner_sources])]
  transfers between devices with their start and end apart: 13 -> 13, of which waited for: 5 -> 7; matrix products, arithmetic and copies ran while one was open for 10% -> 6% of each run, Pallas kernels for 0% -> 0%
where the time goes in v11:
time: 39.1 us; the launch traced here: 39 us
  starting transfers between devices  17 us (43%)
  waiting for transfers between devices  7.61 us (19%)
  local copies, waits for them, and re-layouts  7.08 us (18%)
  matrix products  4.82 us (12%)
  other arithmetic  1.51 us (4%)
  between operations  0.96 us (2%)
    ppermute x9, starting transfers between devices, swap_over_req(): lax.ppermute(blocks[hop], 'req', [(i, i ^ hop) for i in range(n_req)])  12 us
    gather x1, local copies, waits for them, and re-layouts, body(): jnp.take(table, asked.reshape(-1), axis=0, mode='clip')  5.96 us
    ppermute x3, starting transfers between devices, gather_over_cand(): lax.ppermute(rows, 'cand', [(i, (i + hop) % n_cand) for i in range(n_cand)])  4.88 us
    ppermute x3, waiting for transfers between devices, gather_over_cand(): lax.ppermute(rows, 'cand', [(i, (i + hop) % n_cand) for i in range(n_cand)])  4.09 us
    ppermute x9, waiting for transfers between devices, swap_over_req(): lax.ppermute(blocks[hop], 'req', [(i, i ^ hop) for i in range(n_req)])  2.04 us
    dot_general x1, matrix products, attend(): jnp.einsum('bgo,ogl->bgl', gates, values, preferred_element_type=jnp.floa...  1.6 us
    ppermute x1, waiting for transfers between devices, gather_over_cand(): partner = lax.ppermute(mine, 'cand', [(i, i ^ 1) for i in range(n_cand)])  1.48 us
    dot_general x1, matrix products, body(): jnp.dot(hidden, tower_out, preferred_element_type=jnp.float32)[None, :]  1.24 us
  transfers between devices with their start and end apart: 13, of which 7 were waited for; matrix products, arithmetic and copies ran while one was open for 6% of the time, Pallas kernels for 0%

profile of v11, /device:TPU:0, one launch (start us, length us, event | category | flops | bytes accessed | tf_op | source)
XLA Modules:
  0.0 39.0 jit_solution(18146440857826599609)
XLA Ops:
  0.0 0.7 %pad_add_fusion.1 = s32[768]{0:T(1024)S(1)} fusion(s32[256]{0:T(256)} %bitcast.92, s32[256]{0:T(256)} %bitcast.93, s32[128]{0:T(128)} %bitcast.94, s32[128]{0:T(128)} %bitcast.95), kind=kLoop, calls=%fused_computation.58 | loop fusion | flops 2304 | bytes 6144 | tf_op jit(solution)/shard_map/concatenate | solution.py:94
  0.8 0.2 convert_reduce_fusion.1
  1.0 0.2 convert_reduce_fusion
  1.2 0.2 convolution_convert_fusion.5
  1.4 0.3 convolution_convert_fusion.4
  1.8 3.0 %collective-permute-start = (s32[320]{0:T(512)S(1)}, s32[320]{0:T(512)S(1)}, u32[]{:S(2)}, u32[]{:S(2)}) collective-permute-start(s32[320]{0:T(512)S(1)} %get-tuple-element.5), channel_id=1, source_target_pairs={{0,8},{8,0},{16,24},{24,16},{1,9},{9,1},{17,25},{25,17},{2,10},{10... | collective-permute-start | bytes 3848 | tf_op jit(solution)/shard_map/ppermute | solution.py:72
  4.8 1.5 %collective-permute-start.2 = (s32[320]{0:T(512)S(1)}, s32[320]{0:T(512)S(1)}, u32[]{:S(2)}, u32[]{:S(2)}) collective-permute-start(s32[320]{0:T(512)S(1)} %get-tuple-element.6), channel_id=1, source_target_pairs={{0,24},{8,16},{16,8},{24,0},{1,25},{9,17},{17,9},{25,1},{2,26},{10... | collective-permute-start | bytes 3848 | tf_op jit(solution)/shard_map/ppermute | solution.py:72
  7.0 0.1 add_xor_fusion
  7.1 0.1 concatenate.39
  7.3 0.7 %reshape.132 = bf16[1024,1]{0,1:T(2,128)(2,1)S(1)} reshape(bf16[1024]{0:T(1024)(128)(2,1)} %param.21) | data formatting | bytes 4096 | tf_op args[10]
  8.0 1.3 %collective-permute-done.2 = s32[320]{0:T(512)S(1)} collective-permute-done((s32[320]{0:T(512)S(1)}, s32[320]{0:T(512)S(1)}, u32[]{:S(2)}, u32[]{:S(2)}) %collective-permute-start.2) | collective-permute-done | bytes 1312 | tf_op jit(solution)/shard_map/ppermute | solution.py:72
  9.3 0.6 %collective-permute-done.1 = s32[320]{0:T(512)S(1)} collective-permute-done((s32[320]{0:T(512)S(1)}, s32[320]{0:T(512)S(1)}, u32[]{:S(2)}, u32[]{:S(2)}) %collective-permute-start.1) | collective-permute-done | bytes 1312 | tf_op jit(solution)/shard_map/ppermute | solution.py:72
  10.0 6.0 %gather_fusion = bf16[1280,256]{1,0:T(8,128)(2,1)S(1)} fusion(bf16[8192,256]{1,0:T(8,128)(2,1)} %param.11, s32[2048]{0:T(1024)S(1)} %pad_clamp_fusion), kind=kCustom, calls=%fused_computation | custom fusion | bytes 1315840 | tf_op jit(solution)/shard_map/jit(_take)/gather | solution.py:113
  16.0 1.5 %collective-permute-start.8 = (bf16[128,256]{1,0:T(8,128)(2,1)S(1)}, bf16[128,256]{1,0:T(8,128)(2,1)S(1)}, u32[]{:S(2)}, u32[]{:S(2)}) collective-permute-start(bf16[128,256]{1,0:T(8,128)(2,1)S(1)} %get-tuple-element.13), channel_id=1, source_target_pairs={{0,24},{8,16},{16,8},{24,0},{1,25},{9,17},{17,9},{25,1},{2,26},{10... | collective-permute-start | bytes 196616 | tf_op jit(solution)/shard_map/ppermute | solution.py:72
  17.5 1.5 %collective-permute-start.7 = (bf16[128,256]{1,0:T(8,128)(2,1)S(1)}, bf16[128,256]{1,0:T(8,128)(2,1)S(1)}, u32[]{:S(2)}, u32[]{:S(2)}) collective-permute-start(bf16[128,256]{1,0:T(8,128)(2,1)S(1)} %get-tuple-element.14), channel_id=1, source_target_pairs={{0,16},{8,24},{16,0},{24,8},{1,17},{9,25},{17,1},{25,9},{2,18},{10... | collective-permute-start | bytes 196616 | tf_op jit(solution)/shard_map/ppermute | solution.py:72
  19.0 0.5 %collective-permute-start.6 = (bf16[128,256]{1,0:T(8,128)(2,1)S(1)}, bf16[128,256]{1,0:T(8,128)(2,1)S(1)}, u32[]{:S(2)}, u32[]{:S(2)}) collective-permute-start(bf16[128,256]{1,0:T(8,128)(2,1)S(1)} %get-tuple-element.15), channel_id=1, source_target_pairs={{0,8},{8,0},{16,24},{24,16},{1,9},{9,1},{17,25},{25,17},{2,10},{10... | collective-permute-start | bytes 196616 | tf_op jit(solution)/shard_map/ppermute | solution.py:72
  19.6 1.5 %collective-permute-start.5 = (bf16[192,256]{1,0:T(8,128)(2,1)S(1)}, bf16[192,256]{1,0:T(8,128)(2,1)S(1)}, u32[]{:S(2)}, u32[]{:S(2)}) collective-permute-start(bf16[192,256]{1,0:T(8,128)(2,1)S(1)} %get-tuple-element.17), channel_id=1, source_target_pairs={{0,24},{8,16},{16,8},{24,0},{1,25},{9,17},{17,9},{25,1},{2,26},{10... | collective-permute-start | bytes 294920 | tf_op jit(solution)/shard_map/ppermute | solution.py:72
  21.1 1.5 %collective-permute-start.4 = (bf16[192,256]{1,0:T(8,128)(2,1)S(1)}, bf16[192,256]{1,0:T(8,128)(2,1)S(1)}, u32[]{:S(2)}, u32[]{:S(2)}) collective-permute-start(bf16[192,256]{1,0:T(8,128)(2,1)S(1)} %get-tuple-element.18), channel_id=1, source_target_pairs={{0,16},{8,24},{16,0},{24,8},{1,17},{9,25},{17,1},{25,9},{2,18},{10... | collective-permute-start | bytes 294920 | tf_op jit(solution)/shard_map/ppermute | solution.py:72
  22.6 0.9 %collective-permute-start.3 = (bf16[192,256]{1,0:T(8,128)(2,1)S(1)}, bf16[192,256]{1,0:T(8,128)(2,1)S(1)}, u32[]{:S(2)}, u32[]{:S(2)}) collective-permute-start(bf16[192,256]{1,0:T(8,128)(2,1)S(1)} %get-tuple-element.19), channel_id=1, source_target_pairs={{0,8},{8,0},{16,24},{24,16},{1,9},{9,1},{17,25},{25,17},{2,10},{10... | collective-permute-start | bytes 294920 | tf_op jit(solution)/shard_map/ppermute | solution.py:72
  23.6 0.1 collective-permute-done.6
  23.7 0.2 constant_dynamic-update-slice_fusion.4
  23.9 3.9 %collective-permute-start.11 = (bf16[128,256]{1,0:T(8,128)(2,1)S(1)}, bf16[128,256]{1,0:T(8,128)(2,1)S(1)}, u32[]{:S(2)}, u32[]{:S(2)}) collective-permute-start(bf16[128,256]{1,0:T(8,128)(2,1)S(1)} %get-tuple-element.26), channel_id=1, source_target_pairs={{0,6},{1,7},{2,0},{3,1},{4,2},{5,3},{6,4},{7,5},{8,14},{9,15},{10,... | collective-permute-start | bytes 196616 | tf_op jit(solution)/shard_map/ppermute | solution.py:32
  27.8 1.0 %collective-permute-start.9 = (bf16[128,256]{1,0:T(8,128)(2,1)S(1)}, bf16[128,256]{1,0:T(8,128)(2,1)S(1)}, u32[]{:S(2)}, u32[]{:S(2)}) collective-permute-start(bf16[128,256]{1,0:T(8,128)(2,1)S(1)} %get-tuple-element.26), channel_id=1, source_target_pairs={{0,2},{1,3},{2,4},{3,5},{4,6},{5,7},{6,0},{7,1},{8,10},{9,11},{10,... | collective-permute-start | bytes 196616 | tf_op jit(solution)/shard_map/ppermute | solution.py:32
  28.9 0.3 convolution_convert_fusion.1
  29.2 0.3 fusion.12
  29.5 0.2 convolution_convert_fusion.2
  29.8 3.2 %collective-permute-done.10 = bf16[128,256]{1,0:T(8,128)(2,1)S(1)} collective-permute-done((bf16[128,256]{1,0:T(8,128)(2,1)S(1)}, bf16[128,256]{1,0:T(8,128)(2,1)S(1)}, u32[]{:S(2)}, u32[]{:S(2)}) %collective-permute-start.10) | collective-permute-done | bytes 65568 | tf_op jit(solution)/shard_map/ppermute | solution.py:32
  33.0 0.9 %collective-permute-done.9 = bf16[128,256]{1,0:T(8,128)(2,1)S(1)} collective-permute-done((bf16[128,256]{1,0:T(8,128)(2,1)S(1)}, bf16[128,256]{1,0:T(8,128)(2,1)S(1)}, u32[]{:S(2)}, u32[]{:S(2)}) %collective-permute-start.9) | collective-permute-done | bytes 65568 | tf_op jit(solution)/shard_map/ppermute | solution.py:32
  34.0 1.5 %collective-permute-done.12 = bf16[4,128,256]{2,1,0:T(8,128)(2,1)S(1)} collective-permute-done((bf16[4,128,256]{2,1,0:T(8,128)(2,1)S(1)}, bf16[4,128,256]{2,1,0:T(8,128)(2,1)S(1)}, u32[]{:S(2)}, u32[]{:S(2)}) %collective-permute-start.12) | collective-permute-done | bytes 262176 | tf_op jit(solution)/shard_map/ppermute | solution.py:35
  35.6 0.5 %convolution_convert_fusion = bf16[1024,512]{0,1:T(8,128)(2,1)S(1)} fusion(bf16[1024,256]{1,0:T(8,128)(2,1)S(1)} %bitcast.76, bf16[256,256]{1,0:T(8,128)(2,1)S(1)} %copy-done.2, bf16[256,256]{1,0:T(8,128)(2,1)S(1)} %copy-done.3), kind=kOutput, calls=%fused_computation.4 | convolution fusion | flops 269484032 | bytes 1835008 | tf_op jit(solution)/shard_map/dot_general | solution.py:44
  36.1 1.6 %fusion.5 = bf16[4,64,256]{2,1,0:T(8,128)(2,1)S(1)} fusion(bf16[1024,4,64]{0,2,1:T(8,128)(2,1)S(1)} %bitcast.78, bf16[1024,4,64]{0,2,1:T(8,128)(2,1)S(1)} %bitcast.77, bf16[256,4,64]{0,2,1:T(8,128)(2,1)S(1)} %bitcast.84, pred[1024]{0:T(1024)(128)(4,1)S(1)} %fusion.23, f32[]{:T(128)S(6)} %sqrt.3), kind=kOutput, calls=%fused_computation.12 | convolution fusion | flops 274857984 | bytes 1311748 | tf_op jit(solution)/shard_map/bgo,ogl->bgl/dot_general | solution.py:56
  37.7 1.2 %fusion.8 = f32[1,256]{1,0:T(1,128)} fusion(bf16[1024,1]{0,1:T(2,128)(2,1)S(1)} %reshape.132, f32[256,1024]{1,0:T(8,128)S(1)} %fusion.12, bf16[256,256]{0,1:T(8,128)(2,1)S(1)} %bitcast.96, bf16[512,1024]{1,0:T(8,128)(2,1)S(1)} %copy-done.1), kind=kOutput, calls=%fused_computation.14 | convolution fusion | flops 136314880 | bytes 1709056 | tf_op jit(solution)/shard_map/dot_general | solution.py:146
  (47 shorter events, 0.9 us)
Async XLA Ops:
  0.0 29.5 %copy-start = (bf16[256,256]{1,0:T(8,128)(2,1)S(1)}, bf16[256,256]{1,0:T(8,128)(2,1)}, u32[]{:S(2)}) copy-start(bf16[256,256]{1,0:T(8,128)(2,1)} %param.17) | copy-start | bytes 393220
  1.8 6.2 %collective-permute-start = (s32[320]{0:T(512)S(1)}, s32[320]{0:T(512)S(1)}, u32[]{:S(2)}, u32[]{:S(2)}) collective-permute-start(s32[320]{0:T(512)S(1)} %get-tuple-element.5), channel_id=1, source_target_pairs={{0,8},{8,0},{16,24},{24,16},{1,9},{9,1},{17,25},{25,17},{2,10},{10... | collective-permute-start | bytes 3848 | tf_op jit(solution)/shard_map/ppermute | solution.py:72
  4.8 4.5 %collective-permute-start.2 = (s32[320]{0:T(512)S(1)}, s32[320]{0:T(512)S(1)}, u32[]{:S(2)}, u32[]{:S(2)}) collective-permute-start(s32[320]{0:T(512)S(1)} %get-tuple-element.6), channel_id=1, source_target_pairs={{0,24},{8,16},{16,8},{24,0},{1,25},{9,17},{17,9},{25,1},{2,26},{10... | collective-permute-start | bytes 3848 | tf_op jit(solution)/shard_map/ppermute | solution.py:72
  6.3 3.6 %collective-permute-start.1 = (s32[320]{0:T(512)S(1)}, s32[320]{0:T(512)S(1)}, u32[]{:S(2)}, u32[]{:S(2)}) collective-permute-start(s32[320]{0:T(512)S(1)} %get-tuple-element.7), channel_id=1, source_target_pairs={{0,16},{8,24},{16,0},{24,8},{1,17},{9,25},{17,1},{25,9},{2,18},{10... | collective-permute-start | bytes 3848 | tf_op jit(solution)/shard_map/ppermute | solution.py:72
  10.0 19.2 %copy-start.1 = (bf16[512,1024]{1,0:T(8,128)(2,1)S(1)}, bf16[512,1024]{1,0:T(8,128)(2,1)}, u32[]{:S(2)}) copy-start(bf16[512,1024]{1,0:T(8,128)(2,1)} %param.20) | copy-start | bytes 3145732
  15.9 19.6 %copy-start.2 = (bf16[256,256]{1,0:T(8,128)(2,1)S(1)}, bf16[256,256]{1,0:T(8,128)(2,1)}, u32[]{:S(2)}) copy-start(bf16[256,256]{1,0:T(8,128)(2,1)} %param.19) | copy-start | bytes 393220
  15.9 19.6 %copy-start.3 = (bf16[256,256]{1,0:T(8,128)(2,1)S(1)}, bf16[256,256]{1,0:T(8,128)(2,1)}, u32[]{:S(2)}) copy-start(bf16[256,256]{1,0:T(8,128)(2,1)} %param.18) | copy-start | bytes 393220
  16.0 6.6 %collective-permute-start.8 = (bf16[128,256]{1,0:T(8,128)(2,1)S(1)}, bf16[128,256]{1,0:T(8,128)(2,1)S(1)}, u32[]{:S(2)}, u32[]{:S(2)}) collective-permute-start(bf16[128,256]{1,0:T(8,128)(2,1)S(1)} %get-tuple-element.13), channel_id=1, source_target_pairs={{0,24},{8,16},{16,8},{24,0},{1,25},{9,17},{17,9},{25,1},{2,26},{10... | collective-permute-start | bytes 196616 | tf_op jit(solution)/shard_map/ppermute | solution.py:72
  17.5 6.1 %collective-permute-start.7 = (bf16[128,256]{1,0:T(8,128)(2,1)S(1)}, bf16[128,256]{1,0:T(8,128)(2,1)S(1)}, u32[]{:S(2)}, u32[]{:S(2)}) collective-permute-start(bf16[128,256]{1,0:T(8,128)(2,1)S(1)} %get-tuple-element.14), channel_id=1, source_target_pairs={{0,16},{8,24},{16,0},{24,8},{1,17},{9,25},{17,1},{25,9},{2,18},{10... | collective-permute-start | bytes 196616 | tf_op jit(solution)/shard_map/ppermute | solution.py:72
  19.0 4.7 %collective-permute-start.6 = (bf16[128,256]{1,0:T(8,128)(2,1)S(1)}, bf16[128,256]{1,0:T(8,128)(2,1)S(1)}, u32[]{:S(2)}, u32[]{:S(2)}) collective-permute-start(bf16[128,256]{1,0:T(8,128)(2,1)S(1)} %get-tuple-element.15), channel_id=1, source_target_pairs={{0,8},{8,0},{16,24},{24,16},{1,9},{9,1},{17,25},{25,17},{2,10},{10... | collective-permute-start | bytes 196616 | tf_op jit(solution)/shard_map/ppermute | solution.py:72
  19.6 8.2 %collective-permute-start.5 = (bf16[192,256]{1,0:T(8,128)(2,1)S(1)}, bf16[192,256]{1,0:T(8,128)(2,1)S(1)}, u32[]{:S(2)}, u32[]{:S(2)}) collective-permute-start(bf16[192,256]{1,0:T(8,128)(2,1)S(1)} %get-tuple-element.17), channel_id=1, source_target_pairs={{0,24},{8,16},{16,8},{24,0},{1,25},{9,17},{17,9},{25,1},{2,26},{10... | collective-permute-start | bytes 294920 | tf_op jit(solution)/shard_map/ppermute | solution.py:72
  21.1 7.8 %collective-permute-start.4 = (bf16[192,256]{1,0:T(8,128)(2,1)S(1)}, bf16[192,256]{1,0:T(8,128)(2,1)S(1)}, u32[]{:S(2)}, u32[]{:S(2)}) collective-permute-start(bf16[192,256]{1,0:T(8,128)(2,1)S(1)} %get-tuple-element.18), channel_id=1, source_target_pairs={{0,16},{8,24},{16,0},{24,8},{1,17},{9,25},{17,1},{25,9},{2,18},{10... | collective-permute-start | bytes 294920 | tf_op jit(solution)/shard_map/ppermute | solution.py:72
  22.6 6.2 %collective-permute-start.3 = (bf16[192,256]{1,0:T(8,128)(2,1)S(1)}, bf16[192,256]{1,0:T(8,128)(2,1)S(1)}, u32[]{:S(2)}, u32[]{:S(2)}) collective-permute-start(bf16[192,256]{1,0:T(8,128)(2,1)S(1)} %get-tuple-element.19), channel_id=1, source_target_pairs={{0,8},{8,0},{16,24},{24,16},{1,9},{9,1},{17,25},{25,17},{2,10},{10... | collective-permute-start | bytes 294920 | tf_op jit(solution)/shard_map/ppermute | solution.py:72
  23.9 5.8 %collective-permute-start.11 = (bf16[128,256]{1,0:T(8,128)(2,1)S(1)}, bf16[128,256]{1,0:T(8,128)(2,1)S(1)}, u32[]{:S(2)}, u32[]{:S(2)}) collective-permute-start(bf16[128,256]{1,0:T(8,128)(2,1)S(1)} %get-tuple-element.26), channel_id=1, source_target_pairs={{0,6},{1,7},{2,0},{3,1},{4,2},{5,3},{6,4},{7,5},{8,14},{9,15},{10,... | collective-permute-start | bytes 196616 | tf_op jit(solution)/shard_map/ppermute | solution.py:32
  27.8 5.2 %collective-permute-start.10 = (bf16[128,256]{1,0:T(8,128)(2,1)S(1)}, bf16[128,256]{1,0:T(8,128)(2,1)S(1)}, u32[]{:S(2)}, u32[]{:S(2)}) collective-permute-start(bf16[128,256]{1,0:T(8,128)(2,1)S(1)} %get-tuple-element.26), channel_id=1, source_target_pairs={{0,4},{1,5},{2,6},{3,7},{4,0},{5,1},{6,2},{7,3},{8,12},{9,13},{10,... | collective-permute-start | bytes 196616 | tf_op jit(solution)/shard_map/ppermute | solution.py:32
  27.8 6.1 %collective-permute-start.9 = (bf16[128,256]{1,0:T(8,128)(2,1)S(1)}, bf16[128,256]{1,0:T(8,128)(2,1)S(1)}, u32[]{:S(2)}, u32[]{:S(2)}) collective-permute-start(bf16[128,256]{1,0:T(8,128)(2,1)S(1)} %get-tuple-element.26), channel_id=1, source_target_pairs={{0,2},{1,3},{2,4},{3,5},{4,6},{5,7},{6,0},{7,1},{8,10},{9,11},{10,... | collective-permute-start | bytes 196616 | tf_op jit(solution)/shard_map/ppermute | solution.py:32
  33.9 1.6 %collective-permute-start.12 = (bf16[4,128,256]{2,1,0:T(8,128)(2,1)S(1)}, bf16[4,128,256]{2,1,0:T(8,128)(2,1)S(1)}, u32[]{:S(2)}, u32[]{:S(2)}) collective-permute-start(bf16[4,128,256]{2,1,0:T(8,128)(2,1)S(1)} %pad_maximum_fusion.2), channel_id=1, source_target_pairs={{0,1},{1,0},{2,3},{3,2},{4,5},{5,4},{6,7},{7,6},{8,9},{9,8},{10,11... | collective-permute-start | bytes 786440 | tf_op jit(solution)/shard_map/ppermute | solution.py:35

commit v12 on v11

--- a/solution.py
+++ b/solution.py
@@ -37,6 +37,10 @@
     return (mine, source), (partner, source ^ 1)
 
 
+def logistic(x):
+    return 0.5 + 0.5 * jnp.tanh(0.5 * x)
+
+
 def attend(query, blocks, sources, w_pair, length, scale_factor):
     n_blocks, block_rows, d_model = blocks.shape
     count = n_blocks * block_rows
@@ -51,7 +55,7 @@
         count
     )
     gates = jnp.where(
-        (position < length)[None, None, :], jax.nn.sigmoid(scores), jnp.float32(0.0)
+        (position < length)[None, None, :], logistic(scores), jnp.float32(0.0)
     ).astype(jnp.bfloat16)
     return jnp.einsum("bgo,ogl->bgl", gates, values, preferred_element_type=jnp.float32)
 
@@ -142,7 +146,7 @@
     pre_act = jnp.dot(cand_emb, tower_in[:d_model], preferred_element_type=jnp.float32) + jnp.dot(
         attended, tower_in[d_model:], preferred_element_type=jnp.float32
     )
-    hidden = jax.nn.silu(pre_act).astype(jnp.bfloat16)
+    hidden = (pre_act * logistic(pre_act)).astype(jnp.bfloat16)
     return jnp.dot(hidden, tower_out, preferred_element_type=jnp.float32)[None, :]
 
 

time: 39.1 us -> 38.8 us (level)
  no operation moved by 1% of the time
where the time goes in v12:
time: 38.8 us; the launch traced here: 38.6 us
  starting transfers between devices  17 us (44%)
  waiting for transfers between devices  7.61 us (20%)
  local copies, waits for them, and re-layouts  7.08 us (18%)
  matrix products  4.5 us (12%)
  other arithmetic  1.51 us (4%)
  between operations  0.96 us (2%)
    ppermute x9, starting transfers between devices, swap_over_req(): lax.ppermute(blocks[hop], 'req', [(i, i ^ hop) for i in range(n_req)])  12 us
    gather x1, local copies, waits for them, and re-layouts, body(): jnp.take(table, asked.reshape(-1), axis=0, mode='clip')  5.96 us
    ppermute x3, starting transfers between devices, gather_over_cand(): lax.ppermute(rows, 'cand', [(i, (i + hop) % n_cand) for i in range(n_cand)])  4.88 us
    ppermute x3, waiting for transfers between devices, gather_over_cand(): lax.ppermute(rows, 'cand', [(i, (i + hop) % n_cand) for i in range(n_cand)])  4.09 us
    ppermute x9, waiting for transfers between devices, swap_over_req(): lax.ppermute(blocks[hop], 'req', [(i, i ^ hop) for i in range(n_req)])  2.04 us
    ppermute x1, waiting for transfers between devices, gather_over_cand(): partner = lax.ppermute(mine, 'cand', [(i, i ^ 1) for i in range(n_cand)])  1.48 us
    dot_general x1, matrix products, attend(): jnp.einsum('bgo,ogl->bgl', gates, values, preferred_element_type=jnp.floa...  1.32 us
    dot_general x1, matrix products, body(): jnp.dot(hidden, tower_out, preferred_element_type=jnp.float32)[None, :]  1.2 us
  transfers between devices with their start and end apart: 13, of which 7 were waited for; matrix products, arithmetic and copies ran while one was open for 6% of the time, Pallas kernels for 0%

profile of v12, /device:TPU:0, one launch (start us, length us, event | category | flops | bytes accessed | tf_op | source)
XLA Modules:
  0.0 38.6 jit_solution(3973750802305294605)
XLA Ops:
  0.0 0.7 %pad_add_fusion.1 = s32[768]{0:T(1024)S(1)} fusion(s32[256]{0:T(256)} %bitcast.92, s32[256]{0:T(256)} %bitcast.93, s32[128]{0:T(128)} %bitcast.94, s32[128]{0:T(128)} %bitcast.95), kind=kLoop, calls=%fused_computation.58 | loop fusion | flops 2304 | bytes 6144 | tf_op jit(solution)/shard_map/concatenate | solution.py:98
  0.8 0.2 convert_reduce_fusion.1
  1.0 0.2 convert_reduce_fusion
  1.2 0.2 convolution_convert_fusion.5
  1.4 0.3 convolution_convert_fusion.4
  1.8 3.0 %collective-permute-start = (s32[320]{0:T(512)S(1)}, s32[320]{0:T(512)S(1)}, u32[]{:S(2)}, u32[]{:S(2)}) collective-permute-start(s32[320]{0:T(512)S(1)} %get-tuple-element.5), channel_id=1, source_target_pairs={{0,8},{8,0},{16,24},{24,16},{1,9},{9,1},{17,25},{25,17},{2,10},{10... | collective-permute-start | bytes 3848 | tf_op jit(solution)/shard_map/ppermute | solution.py:76
  4.8 1.5 %collective-permute-start.2 = (s32[320]{0:T(512)S(1)}, s32[320]{0:T(512)S(1)}, u32[]{:S(2)}, u32[]{:S(2)}) collective-permute-start(s32[320]{0:T(512)S(1)} %get-tuple-element.6), channel_id=1, source_target_pairs={{0,24},{8,16},{16,8},{24,0},{1,25},{9,17},{17,9},{25,1},{2,26},{10... | collective-permute-start | bytes 3848 | tf_op jit(solution)/shard_map/ppermute | solution.py:76
  7.0 0.1 add_xor_fusion
  7.1 0.1 concatenate.39
  7.3 0.7 %reshape.132 = bf16[1024,1]{0,1:T(2,128)(2,1)S(1)} reshape(bf16[1024]{0:T(1024)(128)(2,1)} %param.21) | data formatting | bytes 4096 | tf_op args[10]
  8.0 1.3 %collective-permute-done.2 = s32[320]{0:T(512)S(1)} collective-permute-done((s32[320]{0:T(512)S(1)}, s32[320]{0:T(512)S(1)}, u32[]{:S(2)}, u32[]{:S(2)}) %collective-permute-start.2) | collective-permute-done | bytes 1312 | tf_op jit(solution)/shard_map/ppermute | solution.py:76
  9.3 0.6 %collective-permute-done.1 = s32[320]{0:T(512)S(1)} collective-permute-done((s32[320]{0:T(512)S(1)}, s32[320]{0:T(512)S(1)}, u32[]{:S(2)}, u32[]{:S(2)}) %collective-permute-start.1) | collective-permute-done | bytes 1312 | tf_op jit(solution)/shard_map/ppermute | solution.py:76
  10.0 6.0 %gather_fusion = bf16[1280,256]{1,0:T(8,128)(2,1)S(1)} fusion(bf16[8192,256]{1,0:T(8,128)(2,1)} %param.11, s32[2048]{0:T(1024)S(1)} %pad_clamp_fusion), kind=kCustom, calls=%fused_computation | custom fusion | bytes 1315840 | tf_op jit(solution)/shard_map/jit(_take)/gather | solution.py:117
  16.0 1.5 %collective-permute-start.8 = (bf16[128,256]{1,0:T(8,128)(2,1)S(1)}, bf16[128,256]{1,0:T(8,128)(2,1)S(1)}, u32[]{:S(2)}, u32[]{:S(2)}) collective-permute-start(bf16[128,256]{1,0:T(8,128)(2,1)S(1)} %get-tuple-element.13), channel_id=1, source_target_pairs={{0,24},{8,16},{16,8},{24,0},{1,25},{9,17},{17,9},{25,1},{2,26},{10... | collective-permute-start | bytes 196616 | tf_op jit(solution)/shard_map/ppermute | solution.py:76
  17.5 1.5 %collective-permute-start.7 = (bf16[128,256]{1,0:T(8,128)(2,1)S(1)}, bf16[128,256]{1,0:T(8,128)(2,1)S(1)}, u32[]{:S(2)}, u32[]{:S(2)}) collective-permute-start(bf16[128,256]{1,0:T(8,128)(2,1)S(1)} %get-tuple-element.14), channel_id=1, source_target_pairs={{0,16},{8,24},{16,0},{24,8},{1,17},{9,25},{17,1},{25,9},{2,18},{10... | collective-permute-start | bytes 196616 | tf_op jit(solution)/shard_map/ppermute | solution.py:76
  19.0 0.5 %collective-permute-start.6 = (bf16[128,256]{1,0:T(8,128)(2,1)S(1)}, bf16[128,256]{1,0:T(8,128)(2,1)S(1)}, u32[]{:S(2)}, u32[]{:S(2)}) collective-permute-start(bf16[128,256]{1,0:T(8,128)(2,1)S(1)} %get-tuple-element.15), channel_id=1, source_target_pairs={{0,8},{8,0},{16,24},{24,16},{1,9},{9,1},{17,25},{25,17},{2,10},{10... | collective-permute-start | bytes 196616 | tf_op jit(solution)/shard_map/ppermute | solution.py:76
  19.6 1.5 %collective-permute-start.5 = (bf16[192,256]{1,0:T(8,128)(2,1)S(1)}, bf16[192,256]{1,0:T(8,128)(2,1)S(1)}, u32[]{:S(2)}, u32[]{:S(2)}) collective-permute-start(bf16[192,256]{1,0:T(8,128)(2,1)S(1)} %get-tuple-element.17), channel_id=1, source_target_pairs={{0,24},{8,16},{16,8},{24,0},{1,25},{9,17},{17,9},{25,1},{2,26},{10... | collective-permute-start | bytes 294920 | tf_op jit(solution)/shard_map/ppermute | solution.py:76
  21.1 1.5 %collective-permute-start.4 = (bf16[192,256]{1,0:T(8,128)(2,1)S(1)}, bf16[192,256]{1,0:T(8,128)(2,1)S(1)}, u32[]{:S(2)}, u32[]{:S(2)}) collective-permute-start(bf16[192,256]{1,0:T(8,128)(2,1)S(1)} %get-tuple-element.18), channel_id=1, source_target_pairs={{0,16},{8,24},{16,0},{24,8},{1,17},{9,25},{17,1},{25,9},{2,18},{10... | collective-permute-start | bytes 294920 | tf_op jit(solution)/shard_map/ppermute | solution.py:76
  22.6 0.9 %collective-permute-start.3 = (bf16[192,256]{1,0:T(8,128)(2,1)S(1)}, bf16[192,256]{1,0:T(8,128)(2,1)S(1)}, u32[]{:S(2)}, u32[]{:S(2)}) collective-permute-start(bf16[192,256]{1,0:T(8,128)(2,1)S(1)} %get-tuple-element.19), channel_id=1, source_target_pairs={{0,8},{8,0},{16,24},{24,16},{1,9},{9,1},{17,25},{25,17},{2,10},{10... | collective-permute-start | bytes 294920 | tf_op jit(solution)/shard_map/ppermute | solution.py:76
  23.6 0.1 collective-permute-done.6
  23.7 0.2 constant_dynamic-update-slice_fusion.4
  23.9 3.9 %collective-permute-start.11 = (bf16[128,256]{1,0:T(8,128)(2,1)S(1)}, bf16[128,256]{1,0:T(8,128)(2,1)S(1)}, u32[]{:S(2)}, u32[]{:S(2)}) collective-permute-start(bf16[128,256]{1,0:T(8,128)(2,1)S(1)} %get-tuple-element.26), channel_id=1, source_target_pairs={{0,6},{1,7},{2,0},{3,1},{4,2},{5,3},{6,4},{7,5},{8,14},{9,15},{10,... | collective-permute-start | bytes 196616 | tf_op jit(solution)/shard_map/ppermute | solution.py:32
  27.8 1.0 %collective-permute-start.9 = (bf16[128,256]{1,0:T(8,128)(2,1)S(1)}, bf16[128,256]{1,0:T(8,128)(2,1)S(1)}, u32[]{:S(2)}, u32[]{:S(2)}) collective-permute-start(bf16[128,256]{1,0:T(8,128)(2,1)S(1)} %get-tuple-element.26), channel_id=1, source_target_pairs={{0,2},{1,3},{2,4},{3,5},{4,6},{5,7},{6,0},{7,1},{8,10},{9,11},{10,... | collective-permute-start | bytes 196616 | tf_op jit(solution)/shard_map/ppermute | solution.py:32
  28.9 0.3 convolution_convert_fusion.1
  29.2 0.3 fusion.12
  29.5 0.2 convolution_convert_fusion.2
  29.8 3.2 %collective-permute-done.10 = bf16[128,256]{1,0:T(8,128)(2,1)S(1)} collective-permute-done((bf16[128,256]{1,0:T(8,128)(2,1)S(1)}, bf16[128,256]{1,0:T(8,128)(2,1)S(1)}, u32[]{:S(2)}, u32[]{:S(2)}) %collective-permute-start.10) | collective-permute-done | bytes 65568 | tf_op jit(solution)/shard_map/ppermute | solution.py:32
  33.0 0.9 %collective-permute-done.9 = bf16[128,256]{1,0:T(8,128)(2,1)S(1)} collective-permute-done((bf16[128,256]{1,0:T(8,128)(2,1)S(1)}, bf16[128,256]{1,0:T(8,128)(2,1)S(1)}, u32[]{:S(2)}, u32[]{:S(2)}) %collective-permute-start.9) | collective-permute-done | bytes 65568 | tf_op jit(solution)/shard_map/ppermute | solution.py:32
  34.0 1.5 %collective-permute-done.12 = bf16[4,128,256]{2,1,0:T(8,128)(2,1)S(1)} collective-permute-done((bf16[4,128,256]{2,1,0:T(8,128)(2,1)S(1)}, bf16[4,128,256]{2,1,0:T(8,128)(2,1)S(1)}, u32[]{:S(2)}, u32[]{:S(2)}) %collective-permute-start.12) | collective-permute-done | bytes 262176 | tf_op jit(solution)/shard_map/ppermute | solution.py:35
  35.6 0.5 %convolution_convert_fusion = bf16[1024,512]{0,1:T(8,128)(2,1)S(1)} fusion(bf16[1024,256]{1,0:T(8,128)(2,1)S(1)} %bitcast.76, bf16[256,256]{1,0:T(8,128)(2,1)S(1)} %copy-done.2, bf16[256,256]{1,0:T(8,128)(2,1)S(1)} %copy-done.3), kind=kOutput, calls=%fused_computation.4 | convolution fusion | flops 269484032 | bytes 1835008 | tf_op jit(solution)/shard_map/dot_general | solution.py:48
  36.1 1.3 %fusion.5 = bf16[4,64,256]{2,1,0:T(8,128)(2,1)S(1)} fusion(bf16[1024,4,64]{0,2,1:T(8,128)(2,1)S(1)} %bitcast.78, bf16[1024,4,64]{0,2,1:T(8,128)(2,1)S(1)} %bitcast.77, bf16[256,4,64]{0,2,1:T(8,128)(2,1)S(1)} %bitcast.84, pred[1024]{0:T(1024)(128)(4,1)S(1)} %fusion.23, f32[]{:T(128)S(6)} %sqrt.3), kind=kOutput, calls=%fused_computation.12 | convolution fusion | flops 273809408 | bytes 1311748 | tf_op jit(solution)/shard_map/bgo,ogl->bgl/dot_general | solution.py:60
  37.4 1.2 %fusion.8 = f32[1,256]{1,0:T(1,128)} fusion(bf16[1024,1]{0,1:T(2,128)(2,1)S(1)} %reshape.132, f32[256,1024]{1,0:T(8,128)S(1)} %fusion.12, bf16[256,256]{0,1:T(8,128)(2,1)S(1)} %bitcast.96, bf16[512,1024]{1,0:T(8,128)(2,1)S(1)} %copy-done.1), kind=kOutput, calls=%fused_computation.14 | convolution fusion | flops 136314880 | bytes 1709056 | tf_op jit(solution)/shard_map/dot_general | solution.py:150
  (47 shorter events, 0.9 us)
Async XLA Ops:
  0.0 29.5 %copy-start = (bf16[256,256]{1,0:T(8,128)(2,1)S(1)}, bf16[256,256]{1,0:T(8,128)(2,1)}, u32[]{:S(2)}) copy-start(bf16[256,256]{1,0:T(8,128)(2,1)} %param.17) | copy-start | bytes 393220
  1.8 6.2 %collective-permute-start = (s32[320]{0:T(512)S(1)}, s32[320]{0:T(512)S(1)}, u32[]{:S(2)}, u32[]{:S(2)}) collective-permute-start(s32[320]{0:T(512)S(1)} %get-tuple-element.5), channel_id=1, source_target_pairs={{0,8},{8,0},{16,24},{24,16},{1,9},{9,1},{17,25},{25,17},{2,10},{10... | collective-permute-start | bytes 3848 | tf_op jit(solution)/shard_map/ppermute | solution.py:76
  4.8 4.5 %collective-permute-start.2 = (s32[320]{0:T(512)S(1)}, s32[320]{0:T(512)S(1)}, u32[]{:S(2)}, u32[]{:S(2)}) collective-permute-start(s32[320]{0:T(512)S(1)} %get-tuple-element.6), channel_id=1, source_target_pairs={{0,24},{8,16},{16,8},{24,0},{1,25},{9,17},{17,9},{25,1},{2,26},{10... | collective-permute-start | bytes 3848 | tf_op jit(solution)/shard_map/ppermute | solution.py:76
  6.3 3.6 %collective-permute-start.1 = (s32[320]{0:T(512)S(1)}, s32[320]{0:T(512)S(1)}, u32[]{:S(2)}, u32[]{:S(2)}) collective-permute-start(s32[320]{0:T(512)S(1)} %get-tuple-element.7), channel_id=1, source_target_pairs={{0,16},{8,24},{16,0},{24,8},{1,17},{9,25},{17,1},{25,9},{2,18},{10... | collective-permute-start | bytes 3848 | tf_op jit(solution)/shard_map/ppermute | solution.py:76
  10.0 19.2 %copy-start.1 = (bf16[512,1024]{1,0:T(8,128)(2,1)S(1)}, bf16[512,1024]{1,0:T(8,128)(2,1)}, u32[]{:S(2)}) copy-start(bf16[512,1024]{1,0:T(8,128)(2,1)} %param.20) | copy-start | bytes 3145732
  15.9 19.6 %copy-start.2 = (bf16[256,256]{1,0:T(8,128)(2,1)S(1)}, bf16[256,256]{1,0:T(8,128)(2,1)}, u32[]{:S(2)}) copy-start(bf16[256,256]{1,0:T(8,128)(2,1)} %param.19) | copy-start | bytes 393220
  15.9 19.6 %copy-start.3 = (bf16[256,256]{1,0:T(8,128)(2,1)S(1)}, bf16[256,256]{1,0:T(8,128)(2,1)}, u32[]{:S(2)}) copy-start(bf16[256,256]{1,0:T(8,128)(2,1)} %param.18) | copy-start | bytes 393220
  16.0 6.6 %collective-permute-start.8 = (bf16[128,256]{1,0:T(8,128)(2,1)S(1)}, bf16[128,256]{1,0:T(8,128)(2,1)S(1)}, u32[]{:S(2)}, u32[]{:S(2)}) collective-permute-start(bf16[128,256]{1,0:T(8,128)(2,1)S(1)} %get-tuple-element.13), channel_id=1, source_target_pairs={{0,24},{8,16},{16,8},{24,0},{1,25},{9,17},{17,9},{25,1},{2,26},{10... | collective-permute-start | bytes 196616 | tf_op jit(solution)/shard_map/ppermute | solution.py:76
  17.5 6.1 %collective-permute-start.7 = (bf16[128,256]{1,0:T(8,128)(2,1)S(1)}, bf16[128,256]{1,0:T(8,128)(2,1)S(1)}, u32[]{:S(2)}, u32[]{:S(2)}) collective-permute-start(bf16[128,256]{1,0:T(8,128)(2,1)S(1)} %get-tuple-element.14), channel_id=1, source_target_pairs={{0,16},{8,24},{16,0},{24,8},{1,17},{9,25},{17,1},{25,9},{2,18},{10... | collective-permute-start | bytes 196616 | tf_op jit(solution)/shard_map/ppermute | solution.py:76
  19.0 4.7 %collective-permute-start.6 = (bf16[128,256]{1,0:T(8,128)(2,1)S(1)}, bf16[128,256]{1,0:T(8,128)(2,1)S(1)}, u32[]{:S(2)}, u32[]{:S(2)}) collective-permute-start(bf16[128,256]{1,0:T(8,128)(2,1)S(1)} %get-tuple-element.15), channel_id=1, source_target_pairs={{0,8},{8,0},{16,24},{24,16},{1,9},{9,1},{17,25},{25,17},{2,10},{10... | collective-permute-start | bytes 196616 | tf_op jit(solution)/shard_map/ppermute | solution.py:76
  19.6 8.2 %collective-permute-start.5 = (bf16[192,256]{1,0:T(8,128)(2,1)S(1)}, bf16[192,256]{1,0:T(8,128)(2,1)S(1)}, u32[]{:S(2)}, u32[]{:S(2)}) collective-permute-start(bf16[192,256]{1,0:T(8,128)(2,1)S(1)} %get-tuple-element.17), channel_id=1, source_target_pairs={{0,24},{8,16},{16,8},{24,0},{1,25},{9,17},{17,9},{25,1},{2,26},{10... | collective-permute-start | bytes 294920 | tf_op jit(solution)/shard_map/ppermute | solution.py:76
  21.1 7.8 %collective-permute-start.4 = (bf16[192,256]{1,0:T(8,128)(2,1)S(1)}, bf16[192,256]{1,0:T(8,128)(2,1)S(1)}, u32[]{:S(2)}, u32[]{:S(2)}) collective-permute-start(bf16[192,256]{1,0:T(8,128)(2,1)S(1)} %get-tuple-element.18), channel_id=1, source_target_pairs={{0,16},{8,24},{16,0},{24,8},{1,17},{9,25},{17,1},{25,9},{2,18},{10... | collective-permute-start | bytes 294920 | tf_op jit(solution)/shard_map/ppermute | solution.py:76
  22.6 6.2 %collective-permute-start.3 = (bf16[192,256]{1,0:T(8,128)(2,1)S(1)}, bf16[192,256]{1,0:T(8,128)(2,1)S(1)}, u32[]{:S(2)}, u32[]{:S(2)}) collective-permute-start(bf16[192,256]{1,0:T(8,128)(2,1)S(1)} %get-tuple-element.19), channel_id=1, source_target_pairs={{0,8},{8,0},{16,24},{24,16},{1,9},{9,1},{17,25},{25,17},{2,10},{10... | collective-permute-start | bytes 294920 | tf_op jit(solution)/shard_map/ppermute | solution.py:76
  23.9 5.8 %collective-permute-start.11 = (bf16[128,256]{1,0:T(8,128)(2,1)S(1)}, bf16[128,256]{1,0:T(8,128)(2,1)S(1)}, u32[]{:S(2)}, u32[]{:S(2)}) collective-permute-start(bf16[128,256]{1,0:T(8,128)(2,1)S(1)} %get-tuple-element.26), channel_id=1, source_target_pairs={{0,6},{1,7},{2,0},{3,1},{4,2},{5,3},{6,4},{7,5},{8,14},{9,15},{10,... | collective-permute-start | bytes 196616 | tf_op jit(solution)/shard_map/ppermute | solution.py:32
  27.8 5.2 %collective-permute-start.10 = (bf16[128,256]{1,0:T(8,128)(2,1)S(1)}, bf16[128,256]{1,0:T(8,128)(2,1)S(1)}, u32[]{:S(2)}, u32[]{:S(2)}) collective-permute-start(bf16[128,256]{1,0:T(8,128)(2,1)S(1)} %get-tuple-element.26), channel_id=1, source_target_pairs={{0,4},{1,5},{2,6},{3,7},{4,0},{5,1},{6,2},{7,3},{8,12},{9,13},{10,... | collective-permute-start | bytes 196616 | tf_op jit(solution)/shard_map/ppermute | solution.py:32
  27.8 6.1 %collective-permute-start.9 = (bf16[128,256]{1,0:T(8,128)(2,1)S(1)}, bf16[128,256]{1,0:T(8,128)(2,1)S(1)}, u32[]{:S(2)}, u32[]{:S(2)}) collective-permute-start(bf16[128,256]{1,0:T(8,128)(2,1)S(1)} %get-tuple-element.26), channel_id=1, source_target_pairs={{0,2},{1,3},{2,4},{3,5},{4,6},{5,7},{6,0},{7,1},{8,10},{9,11},{10,... | collective-permute-start | bytes 196616 | tf_op jit(solution)/shard_map/ppermute | solution.py:32
  33.9 1.6 %collective-permute-start.12 = (bf16[4,128,256]{2,1,0:T(8,128)(2,1)S(1)}, bf16[4,128,256]{2,1,0:T(8,128)(2,1)S(1)}, u32[]{:S(2)}, u32[]{:S(2)}) collective-permute-start(bf16[4,128,256]{2,1,0:T(8,128)(2,1)S(1)} %pad_maximum_fusion.2), channel_id=1, source_target_pairs={{0,1},{1,0},{2,3},{3,2},{4,5},{5,4},{6,7},{7,6},{8,9},{9,8},{10,11... | collective-permute-start | bytes 786440 | tf_op jit(solution)/shard_map/ppermute | solution.py:35

commit v13 on v12

--- a/solution.py
+++ b/solution.py
@@ -41,13 +41,16 @@
     return 0.5 + 0.5 * jnp.tanh(0.5 * x)
 
 
-def attend(query, blocks, sources, w_pair, length, scale_factor):
+def project(blocks, w_pair):
     n_blocks, block_rows, d_model = blocks.shape
-    count = n_blocks * block_rows
+    return jnp.dot(
+        blocks.reshape(n_blocks * block_rows, d_model), w_pair, preferred_element_type=jnp.float32
+    ).astype(jnp.bfloat16)
+
+
+def attend(query, pair_rows, sources, block_rows, length, scale_factor):
+    count, d_model = pair_rows.shape[0], pair_rows.shape[1] // 2
     head_size = d_model // HEADS
-    pair_rows = jnp.dot(
-        blocks.reshape(count, d_model), w_pair, preferred_element_type=jnp.float32
-    ).astype(jnp.bfloat16)
     keys = pair_rows[:, :d_model].reshape(count, HEADS, head_size)
     values = pair_rows[:, d_model:].reshape(count, HEADS, head_size)
     scores = jnp.einsum("zun,aun->zua", query, keys, preferred_element_type=jnp.float32) * scale_factor
@@ -132,9 +135,9 @@
     (mine, mine_sources), (partner, partner_sources) = gather_over_cand(hist_emb)
     weighted_sum = attend(
         query_row_matrix,
-        jnp.concatenate([mine, partner], axis=0),
+        jnp.concatenate([project(mine, w_pair), project(partner, w_pair)], axis=0),
         jnp.concatenate([mine_sources, partner_sources]),
-        w_pair,
+        hist_dev,
         length,
         scale_factor,
     )

time: 38.8 us -> 41 us (1.057)
  local copies, waits for them, and re-layouts: 7.08 us -> 9.2 us
  waiting for transfers between devices: 7.61 us -> 6.29 us
  matrix products: 4.5 us -> 5.64 us
    ppermute x9, waiting for transfers between devices: 2.04 us -> 0.97 us  [swap_over_req(): lax.ppermute(blocks[hop], 'req', [(i, i ^ hop) for i in range(n_req)])]
    dot_general x1, matrix products: 1.2 us -> 2.24 us  [body(): jnp.dot(hidden, tower_out, preferred_element_type=jnp.float32)[None, :]]
    concatenate x1, local copies, waits for them, and re-layouts: 0.02 us -> 0.91 us  [body(): w_pair = jnp.concatenate([w_key, w_value], axis=1)]
    unnamed x12 -> x6, local copies, waits for them, and re-layouts: 0.73 us -> 1.61 us
    ppermute x1, waiting for transfers between devices: 1.48 us -> 0.97 us  [gather_over_cand(): partner = lax.ppermute(mine, 'cand', [(i, i ^ 1) for i in range(n_cand)])]
  transfers between devices with their start and end apart: 13 -> 13, of which waited for: 7 -> 5; matrix products, arithmetic and copies ran while one was open for 6% -> 10% of each run, Pallas kernels for 0% -> 0%
where the time goes in v13:
time: 41 us; the launch traced here: 40.8 us
  starting transfers between devices  17.1 us (42%)
  local copies, waits for them, and re-layouts  9.2 us (22%)
  waiting for transfers between devices  6.29 us (15%)
  matrix products  5.64 us (14%)
  other arithmetic  1.58 us (4%)
  between operations  0.94 us (2%)
    ppermute x9, starting transfers between devices, swap_over_req(): lax.ppermute(blocks[hop], 'req', [(i, i ^ hop) for i in range(n_req)])  12.1 us
    gather x1, local copies, waits for them, and re-layouts, body(): jnp.take(table, asked.reshape(-1), axis=0, mode='clip')  5.96 us
    ppermute x3, starting transfers between devices, gather_over_cand(): lax.ppermute(rows, 'cand', [(i, (i + hop) % n_cand) for i in range(n_cand)])  4.89 us
    ppermute x3, waiting for transfers between devices, gather_over_cand(): lax.ppermute(rows, 'cand', [(i, (i + hop) % n_cand) for i in range(n_cand)])  4.35 us
    dot_general x1, matrix products, body(): jnp.dot(hidden, tower_out, preferred_element_type=jnp.float32)[None, :]  2.24 us
    unnamed x6, local copies, waits for them, and re-layouts  1.61 us
    dot_general x1, matrix products, attend(): jnp.einsum('bgo,ogl->bgl', gates, values, preferred_element_type=jnp.floa...  1.32 us
    ppermute x1, waiting for transfers between devices, gather_over_cand(): partner = lax.ppermute(mine, 'cand', [(i, i ^ 1) for i in range(n_cand)])  0.97 us
  transfers between devices with their start and end apart: 13, of which 5 were waited for; matrix products, arithmetic and copies ran while one was open for 10% of the time, Pallas kernels for 0%

profile of v13, /device:TPU:0, one launch (start us, length us, event | category | flops | bytes accessed | tf_op | source)
XLA Modules:
  0.0 40.8 jit_solution(4844036001092935428)
XLA Ops:
  0.0 0.7 %pad_add_fusion.1 = s32[768]{0:T(1024)S(1)} fusion(s32[256]{0:T(256)} %bitcast.93, s32[256]{0:T(256)} %bitcast.94, s32[128]{0:T(128)} %bitcast.95, s32[128]{0:T(128)} %bitcast.96), kind=kLoop, calls=%fused_computation.55 | loop fusion | flops 2304 | bytes 6144 | tf_op jit(solution)/shard_map/concatenate | solution.py:101
  0.8 0.2 convert_reduce_fusion.1
  1.0 0.2 convert_reduce_fusion
  1.4 0.3 convolution_convert_fusion.5
  1.8 3.0 %collective-permute-start = (s32[320]{0:T(512)S(1)}, s32[320]{0:T(512)S(1)}, u32[]{:S(2)}, u32[]{:S(2)}) collective-permute-start(s32[320]{0:T(512)S(1)} %get-tuple-element.5), channel_id=1, source_target_pairs={{0,8},{8,0},{16,24},{24,16},{1,9},{9,1},{17,25},{25,17},{2,10},{10... | collective-permute-start | bytes 3848 | tf_op jit(solution)/shard_map/ppermute | solution.py:79
  4.8 1.5 %collective-permute-start.2 = (s32[320]{0:T(512)S(1)}, s32[320]{0:T(512)S(1)}, u32[]{:S(2)}, u32[]{:S(2)}) collective-permute-start(s32[320]{0:T(512)S(1)} %get-tuple-element.6), channel_id=1, source_target_pairs={{0,24},{8,16},{16,8},{24,0},{1,25},{9,17},{17,9},{25,1},{2,26},{10... | collective-permute-start | bytes 3848 | tf_op jit(solution)/shard_map/ppermute | solution.py:79
  7.2 0.9 %constant_dynamic-update-slice_fusion.1 = bf16[256,512]{1,0:T(8,128)(2,1)S(1)} fusion(bf16[256,256]{1,0:T(8,128)(2,1)} %param.18), kind=kLoop, calls=%fused_computation.57 | loop fusion | bytes 262144
  8.1 0.9 %constant_dynamic-update-slice_fusion = bf16[256,512]{1,0:T(8,128)(2,1)S(1)} fusion(bf16[256,512]{1,0:T(8,128)(2,1)S(1)} %constant_dynamic-update-slice_fusion.1, bf16[256,256]{1,0:T(8,128)(2,1)} %param.19), kind=kLoop, calls=%fused_computation.56 | loop fusion | bytes 262144 | tf_op jit(solution)/shard_map/concatenate | solution.py:130
  9.1 0.7 %reshape.136 = bf16[1024,1]{0,1:T(2,128)(2,1)S(1)} reshape(bf16[1024]{0:T(1024)(128)(2,1)} %param.21) | data formatting | bytes 4096 | tf_op args[10]
  10.0 6.0 %gather_fusion = bf16[1280,256]{1,0:T(8,128)(2,1)S(1)} fusion(bf16[8192,256]{1,0:T(8,128)(2,1)} %param.11, s32[2048]{0:T(1024)S(1)} %pad_clamp_fusion), kind=kCustom, calls=%fused_computation | custom fusion | bytes 1315840 | tf_op jit(solution)/shard_map/jit(_take)/gather | solution.py:120
  16.0 3.0 %collective-permute-start.8 = (bf16[128,256]{1,0:T(8,128)(2,1)S(1)}, bf16[128,256]{1,0:T(8,128)(2,1)S(1)}, u32[]{:S(2)}, u32[]{:S(2)}) collective-permute-start(bf16[128,256]{1,0:T(8,128)(2,1)S(1)} %get-tuple-element.13), channel_id=1, source_target_pairs={{0,24},{8,16},{16,8},{24,0},{1,25},{9,17},{17,9},{25,1},{2,26},{10... | collective-permute-start | bytes 196616 | tf_op jit(solution)/shard_map/ppermute | solution.py:79
  18.9 0.5 %collective-permute-start.7 = (bf16[128,256]{1,0:T(8,128)(2,1)S(1)}, bf16[128,256]{1,0:T(8,128)(2,1)S(1)}, u32[]{:S(2)}, u32[]{:S(2)}) collective-permute-start(bf16[128,256]{1,0:T(8,128)(2,1)S(1)} %get-tuple-element.14), channel_id=1, source_target_pairs={{0,16},{8,24},{16,0},{24,8},{1,17},{9,25},{17,1},{25,9},{2,18},{10... | collective-permute-start | bytes 196616 | tf_op jit(solution)/shard_map/ppermute | solution.py:79
  19.6 2.9 %collective-permute-start.5 = (bf16[192,256]{1,0:T(8,128)(2,1)S(1)}, bf16[192,256]{1,0:T(8,128)(2,1)S(1)}, u32[]{:S(2)}, u32[]{:S(2)}) collective-permute-start(bf16[192,256]{1,0:T(8,128)(2,1)S(1)} %get-tuple-element.17), channel_id=1, source_target_pairs={{0,24},{8,16},{16,8},{24,0},{1,25},{9,17},{17,9},{25,1},{2,26},{10... | collective-permute-start | bytes 294920 | tf_op jit(solution)/shard_map/ppermute | solution.py:79
  22.5 0.5 %collective-permute-start.4 = (bf16[192,256]{1,0:T(8,128)(2,1)S(1)}, bf16[192,256]{1,0:T(8,128)(2,1)S(1)}, u32[]{:S(2)}, u32[]{:S(2)}) collective-permute-start(bf16[192,256]{1,0:T(8,128)(2,1)S(1)} %get-tuple-element.18), channel_id=1, source_target_pairs={{0,16},{8,24},{16,0},{24,8},{1,17},{9,25},{17,1},{25,9},{2,18},{10... | collective-permute-start | bytes 294920 | tf_op jit(solution)/shard_map/ppermute | solution.py:79
  23.0 0.6 %collective-permute-start.3 = (bf16[192,256]{1,0:T(8,128)(2,1)S(1)}, bf16[192,256]{1,0:T(8,128)(2,1)S(1)}, u32[]{:S(2)}, u32[]{:S(2)}) collective-permute-start(bf16[192,256]{1,0:T(8,128)(2,1)S(1)} %get-tuple-element.19), channel_id=1, source_target_pairs={{0,8},{8,0},{16,24},{24,16},{1,9},{9,1},{17,25},{25,17},{2,10},{10... | collective-permute-start | bytes 294920 | tf_op jit(solution)/shard_map/ppermute | solution.py:79
  23.6 0.9 %collective-permute-done.7 = bf16[128,256]{1,0:T(8,128)(2,1)S(1)} collective-permute-done((bf16[128,256]{1,0:T(8,128)(2,1)S(1)}, bf16[128,256]{1,0:T(8,128)(2,1)S(1)}, u32[]{:S(2)}, u32[]{:S(2)}) %collective-permute-start.7) | collective-permute-done | bytes 65568 | tf_op jit(solution)/shard_map/ppermute | solution.py:79
  24.6 0.2 convolution_convert_fusion.4
  24.8 3.9 %collective-permute-start.11 = (bf16[128,256]{1,0:T(8,128)(2,1)S(1)}, bf16[128,256]{1,0:T(8,128)(2,1)S(1)}, u32[]{:S(2)}, u32[]{:S(2)}) collective-permute-start(bf16[128,256]{1,0:T(8,128)(2,1)S(1)} %convolution_convert_fusion.4), channel_id=1, source_target_pairs={{0,6},{1,7},{2,0},{3,1},{4,2},{5,3},{6,4},{7,5},{8,14},{9,15},{10,... | collective-permute-start | bytes 196616 | tf_op jit(solution)/shard_map/ppermute | solution.py:32
  28.7 1.0 %collective-permute-start.9 = (bf16[128,256]{1,0:T(8,128)(2,1)S(1)}, bf16[128,256]{1,0:T(8,128)(2,1)S(1)}, u32[]{:S(2)}, u32[]{:S(2)}) collective-permute-start(bf16[128,256]{1,0:T(8,128)(2,1)S(1)} %convolution_convert_fusion.4), channel_id=1, source_target_pairs={{0,2},{1,3},{2,4},{3,5},{4,6},{5,7},{6,0},{7,1},{8,10},{9,11},{10,... | collective-permute-start | bytes 196616 | tf_op jit(solution)/shard_map/ppermute | solution.py:32
  29.8 0.3 convolution_convert_fusion.2
  30.1 0.3 fusion.13
  30.4 0.2 collective-permute-done.11
  30.6 3.3 %collective-permute-done.10 = bf16[128,256]{1,0:T(8,128)(2,1)S(1)} collective-permute-done((bf16[128,256]{1,0:T(8,128)(2,1)S(1)}, bf16[128,256]{1,0:T(8,128)(2,1)S(1)}, u32[]{:S(2)}, u32[]{:S(2)}) %collective-permute-start.10) | collective-permute-done | bytes 65568 | tf_op jit(solution)/shard_map/ppermute | solution.py:32
  33.9 0.9 %collective-permute-done.9 = bf16[128,256]{1,0:T(8,128)(2,1)S(1)} collective-permute-done((bf16[128,256]{1,0:T(8,128)(2,1)S(1)}, bf16[128,256]{1,0:T(8,128)(2,1)S(1)}, u32[]{:S(2)}, u32[]{:S(2)}) %collective-permute-start.9) | collective-permute-done | bytes 65568 | tf_op jit(solution)/shard_map/ppermute | solution.py:32
  34.9 0.2 convolution_convert_fusion.3
  35.1 0.3 convolution_convert_fusion.1
  35.4 1.0 %collective-permute-done.12 = bf16[4,128,256]{2,1,0:T(8,128)(2,1)S(1)} collective-permute-done((bf16[4,128,256]{2,1,0:T(8,128)(2,1)S(1)}, bf16[4,128,256]{2,1,0:T(8,128)(2,1)S(1)}, u32[]{:S(2)}, u32[]{:S(2)}) %collective-permute-start.12) | collective-permute-done | bytes 262176 | tf_op jit(solution)/shard_map/ppermute | solution.py:35
  36.4 0.3 convolution_convert_fusion
  36.8 0.2 copy.16
  37.0 0.2 copy.15
  37.2 1.3 %fusion.5 = bf16[4,64,256]{2,1,0:T(8,128)(2,1)S(1)} fusion(bf16[1024,4,64]{0,2,1:T(8,128)(2,1)S(1)} %bitcast.78, bf16[1024,4,64]{0,2,1:T(8,128)(2,1)S(1)} %bitcast.77, bf16[256,4,64]{0,2,1:T(8,128)(2,1)S(1)} %bitcast.82, pred[1024]{0:T(1024)(128)(4,1)S(1)} %fusion.21, f32[]{:T(128)S(6)} %sqrt.3), kind=kOutput, calls=%fused_computation.13 | convolution fusion | flops 273809408 | bytes 1311748 | tf_op jit(solution)/shard_map/bgo,ogl->bgl/dot_general | solution.py:63
  38.5 2.2 %fusion.8 = f32[1,256]{1,0:T(1,128)} fusion(bf16[1024,1]{0,1:T(2,128)(2,1)S(1)} %reshape.136, f32[256,1024]{1,0:T(8,128)S(1)} %fusion.13, bf16[256,256]{0,1:T(8,128)(2,1)S(1)} %bitcast.97, bf16[512,1024]{1,0:T(8,128)(2,1)} %param.20), kind=kOutput, calls=%fused_computation.17 | convolution fusion | flops 136314880 | bytes 1707008 | tf_op jit(solution)/shard_map/dot_general | solution.py:153
  (44 shorter events, 1.3 us)
Async XLA Ops:
  0.0 34.9 %copy-start = (bf16[256,256]{1,0:T(8,128)(2,1)S(1)}, bf16[256,256]{1,0:T(8,128)(2,1)}, u32[]{:S(2)}) copy-start(bf16[256,256]{1,0:T(8,128)(2,1)} %param.17) | copy-start | bytes 393220
  1.8 8.0 %collective-permute-start = (s32[320]{0:T(512)S(1)}, s32[320]{0:T(512)S(1)}, u32[]{:S(2)}, u32[]{:S(2)}) collective-permute-start(s32[320]{0:T(512)S(1)} %get-tuple-element.5), channel_id=1, source_target_pairs={{0,8},{8,0},{16,24},{24,16},{1,9},{9,1},{17,25},{25,17},{2,10},{10... | collective-permute-start | bytes 3848 | tf_op jit(solution)/shard_map/ppermute | solution.py:79
  4.8 5.0 %collective-permute-start.2 = (s32[320]{0:T(512)S(1)}, s32[320]{0:T(512)S(1)}, u32[]{:S(2)}, u32[]{:S(2)}) collective-permute-start(s32[320]{0:T(512)S(1)} %get-tuple-element.6), channel_id=1, source_target_pairs={{0,24},{8,16},{16,8},{24,0},{1,25},{9,17},{17,9},{25,1},{2,26},{10... | collective-permute-start | bytes 3848 | tf_op jit(solution)/shard_map/ppermute | solution.py:79
  6.3 3.6 %collective-permute-start.1 = (s32[320]{0:T(512)S(1)}, s32[320]{0:T(512)S(1)}, u32[]{:S(2)}, u32[]{:S(2)}) collective-permute-start(s32[320]{0:T(512)S(1)} %get-tuple-element.7), channel_id=1, source_target_pairs={{0,16},{8,24},{16,0},{24,8},{1,17},{9,25},{17,1},{25,9},{2,18},{10... | collective-permute-start | bytes 3848 | tf_op jit(solution)/shard_map/ppermute | solution.py:79
  10.0 20.1 %copy-start.1 = (bf16[512,1024]{1,0:T(8,128)(2,1)S(1)}, bf16[512,1024]{1,0:T(8,128)(2,1)}, u32[]{:S(2)}) copy-start(bf16[512,1024]{1,0:T(8,128)(2,1)} %param.20) | copy-start | bytes 3145732
  16.0 7.1 %collective-permute-start.8 = (bf16[128,256]{1,0:T(8,128)(2,1)S(1)}, bf16[128,256]{1,0:T(8,128)(2,1)S(1)}, u32[]{:S(2)}, u32[]{:S(2)}) collective-permute-start(bf16[128,256]{1,0:T(8,128)(2,1)S(1)} %get-tuple-element.13), channel_id=1, source_target_pairs={{0,24},{8,16},{16,8},{24,0},{1,25},{9,17},{17,9},{25,1},{2,26},{10... | collective-permute-start | bytes 196616 | tf_op jit(solution)/shard_map/ppermute | solution.py:79
  18.9 5.6 %collective-permute-start.7 = (bf16[128,256]{1,0:T(8,128)(2,1)S(1)}, bf16[128,256]{1,0:T(8,128)(2,1)S(1)}, u32[]{:S(2)}, u32[]{:S(2)}) collective-permute-start(bf16[128,256]{1,0:T(8,128)(2,1)S(1)} %get-tuple-element.14), channel_id=1, source_target_pairs={{0,16},{8,24},{16,0},{24,8},{1,17},{9,25},{17,1},{25,9},{2,18},{10... | collective-permute-start | bytes 196616 | tf_op jit(solution)/shard_map/ppermute | solution.py:79
  19.4 5.1 %collective-permute-start.6 = (bf16[128,256]{1,0:T(8,128)(2,1)S(1)}, bf16[128,256]{1,0:T(8,128)(2,1)S(1)}, u32[]{:S(2)}, u32[]{:S(2)}) collective-permute-start(bf16[128,256]{1,0:T(8,128)(2,1)S(1)} %get-tuple-element.15), channel_id=1, source_target_pairs={{0,8},{8,0},{16,24},{24,16},{1,9},{9,1},{17,25},{25,17},{2,10},{10... | collective-permute-start | bytes 196616 | tf_op jit(solution)/shard_map/ppermute | solution.py:79
  19.6 9.1 %collective-permute-start.5 = (bf16[192,256]{1,0:T(8,128)(2,1)S(1)}, bf16[192,256]{1,0:T(8,128)(2,1)S(1)}, u32[]{:S(2)}, u32[]{:S(2)}) collective-permute-start(bf16[192,256]{1,0:T(8,128)(2,1)S(1)} %get-tuple-element.17), channel_id=1, source_target_pairs={{0,24},{8,16},{16,8},{24,0},{1,25},{9,17},{17,9},{25,1},{2,26},{10... | collective-permute-start | bytes 294920 | tf_op jit(solution)/shard_map/ppermute | solution.py:79
  22.5 7.2 %collective-permute-start.4 = (bf16[192,256]{1,0:T(8,128)(2,1)S(1)}, bf16[192,256]{1,0:T(8,128)(2,1)S(1)}, u32[]{:S(2)}, u32[]{:S(2)}) collective-permute-start(bf16[192,256]{1,0:T(8,128)(2,1)S(1)} %get-tuple-element.18), channel_id=1, source_target_pairs={{0,16},{8,24},{16,0},{24,8},{1,17},{9,25},{17,1},{25,9},{2,18},{10... | collective-permute-start | bytes 294920 | tf_op jit(solution)/shard_map/ppermute | solution.py:79
  23.0 6.7 %collective-permute-start.3 = (bf16[192,256]{1,0:T(8,128)(2,1)S(1)}, bf16[192,256]{1,0:T(8,128)(2,1)S(1)}, u32[]{:S(2)}, u32[]{:S(2)}) collective-permute-start(bf16[192,256]{1,0:T(8,128)(2,1)S(1)} %get-tuple-element.19), channel_id=1, source_target_pairs={{0,8},{8,0},{16,24},{24,16},{1,9},{9,1},{17,25},{25,17},{2,10},{10... | collective-permute-start | bytes 294920 | tf_op jit(solution)/shard_map/ppermute | solution.py:79
  24.8 5.8 %collective-permute-start.11 = (bf16[128,256]{1,0:T(8,128)(2,1)S(1)}, bf16[128,256]{1,0:T(8,128)(2,1)S(1)}, u32[]{:S(2)}, u32[]{:S(2)}) collective-permute-start(bf16[128,256]{1,0:T(8,128)(2,1)S(1)} %convolution_convert_fusion.4), channel_id=1, source_target_pairs={{0,6},{1,7},{2,0},{3,1},{4,2},{5,3},{6,4},{7,5},{8,14},{9,15},{10,... | collective-permute-start | bytes 196616 | tf_op jit(solution)/shard_map/ppermute | solution.py:32
  28.7 5.2 %collective-permute-start.10 = (bf16[128,256]{1,0:T(8,128)(2,1)S(1)}, bf16[128,256]{1,0:T(8,128)(2,1)S(1)}, u32[]{:S(2)}, u32[]{:S(2)}) collective-permute-start(bf16[128,256]{1,0:T(8,128)(2,1)S(1)} %convolution_convert_fusion.4), channel_id=1, source_target_pairs={{0,4},{1,5},{2,6},{3,7},{4,0},{5,1},{6,2},{7,3},{8,12},{9,13},{10,... | collective-permute-start | bytes 196616 | tf_op jit(solution)/shard_map/ppermute | solution.py:32
  28.7 6.1 %collective-permute-start.9 = (bf16[128,256]{1,0:T(8,128)(2,1)S(1)}, bf16[128,256]{1,0:T(8,128)(2,1)S(1)}, u32[]{:S(2)}, u32[]{:S(2)}) collective-permute-start(bf16[128,256]{1,0:T(8,128)(2,1)S(1)} %convolution_convert_fusion.4), channel_id=1, source_target_pairs={{0,2},{1,3},{2,4},{3,5},{4,6},{5,7},{6,0},{7,1},{8,10},{9,11},{10,... | collective-permute-start | bytes 196616 | tf_op jit(solution)/shard_map/ppermute | solution.py:32
  34.8 1.6 %collective-permute-start.12 = (bf16[4,128,256]{2,1,0:T(8,128)(2,1)S(1)}, bf16[4,128,256]{2,1,0:T(8,128)(2,1)S(1)}, u32[]{:S(2)}, u32[]{:S(2)}) collective-permute-start(bf16[4,128,256]{2,1,0:T(8,128)(2,1)S(1)} %pad_maximum_fusion.3), channel_id=1, source_target_pairs={{0,1},{1,0},{2,3},{3,2},{4,5},{5,4},{6,7},{7,6},{8,9},{9,8},{10,11... | collective-permute-start | bytes 786440 | tf_op jit(solution)/shard_map/ppermute | solution.py:35

commit v14 on v12

--- a/solution.py
+++ b/solution.py
@@ -118,18 +118,19 @@
         n_dest, hist_cap + cand_cap, d_model
     )
     hist_replies = swap_over_req(fetched[:, :hist_cap]).reshape(n_dest * hist_cap, d_model)
-    cand_replies = swap_over_req(fetched[:, hist_cap:]).reshape(n_dest * cand_cap, d_model)
     hist_emb = jnp.dot(hist_pick, hist_replies, preferred_element_type=jnp.float32).astype(jnp.bfloat16)
-    cand_emb = jnp.dot(cand_pick, cand_replies, preferred_element_type=jnp.float32).astype(jnp.bfloat16)
     head_size = d_model // HEADS
     scale_factor = 1.0 / math.sqrt(head_size)
     length = history_length[0]
     w_pair = jnp.concatenate([w_key, w_value], axis=1)
+    (mine, mine_sources), (partner, partner_sources) = gather_over_cand(hist_emb)
+    cand_sent, _ = lax.optimization_barrier((fetched[:, hist_cap:], mine[1]))
+    cand_replies = swap_over_req(cand_sent).reshape(n_dest * cand_cap, d_model)
+    cand_emb = jnp.dot(cand_pick, cand_replies, preferred_element_type=jnp.float32).astype(jnp.bfloat16)
     query_row_matrix = jnp.dot(cand_emb, w_query, preferred_element_type=jnp.float32).astype(
         jnp.bfloat16
     )
     query_row_matrix = query_row_matrix.reshape(cand_dev, HEADS, head_size)
-    (mine, mine_sources), (partner, partner_sources) = gather_over_cand(hist_emb)
     weighted_sum = attend(
         query_row_matrix,
         jnp.concatenate([mine, partner], axis=0),

time: 38.8 us -> 43.1 us (1.11)
  waiting for transfers between devices: 7.61 us -> 10.7 us
  matrix products: 4.5 us -> 6.69 us
  starting transfers between devices: 17 us -> 16.4 us
  local copies, waits for them, and re-layouts: 7.08 us -> 6.62 us
    ppermute x9, waiting for transfers between devices: 2.04 us -> 9.39 us  [swap_over_req(): lax.ppermute(blocks[hop], 'req', [(i, i ^ hop) for i in range(n_req)])]
    ppermute x3, waiting for transfers between devices: 4.09 us -> 1.29 us  [gather_over_cand(): lax.ppermute(rows, 'cand', [(i, (i + hop) % n_cand) for i in range(n_cand)])]
    ppermute x1, waiting for transfers between devices: 1.48 us -> 0.01 us  [gather_over_cand(): partner = lax.ppermute(mine, 'cand', [(i, i ^ 1) for i in range(n_cand)])]
    dot_general x1, matrix products: 1.2 us -> 2.1 us  [body(): jnp.dot(hidden, tower_out, preferred_element_type=jnp.float32)[None, :]]
    dot_general x1, matrix products: 1.32 us -> 1.97 us  [attend(): jnp.einsum('bgo,ogl->bgl', gates, values, preferred_element_type=jnp.floa...]
    dot_general x1, matrix products: 0.23 us -> 0.88 us  [body(): jnp.dot(cand_emb, w_query, preferred_element_type=jnp.float32)]
  transfers between devices with their start and end apart: 13 -> 13, of which waited for: 7 -> 8; matrix products, arithmetic and copies ran while one was open for 6% -> 4% of each run, Pallas kernels for 0% -> 0%
where the time goes in v14:
time: 43.1 us; the launch traced here: 42.9 us
  starting transfers between devices  16.4 us (38%)
  waiting for transfers between devices  10.7 us (25%)
  matrix products  6.69 us (16%)
  local copies, waits for them, and re-layouts  6.62 us (15%)
  other arithmetic  1.51 us (4%)
  between operations  0.98 us (2%)
    ppermute x9, starting transfers between devices, swap_over_req(): lax.ppermute(blocks[hop], 'req', [(i, i ^ hop) for i in range(n_req)])  11.6 us
    ppermute x9, waiting for transfers between devices, swap_over_req(): lax.ppermute(blocks[hop], 'req', [(i, i ^ hop) for i in range(n_req)])  9.39 us
    gather x1, local copies, waits for them, and re-layouts, body(): jnp.take(table, asked.reshape(-1), axis=0, mode='clip')  5.86 us
    ppermute x3, starting transfers between devices, gather_over_cand(): lax.ppermute(rows, 'cand', [(i, (i + hop) % n_cand) for i in range(n_cand)])  4.72 us
    dot_general x1, matrix products, body(): jnp.dot(hidden, tower_out, preferred_element_type=jnp.float32)[None, :]  2.1 us
    dot_general x1, matrix products, attend(): jnp.einsum('bgo,ogl->bgl', gates, values, preferred_element_type=jnp.floa...  1.97 us
    ppermute x3, waiting for transfers between devices, gather_over_cand(): lax.ppermute(rows, 'cand', [(i, (i + hop) % n_cand) for i in range(n_cand)])  1.29 us
    dot_general x1, matrix products, body(): jnp.dot(cand_emb, w_query, preferred_element_type=jnp.float32)  0.88 us
  transfers between devices with their start and end apart: 13, of which 8 were waited for; matrix products, arithmetic and copies ran while one was open for 4% of the time, Pallas kernels for 0%

profile of v14, /device:TPU:0, one launch (start us, length us, event | category | flops | bytes accessed | tf_op | source)
XLA Modules:
  0.0 42.9 jit_solution(9618333734394576691)
XLA Ops:
  0.0 0.8 %pad_add_fusion.1 = s32[768]{0:T(1024)S(1)} fusion(s32[256]{0:T(256)} %bitcast.92, s32[256]{0:T(256)} %bitcast.93, s32[128]{0:T(128)} %bitcast.94, s32[128]{0:T(128)} %bitcast.95), kind=kLoop, calls=%fused_computation.58 | loop fusion | flops 2304 | bytes 6144 | tf_op jit(solution)/shard_map/concatenate | solution.py:98
  0.8 0.2 convert_reduce_fusion.1
  1.0 0.2 convert_reduce_fusion
  1.4 0.3 convolution_convert_fusion.4
  1.8 3.0 %collective-permute-start = (s32[320]{0:T(512)S(1)}, s32[320]{0:T(512)S(1)}, u32[]{:S(2)}, u32[]{:S(2)}) collective-permute-start(s32[320]{0:T(512)S(1)} %get-tuple-element.7), channel_id=1, source_target_pairs={{0,8},{8,0},{16,24},{24,16},{1,9},{9,1},{17,25},{25,17},{2,10},{10... | collective-permute-start | bytes 3848 | tf_op jit(solution)/shard_map/ppermute | solution.py:76
  4.8 1.5 %collective-permute-start.2 = (s32[320]{0:T(512)S(1)}, s32[320]{0:T(512)S(1)}, u32[]{:S(2)}, u32[]{:S(2)}) collective-permute-start(s32[320]{0:T(512)S(1)} %get-tuple-element.8), channel_id=1, source_target_pairs={{0,24},{8,16},{16,8},{24,0},{1,25},{9,17},{17,9},{25,1},{2,26},{10... | collective-permute-start | bytes 3848 | tf_op jit(solution)/shard_map/ppermute | solution.py:76
  6.5 2.8 %collective-permute-done.2 = s32[320]{0:T(512)S(1)} collective-permute-done((s32[320]{0:T(512)S(1)}, s32[320]{0:T(512)S(1)}, u32[]{:S(2)}, u32[]{:S(2)}) %collective-permute-start.2) | collective-permute-done | bytes 1312 | tf_op jit(solution)/shard_map/ppermute | solution.py:76
  9.3 0.6 %collective-permute-done.1 = s32[320]{0:T(512)S(1)} collective-permute-done((s32[320]{0:T(512)S(1)}, s32[320]{0:T(512)S(1)}, u32[]{:S(2)}, u32[]{:S(2)}) %collective-permute-start.1) | collective-permute-done | bytes 1312 | tf_op jit(solution)/shard_map/ppermute | solution.py:76
  10.0 5.9 %gather_fusion = bf16[1280,256]{1,0:T(8,128)(2,1)S(1)} fusion(bf16[8192,256]{1,0:T(8,128)(2,1)} %param.11, s32[2048]{0:T(1024)S(1)} %pad_clamp_fusion), kind=kCustom, calls=%fused_computation | custom fusion | bytes 1315840 | tf_op jit(solution)/shard_map/jit(_take)/gather | solution.py:117
  15.9 1.5 %collective-permute-start.5 = (bf16[128,256]{1,0:T(8,128)(2,1)S(1)}, bf16[128,256]{1,0:T(8,128)(2,1)S(1)}, u32[]{:S(2)}, u32[]{:S(2)}) collective-permute-start(bf16[128,256]{1,0:T(8,128)(2,1)S(1)} %get-tuple-element.15), channel_id=1, source_target_pairs={{0,24},{8,16},{16,8},{24,0},{1,25},{9,17},{17,9},{25,1},{2,26},{10... | collective-permute-start | bytes 196616 | tf_op jit(solution)/shard_map/ppermute | solution.py:76
  17.4 1.5 %collective-permute-start.4 = (bf16[128,256]{1,0:T(8,128)(2,1)S(1)}, bf16[128,256]{1,0:T(8,128)(2,1)S(1)}, u32[]{:S(2)}, u32[]{:S(2)}) collective-permute-start(bf16[128,256]{1,0:T(8,128)(2,1)S(1)} %get-tuple-element.16), channel_id=1, source_target_pairs={{0,16},{8,24},{16,0},{24,8},{1,17},{9,25},{17,1},{25,9},{2,18},{10... | collective-permute-start | bytes 196616 | tf_op jit(solution)/shard_map/ppermute | solution.py:76
  18.9 0.5 %collective-permute-start.3 = (bf16[128,256]{1,0:T(8,128)(2,1)S(1)}, bf16[128,256]{1,0:T(8,128)(2,1)S(1)}, u32[]{:S(2)}, u32[]{:S(2)}) collective-permute-start(bf16[128,256]{1,0:T(8,128)(2,1)S(1)} %get-tuple-element.17), channel_id=1, source_target_pairs={{0,8},{8,0},{16,24},{24,16},{1,9},{9,1},{17,25},{25,17},{2,10},{10... | collective-permute-start | bytes 196616 | tf_op jit(solution)/shard_map/ppermute | solution.py:76
  20.1 1.0 %collective-permute-done.5 = bf16[128,256]{1,0:T(8,128)(2,1)S(1)} collective-permute-done((bf16[128,256]{1,0:T(8,128)(2,1)S(1)}, bf16[128,256]{1,0:T(8,128)(2,1)S(1)}, u32[]{:S(2)}, u32[]{:S(2)}) %collective-permute-start.5) | collective-permute-done | bytes 65568 | tf_op jit(solution)/shard_map/ppermute | solution.py:76
  21.2 0.7 %collective-permute-done.4 = bf16[128,256]{1,0:T(8,128)(2,1)S(1)} collective-permute-done((bf16[128,256]{1,0:T(8,128)(2,1)S(1)}, bf16[128,256]{1,0:T(8,128)(2,1)S(1)}, u32[]{:S(2)}, u32[]{:S(2)}) %collective-permute-start.4) | collective-permute-done | bytes 65568 | tf_op jit(solution)/shard_map/ppermute | solution.py:76
  21.8 1.4 %collective-permute-done.3 = bf16[128,256]{1,0:T(8,128)(2,1)S(1)} collective-permute-done((bf16[128,256]{1,0:T(8,128)(2,1)S(1)}, bf16[128,256]{1,0:T(8,128)(2,1)S(1)}, u32[]{:S(2)}, u32[]{:S(2)}) %collective-permute-start.3) | collective-permute-done | bytes 65568 | tf_op jit(solution)/shard_map/ppermute | solution.py:76
  23.2 0.2 constant_dynamic-update-slice_fusion.4
  23.5 1.6 %collective-permute-start.6 = (bf16[128,256]{1,0:T(8,128)(2,1)S(1)}, bf16[128,256]{1,0:T(8,128)(2,1)S(1)}, u32[]{:S(2)}, u32[]{:S(2)}) collective-permute-start(bf16[128,256]{1,0:T(8,128)(2,1)S(1)} %get-tuple-element.28), channel_id=1, source_target_pairs={{0,2},{1,3},{2,4},{3,5},{4,6},{5,7},{6,0},{7,1},{8,10},{9,11},{10,... | collective-permute-start | bytes 196616 | tf_op jit(solution)/shard_map/ppermute | solution.py:32
  25.3 2.3 %collective-permute-start.11 = (bf16[128,256]{1,0:T(8,128)(2,1)S(1)}, bf16[128,256]{1,0:T(8,128)(2,1)S(1)}, u32[]{:S(2)}, u32[]{:S(2)}) collective-permute-start(bf16[128,256]{1,0:T(8,128)(2,1)S(1)} %get-tuple-element.28), channel_id=1, source_target_pairs={{0,6},{1,7},{2,0},{3,1},{4,2},{5,3},{6,4},{7,5},{8,14},{9,15},{10,... | collective-permute-start | bytes 196616 | tf_op jit(solution)/shard_map/ppermute | solution.py:32
  27.6 0.8 %collective-permute-start.10 = (bf16[128,256]{1,0:T(8,128)(2,1)S(1)}, bf16[128,256]{1,0:T(8,128)(2,1)S(1)}, u32[]{:S(2)}, u32[]{:S(2)}) collective-permute-start(bf16[128,256]{1,0:T(8,128)(2,1)S(1)} %get-tuple-element.28), channel_id=1, source_target_pairs={{0,4},{1,5},{2,6},{3,7},{4,0},{5,1},{6,2},{7,3},{8,12},{9,13},{10,... | collective-permute-start | bytes 196616 | tf_op jit(solution)/shard_map/ppermute | solution.py:32
  28.4 1.3 %collective-permute-done.6 = bf16[128,256]{1,0:T(8,128)(2,1)S(1)} collective-permute-done((bf16[128,256]{1,0:T(8,128)(2,1)S(1)}, bf16[128,256]{1,0:T(8,128)(2,1)S(1)}, u32[]{:S(2)}, u32[]{:S(2)}) %collective-permute-start.6) | collective-permute-done | bytes 65568 | tf_op jit(solution)/shard_map/ppermute | solution.py:32
  29.7 1.0 %collective-permute-start.9 = (bf16[192,256]{1,0:T(8,128)(2,1)S(1)}, bf16[192,256]{1,0:T(8,128)(2,1)S(1)}, u32[]{:S(2)}, u32[]{:S(2)}) collective-permute-start(bf16[192,256]{1,0:T(8,128)(2,1)S(1)} %get-tuple-element.19), channel_id=1, source_target_pairs={{0,24},{8,16},{16,8},{24,0},{1,25},{9,17},{17,9},{25,1},{2,26},{10... | collective-permute-start | bytes 294920 | tf_op jit(solution)/shard_map/ppermute | solution.py:76
  30.7 1.1 %collective-permute-start.8 = (bf16[192,256]{1,0:T(8,128)(2,1)S(1)}, bf16[192,256]{1,0:T(8,128)(2,1)S(1)}, u32[]{:S(2)}, u32[]{:S(2)}) collective-permute-start(bf16[192,256]{1,0:T(8,128)(2,1)S(1)} %get-tuple-element.20), channel_id=1, source_target_pairs={{0,16},{8,24},{16,0},{24,8},{1,17},{9,25},{17,1},{25,9},{2,18},{10... | collective-permute-start | bytes 294920 | tf_op jit(solution)/shard_map/ppermute | solution.py:76
  31.8 1.5 %collective-permute-start.7 = (bf16[192,256]{1,0:T(8,128)(2,1)S(1)}, bf16[192,256]{1,0:T(8,128)(2,1)S(1)}, u32[]{:S(2)}, u32[]{:S(2)}) collective-permute-start(bf16[192,256]{1,0:T(8,128)(2,1)S(1)} %get-tuple-element.21), channel_id=1, source_target_pairs={{0,8},{8,0},{16,24},{24,16},{1,9},{9,1},{17,25},{25,17},{2,10},{10... | collective-permute-start | bytes 294920 | tf_op jit(solution)/shard_map/ppermute | solution.py:76
  33.4 2.0 %collective-permute-done.9 = bf16[192,256]{1,0:T(8,128)(2,1)S(1)} collective-permute-done((bf16[192,256]{1,0:T(8,128)(2,1)S(1)}, bf16[192,256]{1,0:T(8,128)(2,1)S(1)}, u32[]{:S(2)}, u32[]{:S(2)}) %collective-permute-start.9) | collective-permute-done | bytes 98336 | tf_op jit(solution)/shard_map/ppermute | solution.py:76
  35.4 0.9 %collective-permute-done.8 = bf16[192,256]{1,0:T(8,128)(2,1)S(1)} collective-permute-done((bf16[192,256]{1,0:T(8,128)(2,1)S(1)}, bf16[192,256]{1,0:T(8,128)(2,1)S(1)}, u32[]{:S(2)}, u32[]{:S(2)}) %collective-permute-start.8) | collective-permute-done | bytes 98336 | tf_op jit(solution)/shard_map/ppermute | solution.py:76
  36.4 0.3 convolution_convert_fusion.1
  36.8 0.9 %convolution_convert_fusion.2 = bf16[256,256]{0,1:T(8,128)(2,1)} fusion(bf16[256,256]{1,0:T(8,128)(2,1)S(1)} %convolution_convert_fusion.1, bf16[256,256]{1,0:T(8,128)(2,1)S(1)} %copy-done), kind=kOutput, calls=%fused_computation.7 | convolution fusion | flops 33619968 | bytes 393216 | tf_op jit(solution)/shard_map/dot_general | solution.py:130
  37.6 0.3 fusion.12
  38.0 0.5 %convolution_convert_fusion = bf16[1024,512]{0,1:T(8,128)(2,1)S(1)} fusion(bf16[1024,256]{1,0:T(8,128)(2,1)S(1)} %bitcast.76, bf16[256,256]{1,0:T(8,128)(2,1)S(1)} %copy-done.2, bf16[256,256]{1,0:T(8,128)(2,1)S(1)} %copy-done.3), kind=kOutput, calls=%fused_computation.4 | convolution fusion | flops 269484032 | bytes 1835008 | tf_op jit(solution)/shard_map/dot_general | solution.py:48
  38.6 0.3 copy-done.4
  38.9 2.0 %fusion.5 = bf16[4,64,256]{2,1,0:T(8,128)(2,1)} fusion(bf16[1024,4,64]{0,2,1:T(8,128)(2,1)S(1)} %bitcast.78, bf16[1024,4,64]{0,2,1:T(8,128)(2,1)S(1)} %bitcast.77, bf16[256,4,64]{0,2,1:T(8,128)(2,1)S(1)} %bitcast.84, pred[1024]{0:T(1024)(128)(4,1)S(1)} %fusion.23, f32[]{:T(128)S(6)} %sqrt.3), kind=kOutput, calls=%fused_computation.12 | convolution fusion | flops 273809408 | bytes 1311748 | tf_op jit(solution)/shard_map/bgo,ogl->bgl/dot_general | solution.py:60
  40.8 2.1 %fusion.8 = f32[1,256]{1,0:T(1,128)} fusion(bf16[1024,1]{0,1:T(2,128)(2,1)S(1)} %reshape.132, f32[256,1024]{1,0:T(8,128)S(1)} %fusion.12, bf16[256,256]{0,1:T(8,128)(2,1)} %bitcast.96, bf16[512,1024]{1,0:T(8,128)(2,1)S(1)} %copy-done.1), kind=kOutput, calls=%fused_computation.14 | convolution fusion | flops 136314880 | bytes 1709056 | tf_op jit(solution)/shard_map/dot_general | solution.py:151
  (52 shorter events, 1.2 us)
Async XLA Ops:
  0.0 36.8 %copy-start = (bf16[256,256]{1,0:T(8,128)(2,1)S(1)}, bf16[256,256]{1,0:T(8,128)(2,1)}, u32[]{:S(2)}) copy-start(bf16[256,256]{1,0:T(8,128)(2,1)} %param.17) | copy-start | bytes 393220
  0.0 25.2 %copy-start.5 = (bf16[1024]{0:T(1024)(128)(2,1)S(1)}, bf16[1024]{0:T(1024)(128)(2,1)}, u32[]{:S(2)}) copy-start(bf16[1024]{0:T(1024)(128)(2,1)} %param.21) | copy-start | bytes 6148
  1.8 4.7 %collective-permute-start = (s32[320]{0:T(512)S(1)}, s32[320]{0:T(512)S(1)}, u32[]{:S(2)}, u32[]{:S(2)}) collective-permute-start(s32[320]{0:T(512)S(1)} %get-tuple-element.7), channel_id=1, source_target_pairs={{0,8},{8,0},{16,24},{24,16},{1,9},{9,1},{17,25},{25,17},{2,10},{10... | collective-permute-start | bytes 3848 | tf_op jit(solution)/shard_map/ppermute | solution.py:76
  4.8 4.5 %collective-permute-start.2 = (s32[320]{0:T(512)S(1)}, s32[320]{0:T(512)S(1)}, u32[]{:S(2)}, u32[]{:S(2)}) collective-permute-start(s32[320]{0:T(512)S(1)} %get-tuple-element.8), channel_id=1, source_target_pairs={{0,24},{8,16},{16,8},{24,0},{1,25},{9,17},{17,9},{25,1},{2,26},{10... | collective-permute-start | bytes 3848 | tf_op jit(solution)/shard_map/ppermute | solution.py:76
  6.3 3.6 %collective-permute-start.1 = (s32[320]{0:T(512)S(1)}, s32[320]{0:T(512)S(1)}, u32[]{:S(2)}, u32[]{:S(2)}) collective-permute-start(s32[320]{0:T(512)S(1)} %get-tuple-element.9), channel_id=1, source_target_pairs={{0,16},{8,24},{16,0},{24,8},{1,17},{9,25},{17,1},{25,9},{2,18},{10... | collective-permute-start | bytes 3848 | tf_op jit(solution)/shard_map/ppermute | solution.py:76
  15.8 21.8 %copy-start.1 = (bf16[512,1024]{1,0:T(8,128)(2,1)S(1)}, bf16[512,1024]{1,0:T(8,128)(2,1)}, u32[]{:S(2)}) copy-start(bf16[512,1024]{1,0:T(8,128)(2,1)} %param.20) | copy-start | bytes 3145732
  15.9 22.1 %copy-start.2 = (bf16[256,256]{1,0:T(8,128)(2,1)S(1)}, bf16[256,256]{1,0:T(8,128)(2,1)}, u32[]{:S(2)}) copy-start(bf16[256,256]{1,0:T(8,128)(2,1)} %param.19) | copy-start | bytes 393220
  15.9 22.1 %copy-start.3 = (bf16[256,256]{1,0:T(8,128)(2,1)S(1)}, bf16[256,256]{1,0:T(8,128)(2,1)}, u32[]{:S(2)}) copy-start(bf16[256,256]{1,0:T(8,128)(2,1)} %param.18) | copy-start | bytes 393220
  15.9 5.2 %collective-permute-start.5 = (bf16[128,256]{1,0:T(8,128)(2,1)S(1)}, bf16[128,256]{1,0:T(8,128)(2,1)S(1)}, u32[]{:S(2)}, u32[]{:S(2)}) collective-permute-start(bf16[128,256]{1,0:T(8,128)(2,1)S(1)} %get-tuple-element.15), channel_id=1, source_target_pairs={{0,24},{8,16},{16,8},{24,0},{1,25},{9,17},{17,9},{25,1},{2,26},{10... | collective-permute-start | bytes 196616 | tf_op jit(solution)/shard_map/ppermute | solution.py:76
  17.4 4.4 %collective-permute-start.4 = (bf16[128,256]{1,0:T(8,128)(2,1)S(1)}, bf16[128,256]{1,0:T(8,128)(2,1)S(1)}, u32[]{:S(2)}, u32[]{:S(2)}) collective-permute-start(bf16[128,256]{1,0:T(8,128)(2,1)S(1)} %get-tuple-element.16), channel_id=1, source_target_pairs={{0,16},{8,24},{16,0},{24,8},{1,17},{9,25},{17,1},{25,9},{2,18},{10... | collective-permute-start | bytes 196616 | tf_op jit(solution)/shard_map/ppermute | solution.py:76
  18.9 4.3 %collective-permute-start.3 = (bf16[128,256]{1,0:T(8,128)(2,1)S(1)}, bf16[128,256]{1,0:T(8,128)(2,1)S(1)}, u32[]{:S(2)}, u32[]{:S(2)}) collective-permute-start(bf16[128,256]{1,0:T(8,128)(2,1)S(1)} %get-tuple-element.17), channel_id=1, source_target_pairs={{0,8},{8,0},{16,24},{24,16},{1,9},{9,1},{17,25},{25,17},{2,10},{10... | collective-permute-start | bytes 196616 | tf_op jit(solution)/shard_map/ppermute | solution.py:76
  23.5 6.2 %collective-permute-start.6 = (bf16[128,256]{1,0:T(8,128)(2,1)S(1)}, bf16[128,256]{1,0:T(8,128)(2,1)S(1)}, u32[]{:S(2)}, u32[]{:S(2)}) collective-permute-start(bf16[128,256]{1,0:T(8,128)(2,1)S(1)} %get-tuple-element.28), channel_id=1, source_target_pairs={{0,2},{1,3},{2,4},{3,5},{4,6},{5,7},{6,0},{7,1},{8,10},{9,11},{10,... | collective-permute-start | bytes 196616 | tf_op jit(solution)/shard_map/ppermute | solution.py:32
  25.3 8.0 %collective-permute-start.11 = (bf16[128,256]{1,0:T(8,128)(2,1)S(1)}, bf16[128,256]{1,0:T(8,128)(2,1)S(1)}, u32[]{:S(2)}, u32[]{:S(2)}) collective-permute-start(bf16[128,256]{1,0:T(8,128)(2,1)S(1)} %get-tuple-element.28), channel_id=1, source_target_pairs={{0,6},{1,7},{2,0},{3,1},{4,2},{5,3},{6,4},{7,5},{8,14},{9,15},{10,... | collective-permute-start | bytes 196616 | tf_op jit(solution)/shard_map/ppermute | solution.py:32
  27.6 5.7 %collective-permute-start.10 = (bf16[128,256]{1,0:T(8,128)(2,1)S(1)}, bf16[128,256]{1,0:T(8,128)(2,1)S(1)}, u32[]{:S(2)}, u32[]{:S(2)}) collective-permute-start(bf16[128,256]{1,0:T(8,128)(2,1)S(1)} %get-tuple-element.28), channel_id=1, source_target_pairs={{0,4},{1,5},{2,6},{3,7},{4,0},{5,1},{6,2},{7,3},{8,12},{9,13},{10,... | collective-permute-start | bytes 196616 | tf_op jit(solution)/shard_map/ppermute | solution.py:32
  29.7 5.7 %collective-permute-start.9 = (bf16[192,256]{1,0:T(8,128)(2,1)S(1)}, bf16[192,256]{1,0:T(8,128)(2,1)S(1)}, u32[]{:S(2)}, u32[]{:S(2)}) collective-permute-start(bf16[192,256]{1,0:T(8,128)(2,1)S(1)} %get-tuple-element.19), channel_id=1, source_target_pairs={{0,24},{8,16},{16,8},{24,0},{1,25},{9,17},{17,9},{25,1},{2,26},{10... | collective-permute-start | bytes 294920 | tf_op jit(solution)/shard_map/ppermute | solution.py:76
  30.7 5.7 %collective-permute-start.8 = (bf16[192,256]{1,0:T(8,128)(2,1)S(1)}, bf16[192,256]{1,0:T(8,128)(2,1)S(1)}, u32[]{:S(2)}, u32[]{:S(2)}) collective-permute-start(bf16[192,256]{1,0:T(8,128)(2,1)S(1)} %get-tuple-element.20), channel_id=1, source_target_pairs={{0,16},{8,24},{16,0},{24,8},{1,17},{9,25},{17,1},{25,9},{2,18},{10... | collective-permute-start | bytes 294920 | tf_op jit(solution)/shard_map/ppermute | solution.py:76
  31.8 4.6 %collective-permute-start.7 = (bf16[192,256]{1,0:T(8,128)(2,1)S(1)}, bf16[192,256]{1,0:T(8,128)(2,1)S(1)}, u32[]{:S(2)}, u32[]{:S(2)}) collective-permute-start(bf16[192,256]{1,0:T(8,128)(2,1)S(1)} %get-tuple-element.21), channel_id=1, source_target_pairs={{0,8},{8,0},{16,24},{24,16},{1,9},{9,1},{17,25},{25,17},{2,10},{10... | collective-permute-start | bytes 294920 | tf_op jit(solution)/shard_map/ppermute | solution.py:76
  33.3 4.7 %collective-permute-start.12 = (bf16[4,128,256]{2,1,0:T(8,128)(2,1)S(1)}, bf16[4,128,256]{2,1,0:T(8,128)(2,1)S(1)}, u32[]{:S(2)}, u32[]{:S(2)}) collective-permute-start(bf16[4,128,256]{2,1,0:T(8,128)(2,1)S(1)} %pad_maximum_fusion.2), channel_id=1, source_target_pairs={{0,1},{1,0},{2,3},{3,2},{4,5},{5,4},{6,7},{7,6},{8,9},{9,8},{10,11... | collective-permute-start | bytes 786440 | tf_op jit(solution)/shard_map/ppermute | solution.py:35
  38.0 0.9 %copy-start.4 = (bf16[256,256]{0,1:T(8,128)(2,1)S(1)}, bf16[256,256]{0,1:T(8,128)(2,1)}, u32[]{:S(2)}) copy-start(bf16[256,256]{0,1:T(8,128)(2,1)} %convolution_convert_fusion.2) | copy-start | bytes 393220

commit v15 on v12

--- a/solution.py
+++ b/solution.py
@@ -117,8 +117,9 @@
     fetched = jnp.take(table, asked.reshape(-1), axis=0, mode="clip").reshape(
         n_dest, hist_cap + cand_cap, d_model
     )
-    hist_replies = swap_over_req(fetched[:, :hist_cap]).reshape(n_dest * hist_cap, d_model)
-    cand_replies = swap_over_req(fetched[:, hist_cap:]).reshape(n_dest * cand_cap, d_model)
+    replies = swap_over_req(fetched)
+    hist_replies = replies[:, :hist_cap].reshape(n_dest * hist_cap, d_model)
+    cand_replies = replies[:, hist_cap:].reshape(n_dest * cand_cap, d_model)
     hist_emb = jnp.dot(hist_pick, hist_replies, preferred_element_type=jnp.float32).astype(jnp.bfloat16)
     cand_emb = jnp.dot(cand_pick, cand_replies, preferred_element_type=jnp.float32).astype(jnp.bfloat16)
     head_size = d_model // HEADS

time: 38.8 us -> 40 us (1.031)
  waiting for transfers between devices: 7.61 us -> 13 us
  starting transfers between devices: 17 us -> 12.9 us
    ppermute x9 -> x6, waiting for transfers between devices: 2.04 us -> 7.38 us  [swap_over_req(): lax.ppermute(blocks[hop], 'req', [(i, i ^ hop) for i in range(n_req)])]
    ppermute x9 -> x6, starting transfers between devices: 12 us -> 8.1 us  [swap_over_req(): lax.ppermute(blocks[hop], 'req', [(i, i ^ hop) for i in range(n_req)])]
  transfers between devices with their start and end apart: 13 -> 10, of which waited for: 7 -> 8; matrix products, arithmetic and copies ran while one was open for 6% -> 5% of each run, Pallas kernels for 0% -> 0%
where the time goes in v15:
time: 40 us; the launch traced here: 39.8 us
  waiting for transfers between devices  13 us (32%)
  starting transfers between devices  12.9 us (32%)
  local copies, waits for them, and re-layouts  7.02 us (18%)
  matrix products  4.5 us (11%)
  other arithmetic  1.52 us (4%)
  between operations  0.94 us (2%)
    ppermute x6, starting transfers between devices, swap_over_req(): lax.ppermute(blocks[hop], 'req', [(i, i ^ hop) for i in range(n_req)])  8.1 us
    ppermute x6, waiting for transfers between devices, swap_over_req(): lax.ppermute(blocks[hop], 'req', [(i, i ^ hop) for i in range(n_req)])  7.38 us
    gather x1, local copies, waits for them, and re-layouts, body(): jnp.take(table, asked.reshape(-1), axis=0, mode='clip')  5.86 us
    ppermute x3, starting transfers between devices, gather_over_cand(): lax.ppermute(rows, 'cand', [(i, (i + hop) % n_cand) for i in range(n_cand)])  4.71 us
    ppermute x3, waiting for transfers between devices, gather_over_cand(): lax.ppermute(rows, 'cand', [(i, (i + hop) % n_cand) for i in range(n_cand)])  4.13 us
    ppermute x1, waiting for transfers between devices, gather_over_cand(): partner = lax.ppermute(mine, 'cand', [(i, i ^ 1) for i in range(n_cand)])  1.48 us
    dot_general x1, matrix products, attend(): jnp.einsum('bgo,ogl->bgl', gates, values, preferred_element_type=jnp.floa...  1.32 us
    dot_general x1, matrix products, body(): jnp.dot(hidden, tower_out, preferred_element_type=jnp.float32)[None, :]  1.2 us
  transfers between devices with their start and end apart: 10, of which 8 were waited for; matrix products, arithmetic and copies ran while one was open for 5% of the time, Pallas kernels for 0%

profile of v15, /device:TPU:0, one launch (start us, length us, event | category | flops | bytes accessed | tf_op | source)
XLA Modules:
  0.0 39.8 jit_solution(9474028724952293519)
XLA Ops:
  0.0 0.7 %pad_add_fusion.1 = s32[768]{0:T(1024)S(1)} fusion(s32[256]{0:T(256)} %bitcast.76, s32[256]{0:T(256)} %bitcast.77, s32[128]{0:T(128)} %bitcast.78, s32[128]{0:T(128)} %bitcast.79), kind=kLoop, calls=%fused_computation.53 | loop fusion | flops 2304 | bytes 6144 | tf_op jit(solution)/shard_map/concatenate | solution.py:98
  0.8 0.2 convert_reduce_fusion.1
  1.0 0.2 convert_reduce_fusion
  1.2 0.2 convolution_convert_fusion.5
  1.4 0.3 convolution_convert_fusion.4
  1.8 3.0 %collective-permute-start = (s32[320]{0:T(512)S(1)}, s32[320]{0:T(512)S(1)}, u32[]{:S(2)}, u32[]{:S(2)}) collective-permute-start(s32[320]{0:T(512)S(1)} %get-tuple-element.5), channel_id=1, source_target_pairs={{0,8},{8,0},{16,24},{24,16},{1,9},{9,1},{17,25},{25,17},{2,10},{10... | collective-permute-start | bytes 3848 | tf_op jit(solution)/shard_map/ppermute | solution.py:76
  4.8 1.5 %collective-permute-start.2 = (s32[320]{0:T(512)S(1)}, s32[320]{0:T(512)S(1)}, u32[]{:S(2)}, u32[]{:S(2)}) collective-permute-start(s32[320]{0:T(512)S(1)} %get-tuple-element.6), channel_id=1, source_target_pairs={{0,24},{8,16},{16,8},{24,0},{1,25},{9,17},{17,9},{25,1},{2,26},{10... | collective-permute-start | bytes 3848 | tf_op jit(solution)/shard_map/ppermute | solution.py:76
  6.4 0.1 concatenate.39
  7.2 0.7 %reshape.136 = bf16[1024,1]{0,1:T(2,128)(2,1)S(1)} reshape(bf16[1024]{0:T(1024)(128)(2,1)} %param.21) | data formatting | bytes 4096 | tf_op args[10]
  7.9 1.4 %collective-permute-done.2 = s32[320]{0:T(512)S(1)} collective-permute-done((s32[320]{0:T(512)S(1)}, s32[320]{0:T(512)S(1)}, u32[]{:S(2)}, u32[]{:S(2)}) %collective-permute-start.2) | collective-permute-done | bytes 1312 | tf_op jit(solution)/shard_map/ppermute | solution.py:76
  9.3 0.6 %collective-permute-done.1 = s32[320]{0:T(512)S(1)} collective-permute-done((s32[320]{0:T(512)S(1)}, s32[320]{0:T(512)S(1)}, u32[]{:S(2)}, u32[]{:S(2)}) %collective-permute-start.1) | collective-permute-done | bytes 1312 | tf_op jit(solution)/shard_map/ppermute | solution.py:76
  9.9 0.1 reshape.129
  10.0 5.9 %gather_fusion = bf16[1280,256]{1,0:T(8,128)(2,1)S(1)} fusion(bf16[8192,256]{1,0:T(8,128)(2,1)} %param.11, s32[2048]{0:T(1024)S(1)} %pad_clamp_fusion), kind=kCustom, calls=%fused_computation | custom fusion | bytes 1315840 | tf_op jit(solution)/shard_map/jit(_take)/gather | solution.py:117
  15.9 1.0 %collective-permute-start.4 = (bf16[320,256]{1,0:T(8,128)(2,1)S(1)}, bf16[320,256]{1,0:T(8,128)(2,1)S(1)}, u32[]{:S(2)}, u32[]{:S(2)}) collective-permute-start(bf16[320,256]{1,0:T(8,128)(2,1)S(1)} %get-tuple-element.13), channel_id=1, source_target_pairs={{0,16},{8,24},{16,0},{24,8},{1,17},{9,25},{17,1},{25,9},{2,18},{10... | collective-permute-start | bytes 491528 | tf_op jit(solution)/shard_map/ppermute | solution.py:76
  16.9 1.1 %collective-permute-start.3 = (bf16[320,256]{1,0:T(8,128)(2,1)S(1)}, bf16[320,256]{1,0:T(8,128)(2,1)S(1)}, u32[]{:S(2)}, u32[]{:S(2)}) collective-permute-start(bf16[320,256]{1,0:T(8,128)(2,1)S(1)} %get-tuple-element.14), channel_id=1, source_target_pairs={{0,8},{8,0},{16,24},{24,16},{1,9},{9,1},{17,25},{25,17},{2,10},{10... | collective-permute-start | bytes 491528 | tf_op jit(solution)/shard_map/ppermute | solution.py:76
  18.0 1.5 %collective-permute-start.5 = (bf16[320,256]{1,0:T(8,128)(2,1)S(1)}, bf16[320,256]{1,0:T(8,128)(2,1)S(1)}, u32[]{:S(2)}, u32[]{:S(2)}) collective-permute-start(bf16[320,256]{1,0:T(8,128)(2,1)S(1)} %get-tuple-element.15), channel_id=1, source_target_pairs={{0,24},{8,16},{16,8},{24,0},{1,25},{9,17},{17,9},{25,1},{2,26},{10... | collective-permute-start | bytes 491528 | tf_op jit(solution)/shard_map/ppermute | solution.py:76
  19.6 3.5 %collective-permute-done.4 = bf16[320,256]{1,0:T(8,128)(2,1)S(1)} collective-permute-done((bf16[320,256]{1,0:T(8,128)(2,1)S(1)}, bf16[320,256]{1,0:T(8,128)(2,1)S(1)}, u32[]{:S(2)}, u32[]{:S(2)}) %collective-permute-start.4) | collective-permute-done | bytes 163872 | tf_op jit(solution)/shard_map/ppermute | solution.py:76
  23.1 1.9 %collective-permute-done.5 = bf16[320,256]{1,0:T(8,128)(2,1)S(1)} collective-permute-done((bf16[320,256]{1,0:T(8,128)(2,1)S(1)}, bf16[320,256]{1,0:T(8,128)(2,1)S(1)}, u32[]{:S(2)}, u32[]{:S(2)}) %collective-permute-start.5) | collective-permute-done | bytes 163872 | tf_op jit(solution)/shard_map/ppermute | solution.py:76
  25.0 0.1 pad_maximum_fusion
  25.1 0.2 constant_dynamic-update-slice_fusion.4
  25.3 3.7 %collective-permute-start.8 = (bf16[128,256]{1,0:T(8,128)(2,1)S(1)}, bf16[128,256]{1,0:T(8,128)(2,1)S(1)}, u32[]{:S(2)}, u32[]{:S(2)}) collective-permute-start(bf16[128,256]{1,0:T(8,128)(2,1)S(1)} %get-tuple-element.22), channel_id=1, source_target_pairs={{0,6},{1,7},{2,0},{3,1},{4,2},{5,3},{6,4},{7,5},{8,14},{9,15},{10,... | collective-permute-start | bytes 196616 | tf_op jit(solution)/shard_map/ppermute | solution.py:32
  29.0 1.0 %collective-permute-start.6 = (bf16[128,256]{1,0:T(8,128)(2,1)S(1)}, bf16[128,256]{1,0:T(8,128)(2,1)S(1)}, u32[]{:S(2)}, u32[]{:S(2)}) collective-permute-start(bf16[128,256]{1,0:T(8,128)(2,1)S(1)} %get-tuple-element.22), channel_id=1, source_target_pairs={{0,2},{1,3},{2,4},{3,5},{4,6},{5,7},{6,0},{7,1},{8,10},{9,11},{10,... | collective-permute-start | bytes 196616 | tf_op jit(solution)/shard_map/ppermute | solution.py:32
  30.0 0.3 convolution_convert_fusion.1
  30.4 0.3 fusion.12
  30.7 0.2 convolution_convert_fusion.2
  30.9 0.1 collective-permute-done.8
  31.0 3.1 %collective-permute-done.7 = bf16[128,256]{1,0:T(8,128)(2,1)S(1)} collective-permute-done((bf16[128,256]{1,0:T(8,128)(2,1)S(1)}, bf16[128,256]{1,0:T(8,128)(2,1)S(1)}, u32[]{:S(2)}, u32[]{:S(2)}) %collective-permute-start.7) | collective-permute-done | bytes 65568 | tf_op jit(solution)/shard_map/ppermute | solution.py:32
  34.2 0.9 %collective-permute-done.6 = bf16[128,256]{1,0:T(8,128)(2,1)S(1)} collective-permute-done((bf16[128,256]{1,0:T(8,128)(2,1)S(1)}, bf16[128,256]{1,0:T(8,128)(2,1)S(1)}, u32[]{:S(2)}, u32[]{:S(2)}) %collective-permute-start.6) | collective-permute-done | bytes 65568 | tf_op jit(solution)/shard_map/ppermute | solution.py:32
  35.2 1.5 %collective-permute-done.9 = bf16[4,128,256]{2,1,0:T(8,128)(2,1)S(1)} collective-permute-done((bf16[4,128,256]{2,1,0:T(8,128)(2,1)S(1)}, bf16[4,128,256]{2,1,0:T(8,128)(2,1)S(1)}, u32[]{:S(2)}, u32[]{:S(2)}) %collective-permute-start.9) | collective-permute-done | bytes 262176 | tf_op jit(solution)/shard_map/ppermute | solution.py:35
  36.8 0.5 %convolution_convert_fusion = bf16[1024,512]{0,1:T(8,128)(2,1)S(1)} fusion(bf16[1024,256]{1,0:T(8,128)(2,1)S(1)} %bitcast.60, bf16[256,256]{1,0:T(8,128)(2,1)S(1)} %copy-done.2, bf16[256,256]{1,0:T(8,128)(2,1)S(1)} %copy-done.3), kind=kOutput, calls=%fused_computation.4 | convolution fusion | flops 269484032 | bytes 1835008 | tf_op jit(solution)/shard_map/dot_general | solution.py:48
  37.3 1.3 %fusion.5 = bf16[4,64,256]{2,1,0:T(8,128)(2,1)S(1)} fusion(bf16[1024,4,64]{0,2,1:T(8,128)(2,1)S(1)} %bitcast.68, bf16[1024,4,64]{0,2,1:T(8,128)(2,1)S(1)} %bitcast.67, bf16[256,4,64]{0,2,1:T(8,128)(2,1)S(1)} %bitcast.74, pred[1024]{0:T(1024)(128)(4,1)S(1)} %fusion.23, f32[]{:T(128)S(6)} %sqrt.3), kind=kOutput, calls=%fused_computation.12 | convolution fusion | flops 273809408 | bytes 1311748 | tf_op jit(solution)/shard_map/bgo,ogl->bgl/dot_general | solution.py:60
  38.6 1.2 %fusion.8 = f32[1,256]{1,0:T(1,128)} fusion(bf16[1024,1]{0,1:T(2,128)(2,1)S(1)} %reshape.136, f32[256,1024]{1,0:T(8,128)S(1)} %fusion.12, bf16[256,256]{0,1:T(8,128)(2,1)S(1)} %bitcast.80, bf16[512,1024]{1,0:T(8,128)(2,1)S(1)} %copy-done.1), kind=kOutput, calls=%fused_computation.14 | convolution fusion | flops 136314880 | bytes 1709056 | tf_op jit(solution)/shard_map/dot_general | solution.py:151
  (41 shorter events, 0.8 us)
Async XLA Ops:
  0.0 30.7 %copy-start = (bf16[256,256]{1,0:T(8,128)(2,1)S(1)}, bf16[256,256]{1,0:T(8,128)(2,1)}, u32[]{:S(2)}) copy-start(bf16[256,256]{1,0:T(8,128)(2,1)} %param.17) | copy-start | bytes 393220
  1.8 6.1 %collective-permute-start = (s32[320]{0:T(512)S(1)}, s32[320]{0:T(512)S(1)}, u32[]{:S(2)}, u32[]{:S(2)}) collective-permute-start(s32[320]{0:T(512)S(1)} %get-tuple-element.5), channel_id=1, source_target_pairs={{0,8},{8,0},{16,24},{24,16},{1,9},{9,1},{17,25},{25,17},{2,10},{10... | collective-permute-start | bytes 3848 | tf_op jit(solution)/shard_map/ppermute | solution.py:76
  4.8 4.5 %collective-permute-start.2 = (s32[320]{0:T(512)S(1)}, s32[320]{0:T(512)S(1)}, u32[]{:S(2)}, u32[]{:S(2)}) collective-permute-start(s32[320]{0:T(512)S(1)} %get-tuple-element.6), channel_id=1, source_target_pairs={{0,24},{8,16},{16,8},{24,0},{1,25},{9,17},{17,9},{25,1},{2,26},{10... | collective-permute-start | bytes 3848 | tf_op jit(solution)/shard_map/ppermute | solution.py:76
  6.3 3.6 %collective-permute-start.1 = (s32[320]{0:T(512)S(1)}, s32[320]{0:T(512)S(1)}, u32[]{:S(2)}, u32[]{:S(2)}) collective-permute-start(s32[320]{0:T(512)S(1)} %get-tuple-element.7), channel_id=1, source_target_pairs={{0,16},{8,24},{16,0},{24,8},{1,17},{9,25},{17,1},{25,9},{2,18},{10... | collective-permute-start | bytes 3848 | tf_op jit(solution)/shard_map/ppermute | solution.py:76
  15.8 14.5 %copy-start.1 = (bf16[512,1024]{1,0:T(8,128)(2,1)S(1)}, bf16[512,1024]{1,0:T(8,128)(2,1)}, u32[]{:S(2)}) copy-start(bf16[512,1024]{1,0:T(8,128)(2,1)} %param.20) | copy-start | bytes 3145732
  15.8 20.9 %copy-start.2 = (bf16[256,256]{1,0:T(8,128)(2,1)S(1)}, bf16[256,256]{1,0:T(8,128)(2,1)}, u32[]{:S(2)}) copy-start(bf16[256,256]{1,0:T(8,128)(2,1)} %param.19) | copy-start | bytes 393220
  15.9 20.9 %copy-start.3 = (bf16[256,256]{1,0:T(8,128)(2,1)S(1)}, bf16[256,256]{1,0:T(8,128)(2,1)}, u32[]{:S(2)}) copy-start(bf16[256,256]{1,0:T(8,128)(2,1)} %param.18) | copy-start | bytes 393220
  15.9 7.1 %collective-permute-start.4 = (bf16[320,256]{1,0:T(8,128)(2,1)S(1)}, bf16[320,256]{1,0:T(8,128)(2,1)S(1)}, u32[]{:S(2)}, u32[]{:S(2)}) collective-permute-start(bf16[320,256]{1,0:T(8,128)(2,1)S(1)} %get-tuple-element.13), channel_id=1, source_target_pairs={{0,16},{8,24},{16,0},{24,8},{1,17},{9,25},{17,1},{25,9},{2,18},{10... | collective-permute-start | bytes 491528 | tf_op jit(solution)/shard_map/ppermute | solution.py:76
  16.9 6.1 %collective-permute-start.3 = (bf16[320,256]{1,0:T(8,128)(2,1)S(1)}, bf16[320,256]{1,0:T(8,128)(2,1)S(1)}, u32[]{:S(2)}, u32[]{:S(2)}) collective-permute-start(bf16[320,256]{1,0:T(8,128)(2,1)S(1)} %get-tuple-element.14), channel_id=1, source_target_pairs={{0,8},{8,0},{16,24},{24,16},{1,9},{9,1},{17,25},{25,17},{2,10},{10... | collective-permute-start | bytes 491528 | tf_op jit(solution)/shard_map/ppermute | solution.py:76
  18.0 7.0 %collective-permute-start.5 = (bf16[320,256]{1,0:T(8,128)(2,1)S(1)}, bf16[320,256]{1,0:T(8,128)(2,1)S(1)}, u32[]{:S(2)}, u32[]{:S(2)}) collective-permute-start(bf16[320,256]{1,0:T(8,128)(2,1)S(1)} %get-tuple-element.15), channel_id=1, source_target_pairs={{0,24},{8,16},{16,8},{24,0},{1,25},{9,17},{17,9},{25,1},{2,26},{10... | collective-permute-start | bytes 491528 | tf_op jit(solution)/shard_map/ppermute | solution.py:76
  25.3 5.7 %collective-permute-start.8 = (bf16[128,256]{1,0:T(8,128)(2,1)S(1)}, bf16[128,256]{1,0:T(8,128)(2,1)S(1)}, u32[]{:S(2)}, u32[]{:S(2)}) collective-permute-start(bf16[128,256]{1,0:T(8,128)(2,1)S(1)} %get-tuple-element.22), channel_id=1, source_target_pairs={{0,6},{1,7},{2,0},{3,1},{4,2},{5,3},{6,4},{7,5},{8,14},{9,15},{10,... | collective-permute-start | bytes 196616 | tf_op jit(solution)/shard_map/ppermute | solution.py:32
  29.0 5.2 %collective-permute-start.7 = (bf16[128,256]{1,0:T(8,128)(2,1)S(1)}, bf16[128,256]{1,0:T(8,128)(2,1)S(1)}, u32[]{:S(2)}, u32[]{:S(2)}) collective-permute-start(bf16[128,256]{1,0:T(8,128)(2,1)S(1)} %get-tuple-element.22), channel_id=1, source_target_pairs={{0,4},{1,5},{2,6},{3,7},{4,0},{5,1},{6,2},{7,3},{8,12},{9,13},{10,... | collective-permute-start | bytes 196616 | tf_op jit(solution)/shard_map/ppermute | solution.py:32
  29.0 6.1 %collective-permute-start.6 = (bf16[128,256]{1,0:T(8,128)(2,1)S(1)}, bf16[128,256]{1,0:T(8,128)(2,1)S(1)}, u32[]{:S(2)}, u32[]{:S(2)}) collective-permute-start(bf16[128,256]{1,0:T(8,128)(2,1)S(1)} %get-tuple-element.22), channel_id=1, source_target_pairs={{0,2},{1,3},{2,4},{3,5},{4,6},{5,7},{6,0},{7,1},{8,10},{9,11},{10,... | collective-permute-start | bytes 196616 | tf_op jit(solution)/shard_map/ppermute | solution.py:32
  35.1 1.6 %collective-permute-start.9 = (bf16[4,128,256]{2,1,0:T(8,128)(2,1)S(1)}, bf16[4,128,256]{2,1,0:T(8,128)(2,1)S(1)}, u32[]{:S(2)}, u32[]{:S(2)}) collective-permute-start(bf16[4,128,256]{2,1,0:T(8,128)(2,1)S(1)} %pad_maximum_fusion.2), channel_id=1, source_target_pairs={{0,1},{1,0},{2,3},{3,2},{4,5},{5,4},{6,7},{7,6},{8,9},{9,8},{10,11... | collective-permute-start | bytes 786440 | tf_op jit(solution)/shard_map/ppermute | solution.py:35

commit v16 on v12

--- a/solution.py
+++ b/solution.py
@@ -26,11 +26,12 @@
 
 def gather_over_cand(rows):
     n_cand = lax.axis_size("cand")
+    assert n_cand & (n_cand - 1) == 0
     me = lax.axis_index("cand")
     blocks, sources = [rows], [me]
     for hop in range(2, n_cand, 2):
-        blocks.append(lax.ppermute(rows, "cand", [(i, (i + hop) % n_cand) for i in range(n_cand)]))
-        sources.append((me - hop) % n_cand)
+        blocks.append(lax.ppermute(rows, "cand", [(i, i ^ hop) for i in range(n_cand)]))
+        sources.append(me ^ hop)
     mine = jnp.stack(blocks, axis=0)
     partner = lax.ppermute(mine, "cand", [(i, i ^ 1) for i in range(n_cand)])
     source = jnp.stack(sources)

time: 38.8 us -> 37.9 us (0.977)
  waiting for transfers between devices: 7.61 us -> 7.1 us
  starting transfers between devices: 17 us -> 16.6 us
    ppermute x3, waiting for transfers between devices: 4.09 us -> 3.57 us  [gather_over_cand(): lax.ppermute(rows, 'cand', [(i, i ^ hop) for i in range(n_cand)])]
where the time goes in v16:
time: 37.9 us; the launch traced here: 37.8 us
  starting transfers between devices  16.6 us (44%)
  waiting for transfers between devices  7.1 us (19%)
  local copies, waits for them, and re-layouts  7.08 us (19%)
  matrix products  4.5 us (12%)
  other arithmetic  1.51 us (4%)
  between operations  0.95 us (3%)
    ppermute x9, starting transfers between devices, swap_over_req(): lax.ppermute(blocks[hop], 'req', [(i, i ^ hop) for i in range(n_req)])  12 us
    gather x1, local copies, waits for them, and re-layouts, body(): jnp.take(table, asked.reshape(-1), axis=0, mode='clip')  5.96 us
    ppermute x3, starting transfers between devices, gather_over_cand(): lax.ppermute(rows, 'cand', [(i, i ^ hop) for i in range(n_cand)])  4.52 us
    ppermute x3, waiting for transfers between devices, gather_over_cand(): lax.ppermute(rows, 'cand', [(i, i ^ hop) for i in range(n_cand)])  3.57 us
    ppermute x9, waiting for transfers between devices, swap_over_req(): lax.ppermute(blocks[hop], 'req', [(i, i ^ hop) for i in range(n_req)])  2.05 us
    ppermute x1, waiting for transfers between devices, gather_over_cand(): partner = lax.ppermute(mine, 'cand', [(i, i ^ 1) for i in range(n_cand)])  1.48 us
    dot_general x1, matrix products, attend(): jnp.einsum('bgo,ogl->bgl', gates, values, preferred_element_type=jnp.floa...  1.32 us
    dot_general x1, matrix products, body(): jnp.dot(hidden, tower_out, preferred_element_type=jnp.float32)[None, :]  1.2 us
  transfers between devices with their start and end apart: 13, of which 7 were waited for; matrix products, arithmetic and copies ran while one was open for 6% of the time, Pallas kernels for 0%

profile of v16, /device:TPU:0, one launch (start us, length us, event | category | flops | bytes accessed | tf_op | source)
XLA Modules:
  0.0 37.8 jit_solution(5642592848219406820)
XLA Ops:
  0.0 0.7 %pad_add_fusion.1 = s32[768]{0:T(1024)S(1)} fusion(s32[256]{0:T(256)} %bitcast.92, s32[256]{0:T(256)} %bitcast.93, s32[128]{0:T(128)} %bitcast.94, s32[128]{0:T(128)} %bitcast.95), kind=kLoop, calls=%fused_computation.58 | loop fusion | flops 2304 | bytes 6144 | tf_op jit(solution)/shard_map/concatenate | solution.py:99
  0.8 0.2 convert_reduce_fusion.1
  1.0 0.2 convert_reduce_fusion
  1.2 0.2 convolution_convert_fusion.5
  1.4 0.3 convolution_convert_fusion.4
  1.8 3.0 %collective-permute-start = (s32[320]{0:T(512)S(1)}, s32[320]{0:T(512)S(1)}, u32[]{:S(2)}, u32[]{:S(2)}) collective-permute-start(s32[320]{0:T(512)S(1)} %get-tuple-element.5), channel_id=1, source_target_pairs={{0,8},{8,0},{16,24},{24,16},{1,9},{9,1},{17,25},{25,17},{2,10},{10... | collective-permute-start | bytes 3848 | tf_op jit(solution)/shard_map/ppermute | solution.py:77
  4.8 1.5 %collective-permute-start.2 = (s32[320]{0:T(512)S(1)}, s32[320]{0:T(512)S(1)}, u32[]{:S(2)}, u32[]{:S(2)}) collective-permute-start(s32[320]{0:T(512)S(1)} %get-tuple-element.6), channel_id=1, source_target_pairs={{0,24},{8,16},{16,8},{24,0},{1,25},{9,17},{17,9},{25,1},{2,26},{10... | collective-permute-start | bytes 3848 | tf_op jit(solution)/shard_map/ppermute | solution.py:77
  7.0 0.1 concatenate.39
  7.3 0.7 %reshape.132 = bf16[1024,1]{0,1:T(2,128)(2,1)S(1)} reshape(bf16[1024]{0:T(1024)(128)(2,1)} %param.21) | data formatting | bytes 4096 | tf_op args[10]
  8.0 1.3 %collective-permute-done.2 = s32[320]{0:T(512)S(1)} collective-permute-done((s32[320]{0:T(512)S(1)}, s32[320]{0:T(512)S(1)}, u32[]{:S(2)}, u32[]{:S(2)}) %collective-permute-start.2) | collective-permute-done | bytes 1312 | tf_op jit(solution)/shard_map/ppermute | solution.py:77
  9.3 0.6 %collective-permute-done.1 = s32[320]{0:T(512)S(1)} collective-permute-done((s32[320]{0:T(512)S(1)}, s32[320]{0:T(512)S(1)}, u32[]{:S(2)}, u32[]{:S(2)}) %collective-permute-start.1) | collective-permute-done | bytes 1312 | tf_op jit(solution)/shard_map/ppermute | solution.py:77
  9.9 0.1 reshape.125
  10.0 6.0 %gather_fusion = bf16[1280,256]{1,0:T(8,128)(2,1)S(1)} fusion(bf16[8192,256]{1,0:T(8,128)(2,1)} %param.11, s32[2048]{0:T(1024)S(1)} %pad_clamp_fusion), kind=kCustom, calls=%fused_computation | custom fusion | bytes 1315840 | tf_op jit(solution)/shard_map/jit(_take)/gather | solution.py:118
  16.0 1.5 %collective-permute-start.8 = (bf16[128,256]{1,0:T(8,128)(2,1)S(1)}, bf16[128,256]{1,0:T(8,128)(2,1)S(1)}, u32[]{:S(2)}, u32[]{:S(2)}) collective-permute-start(bf16[128,256]{1,0:T(8,128)(2,1)S(1)} %get-tuple-element.13), channel_id=1, source_target_pairs={{0,24},{8,16},{16,8},{24,0},{1,25},{9,17},{17,9},{25,1},{2,26},{10... | collective-permute-start | bytes 196616 | tf_op jit(solution)/shard_map/ppermute | solution.py:77
  17.5 1.5 %collective-permute-start.7 = (bf16[128,256]{1,0:T(8,128)(2,1)S(1)}, bf16[128,256]{1,0:T(8,128)(2,1)S(1)}, u32[]{:S(2)}, u32[]{:S(2)}) collective-permute-start(bf16[128,256]{1,0:T(8,128)(2,1)S(1)} %get-tuple-element.14), channel_id=1, source_target_pairs={{0,16},{8,24},{16,0},{24,8},{1,17},{9,25},{17,1},{25,9},{2,18},{10... | collective-permute-start | bytes 196616 | tf_op jit(solution)/shard_map/ppermute | solution.py:77
  19.0 0.5 %collective-permute-start.6 = (bf16[128,256]{1,0:T(8,128)(2,1)S(1)}, bf16[128,256]{1,0:T(8,128)(2,1)S(1)}, u32[]{:S(2)}, u32[]{:S(2)}) collective-permute-start(bf16[128,256]{1,0:T(8,128)(2,1)S(1)} %get-tuple-element.15), channel_id=1, source_target_pairs={{0,8},{8,0},{16,24},{24,16},{1,9},{9,1},{17,25},{25,17},{2,10},{10... | collective-permute-start | bytes 196616 | tf_op jit(solution)/shard_map/ppermute | solution.py:77
  19.6 1.5 %collective-permute-start.5 = (bf16[192,256]{1,0:T(8,128)(2,1)S(1)}, bf16[192,256]{1,0:T(8,128)(2,1)S(1)}, u32[]{:S(2)}, u32[]{:S(2)}) collective-permute-start(bf16[192,256]{1,0:T(8,128)(2,1)S(1)} %get-tuple-element.17), channel_id=1, source_target_pairs={{0,24},{8,16},{16,8},{24,0},{1,25},{9,17},{17,9},{25,1},{2,26},{10... | collective-permute-start | bytes 294920 | tf_op jit(solution)/shard_map/ppermute | solution.py:77
  21.1 1.5 %collective-permute-start.4 = (bf16[192,256]{1,0:T(8,128)(2,1)S(1)}, bf16[192,256]{1,0:T(8,128)(2,1)S(1)}, u32[]{:S(2)}, u32[]{:S(2)}) collective-permute-start(bf16[192,256]{1,0:T(8,128)(2,1)S(1)} %get-tuple-element.18), channel_id=1, source_target_pairs={{0,16},{8,24},{16,0},{24,8},{1,17},{9,25},{17,1},{25,9},{2,18},{10... | collective-permute-start | bytes 294920 | tf_op jit(solution)/shard_map/ppermute | solution.py:77
  22.6 0.9 %collective-permute-start.3 = (bf16[192,256]{1,0:T(8,128)(2,1)S(1)}, bf16[192,256]{1,0:T(8,128)(2,1)S(1)}, u32[]{:S(2)}, u32[]{:S(2)}) collective-permute-start(bf16[192,256]{1,0:T(8,128)(2,1)S(1)} %get-tuple-element.19), channel_id=1, source_target_pairs={{0,8},{8,0},{16,24},{24,16},{1,9},{9,1},{17,25},{25,17},{2,10},{10... | collective-permute-start | bytes 294920 | tf_op jit(solution)/shard_map/ppermute | solution.py:77
  23.6 0.1 collective-permute-done.6
  23.7 0.2 constant_dynamic-update-slice_fusion.4
  23.9 3.9 %collective-permute-start.11 = (bf16[128,256]{1,0:T(8,128)(2,1)S(1)}, bf16[128,256]{1,0:T(8,128)(2,1)S(1)}, u32[]{:S(2)}, u32[]{:S(2)}) collective-permute-start(bf16[128,256]{1,0:T(8,128)(2,1)S(1)} %get-tuple-element.26), channel_id=1, source_target_pairs={{0,6},{1,7},{2,4},{3,5},{4,2},{5,3},{6,0},{7,1},{8,14},{9,15},{10,... | collective-permute-start | bytes 196616 | tf_op jit(solution)/shard_map/ppermute | solution.py:33
  27.8 0.6 %collective-permute-start.9 = (bf16[128,256]{1,0:T(8,128)(2,1)S(1)}, bf16[128,256]{1,0:T(8,128)(2,1)S(1)}, u32[]{:S(2)}, u32[]{:S(2)}) collective-permute-start(bf16[128,256]{1,0:T(8,128)(2,1)S(1)} %get-tuple-element.26), channel_id=1, source_target_pairs={{0,2},{1,3},{2,0},{3,1},{4,6},{5,7},{6,4},{7,5},{8,10},{9,11},{10,... | collective-permute-start | bytes 196616 | tf_op jit(solution)/shard_map/ppermute | solution.py:33
  28.5 0.3 convolution_convert_fusion.1
  28.9 0.3 fusion.12
  29.2 0.2 convolution_convert_fusion.2
  29.4 0.8 %collective-permute-done.11 = bf16[128,256]{1,0:T(8,128)(2,1)S(1)} collective-permute-done((bf16[128,256]{1,0:T(8,128)(2,1)S(1)}, bf16[128,256]{1,0:T(8,128)(2,1)S(1)}, u32[]{:S(2)}, u32[]{:S(2)}) %collective-permute-start.11) | collective-permute-done | bytes 65568 | tf_op jit(solution)/shard_map/ppermute | solution.py:33
  30.2 2.8 %collective-permute-done.10 = bf16[128,256]{1,0:T(8,128)(2,1)S(1)} collective-permute-done((bf16[128,256]{1,0:T(8,128)(2,1)S(1)}, bf16[128,256]{1,0:T(8,128)(2,1)S(1)}, u32[]{:S(2)}, u32[]{:S(2)}) %collective-permute-start.10) | collective-permute-done | bytes 65568 | tf_op jit(solution)/shard_map/ppermute | solution.py:33
  33.1 1.5 %collective-permute-done.12 = bf16[4,128,256]{2,1,0:T(8,128)(2,1)S(1)} collective-permute-done((bf16[4,128,256]{2,1,0:T(8,128)(2,1)S(1)}, bf16[4,128,256]{2,1,0:T(8,128)(2,1)S(1)}, u32[]{:S(2)}, u32[]{:S(2)}) %collective-permute-start.12) | collective-permute-done | bytes 262176 | tf_op jit(solution)/shard_map/ppermute | solution.py:36
  34.7 0.5 %convolution_convert_fusion = bf16[1024,512]{0,1:T(8,128)(2,1)S(1)} fusion(bf16[1024,256]{1,0:T(8,128)(2,1)S(1)} %bitcast.76, bf16[256,256]{1,0:T(8,128)(2,1)S(1)} %copy-done.2, bf16[256,256]{1,0:T(8,128)(2,1)S(1)} %copy-done.3), kind=kOutput, calls=%fused_computation.4 | convolution fusion | flops 269484032 | bytes 1835008 | tf_op jit(solution)/shard_map/dot_general | solution.py:49
  35.2 1.3 %fusion.5 = bf16[4,64,256]{2,1,0:T(8,128)(2,1)S(1)} fusion(bf16[1024,4,64]{0,2,1:T(8,128)(2,1)S(1)} %bitcast.78, bf16[1024,4,64]{0,2,1:T(8,128)(2,1)S(1)} %bitcast.77, bf16[256,4,64]{0,2,1:T(8,128)(2,1)S(1)} %bitcast.84, pred[1024]{0:T(1024)(128)(4,1)S(1)} %fusion.23, f32[]{:T(128)S(6)} %sqrt.3), kind=kOutput, calls=%fused_computation.12 | convolution fusion | flops 273809408 | bytes 1311748 | tf_op jit(solution)/shard_map/bgo,ogl->bgl/dot_general | solution.py:61
  36.6 1.2 %fusion.8 = f32[1,256]{1,0:T(1,128)} fusion(bf16[1024,1]{0,1:T(2,128)(2,1)S(1)} %reshape.132, f32[256,1024]{1,0:T(8,128)S(1)} %fusion.12, bf16[256,256]{0,1:T(8,128)(2,1)S(1)} %bitcast.96, bf16[512,1024]{1,0:T(8,128)(2,1)S(1)} %copy-done.1), kind=kOutput, calls=%fused_computation.14 | convolution fusion | flops 136314880 | bytes 1709056 | tf_op jit(solution)/shard_map/dot_general | solution.py:151
  (47 shorter events, 0.9 us)
Async XLA Ops:
  0.0 29.2 %copy-start = (bf16[256,256]{1,0:T(8,128)(2,1)S(1)}, bf16[256,256]{1,0:T(8,128)(2,1)}, u32[]{:S(2)}) copy-start(bf16[256,256]{1,0:T(8,128)(2,1)} %param.17) | copy-start | bytes 393220
  1.8 6.2 %collective-permute-start = (s32[320]{0:T(512)S(1)}, s32[320]{0:T(512)S(1)}, u32[]{:S(2)}, u32[]{:S(2)}) collective-permute-start(s32[320]{0:T(512)S(1)} %get-tuple-element.5), channel_id=1, source_target_pairs={{0,8},{8,0},{16,24},{24,16},{1,9},{9,1},{17,25},{25,17},{2,10},{10... | collective-permute-start | bytes 3848 | tf_op jit(solution)/shard_map/ppermute | solution.py:77
  4.8 4.5 %collective-permute-start.2 = (s32[320]{0:T(512)S(1)}, s32[320]{0:T(512)S(1)}, u32[]{:S(2)}, u32[]{:S(2)}) collective-permute-start(s32[320]{0:T(512)S(1)} %get-tuple-element.6), channel_id=1, source_target_pairs={{0,24},{8,16},{16,8},{24,0},{1,25},{9,17},{17,9},{25,1},{2,26},{10... | collective-permute-start | bytes 3848 | tf_op jit(solution)/shard_map/ppermute | solution.py:77
  6.3 3.6 %collective-permute-start.1 = (s32[320]{0:T(512)S(1)}, s32[320]{0:T(512)S(1)}, u32[]{:S(2)}, u32[]{:S(2)}) collective-permute-start(s32[320]{0:T(512)S(1)} %get-tuple-element.7), channel_id=1, source_target_pairs={{0,16},{8,24},{16,0},{24,8},{1,17},{9,25},{17,1},{25,9},{2,18},{10... | collective-permute-start | bytes 3848 | tf_op jit(solution)/shard_map/ppermute | solution.py:77
  10.0 18.9 %copy-start.1 = (bf16[512,1024]{1,0:T(8,128)(2,1)S(1)}, bf16[512,1024]{1,0:T(8,128)(2,1)}, u32[]{:S(2)}) copy-start(bf16[512,1024]{1,0:T(8,128)(2,1)} %param.20) | copy-start | bytes 3145732
  15.9 18.7 %copy-start.2 = (bf16[256,256]{1,0:T(8,128)(2,1)S(1)}, bf16[256,256]{1,0:T(8,128)(2,1)}, u32[]{:S(2)}) copy-start(bf16[256,256]{1,0:T(8,128)(2,1)} %param.19) | copy-start | bytes 393220
  15.9 18.7 %copy-start.3 = (bf16[256,256]{1,0:T(8,128)(2,1)S(1)}, bf16[256,256]{1,0:T(8,128)(2,1)}, u32[]{:S(2)}) copy-start(bf16[256,256]{1,0:T(8,128)(2,1)} %param.18) | copy-start | bytes 393220
  16.0 6.6 %collective-permute-start.8 = (bf16[128,256]{1,0:T(8,128)(2,1)S(1)}, bf16[128,256]{1,0:T(8,128)(2,1)S(1)}, u32[]{:S(2)}, u32[]{:S(2)}) collective-permute-start(bf16[128,256]{1,0:T(8,128)(2,1)S(1)} %get-tuple-element.13), channel_id=1, source_target_pairs={{0,24},{8,16},{16,8},{24,0},{1,25},{9,17},{17,9},{25,1},{2,26},{10... | collective-permute-start | bytes 196616 | tf_op jit(solution)/shard_map/ppermute | solution.py:77
  17.5 6.1 %collective-permute-start.7 = (bf16[128,256]{1,0:T(8,128)(2,1)S(1)}, bf16[128,256]{1,0:T(8,128)(2,1)S(1)}, u32[]{:S(2)}, u32[]{:S(2)}) collective-permute-start(bf16[128,256]{1,0:T(8,128)(2,1)S(1)} %get-tuple-element.14), channel_id=1, source_target_pairs={{0,16},{8,24},{16,0},{24,8},{1,17},{9,25},{17,1},{25,9},{2,18},{10... | collective-permute-start | bytes 196616 | tf_op jit(solution)/shard_map/ppermute | solution.py:77
  19.0 4.7 %collective-permute-start.6 = (bf16[128,256]{1,0:T(8,128)(2,1)S(1)}, bf16[128,256]{1,0:T(8,128)(2,1)S(1)}, u32[]{:S(2)}, u32[]{:S(2)}) collective-permute-start(bf16[128,256]{1,0:T(8,128)(2,1)S(1)} %get-tuple-element.15), channel_id=1, source_target_pairs={{0,8},{8,0},{16,24},{24,16},{1,9},{9,1},{17,25},{25,17},{2,10},{10... | collective-permute-start | bytes 196616 | tf_op jit(solution)/shard_map/ppermute | solution.py:77
  19.6 8.3 %collective-permute-start.5 = (bf16[192,256]{1,0:T(8,128)(2,1)S(1)}, bf16[192,256]{1,0:T(8,128)(2,1)S(1)}, u32[]{:S(2)}, u32[]{:S(2)}) collective-permute-start(bf16[192,256]{1,0:T(8,128)(2,1)S(1)} %get-tuple-element.17), channel_id=1, source_target_pairs={{0,24},{8,16},{16,8},{24,0},{1,25},{9,17},{17,9},{25,1},{2,26},{10... | collective-permute-start | bytes 294920 | tf_op jit(solution)/shard_map/ppermute | solution.py:77
  21.1 7.4 %collective-permute-start.4 = (bf16[192,256]{1,0:T(8,128)(2,1)S(1)}, bf16[192,256]{1,0:T(8,128)(2,1)S(1)}, u32[]{:S(2)}, u32[]{:S(2)}) collective-permute-start(bf16[192,256]{1,0:T(8,128)(2,1)S(1)} %get-tuple-element.18), channel_id=1, source_target_pairs={{0,16},{8,24},{16,0},{24,8},{1,17},{9,25},{17,1},{25,9},{2,18},{10... | collective-permute-start | bytes 294920 | tf_op jit(solution)/shard_map/ppermute | solution.py:77
  22.6 5.9 %collective-permute-start.3 = (bf16[192,256]{1,0:T(8,128)(2,1)S(1)}, bf16[192,256]{1,0:T(8,128)(2,1)S(1)}, u32[]{:S(2)}, u32[]{:S(2)}) collective-permute-start(bf16[192,256]{1,0:T(8,128)(2,1)S(1)} %get-tuple-element.19), channel_id=1, source_target_pairs={{0,8},{8,0},{16,24},{24,16},{1,9},{9,1},{17,25},{25,17},{2,10},{10... | collective-permute-start | bytes 294920 | tf_op jit(solution)/shard_map/ppermute | solution.py:77
  23.9 6.2 %collective-permute-start.11 = (bf16[128,256]{1,0:T(8,128)(2,1)S(1)}, bf16[128,256]{1,0:T(8,128)(2,1)S(1)}, u32[]{:S(2)}, u32[]{:S(2)}) collective-permute-start(bf16[128,256]{1,0:T(8,128)(2,1)S(1)} %get-tuple-element.26), channel_id=1, source_target_pairs={{0,6},{1,7},{2,4},{3,5},{4,2},{5,3},{6,0},{7,1},{8,14},{9,15},{10,... | collective-permute-start | bytes 196616 | tf_op jit(solution)/shard_map/ppermute | solution.py:33
  27.8 5.2 %collective-permute-start.10 = (bf16[128,256]{1,0:T(8,128)(2,1)S(1)}, bf16[128,256]{1,0:T(8,128)(2,1)S(1)}, u32[]{:S(2)}, u32[]{:S(2)}) collective-permute-start(bf16[128,256]{1,0:T(8,128)(2,1)S(1)} %get-tuple-element.26), channel_id=1, source_target_pairs={{0,4},{1,5},{2,6},{3,7},{4,0},{5,1},{6,2},{7,3},{8,12},{9,13},{10,... | collective-permute-start | bytes 196616 | tf_op jit(solution)/shard_map/ppermute | solution.py:33
  27.8 5.2 %collective-permute-start.9 = (bf16[128,256]{1,0:T(8,128)(2,1)S(1)}, bf16[128,256]{1,0:T(8,128)(2,1)S(1)}, u32[]{:S(2)}, u32[]{:S(2)}) collective-permute-start(bf16[128,256]{1,0:T(8,128)(2,1)S(1)} %get-tuple-element.26), channel_id=1, source_target_pairs={{0,2},{1,3},{2,0},{3,1},{4,6},{5,7},{6,4},{7,5},{8,10},{9,11},{10,... | collective-permute-start | bytes 196616 | tf_op jit(solution)/shard_map/ppermute | solution.py:33
  33.0 1.6 %collective-permute-start.12 = (bf16[4,128,256]{2,1,0:T(8,128)(2,1)S(1)}, bf16[4,128,256]{2,1,0:T(8,128)(2,1)S(1)}, u32[]{:S(2)}, u32[]{:S(2)}) collective-permute-start(bf16[4,128,256]{2,1,0:T(8,128)(2,1)S(1)} %pad_maximum_fusion.2), channel_id=1, source_target_pairs={{0,1},{1,0},{2,3},{3,2},{4,5},{5,4},{6,7},{7,6},{8,9},{9,8},{10,11... | collective-permute-start | bytes 786440 | tf_op jit(solution)/shard_map/ppermute | solution.py:36

commit v17 on v16

--- a/solution.py
+++ b/solution.py
@@ -32,10 +32,9 @@
     for hop in range(2, n_cand, 2):
         blocks.append(lax.ppermute(rows, "cand", [(i, i ^ hop) for i in range(n_cand)]))
         sources.append(me ^ hop)
-    mine = jnp.stack(blocks, axis=0)
-    partner = lax.ppermute(mine, "cand", [(i, i ^ 1) for i in range(n_cand)])
+    forwarded = [lax.ppermute(block, "cand", [(i, i ^ 1) for i in range(n_cand)]) for block in blocks]
     source = jnp.stack(sources)
-    return (mine, source), (partner, source ^ 1)
+    return (jnp.stack(blocks, axis=0), source), (jnp.stack(forwarded, axis=0), source ^ 1)
 
 
 def logistic(x):

time: 37.9 us -> 37.7 us (level)
  waiting for transfers between devices: 7.1 us -> 6.47 us
  starting transfers between devices: 16.6 us -> 17.1 us
    ppermute x1 -> x4, waiting for transfers between devices: 1.48 us -> 0.86 us  [gather_over_cand(): lax.ppermute(block, 'cand', [(i, i ^ 1) for i in range(n_cand)])]
    ppermute x1 -> x4, starting transfers between devices: 0.07 us -> 0.52 us  [gather_over_cand(): lax.ppermute(block, 'cand', [(i, i ^ 1) for i in range(n_cand)])]
  transfers between devices with their start and end apart: 13 -> 16, of which waited for: 7 -> 7; matrix products, arithmetic and copies ran while one was open for 6% -> 6% of each run, Pallas kernels for 0% -> 0%
where the time goes in v17:
time: 37.7 us; the launch traced here: 37.6 us
  starting transfers between devices  17.1 us (45%)
  local copies, waits for them, and re-layouts  7.08 us (19%)
  waiting for transfers between devices  6.47 us (17%)
  matrix products  4.5 us (12%)
  other arithmetic  1.48 us (4%)
  between operations  0.97 us (3%)
    ppermute x9, starting transfers between devices, swap_over_req(): lax.ppermute(blocks[hop], 'req', [(i, i ^ hop) for i in range(n_req)])  12 us
    gather x1, local copies, waits for them, and re-layouts, body(): jnp.take(table, asked.reshape(-1), axis=0, mode='clip')  5.96 us
    ppermute x3, starting transfers between devices, gather_over_cand(): lax.ppermute(rows, 'cand', [(i, i ^ hop) for i in range(n_cand)])  4.52 us
    ppermute x3, waiting for transfers between devices, gather_over_cand(): lax.ppermute(rows, 'cand', [(i, i ^ hop) for i in range(n_cand)])  3.56 us
    ppermute x9, waiting for transfers between devices, swap_over_req(): lax.ppermute(blocks[hop], 'req', [(i, i ^ hop) for i in range(n_req)])  2.05 us
    dot_general x1, matrix products, attend(): jnp.einsum('bgo,ogl->bgl', gates, values, preferred_element_type=jnp.floa...  1.32 us
    dot_general x1, matrix products, body(): jnp.dot(hidden, tower_out, preferred_element_type=jnp.float32)[None, :]  1.2 us
    ppermute x4, waiting for transfers between devices, gather_over_cand(): lax.ppermute(block, 'cand', [(i, i ^ 1) for i in range(n_cand)])  0.86 us
  transfers between devices with their start and end apart: 16, of which 7 were waited for; matrix products, arithmetic and copies ran while one was open for 6% of the time, Pallas kernels for 0%

profile of v17, /device:TPU:0, one launch (start us, length us, event | category | flops | bytes accessed | tf_op | source)
XLA Modules:
  0.0 37.6 jit_solution(7215698751351016736)
XLA Ops:
  0.0 0.7 %pad_add_fusion.1 = s32[768]{0:T(1024)S(1)} fusion(s32[256]{0:T(256)} %bitcast.96, s32[256]{0:T(256)} %bitcast.97, s32[128]{0:T(128)} %bitcast.98, s32[128]{0:T(128)} %bitcast.99), kind=kLoop, calls=%fused_computation.60 | loop fusion | flops 2304 | bytes 6144 | tf_op jit(solution)/shard_map/concatenate | solution.py:98
  0.8 0.2 convert_reduce_fusion.1
  1.0 0.2 convert_reduce_fusion
  1.2 0.2 convolution_convert_fusion.5
  1.4 0.3 convolution_convert_fusion.4
  1.8 3.0 %collective-permute-start = (s32[320]{0:T(512)S(1)}, s32[320]{0:T(512)S(1)}, u32[]{:S(2)}, u32[]{:S(2)}) collective-permute-start(s32[320]{0:T(512)S(1)} %get-tuple-element.5), channel_id=1, source_target_pairs={{0,8},{8,0},{16,24},{24,16},{1,9},{9,1},{17,25},{25,17},{2,10},{10... | collective-permute-start | bytes 3848 | tf_op jit(solution)/shard_map/ppermute | solution.py:76
  4.8 1.5 %collective-permute-start.2 = (s32[320]{0:T(512)S(1)}, s32[320]{0:T(512)S(1)}, u32[]{:S(2)}, u32[]{:S(2)}) collective-permute-start(s32[320]{0:T(512)S(1)} %get-tuple-element.6), channel_id=1, source_target_pairs={{0,24},{8,16},{16,8},{24,0},{1,25},{9,17},{17,9},{25,1},{2,26},{10... | collective-permute-start | bytes 3848 | tf_op jit(solution)/shard_map/ppermute | solution.py:76
  7.0 0.1 concatenate.38
  7.3 0.7 %reshape.132 = bf16[1024,1]{0,1:T(2,128)(2,1)S(1)} reshape(bf16[1024]{0:T(1024)(128)(2,1)} %param.21) | data formatting | bytes 4096 | tf_op args[10]
  8.0 1.3 %collective-permute-done.2 = s32[320]{0:T(512)S(1)} collective-permute-done((s32[320]{0:T(512)S(1)}, s32[320]{0:T(512)S(1)}, u32[]{:S(2)}, u32[]{:S(2)}) %collective-permute-start.2) | collective-permute-done | bytes 1312 | tf_op jit(solution)/shard_map/ppermute | solution.py:76
  9.3 0.6 %collective-permute-done.1 = s32[320]{0:T(512)S(1)} collective-permute-done((s32[320]{0:T(512)S(1)}, s32[320]{0:T(512)S(1)}, u32[]{:S(2)}, u32[]{:S(2)}) %collective-permute-start.1) | collective-permute-done | bytes 1312 | tf_op jit(solution)/shard_map/ppermute | solution.py:76
  10.0 6.0 %gather_fusion = bf16[1280,256]{1,0:T(8,128)(2,1)S(1)} fusion(bf16[8192,256]{1,0:T(8,128)(2,1)} %param.11, s32[2048]{0:T(1024)S(1)} %pad_clamp_fusion), kind=kCustom, calls=%fused_computation | custom fusion | bytes 1315840 | tf_op jit(solution)/shard_map/jit(_take)/gather | solution.py:117
  16.0 1.5 %collective-permute-start.8 = (bf16[128,256]{1,0:T(8,128)(2,1)S(1)}, bf16[128,256]{1,0:T(8,128)(2,1)S(1)}, u32[]{:S(2)}, u32[]{:S(2)}) collective-permute-start(bf16[128,256]{1,0:T(8,128)(2,1)S(1)} %get-tuple-element.13), channel_id=1, source_target_pairs={{0,24},{8,16},{16,8},{24,0},{1,25},{9,17},{17,9},{25,1},{2,26},{10... | collective-permute-start | bytes 196616 | tf_op jit(solution)/shard_map/ppermute | solution.py:76
  17.5 1.5 %collective-permute-start.7 = (bf16[128,256]{1,0:T(8,128)(2,1)S(1)}, bf16[128,256]{1,0:T(8,128)(2,1)S(1)}, u32[]{:S(2)}, u32[]{:S(2)}) collective-permute-start(bf16[128,256]{1,0:T(8,128)(2,1)S(1)} %get-tuple-element.14), channel_id=1, source_target_pairs={{0,16},{8,24},{16,0},{24,8},{1,17},{9,25},{17,1},{25,9},{2,18},{10... | collective-permute-start | bytes 196616 | tf_op jit(solution)/shard_map/ppermute | solution.py:76
  19.0 0.5 %collective-permute-start.6 = (bf16[128,256]{1,0:T(8,128)(2,1)S(1)}, bf16[128,256]{1,0:T(8,128)(2,1)S(1)}, u32[]{:S(2)}, u32[]{:S(2)}) collective-permute-start(bf16[128,256]{1,0:T(8,128)(2,1)S(1)} %get-tuple-element.15), channel_id=1, source_target_pairs={{0,8},{8,0},{16,24},{24,16},{1,9},{9,1},{17,25},{25,17},{2,10},{10... | collective-permute-start | bytes 196616 | tf_op jit(solution)/shard_map/ppermute | solution.py:76
  19.6 1.5 %collective-permute-start.5 = (bf16[192,256]{1,0:T(8,128)(2,1)S(1)}, bf16[192,256]{1,0:T(8,128)(2,1)S(1)}, u32[]{:S(2)}, u32[]{:S(2)}) collective-permute-start(bf16[192,256]{1,0:T(8,128)(2,1)S(1)} %get-tuple-element.17), channel_id=1, source_target_pairs={{0,24},{8,16},{16,8},{24,0},{1,25},{9,17},{17,9},{25,1},{2,26},{10... | collective-permute-start | bytes 294920 | tf_op jit(solution)/shard_map/ppermute | solution.py:76
  21.1 1.5 %collective-permute-start.4 = (bf16[192,256]{1,0:T(8,128)(2,1)S(1)}, bf16[192,256]{1,0:T(8,128)(2,1)S(1)}, u32[]{:S(2)}, u32[]{:S(2)}) collective-permute-start(bf16[192,256]{1,0:T(8,128)(2,1)S(1)} %get-tuple-element.18), channel_id=1, source_target_pairs={{0,16},{8,24},{16,0},{24,8},{1,17},{9,25},{17,1},{25,9},{2,18},{10... | collective-permute-start | bytes 294920 | tf_op jit(solution)/shard_map/ppermute | solution.py:76
  22.6 0.9 %collective-permute-start.3 = (bf16[192,256]{1,0:T(8,128)(2,1)S(1)}, bf16[192,256]{1,0:T(8,128)(2,1)S(1)}, u32[]{:S(2)}, u32[]{:S(2)}) collective-permute-start(bf16[192,256]{1,0:T(8,128)(2,1)S(1)} %get-tuple-element.19), channel_id=1, source_target_pairs={{0,8},{8,0},{16,24},{24,16},{1,9},{9,1},{17,25},{25,17},{2,10},{10... | collective-permute-start | bytes 294920 | tf_op jit(solution)/shard_map/ppermute | solution.py:76
  23.6 0.1 collective-permute-done.6
  23.7 0.2 bitcast_dynamic-update-slice_fusion.7
  23.9 3.9 %collective-permute-start.11 = (bf16[128,256]{1,0:T(8,128)(2,1)S(1)}, bf16[128,256]{1,0:T(8,128)(2,1)S(1)}, u32[]{:S(2)}, u32[]{:S(2)}) collective-permute-start(bf16[128,256]{1,0:T(8,128)(2,1)S(1)} %get-tuple-element.26), channel_id=1, source_target_pairs={{0,6},{1,7},{2,4},{3,5},{4,2},{5,3},{6,0},{7,1},{8,14},{9,15},{10,... | collective-permute-start | bytes 196616 | tf_op jit(solution)/shard_map/ppermute | solution.py:33
  27.8 0.6 %collective-permute-start.9 = (bf16[128,256]{1,0:T(8,128)(2,1)S(1)}, bf16[128,256]{1,0:T(8,128)(2,1)S(1)}, u32[]{:S(2)}, u32[]{:S(2)}) collective-permute-start(bf16[128,256]{1,0:T(8,128)(2,1)S(1)} %get-tuple-element.26), channel_id=1, source_target_pairs={{0,2},{1,3},{2,0},{3,1},{4,6},{5,7},{6,4},{7,5},{8,10},{9,11},{10,... | collective-permute-start | bytes 196616 | tf_op jit(solution)/shard_map/ppermute | solution.py:33
  28.5 0.3 convolution_convert_fusion.1
  28.9 0.3 fusion.12
  29.2 0.2 convolution_convert_fusion.2
  29.4 0.7 %collective-permute-done.11 = bf16[128,256]{1,0:T(8,128)(2,1)S(1)} collective-permute-done((bf16[128,256]{1,0:T(8,128)(2,1)S(1)}, bf16[128,256]{1,0:T(8,128)(2,1)S(1)}, u32[]{:S(2)}, u32[]{:S(2)}) %collective-permute-start.11) | collective-permute-done | bytes 65568 | tf_op jit(solution)/shard_map/ppermute | solution.py:33
  30.2 2.8 %collective-permute-done.10 = bf16[128,256]{1,0:T(8,128)(2,1)S(1)} collective-permute-done((bf16[128,256]{1,0:T(8,128)(2,1)S(1)}, bf16[128,256]{1,0:T(8,128)(2,1)S(1)}, u32[]{:S(2)}, u32[]{:S(2)}) %collective-permute-start.10) | collective-permute-done | bytes 65568 | tf_op jit(solution)/shard_map/ppermute | solution.py:33
  33.0 0.5 %collective-permute-start.13 = (bf16[128,256]{1,0:T(8,128)(2,1)S(1)}, bf16[128,256]{1,0:T(8,128)(2,1)S(1)}, u32[]{:S(2)}, u32[]{:S(2)}) collective-permute-start(bf16[128,256]{1,0:T(8,128)(2,1)S(1)} %collective-permute-done.9), channel_id=1, source_target_pairs={{0,1},{1,0},{2,3},{3,2},{4,5},{5,4},{6,7},{7,6},{8,9},{9,8},{10,11... | collective-permute-start | bytes 196616 | tf_op jit(solution)/shard_map/ppermute | solution.py:35
  33.6 0.8 %collective-permute-done.13 = bf16[128,256]{1,0:T(8,128)(2,1)S(1)} collective-permute-done((bf16[128,256]{1,0:T(8,128)(2,1)S(1)}, bf16[128,256]{1,0:T(8,128)(2,1)S(1)}, u32[]{:S(2)}, u32[]{:S(2)}) %collective-permute-start.13) | collective-permute-done | bytes 65568 | tf_op jit(solution)/shard_map/ppermute | solution.py:35
  34.5 0.5 %convolution_convert_fusion = bf16[1024,512]{0,1:T(8,128)(2,1)S(1)} fusion(bf16[1024,256]{1,0:T(8,128)(2,1)S(1)} %bitcast.84, bf16[256,256]{1,0:T(8,128)(2,1)S(1)} %copy-done.2, bf16[256,256]{1,0:T(8,128)(2,1)S(1)} %copy-done.3), kind=kOutput, calls=%fused_computation.4 | convolution fusion | flops 269484032 | bytes 1835008 | tf_op jit(solution)/shard_map/dot_general | solution.py:48
  35.0 1.3 %fusion.5 = bf16[4,64,256]{2,1,0:T(8,128)(2,1)S(1)} fusion(bf16[1024,4,64]{0,2,1:T(8,128)(2,1)S(1)} %bitcast.86, bf16[1024,4,64]{0,2,1:T(8,128)(2,1)S(1)} %bitcast.85, bf16[256,4,64]{0,2,1:T(8,128)(2,1)S(1)} %bitcast.88, pred[1024]{0:T(1024)(128)(4,1)S(1)} %fusion.23, f32[]{:T(128)S(6)} %sqrt.3), kind=kOutput, calls=%fused_computation.12 | convolution fusion | flops 273809408 | bytes 1311748 | tf_op jit(solution)/shard_map/bgo,ogl->bgl/dot_general | solution.py:60
  36.4 1.2 %fusion.8 = f32[1,256]{1,0:T(1,128)} fusion(bf16[1024,1]{0,1:T(2,128)(2,1)S(1)} %reshape.132, f32[256,1024]{1,0:T(8,128)S(1)} %fusion.12, bf16[256,256]{0,1:T(8,128)(2,1)S(1)} %bitcast.100, bf16[512,1024]{1,0:T(8,128)(2,1)S(1)} %copy-done.1), kind=kOutput, calls=%fused_computation.14 | convolution fusion | flops 136314880 | bytes 1709056 | tf_op jit(solution)/shard_map/dot_general | solution.py:150
  (55 shorter events, 0.9 us)
Async XLA Ops:
  0.0 29.2 %copy-start = (bf16[256,256]{1,0:T(8,128)(2,1)S(1)}, bf16[256,256]{1,0:T(8,128)(2,1)}, u32[]{:S(2)}) copy-start(bf16[256,256]{1,0:T(8,128)(2,1)} %param.17) | copy-start | bytes 393220
  1.8 6.2 %collective-permute-start = (s32[320]{0:T(512)S(1)}, s32[320]{0:T(512)S(1)}, u32[]{:S(2)}, u32[]{:S(2)}) collective-permute-start(s32[320]{0:T(512)S(1)} %get-tuple-element.5), channel_id=1, source_target_pairs={{0,8},{8,0},{16,24},{24,16},{1,9},{9,1},{17,25},{25,17},{2,10},{10... | collective-permute-start | bytes 3848 | tf_op jit(solution)/shard_map/ppermute | solution.py:76
  4.8 4.5 %collective-permute-start.2 = (s32[320]{0:T(512)S(1)}, s32[320]{0:T(512)S(1)}, u32[]{:S(2)}, u32[]{:S(2)}) collective-permute-start(s32[320]{0:T(512)S(1)} %get-tuple-element.6), channel_id=1, source_target_pairs={{0,24},{8,16},{16,8},{24,0},{1,25},{9,17},{17,9},{25,1},{2,26},{10... | collective-permute-start | bytes 3848 | tf_op jit(solution)/shard_map/ppermute | solution.py:76
  6.3 3.6 %collective-permute-start.1 = (s32[320]{0:T(512)S(1)}, s32[320]{0:T(512)S(1)}, u32[]{:S(2)}, u32[]{:S(2)}) collective-permute-start(s32[320]{0:T(512)S(1)} %get-tuple-element.7), channel_id=1, source_target_pairs={{0,16},{8,24},{16,0},{24,8},{1,17},{9,25},{17,1},{25,9},{2,18},{10... | collective-permute-start | bytes 3848 | tf_op jit(solution)/shard_map/ppermute | solution.py:76
  10.0 18.9 %copy-start.1 = (bf16[512,1024]{1,0:T(8,128)(2,1)S(1)}, bf16[512,1024]{1,0:T(8,128)(2,1)}, u32[]{:S(2)}) copy-start(bf16[512,1024]{1,0:T(8,128)(2,1)} %param.20) | copy-start | bytes 3145732
  15.9 18.5 %copy-start.2 = (bf16[256,256]{1,0:T(8,128)(2,1)S(1)}, bf16[256,256]{1,0:T(8,128)(2,1)}, u32[]{:S(2)}) copy-start(bf16[256,256]{1,0:T(8,128)(2,1)} %param.19) | copy-start | bytes 393220
  15.9 18.5 %copy-start.3 = (bf16[256,256]{1,0:T(8,128)(2,1)S(1)}, bf16[256,256]{1,0:T(8,128)(2,1)}, u32[]{:S(2)}) copy-start(bf16[256,256]{1,0:T(8,128)(2,1)} %param.18) | copy-start | bytes 393220
  16.0 6.6 %collective-permute-start.8 = (bf16[128,256]{1,0:T(8,128)(2,1)S(1)}, bf16[128,256]{1,0:T(8,128)(2,1)S(1)}, u32[]{:S(2)}, u32[]{:S(2)}) collective-permute-start(bf16[128,256]{1,0:T(8,128)(2,1)S(1)} %get-tuple-element.13), channel_id=1, source_target_pairs={{0,24},{8,16},{16,8},{24,0},{1,25},{9,17},{17,9},{25,1},{2,26},{10... | collective-permute-start | bytes 196616 | tf_op jit(solution)/shard_map/ppermute | solution.py:76
  17.5 6.1 %collective-permute-start.7 = (bf16[128,256]{1,0:T(8,128)(2,1)S(1)}, bf16[128,256]{1,0:T(8,128)(2,1)S(1)}, u32[]{:S(2)}, u32[]{:S(2)}) collective-permute-start(bf16[128,256]{1,0:T(8,128)(2,1)S(1)} %get-tuple-element.14), channel_id=1, source_target_pairs={{0,16},{8,24},{16,0},{24,8},{1,17},{9,25},{17,1},{25,9},{2,18},{10... | collective-permute-start | bytes 196616 | tf_op jit(solution)/shard_map/ppermute | solution.py:76
  19.0 4.7 %collective-permute-start.6 = (bf16[128,256]{1,0:T(8,128)(2,1)S(1)}, bf16[128,256]{1,0:T(8,128)(2,1)S(1)}, u32[]{:S(2)}, u32[]{:S(2)}) collective-permute-start(bf16[128,256]{1,0:T(8,128)(2,1)S(1)} %get-tuple-element.15), channel_id=1, source_target_pairs={{0,8},{8,0},{16,24},{24,16},{1,9},{9,1},{17,25},{25,17},{2,10},{10... | collective-permute-start | bytes 196616 | tf_op jit(solution)/shard_map/ppermute | solution.py:76
  19.6 8.3 %collective-permute-start.5 = (bf16[192,256]{1,0:T(8,128)(2,1)S(1)}, bf16[192,256]{1,0:T(8,128)(2,1)S(1)}, u32[]{:S(2)}, u32[]{:S(2)}) collective-permute-start(bf16[192,256]{1,0:T(8,128)(2,1)S(1)} %get-tuple-element.17), channel_id=1, source_target_pairs={{0,24},{8,16},{16,8},{24,0},{1,25},{9,17},{17,9},{25,1},{2,26},{10... | collective-permute-start | bytes 294920 | tf_op jit(solution)/shard_map/ppermute | solution.py:76
  21.1 7.4 %collective-permute-start.4 = (bf16[192,256]{1,0:T(8,128)(2,1)S(1)}, bf16[192,256]{1,0:T(8,128)(2,1)S(1)}, u32[]{:S(2)}, u32[]{:S(2)}) collective-permute-start(bf16[192,256]{1,0:T(8,128)(2,1)S(1)} %get-tuple-element.18), channel_id=1, source_target_pairs={{0,16},{8,24},{16,0},{24,8},{1,17},{9,25},{17,1},{25,9},{2,18},{10... | collective-permute-start | bytes 294920 | tf_op jit(solution)/shard_map/ppermute | solution.py:76
  22.6 5.9 %collective-permute-start.3 = (bf16[192,256]{1,0:T(8,128)(2,1)S(1)}, bf16[192,256]{1,0:T(8,128)(2,1)S(1)}, u32[]{:S(2)}, u32[]{:S(2)}) collective-permute-start(bf16[192,256]{1,0:T(8,128)(2,1)S(1)} %get-tuple-element.19), channel_id=1, source_target_pairs={{0,8},{8,0},{16,24},{24,16},{1,9},{9,1},{17,25},{25,17},{2,10},{10... | collective-permute-start | bytes 294920 | tf_op jit(solution)/shard_map/ppermute | solution.py:76
  23.9 6.2 %collective-permute-start.11 = (bf16[128,256]{1,0:T(8,128)(2,1)S(1)}, bf16[128,256]{1,0:T(8,128)(2,1)S(1)}, u32[]{:S(2)}, u32[]{:S(2)}) collective-permute-start(bf16[128,256]{1,0:T(8,128)(2,1)S(1)} %get-tuple-element.26), channel_id=1, source_target_pairs={{0,6},{1,7},{2,4},{3,5},{4,2},{5,3},{6,0},{7,1},{8,14},{9,15},{10,... | collective-permute-start | bytes 196616 | tf_op jit(solution)/shard_map/ppermute | solution.py:33
  27.8 5.2 %collective-permute-start.10 = (bf16[128,256]{1,0:T(8,128)(2,1)S(1)}, bf16[128,256]{1,0:T(8,128)(2,1)S(1)}, u32[]{:S(2)}, u32[]{:S(2)}) collective-permute-start(bf16[128,256]{1,0:T(8,128)(2,1)S(1)} %get-tuple-element.26), channel_id=1, source_target_pairs={{0,4},{1,5},{2,6},{3,7},{4,0},{5,1},{6,2},{7,3},{8,12},{9,13},{10,... | collective-permute-start | bytes 196616 | tf_op jit(solution)/shard_map/ppermute | solution.py:33
  27.8 5.2 %collective-permute-start.9 = (bf16[128,256]{1,0:T(8,128)(2,1)S(1)}, bf16[128,256]{1,0:T(8,128)(2,1)S(1)}, u32[]{:S(2)}, u32[]{:S(2)}) collective-permute-start(bf16[128,256]{1,0:T(8,128)(2,1)S(1)} %get-tuple-element.26), channel_id=1, source_target_pairs={{0,2},{1,3},{2,0},{3,1},{4,6},{5,7},{6,4},{7,5},{8,10},{9,11},{10,... | collective-permute-start | bytes 196616 | tf_op jit(solution)/shard_map/ppermute | solution.py:33
  28.5 5.1 %collective-permute-start.12 = (bf16[128,256]{1,0:T(8,128)(2,1)S(1)}, bf16[128,256]{1,0:T(8,128)(2,1)S(1)}, u32[]{:S(2)}, u32[]{:S(2)}) collective-permute-start(bf16[128,256]{1,0:T(8,128)(2,1)S(1)} %get-tuple-element.26), channel_id=1, source_target_pairs={{0,1},{1,0},{2,3},{3,2},{4,5},{5,4},{6,7},{7,6},{8,9},{9,8},{10,11... | collective-permute-start | bytes 196616 | tf_op jit(solution)/shard_map/ppermute | solution.py:35
  30.2 4.3 %collective-permute-start.15 = (bf16[128,256]{1,0:T(8,128)(2,1)S(1)}, bf16[128,256]{1,0:T(8,128)(2,1)S(1)}, u32[]{:S(2)}, u32[]{:S(2)}) collective-permute-start(bf16[128,256]{1,0:T(8,128)(2,1)S(1)} %collective-permute-done.11), channel_id=1, source_target_pairs={{0,1},{1,0},{2,3},{3,2},{4,5},{5,4},{6,7},{7,6},{8,9},{9,8},{10,11... | collective-permute-start | bytes 196616 | tf_op jit(solution)/shard_map/ppermute | solution.py:35
  33.0 1.4 %collective-permute-start.14 = (bf16[128,256]{1,0:T(8,128)(2,1)S(1)}, bf16[128,256]{1,0:T(8,128)(2,1)S(1)}, u32[]{:S(2)}, u32[]{:S(2)}) collective-permute-start(bf16[128,256]{1,0:T(8,128)(2,1)S(1)} %collective-permute-done.10), channel_id=1, source_target_pairs={{0,1},{1,0},{2,3},{3,2},{4,5},{5,4},{6,7},{7,6},{8,9},{9,8},{10,11... | collective-permute-start | bytes 196616 | tf_op jit(solution)/shard_map/ppermute | solution.py:35
  33.0 1.4 %collective-permute-start.13 = (bf16[128,256]{1,0:T(8,128)(2,1)S(1)}, bf16[128,256]{1,0:T(8,128)(2,1)S(1)}, u32[]{:S(2)}, u32[]{:S(2)}) collective-permute-start(bf16[128,256]{1,0:T(8,128)(2,1)S(1)} %collective-permute-done.9), channel_id=1, source_target_pairs={{0,1},{1,0},{2,3},{3,2},{4,5},{5,4},{6,7},{7,6},{8,9},{9,8},{10,11... | collective-permute-start | bytes 196616 | tf_op jit(solution)/shard_map/ppermute | solution.py:35

commit v18 on v17

--- a/solution.py
+++ b/solution.py
@@ -118,8 +118,9 @@
         n_dest, hist_cap + cand_cap, d_model
     )
     hist_replies = swap_over_req(fetched[:, :hist_cap]).reshape(n_dest * hist_cap, d_model)
-    cand_replies = swap_over_req(fetched[:, hist_cap:]).reshape(n_dest * cand_cap, d_model)
     hist_emb = jnp.dot(hist_pick, hist_replies, preferred_element_type=jnp.float32).astype(jnp.bfloat16)
+    cand_sent, hist_emb = lax.optimization_barrier((fetched[:, hist_cap:], hist_emb))
+    cand_replies = swap_over_req(cand_sent).reshape(n_dest * cand_cap, d_model)
     cand_emb = jnp.dot(cand_pick, cand_replies, preferred_element_type=jnp.float32).astype(jnp.bfloat16)
     head_size = d_model // HEADS
     scale_factor = 1.0 / math.sqrt(head_size)

time: 37.7 us -> 41.6 us (1.10)
  waiting for transfers between devices: 6.47 us -> 12.2 us
  starting transfers between devices: 17.1 us -> 15.8 us
  local copies, waits for them, and re-layouts: 7.08 us -> 6.44 us
    ppermute x9, waiting for transfers between devices: 2.05 us -> 9.18 us  [swap_over_req(): lax.ppermute(blocks[hop], 'req', [(i, i ^ hop) for i in range(n_req)])]
    ppermute x9, starting transfers between devices: 12 us -> 10.6 us  [swap_over_req(): lax.ppermute(blocks[hop], 'req', [(i, i ^ hop) for i in range(n_req)])]
    ppermute x4, waiting for transfers between devices: 0.86 us -> 0.01 us  [gather_over_cand(): lax.ppermute(block, 'cand', [(i, i ^ 1) for i in range(n_cand)])]
    unnamed x15 -> x18, local copies, waits for them, and re-layouts: 0.75 us -> 0.07 us
    ppermute x3, waiting for transfers between devices: 3.56 us -> 3.02 us  [gather_over_cand(): lax.ppermute(rows, 'cand', [(i, i ^ hop) for i in range(n_cand)])]
  transfers between devices with their start and end apart: 16 -> 16, of which waited for: 7 -> 8; matrix products, arithmetic and copies ran while one was open for 6% -> 3% of each run, Pallas kernels for 0% -> 0%
where the time goes in v18:
time: 41.6 us; the launch traced here: 41.4 us
  starting transfers between devices  15.8 us (38%)
  waiting for transfers between devices  12.2 us (29%)
  local copies, waits for them, and re-layouts  6.44 us (15%)
  matrix products  4.5 us (11%)
  other arithmetic  1.48 us (4%)
  between operations  1.03 us (2%)
    ppermute x9, starting transfers between devices, swap_over_req(): lax.ppermute(blocks[hop], 'req', [(i, i ^ hop) for i in range(n_req)])  10.6 us
    ppermute x9, waiting for transfers between devices, swap_over_req(): lax.ppermute(blocks[hop], 'req', [(i, i ^ hop) for i in range(n_req)])  9.18 us
    gather x1, local copies, waits for them, and re-layouts, body(): jnp.take(table, asked.reshape(-1), axis=0, mode='clip')  5.96 us
    ppermute x3, starting transfers between devices, gather_over_cand(): lax.ppermute(rows, 'cand', [(i, i ^ hop) for i in range(n_cand)])  4.45 us
    ppermute x3, waiting for transfers between devices, gather_over_cand(): lax.ppermute(rows, 'cand', [(i, i ^ hop) for i in range(n_cand)])  3.02 us
    dot_general x1, matrix products, attend(): jnp.einsum('bgo,ogl->bgl', gates, values, preferred_element_type=jnp.floa...  1.32 us
    dot_general x1, matrix products, body(): jnp.dot(hidden, tower_out, preferred_element_type=jnp.float32)[None, :]  1.2 us
  transfers between devices with their start and end apart: 16, of which 8 were waited for; matrix products, arithmetic and copies ran while one was open for 3% of the time, Pallas kernels for 0%

profile of v18, /device:TPU:0, one launch (start us, length us, event | category | flops | bytes accessed | tf_op | source)
XLA Modules:
  0.0 41.4 jit_solution(10663141385494202279)
XLA Ops:
  0.0 0.8 %pad_add_fusion.1 = s32[768]{0:T(1024)S(1)} fusion(s32[256]{0:T(256)} %bitcast.96, s32[256]{0:T(256)} %bitcast.97, s32[128]{0:T(128)} %bitcast.98, s32[128]{0:T(128)} %bitcast.99), kind=kLoop, calls=%fused_computation.60 | loop fusion | flops 2304 | bytes 6144 | tf_op jit(solution)/shard_map/concatenate | solution.py:98
  0.8 0.2 convert_reduce_fusion.1
  1.0 0.2 convert_reduce_fusion
  1.2 0.2 convolution_convert_fusion.5
  1.4 0.3 convolution_convert_fusion.4
  1.8 3.0 %collective-permute-start = (s32[320]{0:T(512)S(1)}, s32[320]{0:T(512)S(1)}, u32[]{:S(2)}, u32[]{:S(2)}) collective-permute-start(s32[320]{0:T(512)S(1)} %get-tuple-element.9), channel_id=1, source_target_pairs={{0,8},{8,0},{16,24},{24,16},{1,9},{9,1},{17,25},{25,17},{2,10},{10... | collective-permute-start | bytes 3848 | tf_op jit(solution)/shard_map/ppermute | solution.py:76
  4.8 1.5 %collective-permute-start.2 = (s32[320]{0:T(512)S(1)}, s32[320]{0:T(512)S(1)}, u32[]{:S(2)}, u32[]{:S(2)}) collective-permute-start(s32[320]{0:T(512)S(1)} %get-tuple-element.10), channel_id=1, source_target_pairs={{0,24},{8,16},{16,8},{24,0},{1,25},{9,17},{17,9},{25,1},{2,26},{10... | collective-permute-start | bytes 3848 | tf_op jit(solution)/shard_map/ppermute | solution.py:76
  7.2 2.1 %collective-permute-done.2 = s32[320]{0:T(512)S(1)} collective-permute-done((s32[320]{0:T(512)S(1)}, s32[320]{0:T(512)S(1)}, u32[]{:S(2)}, u32[]{:S(2)}) %collective-permute-start.2) | collective-permute-done | bytes 1312 | tf_op jit(solution)/shard_map/ppermute | solution.py:76
  9.3 0.6 %collective-permute-done.1 = s32[320]{0:T(512)S(1)} collective-permute-done((s32[320]{0:T(512)S(1)}, s32[320]{0:T(512)S(1)}, u32[]{:S(2)}, u32[]{:S(2)}) %collective-permute-start.1) | collective-permute-done | bytes 1312 | tf_op jit(solution)/shard_map/ppermute | solution.py:76
  10.0 6.0 %gather_fusion = bf16[1280,256]{1,0:T(8,128)(2,1)S(1)} fusion(bf16[8192,256]{1,0:T(8,128)(2,1)} %param.11, s32[2048]{0:T(1024)S(1)} %pad_clamp_fusion), kind=kCustom, calls=%fused_computation | custom fusion | bytes 1315840 | tf_op jit(solution)/shard_map/jit(_take)/gather | solution.py:117
  16.0 1.5 %collective-permute-start.5 = (bf16[128,256]{1,0:T(8,128)(2,1)S(1)}, bf16[128,256]{1,0:T(8,128)(2,1)S(1)}, u32[]{:S(2)}, u32[]{:S(2)}) collective-permute-start(bf16[128,256]{1,0:T(8,128)(2,1)S(1)} %get-tuple-element.17), channel_id=1, source_target_pairs={{0,24},{8,16},{16,8},{24,0},{1,25},{9,17},{17,9},{25,1},{2,26},{10... | collective-permute-start | bytes 196616 | tf_op jit(solution)/shard_map/ppermute | solution.py:76
  17.5 1.5 %collective-permute-start.4 = (bf16[128,256]{1,0:T(8,128)(2,1)S(1)}, bf16[128,256]{1,0:T(8,128)(2,1)S(1)}, u32[]{:S(2)}, u32[]{:S(2)}) collective-permute-start(bf16[128,256]{1,0:T(8,128)(2,1)S(1)} %get-tuple-element.18), channel_id=1, source_target_pairs={{0,16},{8,24},{16,0},{24,8},{1,17},{9,25},{17,1},{25,9},{2,18},{10... | collective-permute-start | bytes 196616 | tf_op jit(solution)/shard_map/ppermute | solution.py:76
  19.0 0.5 %collective-permute-start.3 = (bf16[128,256]{1,0:T(8,128)(2,1)S(1)}, bf16[128,256]{1,0:T(8,128)(2,1)S(1)}, u32[]{:S(2)}, u32[]{:S(2)}) collective-permute-start(bf16[128,256]{1,0:T(8,128)(2,1)S(1)} %get-tuple-element.19), channel_id=1, source_target_pairs={{0,8},{8,0},{16,24},{24,16},{1,9},{9,1},{17,25},{25,17},{2,10},{10... | collective-permute-start | bytes 196616 | tf_op jit(solution)/shard_map/ppermute | solution.py:76
  19.7 1.5 %collective-permute-done.5 = bf16[128,256]{1,0:T(8,128)(2,1)S(1)} collective-permute-done((bf16[128,256]{1,0:T(8,128)(2,1)S(1)}, bf16[128,256]{1,0:T(8,128)(2,1)S(1)}, u32[]{:S(2)}, u32[]{:S(2)}) %collective-permute-start.5) | collective-permute-done | bytes 65568 | tf_op jit(solution)/shard_map/ppermute | solution.py:76
  21.2 0.7 %collective-permute-done.4 = bf16[128,256]{1,0:T(8,128)(2,1)S(1)} collective-permute-done((bf16[128,256]{1,0:T(8,128)(2,1)S(1)}, bf16[128,256]{1,0:T(8,128)(2,1)S(1)}, u32[]{:S(2)}, u32[]{:S(2)}) %collective-permute-start.4) | collective-permute-done | bytes 65568 | tf_op jit(solution)/shard_map/ppermute | solution.py:76
  21.9 1.4 %collective-permute-done.3 = bf16[128,256]{1,0:T(8,128)(2,1)S(1)} collective-permute-done((bf16[128,256]{1,0:T(8,128)(2,1)S(1)}, bf16[128,256]{1,0:T(8,128)(2,1)S(1)}, u32[]{:S(2)}, u32[]{:S(2)}) %collective-permute-start.3) | collective-permute-done | bytes 65568 | tf_op jit(solution)/shard_map/ppermute | solution.py:76
  23.3 0.2 convolution_convert_fusion.3
  23.6 3.7 %collective-permute-start.11 = (bf16[128,256]{1,0:T(8,128)(2,1)S(1)}, bf16[128,256]{1,0:T(8,128)(2,1)S(1)}, u32[]{:S(2)}, u32[]{:S(2)}) collective-permute-start(bf16[128,256]{1,0:T(8,128)(2,1)S(1)} %convolution_convert_fusion.3), channel_id=1, source_target_pairs={{0,6},{1,7},{2,4},{3,5},{4,2},{5,3},{6,0},{7,1},{8,14},{9,15},{10,... | collective-permute-start | bytes 196616 | tf_op jit(solution)/shard_map/ppermute | solution.py:33
  27.3 0.8 %collective-permute-start.9 = (bf16[128,256]{1,0:T(8,128)(2,1)S(1)}, bf16[128,256]{1,0:T(8,128)(2,1)S(1)}, u32[]{:S(2)}, u32[]{:S(2)}) collective-permute-start(bf16[128,256]{1,0:T(8,128)(2,1)S(1)} %convolution_convert_fusion.3), channel_id=1, source_target_pairs={{0,2},{1,3},{2,0},{3,1},{4,6},{5,7},{6,4},{7,5},{8,10},{9,11},{10,... | collective-permute-start | bytes 196616 | tf_op jit(solution)/shard_map/ppermute | solution.py:33
  28.1 1.0 %collective-permute-start.8 = (bf16[192,256]{1,0:T(8,128)(2,1)S(1)}, bf16[192,256]{1,0:T(8,128)(2,1)S(1)}, u32[]{:S(2)}, u32[]{:S(2)}) collective-permute-start(bf16[192,256]{1,0:T(8,128)(2,1)S(1)} %get-tuple-element.21), channel_id=1, source_target_pairs={{0,24},{8,16},{16,8},{24,0},{1,25},{9,17},{17,9},{25,1},{2,26},{10... | collective-permute-start | bytes 294920 | tf_op jit(solution)/shard_map/ppermute | solution.py:76
  29.1 3.0 %collective-permute-done.9 = bf16[128,256]{1,0:T(8,128)(2,1)S(1)} collective-permute-done((bf16[128,256]{1,0:T(8,128)(2,1)S(1)}, bf16[128,256]{1,0:T(8,128)(2,1)S(1)}, u32[]{:S(2)}, u32[]{:S(2)}) %collective-permute-start.9) | collective-permute-done | bytes 65568 | tf_op jit(solution)/shard_map/ppermute | solution.py:33
  32.1 0.5 %collective-permute-start.7 = (bf16[192,256]{1,0:T(8,128)(2,1)S(1)}, bf16[192,256]{1,0:T(8,128)(2,1)S(1)}, u32[]{:S(2)}, u32[]{:S(2)}) collective-permute-start(bf16[192,256]{1,0:T(8,128)(2,1)S(1)} %get-tuple-element.22), channel_id=1, source_target_pairs={{0,16},{8,24},{16,0},{24,8},{1,17},{9,25},{17,1},{25,9},{2,18},{10... | collective-permute-start | bytes 294920 | tf_op jit(solution)/shard_map/ppermute | solution.py:76
  32.6 1.0 %collective-permute-start.6 = (bf16[192,256]{1,0:T(8,128)(2,1)S(1)}, bf16[192,256]{1,0:T(8,128)(2,1)S(1)}, u32[]{:S(2)}, u32[]{:S(2)}) collective-permute-start(bf16[192,256]{1,0:T(8,128)(2,1)S(1)} %get-tuple-element.23), channel_id=1, source_target_pairs={{0,8},{8,0},{16,24},{24,16},{1,9},{9,1},{17,25},{25,17},{2,10},{10... | collective-permute-start | bytes 294920 | tf_op jit(solution)/shard_map/ppermute | solution.py:76
  33.7 0.6 %collective-permute-start.14 = (bf16[128,256]{1,0:T(8,128)(2,1)S(1)}, bf16[128,256]{1,0:T(8,128)(2,1)S(1)}, u32[]{:S(2)}, u32[]{:S(2)}) collective-permute-start(bf16[128,256]{1,0:T(8,128)(2,1)S(1)} %collective-permute-done.10), channel_id=1, source_target_pairs={{0,1},{1,0},{2,3},{3,2},{4,5},{5,4},{6,7},{7,6},{8,9},{9,8},{10,11... | collective-permute-start | bytes 196616 | tf_op jit(solution)/shard_map/ppermute | solution.py:35
  34.4 2.4 %collective-permute-done.7 = bf16[192,256]{1,0:T(8,128)(2,1)S(1)} collective-permute-done((bf16[192,256]{1,0:T(8,128)(2,1)S(1)}, bf16[192,256]{1,0:T(8,128)(2,1)S(1)}, u32[]{:S(2)}, u32[]{:S(2)}) %collective-permute-start.7) | collective-permute-done | bytes 98336 | tf_op jit(solution)/shard_map/ppermute | solution.py:76
  36.7 0.6 %collective-permute-done.6 = bf16[192,256]{1,0:T(8,128)(2,1)S(1)} collective-permute-done((bf16[192,256]{1,0:T(8,128)(2,1)S(1)}, bf16[192,256]{1,0:T(8,128)(2,1)S(1)}, u32[]{:S(2)}, u32[]{:S(2)}) %collective-permute-start.6) | collective-permute-done | bytes 98336 | tf_op jit(solution)/shard_map/ppermute | solution.py:76
  37.4 0.3 convolution_convert_fusion.1
  37.7 0.3 fusion.12
  38.0 0.2 convolution_convert_fusion.2
  38.4 0.5 %convolution_convert_fusion = bf16[1024,512]{0,1:T(8,128)(2,1)S(1)} fusion(bf16[1024,256]{1,0:T(8,128)(2,1)S(1)} %bitcast.84, bf16[256,256]{1,0:T(8,128)(2,1)S(1)} %copy-done.2, bf16[256,256]{1,0:T(8,128)(2,1)S(1)} %copy-done.3), kind=kOutput, calls=%fused_computation.4 | convolution fusion | flops 269484032 | bytes 1835008 | tf_op jit(solution)/shard_map/dot_general | solution.py:48
  38.9 1.3 %fusion.5 = bf16[4,64,256]{2,1,0:T(8,128)(2,1)S(1)} fusion(bf16[1024,4,64]{0,2,1:T(8,128)(2,1)S(1)} %bitcast.86, bf16[1024,4,64]{0,2,1:T(8,128)(2,1)S(1)} %bitcast.85, bf16[256,4,64]{0,2,1:T(8,128)(2,1)S(1)} %bitcast.88, pred[1024]{0:T(1024)(128)(4,1)S(1)} %fusion.23, f32[]{:T(128)S(6)} %sqrt.3), kind=kOutput, calls=%fused_computation.12 | convolution fusion | flops 273809408 | bytes 1311748 | tf_op jit(solution)/shard_map/bgo,ogl->bgl/dot_general | solution.py:60
  40.2 1.2 %fusion.8 = f32[1,256]{1,0:T(1,128)} fusion(bf16[1024,1]{0,1:T(2,128)(2,1)S(1)} %reshape.132, f32[256,1024]{1,0:T(8,128)S(1)} %fusion.12, bf16[256,256]{0,1:T(8,128)(2,1)S(1)} %bitcast.100, bf16[512,1024]{1,0:T(8,128)(2,1)S(1)} %copy-done.1), kind=kOutput, calls=%fused_computation.14 | convolution fusion | flops 136314880 | bytes 1709056 | tf_op jit(solution)/shard_map/dot_general | solution.py:151
  (59 shorter events, 1.1 us)
Async XLA Ops:
  0.0 38.0 %copy-start = (bf16[256,256]{1,0:T(8,128)(2,1)S(1)}, bf16[256,256]{1,0:T(8,128)(2,1)}, u32[]{:S(2)}) copy-start(bf16[256,256]{1,0:T(8,128)(2,1)} %param.17) | copy-start | bytes 393220
  0.0 19.7 %copy-start.4 = (bf16[1024]{0:T(1024)(128)(2,1)S(1)}, bf16[1024]{0:T(1024)(128)(2,1)}, u32[]{:S(2)}) copy-start(bf16[1024]{0:T(1024)(128)(2,1)} %param.21) | copy-start | bytes 6148
  1.8 5.4 %collective-permute-start = (s32[320]{0:T(512)S(1)}, s32[320]{0:T(512)S(1)}, u32[]{:S(2)}, u32[]{:S(2)}) collective-permute-start(s32[320]{0:T(512)S(1)} %get-tuple-element.9), channel_id=1, source_target_pairs={{0,8},{8,0},{16,24},{24,16},{1,9},{9,1},{17,25},{25,17},{2,10},{10... | collective-permute-start | bytes 3848 | tf_op jit(solution)/shard_map/ppermute | solution.py:76
  4.8 4.5 %collective-permute-start.2 = (s32[320]{0:T(512)S(1)}, s32[320]{0:T(512)S(1)}, u32[]{:S(2)}, u32[]{:S(2)}) collective-permute-start(s32[320]{0:T(512)S(1)} %get-tuple-element.10), channel_id=1, source_target_pairs={{0,24},{8,16},{16,8},{24,0},{1,25},{9,17},{17,9},{25,1},{2,26},{10... | collective-permute-start | bytes 3848 | tf_op jit(solution)/shard_map/ppermute | solution.py:76
  6.3 3.6 %collective-permute-start.1 = (s32[320]{0:T(512)S(1)}, s32[320]{0:T(512)S(1)}, u32[]{:S(2)}, u32[]{:S(2)}) collective-permute-start(s32[320]{0:T(512)S(1)} %get-tuple-element.11), channel_id=1, source_target_pairs={{0,16},{8,24},{16,0},{24,8},{1,17},{9,25},{17,1},{25,9},{2,18},{10... | collective-permute-start | bytes 3848 | tf_op jit(solution)/shard_map/ppermute | solution.py:76
  10.0 27.7 %copy-start.1 = (bf16[512,1024]{1,0:T(8,128)(2,1)S(1)}, bf16[512,1024]{1,0:T(8,128)(2,1)}, u32[]{:S(2)}) copy-start(bf16[512,1024]{1,0:T(8,128)(2,1)} %param.20) | copy-start | bytes 3145732
  15.9 22.4 %copy-start.2 = (bf16[256,256]{1,0:T(8,128)(2,1)S(1)}, bf16[256,256]{1,0:T(8,128)(2,1)}, u32[]{:S(2)}) copy-start(bf16[256,256]{1,0:T(8,128)(2,1)} %param.19) | copy-start | bytes 393220
  16.0 22.4 %copy-start.3 = (bf16[256,256]{1,0:T(8,128)(2,1)S(1)}, bf16[256,256]{1,0:T(8,128)(2,1)}, u32[]{:S(2)}) copy-start(bf16[256,256]{1,0:T(8,128)(2,1)} %param.18) | copy-start | bytes 393220
  16.0 5.2 %collective-permute-start.5 = (bf16[128,256]{1,0:T(8,128)(2,1)S(1)}, bf16[128,256]{1,0:T(8,128)(2,1)S(1)}, u32[]{:S(2)}, u32[]{:S(2)}) collective-permute-start(bf16[128,256]{1,0:T(8,128)(2,1)S(1)} %get-tuple-element.17), channel_id=1, source_target_pairs={{0,24},{8,16},{16,8},{24,0},{1,25},{9,17},{17,9},{25,1},{2,26},{10... | collective-permute-start | bytes 196616 | tf_op jit(solution)/shard_map/ppermute | solution.py:76
  17.5 4.4 %collective-permute-start.4 = (bf16[128,256]{1,0:T(8,128)(2,1)S(1)}, bf16[128,256]{1,0:T(8,128)(2,1)S(1)}, u32[]{:S(2)}, u32[]{:S(2)}) collective-permute-start(bf16[128,256]{1,0:T(8,128)(2,1)S(1)} %get-tuple-element.18), channel_id=1, source_target_pairs={{0,16},{8,24},{16,0},{24,8},{1,17},{9,25},{17,1},{25,9},{2,18},{10... | collective-permute-start | bytes 196616 | tf_op jit(solution)/shard_map/ppermute | solution.py:76
  19.0 4.3 %collective-permute-start.3 = (bf16[128,256]{1,0:T(8,128)(2,1)S(1)}, bf16[128,256]{1,0:T(8,128)(2,1)S(1)}, u32[]{:S(2)}, u32[]{:S(2)}) collective-permute-start(bf16[128,256]{1,0:T(8,128)(2,1)S(1)} %get-tuple-element.19), channel_id=1, source_target_pairs={{0,8},{8,0},{16,24},{24,16},{1,9},{9,1},{17,25},{25,17},{2,10},{10... | collective-permute-start | bytes 196616 | tf_op jit(solution)/shard_map/ppermute | solution.py:76
  23.6 10.1 %collective-permute-start.12 = (bf16[128,256]{1,0:T(8,128)(2,1)S(1)}, bf16[128,256]{1,0:T(8,128)(2,1)S(1)}, u32[]{:S(2)}, u32[]{:S(2)}) collective-permute-start(bf16[128,256]{1,0:T(8,128)(2,1)S(1)} %convolution_convert_fusion.3), channel_id=1, source_target_pairs={{0,1},{1,0},{2,3},{3,2},{4,5},{5,4},{6,7},{7,6},{8,9},{9,8},{10,11... | collective-permute-start | bytes 196616 | tf_op jit(solution)/shard_map/ppermute | solution.py:35
  23.6 9.0 %collective-permute-start.11 = (bf16[128,256]{1,0:T(8,128)(2,1)S(1)}, bf16[128,256]{1,0:T(8,128)(2,1)S(1)}, u32[]{:S(2)}, u32[]{:S(2)}) collective-permute-start(bf16[128,256]{1,0:T(8,128)(2,1)S(1)} %convolution_convert_fusion.3), channel_id=1, source_target_pairs={{0,6},{1,7},{2,4},{3,5},{4,2},{5,3},{6,0},{7,1},{8,14},{9,15},{10,... | collective-permute-start | bytes 196616 | tf_op jit(solution)/shard_map/ppermute | solution.py:33
  27.3 6.4 %collective-permute-start.10 = (bf16[128,256]{1,0:T(8,128)(2,1)S(1)}, bf16[128,256]{1,0:T(8,128)(2,1)S(1)}, u32[]{:S(2)}, u32[]{:S(2)}) collective-permute-start(bf16[128,256]{1,0:T(8,128)(2,1)S(1)} %convolution_convert_fusion.3), channel_id=1, source_target_pairs={{0,4},{1,5},{2,6},{3,7},{4,0},{5,1},{6,2},{7,3},{8,12},{9,13},{10,... | collective-permute-start | bytes 196616 | tf_op jit(solution)/shard_map/ppermute | solution.py:33
  27.3 4.8 %collective-permute-start.9 = (bf16[128,256]{1,0:T(8,128)(2,1)S(1)}, bf16[128,256]{1,0:T(8,128)(2,1)S(1)}, u32[]{:S(2)}, u32[]{:S(2)}) collective-permute-start(bf16[128,256]{1,0:T(8,128)(2,1)S(1)} %convolution_convert_fusion.3), channel_id=1, source_target_pairs={{0,2},{1,3},{2,0},{3,1},{4,6},{5,7},{6,4},{7,5},{8,10},{9,11},{10,... | collective-permute-start | bytes 196616 | tf_op jit(solution)/shard_map/ppermute | solution.py:33
  28.1 6.2 %collective-permute-start.8 = (bf16[192,256]{1,0:T(8,128)(2,1)S(1)}, bf16[192,256]{1,0:T(8,128)(2,1)S(1)}, u32[]{:S(2)}, u32[]{:S(2)}) collective-permute-start(bf16[192,256]{1,0:T(8,128)(2,1)S(1)} %get-tuple-element.21), channel_id=1, source_target_pairs={{0,24},{8,16},{16,8},{24,0},{1,25},{9,17},{17,9},{25,1},{2,26},{10... | collective-permute-start | bytes 294920 | tf_op jit(solution)/shard_map/ppermute | solution.py:76
  32.1 4.6 %collective-permute-start.7 = (bf16[192,256]{1,0:T(8,128)(2,1)S(1)}, bf16[192,256]{1,0:T(8,128)(2,1)S(1)}, u32[]{:S(2)}, u32[]{:S(2)}) collective-permute-start(bf16[192,256]{1,0:T(8,128)(2,1)S(1)} %get-tuple-element.22), channel_id=1, source_target_pairs={{0,16},{8,24},{16,0},{24,8},{1,17},{9,25},{17,1},{25,9},{2,18},{10... | collective-permute-start | bytes 294920 | tf_op jit(solution)/shard_map/ppermute | solution.py:76
  32.6 4.7 %collective-permute-start.6 = (bf16[192,256]{1,0:T(8,128)(2,1)S(1)}, bf16[192,256]{1,0:T(8,128)(2,1)S(1)}, u32[]{:S(2)}, u32[]{:S(2)}) collective-permute-start(bf16[192,256]{1,0:T(8,128)(2,1)S(1)} %get-tuple-element.23), channel_id=1, source_target_pairs={{0,8},{8,0},{16,24},{24,16},{1,9},{9,1},{17,25},{25,17},{2,10},{10... | collective-permute-start | bytes 294920 | tf_op jit(solution)/shard_map/ppermute | solution.py:76
  33.7 4.6 %collective-permute-start.15 = (bf16[128,256]{1,0:T(8,128)(2,1)S(1)}, bf16[128,256]{1,0:T(8,128)(2,1)S(1)}, u32[]{:S(2)}, u32[]{:S(2)}) collective-permute-start(bf16[128,256]{1,0:T(8,128)(2,1)S(1)} %collective-permute-done.11), channel_id=1, source_target_pairs={{0,1},{1,0},{2,3},{3,2},{4,5},{5,4},{6,7},{7,6},{8,9},{9,8},{10,11... | collective-permute-start | bytes 196616 | tf_op jit(solution)/shard_map/ppermute | solution.py:35
  33.7 4.6 %collective-permute-start.14 = (bf16[128,256]{1,0:T(8,128)(2,1)S(1)}, bf16[128,256]{1,0:T(8,128)(2,1)S(1)}, u32[]{:S(2)}, u32[]{:S(2)}) collective-permute-start(bf16[128,256]{1,0:T(8,128)(2,1)S(1)} %collective-permute-done.10), channel_id=1, source_target_pairs={{0,1},{1,0},{2,3},{3,2},{4,5},{5,4},{6,7},{7,6},{8,9},{9,8},{10,11... | collective-permute-start | bytes 196616 | tf_op jit(solution)/shard_map/ppermute | solution.py:35
  34.3 4.0 %collective-permute-start.13 = (bf16[128,256]{1,0:T(8,128)(2,1)S(1)}, bf16[128,256]{1,0:T(8,128)(2,1)S(1)}, u32[]{:S(2)}, u32[]{:S(2)}) collective-permute-start(bf16[128,256]{1,0:T(8,128)(2,1)S(1)} %collective-permute-done.9), channel_id=1, source_target_pairs={{0,1},{1,0},{2,3},{3,2},{4,5},{5,4},{6,7},{7,6},{8,9},{9,8},{10,11... | collective-permute-start | bytes 196616 | tf_op jit(solution)/shard_map/ppermute | solution.py:35

commit v19 on v17

--- a/solution.py
+++ b/solution.py
@@ -50,14 +50,14 @@
     ).astype(jnp.bfloat16)
     keys = pair_rows[:, :d_model].reshape(count, HEADS, head_size)
     values = pair_rows[:, d_model:].reshape(count, HEADS, head_size)
-    scores = jnp.einsum("zun,aun->zua", query, keys, preferred_element_type=jnp.float32) * scale_factor
+    scores = jnp.einsum("zun,aun->uza", query, keys, preferred_element_type=jnp.float32) * scale_factor
     position = (sources[:, None] * block_rows + jnp.arange(block_rows, dtype=jnp.int32)[None, :]).reshape(
         count
     )
     gates = jnp.where(
         (position < length)[None, None, :], logistic(scores), jnp.float32(0.0)
     ).astype(jnp.bfloat16)
-    return jnp.einsum("bgo,ogl->bgl", gates, values, preferred_element_type=jnp.float32)
+    return jnp.einsum("gbo,ogl->bgl", gates, values, preferred_element_type=jnp.float32)
 
 
 def wanted_rows(slots, n_slots, rows):

time: 37.7 us -> 37.8 us (level)
  no operation moved by 1% of the time
where the time goes in v19:
time: 37.8 us; the launch traced here: 37.7 us
  starting transfers between devices  17.1 us (45%)
  local copies, waits for them, and re-layouts  7.08 us (19%)
  waiting for transfers between devices  6.47 us (17%)
  matrix products  4.59 us (12%)
  other arithmetic  1.48 us (4%)
  between operations  0.97 us (3%)
    ppermute x9, starting transfers between devices, swap_over_req(): lax.ppermute(blocks[hop], 'req', [(i, i ^ hop) for i in range(n_req)])  12 us
    gather x1, local copies, waits for them, and re-layouts, body(): jnp.take(table, asked.reshape(-1), axis=0, mode='clip')  5.96 us
    ppermute x3, starting transfers between devices, gather_over_cand(): lax.ppermute(rows, 'cand', [(i, i ^ hop) for i in range(n_cand)])  4.52 us
    ppermute x3, waiting for transfers between devices, gather_over_cand(): lax.ppermute(rows, 'cand', [(i, i ^ hop) for i in range(n_cand)])  3.56 us
    ppermute x9, waiting for transfers between devices, swap_over_req(): lax.ppermute(blocks[hop], 'req', [(i, i ^ hop) for i in range(n_req)])  2.05 us
    dot_general x1, matrix products, attend(): jnp.einsum('gbo,ogl->bgl', gates, values, preferred_element_type=jnp.floa...  1.41 us
    dot_general x1, matrix products, body(): jnp.dot(hidden, tower_out, preferred_element_type=jnp.float32)[None, :]  1.2 us
    ppermute x4, waiting for transfers between devices, gather_over_cand(): lax.ppermute(block, 'cand', [(i, i ^ 1) for i in range(n_cand)])  0.86 us
  transfers between devices with their start and end apart: 16, of which 7 were waited for; matrix products, arithmetic and copies ran while one was open for 6% of the time, Pallas kernels for 0%

profile of v19, /device:TPU:0, one launch (start us, length us, event | category | flops | bytes accessed | tf_op | source)
XLA Modules:
  0.0 37.7 jit_solution(15239805215186497991)
XLA Ops:
  0.0 0.7 %pad_add_fusion.1 = s32[768]{0:T(1024)S(1)} fusion(s32[256]{0:T(256)} %bitcast.89, s32[256]{0:T(256)} %bitcast.90, s32[128]{0:T(128)} %bitcast.91, s32[128]{0:T(128)} %bitcast.92), kind=kLoop, calls=%fused_computation.59 | loop fusion | flops 2304 | bytes 6144 | tf_op jit(solution)/shard_map/concatenate | solution.py:98
  0.8 0.2 convert_reduce_fusion.1
  1.0 0.2 convert_reduce_fusion
  1.2 0.2 convolution_convert_fusion.5
  1.4 0.3 convolution_convert_fusion.4
  1.8 3.0 %collective-permute-start = (s32[320]{0:T(512)S(1)}, s32[320]{0:T(512)S(1)}, u32[]{:S(2)}, u32[]{:S(2)}) collective-permute-start(s32[320]{0:T(512)S(1)} %get-tuple-element.5), channel_id=1, source_target_pairs={{0,8},{8,0},{16,24},{24,16},{1,9},{9,1},{17,25},{25,17},{2,10},{10... | collective-permute-start | bytes 3848 | tf_op jit(solution)/shard_map/ppermute | solution.py:76
  4.8 1.5 %collective-permute-start.2 = (s32[320]{0:T(512)S(1)}, s32[320]{0:T(512)S(1)}, u32[]{:S(2)}, u32[]{:S(2)}) collective-permute-start(s32[320]{0:T(512)S(1)} %get-tuple-element.6), channel_id=1, source_target_pairs={{0,24},{8,16},{16,8},{24,0},{1,25},{9,17},{17,9},{25,1},{2,26},{10... | collective-permute-start | bytes 3848 | tf_op jit(solution)/shard_map/ppermute | solution.py:76
  7.0 0.1 concatenate.38
  7.3 0.7 %reshape.132 = bf16[1024,1]{0,1:T(2,128)(2,1)S(1)} reshape(bf16[1024]{0:T(1024)(128)(2,1)} %param.21) | data formatting | bytes 4096 | tf_op args[10]
  8.0 1.3 %collective-permute-done.2 = s32[320]{0:T(512)S(1)} collective-permute-done((s32[320]{0:T(512)S(1)}, s32[320]{0:T(512)S(1)}, u32[]{:S(2)}, u32[]{:S(2)}) %collective-permute-start.2) | collective-permute-done | bytes 1312 | tf_op jit(solution)/shard_map/ppermute | solution.py:76
  9.3 0.6 %collective-permute-done.1 = s32[320]{0:T(512)S(1)} collective-permute-done((s32[320]{0:T(512)S(1)}, s32[320]{0:T(512)S(1)}, u32[]{:S(2)}, u32[]{:S(2)}) %collective-permute-start.1) | collective-permute-done | bytes 1312 | tf_op jit(solution)/shard_map/ppermute | solution.py:76
  10.0 6.0 %gather_fusion = bf16[1280,256]{1,0:T(8,128)(2,1)S(1)} fusion(bf16[8192,256]{1,0:T(8,128)(2,1)} %param.11, s32[2048]{0:T(1024)S(1)} %pad_clamp_fusion), kind=kCustom, calls=%fused_computation | custom fusion | bytes 1315840 | tf_op jit(solution)/shard_map/jit(_take)/gather | solution.py:117
  16.0 1.5 %collective-permute-start.8 = (bf16[128,256]{1,0:T(8,128)(2,1)S(1)}, bf16[128,256]{1,0:T(8,128)(2,1)S(1)}, u32[]{:S(2)}, u32[]{:S(2)}) collective-permute-start(bf16[128,256]{1,0:T(8,128)(2,1)S(1)} %get-tuple-element.13), channel_id=1, source_target_pairs={{0,24},{8,16},{16,8},{24,0},{1,25},{9,17},{17,9},{25,1},{2,26},{10... | collective-permute-start | bytes 196616 | tf_op jit(solution)/shard_map/ppermute | solution.py:76
  17.5 1.5 %collective-permute-start.7 = (bf16[128,256]{1,0:T(8,128)(2,1)S(1)}, bf16[128,256]{1,0:T(8,128)(2,1)S(1)}, u32[]{:S(2)}, u32[]{:S(2)}) collective-permute-start(bf16[128,256]{1,0:T(8,128)(2,1)S(1)} %get-tuple-element.14), channel_id=1, source_target_pairs={{0,16},{8,24},{16,0},{24,8},{1,17},{9,25},{17,1},{25,9},{2,18},{10... | collective-permute-start | bytes 196616 | tf_op jit(solution)/shard_map/ppermute | solution.py:76
  19.0 0.5 %collective-permute-start.6 = (bf16[128,256]{1,0:T(8,128)(2,1)S(1)}, bf16[128,256]{1,0:T(8,128)(2,1)S(1)}, u32[]{:S(2)}, u32[]{:S(2)}) collective-permute-start(bf16[128,256]{1,0:T(8,128)(2,1)S(1)} %get-tuple-element.15), channel_id=1, source_target_pairs={{0,8},{8,0},{16,24},{24,16},{1,9},{9,1},{17,25},{25,17},{2,10},{10... | collective-permute-start | bytes 196616 | tf_op jit(solution)/shard_map/ppermute | solution.py:76
  19.6 1.5 %collective-permute-start.5 = (bf16[192,256]{1,0:T(8,128)(2,1)S(1)}, bf16[192,256]{1,0:T(8,128)(2,1)S(1)}, u32[]{:S(2)}, u32[]{:S(2)}) collective-permute-start(bf16[192,256]{1,0:T(8,128)(2,1)S(1)} %get-tuple-element.17), channel_id=1, source_target_pairs={{0,24},{8,16},{16,8},{24,0},{1,25},{9,17},{17,9},{25,1},{2,26},{10... | collective-permute-start | bytes 294920 | tf_op jit(solution)/shard_map/ppermute | solution.py:76
  21.1 1.5 %collective-permute-start.4 = (bf16[192,256]{1,0:T(8,128)(2,1)S(1)}, bf16[192,256]{1,0:T(8,128)(2,1)S(1)}, u32[]{:S(2)}, u32[]{:S(2)}) collective-permute-start(bf16[192,256]{1,0:T(8,128)(2,1)S(1)} %get-tuple-element.18), channel_id=1, source_target_pairs={{0,16},{8,24},{16,0},{24,8},{1,17},{9,25},{17,1},{25,9},{2,18},{10... | collective-permute-start | bytes 294920 | tf_op jit(solution)/shard_map/ppermute | solution.py:76
  22.6 0.9 %collective-permute-start.3 = (bf16[192,256]{1,0:T(8,128)(2,1)S(1)}, bf16[192,256]{1,0:T(8,128)(2,1)S(1)}, u32[]{:S(2)}, u32[]{:S(2)}) collective-permute-start(bf16[192,256]{1,0:T(8,128)(2,1)S(1)} %get-tuple-element.19), channel_id=1, source_target_pairs={{0,8},{8,0},{16,24},{24,16},{1,9},{9,1},{17,25},{25,17},{2,10},{10... | collective-permute-start | bytes 294920 | tf_op jit(solution)/shard_map/ppermute | solution.py:76
  23.6 0.1 collective-permute-done.6
  23.7 0.2 bitcast_dynamic-update-slice_fusion.7
  23.9 3.9 %collective-permute-start.11 = (bf16[128,256]{1,0:T(8,128)(2,1)S(1)}, bf16[128,256]{1,0:T(8,128)(2,1)S(1)}, u32[]{:S(2)}, u32[]{:S(2)}) collective-permute-start(bf16[128,256]{1,0:T(8,128)(2,1)S(1)} %get-tuple-element.26), channel_id=1, source_target_pairs={{0,6},{1,7},{2,4},{3,5},{4,2},{5,3},{6,0},{7,1},{8,14},{9,15},{10,... | collective-permute-start | bytes 196616 | tf_op jit(solution)/shard_map/ppermute | solution.py:33
  27.8 0.6 %collective-permute-start.9 = (bf16[128,256]{1,0:T(8,128)(2,1)S(1)}, bf16[128,256]{1,0:T(8,128)(2,1)S(1)}, u32[]{:S(2)}, u32[]{:S(2)}) collective-permute-start(bf16[128,256]{1,0:T(8,128)(2,1)S(1)} %get-tuple-element.26), channel_id=1, source_target_pairs={{0,2},{1,3},{2,0},{3,1},{4,6},{5,7},{6,4},{7,5},{8,10},{9,11},{10,... | collective-permute-start | bytes 196616 | tf_op jit(solution)/shard_map/ppermute | solution.py:33
  28.5 0.3 convolution_convert_fusion.1
  28.9 0.3 fusion.7
  29.2 0.2 convolution_convert_fusion.2
  29.4 0.7 %collective-permute-done.11 = bf16[128,256]{1,0:T(8,128)(2,1)S(1)} collective-permute-done((bf16[128,256]{1,0:T(8,128)(2,1)S(1)}, bf16[128,256]{1,0:T(8,128)(2,1)S(1)}, u32[]{:S(2)}, u32[]{:S(2)}) %collective-permute-start.11) | collective-permute-done | bytes 65568 | tf_op jit(solution)/shard_map/ppermute | solution.py:33
  30.2 2.8 %collective-permute-done.10 = bf16[128,256]{1,0:T(8,128)(2,1)S(1)} collective-permute-done((bf16[128,256]{1,0:T(8,128)(2,1)S(1)}, bf16[128,256]{1,0:T(8,128)(2,1)S(1)}, u32[]{:S(2)}, u32[]{:S(2)}) %collective-permute-start.10) | collective-permute-done | bytes 65568 | tf_op jit(solution)/shard_map/ppermute | solution.py:33
  33.0 0.5 %collective-permute-start.13 = (bf16[128,256]{1,0:T(8,128)(2,1)S(1)}, bf16[128,256]{1,0:T(8,128)(2,1)S(1)}, u32[]{:S(2)}, u32[]{:S(2)}) collective-permute-start(bf16[128,256]{1,0:T(8,128)(2,1)S(1)} %collective-permute-done.9), channel_id=1, source_target_pairs={{0,1},{1,0},{2,3},{3,2},{4,5},{5,4},{6,7},{7,6},{8,9},{9,8},{10,11... | collective-permute-start | bytes 196616 | tf_op jit(solution)/shard_map/ppermute | solution.py:35
  33.6 0.8 %collective-permute-done.13 = bf16[128,256]{1,0:T(8,128)(2,1)S(1)} collective-permute-done((bf16[128,256]{1,0:T(8,128)(2,1)S(1)}, bf16[128,256]{1,0:T(8,128)(2,1)S(1)}, u32[]{:S(2)}, u32[]{:S(2)}) %collective-permute-start.13) | collective-permute-done | bytes 65568 | tf_op jit(solution)/shard_map/ppermute | solution.py:35
  34.5 0.5 %convolution_convert_fusion = bf16[1024,512]{0,1:T(8,128)(2,1)S(1)} fusion(bf16[1024,256]{1,0:T(8,128)(2,1)S(1)} %bitcast.77, bf16[256,256]{1,0:T(8,128)(2,1)S(1)} %copy-done.2, bf16[256,256]{1,0:T(8,128)(2,1)S(1)} %copy-done.3), kind=kOutput, calls=%fused_computation.2 | convolution fusion | flops 269484032 | bytes 1835008 | tf_op jit(solution)/shard_map/dot_general | solution.py:48
  35.0 1.4 %fusion.2 = bf16[4,64,256]{2,1,0:T(8,128)(2,1)S(1)} fusion(bf16[1024,4,64]{0,2,1:T(8,128)(2,1)S(1)} %bitcast.79, bf16[256,4,64]{0,2,1:T(8,128)(2,1)S(1)} %bitcast.81, bf16[1024,4,64]{0,2,1:T(8,128)(2,1)S(1)} %bitcast.78, pred[1024]{0:T(1024)(128)(4,1)S(1)} %fusion.18, f32[]{:T(128)S(6)} %sqrt.3), kind=kOutput, calls=%fused_computation.11 | convolution fusion | flops 273809408 | bytes 1311748 | tf_op jit(solution)/shard_map/gbo,ogl->bgl/dot_general | solution.py:60
  36.5 1.2 %fusion.3 = f32[1,256]{1,0:T(1,128)} fusion(bf16[1024,1]{0,1:T(2,128)(2,1)S(1)} %reshape.132, f32[256,1024]{1,0:T(8,128)S(1)} %fusion.7, bf16[256,256]{0,1:T(8,128)(2,1)S(1)} %bitcast.93, bf16[512,1024]{1,0:T(8,128)(2,1)S(1)} %copy-done.1), kind=kOutput, calls=%fused_computation.13 | convolution fusion | flops 136314880 | bytes 1709056 | tf_op jit(solution)/shard_map/dot_general | solution.py:150
  (55 shorter events, 0.9 us)
Async XLA Ops:
  0.0 29.2 %copy-start = (bf16[256,256]{1,0:T(8,128)(2,1)S(1)}, bf16[256,256]{1,0:T(8,128)(2,1)}, u32[]{:S(2)}) copy-start(bf16[256,256]{1,0:T(8,128)(2,1)} %param.17) | copy-start | bytes 393220
  1.8 6.2 %collective-permute-start = (s32[320]{0:T(512)S(1)}, s32[320]{0:T(512)S(1)}, u32[]{:S(2)}, u32[]{:S(2)}) collective-permute-start(s32[320]{0:T(512)S(1)} %get-tuple-element.5), channel_id=1, source_target_pairs={{0,8},{8,0},{16,24},{24,16},{1,9},{9,1},{17,25},{25,17},{2,10},{10... | collective-permute-start | bytes 3848 | tf_op jit(solution)/shard_map/ppermute | solution.py:76
  4.8 4.5 %collective-permute-start.2 = (s32[320]{0:T(512)S(1)}, s32[320]{0:T(512)S(1)}, u32[]{:S(2)}, u32[]{:S(2)}) collective-permute-start(s32[320]{0:T(512)S(1)} %get-tuple-element.6), channel_id=1, source_target_pairs={{0,24},{8,16},{16,8},{24,0},{1,25},{9,17},{17,9},{25,1},{2,26},{10... | collective-permute-start | bytes 3848 | tf_op jit(solution)/shard_map/ppermute | solution.py:76
  6.3 3.6 %collective-permute-start.1 = (s32[320]{0:T(512)S(1)}, s32[320]{0:T(512)S(1)}, u32[]{:S(2)}, u32[]{:S(2)}) collective-permute-start(s32[320]{0:T(512)S(1)} %get-tuple-element.7), channel_id=1, source_target_pairs={{0,16},{8,24},{16,0},{24,8},{1,17},{9,25},{17,1},{25,9},{2,18},{10... | collective-permute-start | bytes 3848 | tf_op jit(solution)/shard_map/ppermute | solution.py:76
  10.0 18.9 %copy-start.1 = (bf16[512,1024]{1,0:T(8,128)(2,1)S(1)}, bf16[512,1024]{1,0:T(8,128)(2,1)}, u32[]{:S(2)}) copy-start(bf16[512,1024]{1,0:T(8,128)(2,1)} %param.20) | copy-start | bytes 3145732
  15.9 18.5 %copy-start.2 = (bf16[256,256]{1,0:T(8,128)(2,1)S(1)}, bf16[256,256]{1,0:T(8,128)(2,1)}, u32[]{:S(2)}) copy-start(bf16[256,256]{1,0:T(8,128)(2,1)} %param.19) | copy-start | bytes 393220
  15.9 18.5 %copy-start.3 = (bf16[256,256]{1,0:T(8,128)(2,1)S(1)}, bf16[256,256]{1,0:T(8,128)(2,1)}, u32[]{:S(2)}) copy-start(bf16[256,256]{1,0:T(8,128)(2,1)} %param.18) | copy-start | bytes 393220
  16.0 6.6 %collective-permute-start.8 = (bf16[128,256]{1,0:T(8,128)(2,1)S(1)}, bf16[128,256]{1,0:T(8,128)(2,1)S(1)}, u32[]{:S(2)}, u32[]{:S(2)}) collective-permute-start(bf16[128,256]{1,0:T(8,128)(2,1)S(1)} %get-tuple-element.13), channel_id=1, source_target_pairs={{0,24},{8,16},{16,8},{24,0},{1,25},{9,17},{17,9},{25,1},{2,26},{10... | collective-permute-start | bytes 196616 | tf_op jit(solution)/shard_map/ppermute | solution.py:76
  17.5 6.1 %collective-permute-start.7 = (bf16[128,256]{1,0:T(8,128)(2,1)S(1)}, bf16[128,256]{1,0:T(8,128)(2,1)S(1)}, u32[]{:S(2)}, u32[]{:S(2)}) collective-permute-start(bf16[128,256]{1,0:T(8,128)(2,1)S(1)} %get-tuple-element.14), channel_id=1, source_target_pairs={{0,16},{8,24},{16,0},{24,8},{1,17},{9,25},{17,1},{25,9},{2,18},{10... | collective-permute-start | bytes 196616 | tf_op jit(solution)/shard_map/ppermute | solution.py:76
  19.0 4.7 %collective-permute-start.6 = (bf16[128,256]{1,0:T(8,128)(2,1)S(1)}, bf16[128,256]{1,0:T(8,128)(2,1)S(1)}, u32[]{:S(2)}, u32[]{:S(2)}) collective-permute-start(bf16[128,256]{1,0:T(8,128)(2,1)S(1)} %get-tuple-element.15), channel_id=1, source_target_pairs={{0,8},{8,0},{16,24},{24,16},{1,9},{9,1},{17,25},{25,17},{2,10},{10... | collective-permute-start | bytes 196616 | tf_op jit(solution)/shard_map/ppermute | solution.py:76
  19.6 8.3 %collective-permute-start.5 = (bf16[192,256]{1,0:T(8,128)(2,1)S(1)}, bf16[192,256]{1,0:T(8,128)(2,1)S(1)}, u32[]{:S(2)}, u32[]{:S(2)}) collective-permute-start(bf16[192,256]{1,0:T(8,128)(2,1)S(1)} %get-tuple-element.17), channel_id=1, source_target_pairs={{0,24},{8,16},{16,8},{24,0},{1,25},{9,17},{17,9},{25,1},{2,26},{10... | collective-permute-start | bytes 294920 | tf_op jit(solution)/shard_map/ppermute | solution.py:76
  21.1 7.4 %collective-permute-start.4 = (bf16[192,256]{1,0:T(8,128)(2,1)S(1)}, bf16[192,256]{1,0:T(8,128)(2,1)S(1)}, u32[]{:S(2)}, u32[]{:S(2)}) collective-permute-start(bf16[192,256]{1,0:T(8,128)(2,1)S(1)} %get-tuple-element.18), channel_id=1, source_target_pairs={{0,16},{8,24},{16,0},{24,8},{1,17},{9,25},{17,1},{25,9},{2,18},{10... | collective-permute-start | bytes 294920 | tf_op jit(solution)/shard_map/ppermute | solution.py:76
  22.6 5.9 %collective-permute-start.3 = (bf16[192,256]{1,0:T(8,128)(2,1)S(1)}, bf16[192,256]{1,0:T(8,128)(2,1)S(1)}, u32[]{:S(2)}, u32[]{:S(2)}) collective-permute-start(bf16[192,256]{1,0:T(8,128)(2,1)S(1)} %get-tuple-element.19), channel_id=1, source_target_pairs={{0,8},{8,0},{16,24},{24,16},{1,9},{9,1},{17,25},{25,17},{2,10},{10... | collective-permute-start | bytes 294920 | tf_op jit(solution)/shard_map/ppermute | solution.py:76
  23.9 6.2 %collective-permute-start.11 = (bf16[128,256]{1,0:T(8,128)(2,1)S(1)}, bf16[128,256]{1,0:T(8,128)(2,1)S(1)}, u32[]{:S(2)}, u32[]{:S(2)}) collective-permute-start(bf16[128,256]{1,0:T(8,128)(2,1)S(1)} %get-tuple-element.26), channel_id=1, source_target_pairs={{0,6},{1,7},{2,4},{3,5},{4,2},{5,3},{6,0},{7,1},{8,14},{9,15},{10,... | collective-permute-start | bytes 196616 | tf_op jit(solution)/shard_map/ppermute | solution.py:33
  27.8 5.2 %collective-permute-start.10 = (bf16[128,256]{1,0:T(8,128)(2,1)S(1)}, bf16[128,256]{1,0:T(8,128)(2,1)S(1)}, u32[]{:S(2)}, u32[]{:S(2)}) collective-permute-start(bf16[128,256]{1,0:T(8,128)(2,1)S(1)} %get-tuple-element.26), channel_id=1, source_target_pairs={{0,4},{1,5},{2,6},{3,7},{4,0},{5,1},{6,2},{7,3},{8,12},{9,13},{10,... | collective-permute-start | bytes 196616 | tf_op jit(solution)/shard_map/ppermute | solution.py:33
  27.8 5.2 %collective-permute-start.9 = (bf16[128,256]{1,0:T(8,128)(2,1)S(1)}, bf16[128,256]{1,0:T(8,128)(2,1)S(1)}, u32[]{:S(2)}, u32[]{:S(2)}) collective-permute-start(bf16[128,256]{1,0:T(8,128)(2,1)S(1)} %get-tuple-element.26), channel_id=1, source_target_pairs={{0,2},{1,3},{2,0},{3,1},{4,6},{5,7},{6,4},{7,5},{8,10},{9,11},{10,... | collective-permute-start | bytes 196616 | tf_op jit(solution)/shard_map/ppermute | solution.py:33
  28.5 5.1 %collective-permute-start.12 = (bf16[128,256]{1,0:T(8,128)(2,1)S(1)}, bf16[128,256]{1,0:T(8,128)(2,1)S(1)}, u32[]{:S(2)}, u32[]{:S(2)}) collective-permute-start(bf16[128,256]{1,0:T(8,128)(2,1)S(1)} %get-tuple-element.26), channel_id=1, source_target_pairs={{0,1},{1,0},{2,3},{3,2},{4,5},{5,4},{6,7},{7,6},{8,9},{9,8},{10,11... | collective-permute-start | bytes 196616 | tf_op jit(solution)/shard_map/ppermute | solution.py:35
  30.2 4.3 %collective-permute-start.15 = (bf16[128,256]{1,0:T(8,128)(2,1)S(1)}, bf16[128,256]{1,0:T(8,128)(2,1)S(1)}, u32[]{:S(2)}, u32[]{:S(2)}) collective-permute-start(bf16[128,256]{1,0:T(8,128)(2,1)S(1)} %collective-permute-done.11), channel_id=1, source_target_pairs={{0,1},{1,0},{2,3},{3,2},{4,5},{5,4},{6,7},{7,6},{8,9},{9,8},{10,11... | collective-permute-start | bytes 196616 | tf_op jit(solution)/shard_map/ppermute | solution.py:35
  33.0 1.4 %collective-permute-start.14 = (bf16[128,256]{1,0:T(8,128)(2,1)S(1)}, bf16[128,256]{1,0:T(8,128)(2,1)S(1)}, u32[]{:S(2)}, u32[]{:S(2)}) collective-permute-start(bf16[128,256]{1,0:T(8,128)(2,1)S(1)} %collective-permute-done.10), channel_id=1, source_target_pairs={{0,1},{1,0},{2,3},{3,2},{4,5},{5,4},{6,7},{7,6},{8,9},{9,8},{10,11... | collective-permute-start | bytes 196616 | tf_op jit(solution)/shard_map/ppermute | solution.py:35
  33.0 1.4 %collective-permute-start.13 = (bf16[128,256]{1,0:T(8,128)(2,1)S(1)}, bf16[128,256]{1,0:T(8,128)(2,1)S(1)}, u32[]{:S(2)}, u32[]{:S(2)}) collective-permute-start(bf16[128,256]{1,0:T(8,128)(2,1)S(1)} %collective-permute-done.9), channel_id=1, source_target_pairs={{0,1},{1,0},{2,3},{3,2},{4,5},{5,4},{6,7},{7,6},{8,9},{9,8},{10,11... | collective-permute-start | bytes 196616 | tf_op jit(solution)/shard_map/ppermute | solution.py:35

commit v20 on v17

--- a/solution.py
+++ b/solution.py
@@ -147,7 +147,8 @@
         attended, tower_in[d_model:], preferred_element_type=jnp.float32
     )
     hidden = (pre_act * logistic(pre_act)).astype(jnp.bfloat16)
-    return jnp.dot(hidden, tower_out, preferred_element_type=jnp.float32)[None, :]
+    products = hidden.astype(jnp.float32) * tower_out.astype(jnp.float32)[None, :]
+    return jnp.sum(products, axis=1)[None, :]
 
 
 def solution(mesh):

time: 37.7 us -> 37.7 us (level)
  other arithmetic: 1.48 us -> 2.16 us
  local copies, waits for them, and re-layouts: 7.08 us -> 6.4 us
    unnamed x15 -> x14, local copies, waits for them, and re-layouts: 0.75 us -> 0.06 us
    convert_element_type x0 -> x1, other arithmetic: none -> 0.69 us  [body(): tower_out.astype(jnp.float32)[None, :]]
where the time goes in v20:
time: 37.7 us; the launch traced here: 37.5 us
  starting transfers between devices  17.1 us (45%)
  waiting for transfers between devices  6.47 us (17%)
  local copies, waits for them, and re-layouts  6.4 us (17%)
  matrix products  4.42 us (12%)
  other arithmetic  2.16 us (6%)
  between operations  0.96 us (3%)
    ppermute x9, starting transfers between devices, swap_over_req(): lax.ppermute(blocks[hop], 'req', [(i, i ^ hop) for i in range(n_req)])  12 us
    gather x1, local copies, waits for them, and re-layouts, body(): jnp.take(table, asked.reshape(-1), axis=0, mode='clip')  5.96 us
    ppermute x3, starting transfers between devices, gather_over_cand(): lax.ppermute(rows, 'cand', [(i, i ^ hop) for i in range(n_cand)])  4.52 us
    ppermute x3, waiting for transfers between devices, gather_over_cand(): lax.ppermute(rows, 'cand', [(i, i ^ hop) for i in range(n_cand)])  3.56 us
    ppermute x9, waiting for transfers between devices, swap_over_req(): lax.ppermute(blocks[hop], 'req', [(i, i ^ hop) for i in range(n_req)])  2.06 us
    dot_general x1, matrix products, attend(): jnp.einsum('bgo,ogl->bgl', gates, values, preferred_element_type=jnp.floa...  1.32 us
    dot_general x1, matrix products, body(): jnp.dot(attended, tower_in[d_model:], preferred_element_type=jnp.float32)  1.12 us
    ppermute x4, waiting for transfers between devices, gather_over_cand(): lax.ppermute(block, 'cand', [(i, i ^ 1) for i in range(n_cand)])  0.86 us
  transfers between devices with their start and end apart: 16, of which 7 were waited for; matrix products, arithmetic and copies ran while one was open for 6% of the time, Pallas kernels for 0%

profile of v20, /device:TPU:0, one launch (start us, length us, event | category | flops | bytes accessed | tf_op | source)
XLA Modules:
  0.0 37.5 jit_solution(16669067115134863154)
XLA Ops:
  0.0 0.7 %pad_add_fusion.1 = s32[768]{0:T(1024)S(1)} fusion(s32[256]{0:T(256)} %bitcast.95, s32[256]{0:T(256)} %bitcast.96, s32[128]{0:T(128)} %bitcast.97, s32[128]{0:T(128)} %bitcast.98), kind=kLoop, calls=%fused_computation.59 | loop fusion | flops 2304 | bytes 6144 | tf_op jit(solution)/shard_map/concatenate | solution.py:98
  0.8 0.2 convert_reduce_fusion.1
  1.0 0.2 convert_reduce_fusion
  1.2 0.2 convolution_convert_fusion.5
  1.4 0.3 convolution_convert_fusion.4
  1.8 3.0 %collective-permute-start = (s32[320]{0:T(512)S(1)}, s32[320]{0:T(512)S(1)}, u32[]{:S(2)}, u32[]{:S(2)}) collective-permute-start(s32[320]{0:T(512)S(1)} %get-tuple-element.5), channel_id=1, source_target_pairs={{0,8},{8,0},{16,24},{24,16},{1,9},{9,1},{17,25},{25,17},{2,10},{10... | collective-permute-start | bytes 3848 | tf_op jit(solution)/shard_map/ppermute | solution.py:76
  4.8 1.5 %collective-permute-start.2 = (s32[320]{0:T(512)S(1)}, s32[320]{0:T(512)S(1)}, u32[]{:S(2)}, u32[]{:S(2)}) collective-permute-start(s32[320]{0:T(512)S(1)} %get-tuple-element.6), channel_id=1, source_target_pairs={{0,24},{8,16},{16,8},{24,0},{1,25},{9,17},{17,9},{25,1},{2,26},{10... | collective-permute-start | bytes 3848 | tf_op jit(solution)/shard_map/ppermute | solution.py:76
  7.0 0.1 concatenate.38
  7.3 0.7 %convert_element_type.69 = f32[1024]{0:T(1024)S(1)} convert(bf16[1024]{0:T(1024)(128)(2,1)} %param.21) | non-fusion elementwise | flops 1024 | bytes 6144 | tf_op jit(solution)/shard_map/convert_element_type | solution.py:150
  8.0 1.3 %collective-permute-done.2 = s32[320]{0:T(512)S(1)} collective-permute-done((s32[320]{0:T(512)S(1)}, s32[320]{0:T(512)S(1)}, u32[]{:S(2)}, u32[]{:S(2)}) %collective-permute-start.2) | collective-permute-done | bytes 1312 | tf_op jit(solution)/shard_map/ppermute | solution.py:76
  9.3 0.6 %collective-permute-done.1 = s32[320]{0:T(512)S(1)} collective-permute-done((s32[320]{0:T(512)S(1)}, s32[320]{0:T(512)S(1)}, u32[]{:S(2)}, u32[]{:S(2)}) %collective-permute-start.1) | collective-permute-done | bytes 1312 | tf_op jit(solution)/shard_map/ppermute | solution.py:76
  10.0 6.0 %gather_fusion = bf16[1280,256]{1,0:T(8,128)(2,1)S(1)} fusion(bf16[8192,256]{1,0:T(8,128)(2,1)} %param.11, s32[2048]{0:T(1024)S(1)} %pad_clamp_fusion), kind=kCustom, calls=%fused_computation | custom fusion | bytes 1315840 | tf_op jit(solution)/shard_map/jit(_take)/gather | solution.py:117
  16.0 1.5 %collective-permute-start.8 = (bf16[128,256]{1,0:T(8,128)(2,1)S(1)}, bf16[128,256]{1,0:T(8,128)(2,1)S(1)}, u32[]{:S(2)}, u32[]{:S(2)}) collective-permute-start(bf16[128,256]{1,0:T(8,128)(2,1)S(1)} %get-tuple-element.13), channel_id=1, source_target_pairs={{0,24},{8,16},{16,8},{24,0},{1,25},{9,17},{17,9},{25,1},{2,26},{10... | collective-permute-start | bytes 196616 | tf_op jit(solution)/shard_map/ppermute | solution.py:76
  17.5 1.5 %collective-permute-start.7 = (bf16[128,256]{1,0:T(8,128)(2,1)S(1)}, bf16[128,256]{1,0:T(8,128)(2,1)S(1)}, u32[]{:S(2)}, u32[]{:S(2)}) collective-permute-start(bf16[128,256]{1,0:T(8,128)(2,1)S(1)} %get-tuple-element.14), channel_id=1, source_target_pairs={{0,16},{8,24},{16,0},{24,8},{1,17},{9,25},{17,1},{25,9},{2,18},{10... | collective-permute-start | bytes 196616 | tf_op jit(solution)/shard_map/ppermute | solution.py:76
  19.0 0.5 %collective-permute-start.6 = (bf16[128,256]{1,0:T(8,128)(2,1)S(1)}, bf16[128,256]{1,0:T(8,128)(2,1)S(1)}, u32[]{:S(2)}, u32[]{:S(2)}) collective-permute-start(bf16[128,256]{1,0:T(8,128)(2,1)S(1)} %get-tuple-element.15), channel_id=1, source_target_pairs={{0,8},{8,0},{16,24},{24,16},{1,9},{9,1},{17,25},{25,17},{2,10},{10... | collective-permute-start | bytes 196616 | tf_op jit(solution)/shard_map/ppermute | solution.py:76
  19.6 1.5 %collective-permute-start.5 = (bf16[192,256]{1,0:T(8,128)(2,1)S(1)}, bf16[192,256]{1,0:T(8,128)(2,1)S(1)}, u32[]{:S(2)}, u32[]{:S(2)}) collective-permute-start(bf16[192,256]{1,0:T(8,128)(2,1)S(1)} %get-tuple-element.17), channel_id=1, source_target_pairs={{0,24},{8,16},{16,8},{24,0},{1,25},{9,17},{17,9},{25,1},{2,26},{10... | collective-permute-start | bytes 294920 | tf_op jit(solution)/shard_map/ppermute | solution.py:76
  21.1 1.5 %collective-permute-start.4 = (bf16[192,256]{1,0:T(8,128)(2,1)S(1)}, bf16[192,256]{1,0:T(8,128)(2,1)S(1)}, u32[]{:S(2)}, u32[]{:S(2)}) collective-permute-start(bf16[192,256]{1,0:T(8,128)(2,1)S(1)} %get-tuple-element.18), channel_id=1, source_target_pairs={{0,16},{8,24},{16,0},{24,8},{1,17},{9,25},{17,1},{25,9},{2,18},{10... | collective-permute-start | bytes 294920 | tf_op jit(solution)/shard_map/ppermute | solution.py:76
  22.6 0.9 %collective-permute-start.3 = (bf16[192,256]{1,0:T(8,128)(2,1)S(1)}, bf16[192,256]{1,0:T(8,128)(2,1)S(1)}, u32[]{:S(2)}, u32[]{:S(2)}) collective-permute-start(bf16[192,256]{1,0:T(8,128)(2,1)S(1)} %get-tuple-element.19), channel_id=1, source_target_pairs={{0,8},{8,0},{16,24},{24,16},{1,9},{9,1},{17,25},{25,17},{2,10},{10... | collective-permute-start | bytes 294920 | tf_op jit(solution)/shard_map/ppermute | solution.py:76
  23.6 0.1 collective-permute-done.6
  23.7 0.2 bitcast_dynamic-update-slice_fusion.7
  23.9 3.9 %collective-permute-start.11 = (bf16[128,256]{1,0:T(8,128)(2,1)S(1)}, bf16[128,256]{1,0:T(8,128)(2,1)S(1)}, u32[]{:S(2)}, u32[]{:S(2)}) collective-permute-start(bf16[128,256]{1,0:T(8,128)(2,1)S(1)} %get-tuple-element.26), channel_id=1, source_target_pairs={{0,6},{1,7},{2,4},{3,5},{4,2},{5,3},{6,0},{7,1},{8,14},{9,15},{10,... | collective-permute-start | bytes 196616 | tf_op jit(solution)/shard_map/ppermute | solution.py:33
  27.8 0.6 %collective-permute-start.9 = (bf16[128,256]{1,0:T(8,128)(2,1)S(1)}, bf16[128,256]{1,0:T(8,128)(2,1)S(1)}, u32[]{:S(2)}, u32[]{:S(2)}) collective-permute-start(bf16[128,256]{1,0:T(8,128)(2,1)S(1)} %get-tuple-element.26), channel_id=1, source_target_pairs={{0,2},{1,3},{2,0},{3,1},{4,6},{5,7},{6,4},{7,5},{8,10},{9,11},{10,... | collective-permute-start | bytes 196616 | tf_op jit(solution)/shard_map/ppermute | solution.py:33
  28.5 0.3 convolution_convert_fusion.1
  28.9 0.3 fusion.9
  29.2 0.2 convolution_convert_fusion.2
  29.4 0.7 %collective-permute-done.11 = bf16[128,256]{1,0:T(8,128)(2,1)S(1)} collective-permute-done((bf16[128,256]{1,0:T(8,128)(2,1)S(1)}, bf16[128,256]{1,0:T(8,128)(2,1)S(1)}, u32[]{:S(2)}, u32[]{:S(2)}) %collective-permute-start.11) | collective-permute-done | bytes 65568 | tf_op jit(solution)/shard_map/ppermute | solution.py:33
  30.2 2.8 %collective-permute-done.10 = bf16[128,256]{1,0:T(8,128)(2,1)S(1)} collective-permute-done((bf16[128,256]{1,0:T(8,128)(2,1)S(1)}, bf16[128,256]{1,0:T(8,128)(2,1)S(1)}, u32[]{:S(2)}, u32[]{:S(2)}) %collective-permute-start.10) | collective-permute-done | bytes 65568 | tf_op jit(solution)/shard_map/ppermute | solution.py:33
  33.0 0.5 %collective-permute-start.13 = (bf16[128,256]{1,0:T(8,128)(2,1)S(1)}, bf16[128,256]{1,0:T(8,128)(2,1)S(1)}, u32[]{:S(2)}, u32[]{:S(2)}) collective-permute-start(bf16[128,256]{1,0:T(8,128)(2,1)S(1)} %collective-permute-done.9), channel_id=1, source_target_pairs={{0,1},{1,0},{2,3},{3,2},{4,5},{5,4},{6,7},{7,6},{8,9},{9,8},{10,11... | collective-permute-start | bytes 196616 | tf_op jit(solution)/shard_map/ppermute | solution.py:35
  33.6 0.8 %collective-permute-done.13 = bf16[128,256]{1,0:T(8,128)(2,1)S(1)} collective-permute-done((bf16[128,256]{1,0:T(8,128)(2,1)S(1)}, bf16[128,256]{1,0:T(8,128)(2,1)S(1)}, u32[]{:S(2)}, u32[]{:S(2)}) %collective-permute-start.13) | collective-permute-done | bytes 65568 | tf_op jit(solution)/shard_map/ppermute | solution.py:35
  34.5 0.5 %convolution_convert_fusion = bf16[1024,512]{0,1:T(8,128)(2,1)S(1)} fusion(bf16[1024,256]{1,0:T(8,128)(2,1)S(1)} %bitcast.83, bf16[256,256]{1,0:T(8,128)(2,1)S(1)} %copy-done.2, bf16[256,256]{1,0:T(8,128)(2,1)S(1)} %copy-done.3), kind=kOutput, calls=%fused_computation.4 | convolution fusion | flops 269484032 | bytes 1835008 | tf_op jit(solution)/shard_map/dot_general | solution.py:48
  35.0 1.3 %fusion.5 = bf16[4,64,256]{2,1,0:T(8,128)(2,1)S(1)} fusion(bf16[1024,4,64]{0,2,1:T(8,128)(2,1)S(1)} %bitcast.85, bf16[1024,4,64]{0,2,1:T(8,128)(2,1)S(1)} %bitcast.84, bf16[256,4,64]{0,2,1:T(8,128)(2,1)S(1)} %bitcast.87, pred[1024]{0:T(1024)(128)(4,1)S(1)} %fusion.20, f32[]{:T(128)S(6)} %sqrt.3), kind=kOutput, calls=%fused_computation.12 | convolution fusion | flops 273809408 | bytes 1311748 | tf_op jit(solution)/shard_map/bgo,ogl->bgl/dot_general | solution.py:60
  36.4 1.1 %multiply_reduce_fusion = f32[256]{0:T(256)} fusion(f32[256,1024]{1,0:T(8,128)S(1)} %fusion.9, bf16[256,256]{0,1:T(8,128)(2,1)S(1)} %bitcast.99, f32[1024]{0:T(1024)S(1)} %convert_element_type.69, bf16[512,1024]{1,0:T(8,128)(2,1)S(1)} %copy-done.1), kind=kOutput, calls=%fused_computation.13 | convolution fusion | flops 136576768 | bytes 1709056 | tf_op jit(solution)/shard_map/dot_general | solution.py:146
  (55 shorter events, 0.9 us)
Async XLA Ops:
  0.0 29.2 %copy-start = (bf16[256,256]{1,0:T(8,128)(2,1)S(1)}, bf16[256,256]{1,0:T(8,128)(2,1)}, u32[]{:S(2)}) copy-start(bf16[256,256]{1,0:T(8,128)(2,1)} %param.17) | copy-start | bytes 393220
  1.8 6.2 %collective-permute-start = (s32[320]{0:T(512)S(1)}, s32[320]{0:T(512)S(1)}, u32[]{:S(2)}, u32[]{:S(2)}) collective-permute-start(s32[320]{0:T(512)S(1)} %get-tuple-element.5), channel_id=1, source_target_pairs={{0,8},{8,0},{16,24},{24,16},{1,9},{9,1},{17,25},{25,17},{2,10},{10... | collective-permute-start | bytes 3848 | tf_op jit(solution)/shard_map/ppermute | solution.py:76
  4.8 4.5 %collective-permute-start.2 = (s32[320]{0:T(512)S(1)}, s32[320]{0:T(512)S(1)}, u32[]{:S(2)}, u32[]{:S(2)}) collective-permute-start(s32[320]{0:T(512)S(1)} %get-tuple-element.6), channel_id=1, source_target_pairs={{0,24},{8,16},{16,8},{24,0},{1,25},{9,17},{17,9},{25,1},{2,26},{10... | collective-permute-start | bytes 3848 | tf_op jit(solution)/shard_map/ppermute | solution.py:76
  6.3 3.6 %collective-permute-start.1 = (s32[320]{0:T(512)S(1)}, s32[320]{0:T(512)S(1)}, u32[]{:S(2)}, u32[]{:S(2)}) collective-permute-start(s32[320]{0:T(512)S(1)} %get-tuple-element.7), channel_id=1, source_target_pairs={{0,16},{8,24},{16,0},{24,8},{1,17},{9,25},{17,1},{25,9},{2,18},{10... | collective-permute-start | bytes 3848 | tf_op jit(solution)/shard_map/ppermute | solution.py:76
  10.0 18.9 %copy-start.1 = (bf16[512,1024]{1,0:T(8,128)(2,1)S(1)}, bf16[512,1024]{1,0:T(8,128)(2,1)}, u32[]{:S(2)}) copy-start(bf16[512,1024]{1,0:T(8,128)(2,1)} %param.20) | copy-start | bytes 3145732
  15.9 18.5 %copy-start.2 = (bf16[256,256]{1,0:T(8,128)(2,1)S(1)}, bf16[256,256]{1,0:T(8,128)(2,1)}, u32[]{:S(2)}) copy-start(bf16[256,256]{1,0:T(8,128)(2,1)} %param.19) | copy-start | bytes 393220
  15.9 18.5 %copy-start.3 = (bf16[256,256]{1,0:T(8,128)(2,1)S(1)}, bf16[256,256]{1,0:T(8,128)(2,1)}, u32[]{:S(2)}) copy-start(bf16[256,256]{1,0:T(8,128)(2,1)} %param.18) | copy-start | bytes 393220
  16.0 6.6 %collective-permute-start.8 = (bf16[128,256]{1,0:T(8,128)(2,1)S(1)}, bf16[128,256]{1,0:T(8,128)(2,1)S(1)}, u32[]{:S(2)}, u32[]{:S(2)}) collective-permute-start(bf16[128,256]{1,0:T(8,128)(2,1)S(1)} %get-tuple-element.13), channel_id=1, source_target_pairs={{0,24},{8,16},{16,8},{24,0},{1,25},{9,17},{17,9},{25,1},{2,26},{10... | collective-permute-start | bytes 196616 | tf_op jit(solution)/shard_map/ppermute | solution.py:76
  17.5 6.1 %collective-permute-start.7 = (bf16[128,256]{1,0:T(8,128)(2,1)S(1)}, bf16[128,256]{1,0:T(8,128)(2,1)S(1)}, u32[]{:S(2)}, u32[]{:S(2)}) collective-permute-start(bf16[128,256]{1,0:T(8,128)(2,1)S(1)} %get-tuple-element.14), channel_id=1, source_target_pairs={{0,16},{8,24},{16,0},{24,8},{1,17},{9,25},{17,1},{25,9},{2,18},{10... | collective-permute-start | bytes 196616 | tf_op jit(solution)/shard_map/ppermute | solution.py:76
  19.0 4.7 %collective-permute-start.6 = (bf16[128,256]{1,0:T(8,128)(2,1)S(1)}, bf16[128,256]{1,0:T(8,128)(2,1)S(1)}, u32[]{:S(2)}, u32[]{:S(2)}) collective-permute-start(bf16[128,256]{1,0:T(8,128)(2,1)S(1)} %get-tuple-element.15), channel_id=1, source_target_pairs={{0,8},{8,0},{16,24},{24,16},{1,9},{9,1},{17,25},{25,17},{2,10},{10... | collective-permute-start | bytes 196616 | tf_op jit(solution)/shard_map/ppermute | solution.py:76
  19.6 8.3 %collective-permute-start.5 = (bf16[192,256]{1,0:T(8,128)(2,1)S(1)}, bf16[192,256]{1,0:T(8,128)(2,1)S(1)}, u32[]{:S(2)}, u32[]{:S(2)}) collective-permute-start(bf16[192,256]{1,0:T(8,128)(2,1)S(1)} %get-tuple-element.17), channel_id=1, source_target_pairs={{0,24},{8,16},{16,8},{24,0},{1,25},{9,17},{17,9},{25,1},{2,26},{10... | collective-permute-start | bytes 294920 | tf_op jit(solution)/shard_map/ppermute | solution.py:76
  21.1 7.4 %collective-permute-start.4 = (bf16[192,256]{1,0:T(8,128)(2,1)S(1)}, bf16[192,256]{1,0:T(8,128)(2,1)S(1)}, u32[]{:S(2)}, u32[]{:S(2)}) collective-permute-start(bf16[192,256]{1,0:T(8,128)(2,1)S(1)} %get-tuple-element.18), channel_id=1, source_target_pairs={{0,16},{8,24},{16,0},{24,8},{1,17},{9,25},{17,1},{25,9},{2,18},{10... | collective-permute-start | bytes 294920 | tf_op jit(solution)/shard_map/ppermute | solution.py:76
  22.6 5.9 %collective-permute-start.3 = (bf16[192,256]{1,0:T(8,128)(2,1)S(1)}, bf16[192,256]{1,0:T(8,128)(2,1)S(1)}, u32[]{:S(2)}, u32[]{:S(2)}) collective-permute-start(bf16[192,256]{1,0:T(8,128)(2,1)S(1)} %get-tuple-element.19), channel_id=1, source_target_pairs={{0,8},{8,0},{16,24},{24,16},{1,9},{9,1},{17,25},{25,17},{2,10},{10... | collective-permute-start | bytes 294920 | tf_op jit(solution)/shard_map/ppermute | solution.py:76
  23.9 6.2 %collective-permute-start.11 = (bf16[128,256]{1,0:T(8,128)(2,1)S(1)}, bf16[128,256]{1,0:T(8,128)(2,1)S(1)}, u32[]{:S(2)}, u32[]{:S(2)}) collective-permute-start(bf16[128,256]{1,0:T(8,128)(2,1)S(1)} %get-tuple-element.26), channel_id=1, source_target_pairs={{0,6},{1,7},{2,4},{3,5},{4,2},{5,3},{6,0},{7,1},{8,14},{9,15},{10,... | collective-permute-start | bytes 196616 | tf_op jit(solution)/shard_map/ppermute | solution.py:33
  27.8 5.2 %collective-permute-start.10 = (bf16[128,256]{1,0:T(8,128)(2,1)S(1)}, bf16[128,256]{1,0:T(8,128)(2,1)S(1)}, u32[]{:S(2)}, u32[]{:S(2)}) collective-permute-start(bf16[128,256]{1,0:T(8,128)(2,1)S(1)} %get-tuple-element.26), channel_id=1, source_target_pairs={{0,4},{1,5},{2,6},{3,7},{4,0},{5,1},{6,2},{7,3},{8,12},{9,13},{10,... | collective-permute-start | bytes 196616 | tf_op jit(solution)/shard_map/ppermute | solution.py:33
  27.8 5.2 %collective-permute-start.9 = (bf16[128,256]{1,0:T(8,128)(2,1)S(1)}, bf16[128,256]{1,0:T(8,128)(2,1)S(1)}, u32[]{:S(2)}, u32[]{:S(2)}) collective-permute-start(bf16[128,256]{1,0:T(8,128)(2,1)S(1)} %get-tuple-element.26), channel_id=1, source_target_pairs={{0,2},{1,3},{2,0},{3,1},{4,6},{5,7},{6,4},{7,5},{8,10},{9,11},{10,... | collective-permute-start | bytes 196616 | tf_op jit(solution)/shard_map/ppermute | solution.py:33
  28.5 5.1 %collective-permute-start.12 = (bf16[128,256]{1,0:T(8,128)(2,1)S(1)}, bf16[128,256]{1,0:T(8,128)(2,1)S(1)}, u32[]{:S(2)}, u32[]{:S(2)}) collective-permute-start(bf16[128,256]{1,0:T(8,128)(2,1)S(1)} %get-tuple-element.26), channel_id=1, source_target_pairs={{0,1},{1,0},{2,3},{3,2},{4,5},{5,4},{6,7},{7,6},{8,9},{9,8},{10,11... | collective-permute-start | bytes 196616 | tf_op jit(solution)/shard_map/ppermute | solution.py:35
  30.2 4.3 %collective-permute-start.15 = (bf16[128,256]{1,0:T(8,128)(2,1)S(1)}, bf16[128,256]{1,0:T(8,128)(2,1)S(1)}, u32[]{:S(2)}, u32[]{:S(2)}) collective-permute-start(bf16[128,256]{1,0:T(8,128)(2,1)S(1)} %collective-permute-done.11), channel_id=1, source_target_pairs={{0,1},{1,0},{2,3},{3,2},{4,5},{5,4},{6,7},{7,6},{8,9},{9,8},{10,11... | collective-permute-start | bytes 196616 | tf_op jit(solution)/shard_map/ppermute | solution.py:35
  33.0 1.4 %collective-permute-start.14 = (bf16[128,256]{1,0:T(8,128)(2,1)S(1)}, bf16[128,256]{1,0:T(8,128)(2,1)S(1)}, u32[]{:S(2)}, u32[]{:S(2)}) collective-permute-start(bf16[128,256]{1,0:T(8,128)(2,1)S(1)} %collective-permute-done.10), channel_id=1, source_target_pairs={{0,1},{1,0},{2,3},{3,2},{4,5},{5,4},{6,7},{7,6},{8,9},{9,8},{10,11... | collective-permute-start | bytes 196616 | tf_op jit(solution)/shard_map/ppermute | solution.py:35
  33.0 1.4 %collective-permute-start.13 = (bf16[128,256]{1,0:T(8,128)(2,1)S(1)}, bf16[128,256]{1,0:T(8,128)(2,1)S(1)}, u32[]{:S(2)}, u32[]{:S(2)}) collective-permute-start(bf16[128,256]{1,0:T(8,128)(2,1)S(1)} %collective-permute-done.9), channel_id=1, source_target_pairs={{0,1},{1,0},{2,3},{3,2},{4,5},{5,4},{6,7},{7,6},{8,9},{9,8},{10,11... | collective-permute-start | bytes 196616 | tf_op jit(solution)/shard_map/ppermute | solution.py:35

commit v21 on v13

--- a/solution.py
+++ b/solution.py
@@ -26,15 +26,15 @@
 
 def gather_over_cand(rows):
     n_cand = lax.axis_size("cand")
+    assert n_cand & (n_cand - 1) == 0
     me = lax.axis_index("cand")
     blocks, sources = [rows], [me]
     for hop in range(2, n_cand, 2):
-        blocks.append(lax.ppermute(rows, "cand", [(i, (i + hop) % n_cand) for i in range(n_cand)]))
-        sources.append((me - hop) % n_cand)
-    mine = jnp.stack(blocks, axis=0)
-    partner = lax.ppermute(mine, "cand", [(i, i ^ 1) for i in range(n_cand)])
+        blocks.append(lax.ppermute(rows, "cand", [(i, i ^ hop) for i in range(n_cand)]))
+        sources.append(me ^ hop)
+    forwarded = [lax.ppermute(block, "cand", [(i, i ^ 1) for i in range(n_cand)]) for block in blocks]
     source = jnp.stack(sources)
-    return (mine, source), (partner, source ^ 1)
+    return (jnp.stack(blocks, axis=0), source), (jnp.stack(forwarded, axis=0), source ^ 1)
 
 
 def logistic(x):

time: 41 us -> 41.6 us (1.015)
  starting transfers between devices: 17.1 us -> 19 us
  waiting for transfers between devices: 6.29 us -> 4.99 us
    ppermute x4 -> x7, starting transfers between devices: 4.97 us -> 6.85 us  [the longest x3 6.14 us: gather_over_cand(): lax.ppermute(rows, 'cand', [(i, i ^ hop) for i in range(n_cand)])]
    ppermute x4 -> x7, waiting for transfers between devices: 5.32 us -> 4 us  [the longest x3 3.14 us: gather_over_cand(): lax.ppermute(rows, 'cand', [(i, i ^ hop) for i in range(n_cand)])]
  transfers between devices with their start and end apart: 13 -> 16, of which waited for: 5 -> 6; matrix products, arithmetic and copies ran while one was open for 10% -> 10% of each run, Pallas kernels for 0% -> 0%
where the time goes in v21:
time: 41.6 us; the launch traced here: 41.4 us
  starting transfers between devices  19 us (46%)
  local copies, waits for them, and re-layouts  9.2 us (22%)
  matrix products  5.64 us (14%)
  waiting for transfers between devices  4.99 us (12%)
  other arithmetic  1.61 us (4%)
  between operations  0.95 us (2%)
    ppermute x9, starting transfers between devices, swap_over_req(): lax.ppermute(blocks[hop], 'req', [(i, i ^ hop) for i in range(n_req)])  12.1 us
    ppermute x3, starting transfers between devices, gather_over_cand(): lax.ppermute(rows, 'cand', [(i, i ^ hop) for i in range(n_cand)])  6.14 us
    gather x1, local copies, waits for them, and re-layouts, body(): jnp.take(table, asked.reshape(-1), axis=0, mode='clip')  5.96 us
    ppermute x3, waiting for transfers between devices, gather_over_cand(): lax.ppermute(rows, 'cand', [(i, i ^ hop) for i in range(n_cand)])  3.14 us
    dot_general x1, matrix products, body(): jnp.dot(hidden, tower_out, preferred_element_type=jnp.float32)[None, :]  2.24 us
    unnamed x6, local copies, waits for them, and re-layouts  1.61 us
    dot_general x1, matrix products, attend(): jnp.einsum('bgo,ogl->bgl', gates, values, preferred_element_type=jnp.floa...  1.32 us
    ppermute x9, waiting for transfers between devices, swap_over_req(): lax.ppermute(blocks[hop], 'req', [(i, i ^ hop) for i in range(n_req)])  0.99 us
  transfers between devices with their start and end apart: 16, of which 6 were waited for; matrix products, arithmetic and copies ran while one was open for 10% of the time, Pallas kernels for 0%

profile of v21, /device:TPU:0, one launch (start us, length us, event | category | flops | bytes accessed | tf_op | source)
XLA Modules:
  0.0 41.4 jit_solution(10554782279886866438)
XLA Ops:
  0.0 0.7 %pad_add_fusion.1 = s32[768]{0:T(1024)S(1)} fusion(s32[256]{0:T(256)} %bitcast.101, s32[256]{0:T(256)} %bitcast.102, s32[128]{0:T(128)} %bitcast.103, s32[128]{0:T(128)} %bitcast.104), kind=kLoop, calls=%fused_computation.56 | loop fusion | flops 2304 | bytes 6144 | tf_op jit(solution)/shard_map/concatenate | solution.py:101
  1.0 0.2 convert_reduce_fusion
  1.4 0.3 convolution_convert_fusion.5
  1.8 3.0 %collective-permute-start = (s32[320]{0:T(512)S(1)}, s32[320]{0:T(512)S(1)}, u32[]{:S(2)}, u32[]{:S(2)}) collective-permute-start(s32[320]{0:T(512)S(1)} %get-tuple-element.5), channel_id=1, source_target_pairs={{0,8},{8,0},{16,24},{24,16},{1,9},{9,1},{17,25},{25,17},{2,10},{10... | collective-permute-start | bytes 3848 | tf_op jit(solution)/shard_map/ppermute | solution.py:79
  4.8 1.5 %collective-permute-start.2 = (s32[320]{0:T(512)S(1)}, s32[320]{0:T(512)S(1)}, u32[]{:S(2)}, u32[]{:S(2)}) collective-permute-start(s32[320]{0:T(512)S(1)} %get-tuple-element.6), channel_id=1, source_target_pairs={{0,24},{8,16},{16,8},{24,0},{1,25},{9,17},{17,9},{25,1},{2,26},{10... | collective-permute-start | bytes 3848 | tf_op jit(solution)/shard_map/ppermute | solution.py:79
  7.1 0.9 %constant_dynamic-update-slice_fusion.1 = bf16[256,512]{1,0:T(8,128)(2,1)S(1)} fusion(bf16[256,256]{1,0:T(8,128)(2,1)} %param.18), kind=kLoop, calls=%fused_computation.58 | loop fusion | bytes 262144
  8.1 0.9 %constant_dynamic-update-slice_fusion = bf16[256,512]{1,0:T(8,128)(2,1)S(1)} fusion(bf16[256,512]{1,0:T(8,128)(2,1)S(1)} %constant_dynamic-update-slice_fusion.1, bf16[256,256]{1,0:T(8,128)(2,1)} %param.19), kind=kLoop, calls=%fused_computation.57 | loop fusion | bytes 262144 | tf_op jit(solution)/shard_map/concatenate | solution.py:130
  9.1 0.7 %reshape.136 = bf16[1024,1]{0,1:T(2,128)(2,1)S(1)} reshape(bf16[1024]{0:T(1024)(128)(2,1)} %param.21) | data formatting | bytes 4096 | tf_op args[10]
  10.0 6.0 %gather_fusion = bf16[1280,256]{1,0:T(8,128)(2,1)S(1)} fusion(bf16[8192,256]{1,0:T(8,128)(2,1)} %param.11, s32[2048]{0:T(1024)S(1)} %pad_clamp_fusion), kind=kCustom, calls=%fused_computation | custom fusion | bytes 1315840 | tf_op jit(solution)/shard_map/jit(_take)/gather | solution.py:120
  16.0 3.0 %collective-permute-start.8 = (bf16[128,256]{1,0:T(8,128)(2,1)S(1)}, bf16[128,256]{1,0:T(8,128)(2,1)S(1)}, u32[]{:S(2)}, u32[]{:S(2)}) collective-permute-start(bf16[128,256]{1,0:T(8,128)(2,1)S(1)} %get-tuple-element.13), channel_id=1, source_target_pairs={{0,24},{8,16},{16,8},{24,0},{1,25},{9,17},{17,9},{25,1},{2,26},{10... | collective-permute-start | bytes 196616 | tf_op jit(solution)/shard_map/ppermute | solution.py:79
  18.9 0.5 %collective-permute-start.7 = (bf16[128,256]{1,0:T(8,128)(2,1)S(1)}, bf16[128,256]{1,0:T(8,128)(2,1)S(1)}, u32[]{:S(2)}, u32[]{:S(2)}) collective-permute-start(bf16[128,256]{1,0:T(8,128)(2,1)S(1)} %get-tuple-element.14), channel_id=1, source_target_pairs={{0,16},{8,24},{16,0},{24,8},{1,17},{9,25},{17,1},{25,9},{2,18},{10... | collective-permute-start | bytes 196616 | tf_op jit(solution)/shard_map/ppermute | solution.py:79
  19.6 2.9 %collective-permute-start.5 = (bf16[192,256]{1,0:T(8,128)(2,1)S(1)}, bf16[192,256]{1,0:T(8,128)(2,1)S(1)}, u32[]{:S(2)}, u32[]{:S(2)}) collective-permute-start(bf16[192,256]{1,0:T(8,128)(2,1)S(1)} %get-tuple-element.17), channel_id=1, source_target_pairs={{0,24},{8,16},{16,8},{24,0},{1,25},{9,17},{17,9},{25,1},{2,26},{10... | collective-permute-start | bytes 294920 | tf_op jit(solution)/shard_map/ppermute | solution.py:79
  22.5 0.5 %collective-permute-start.4 = (bf16[192,256]{1,0:T(8,128)(2,1)S(1)}, bf16[192,256]{1,0:T(8,128)(2,1)S(1)}, u32[]{:S(2)}, u32[]{:S(2)}) collective-permute-start(bf16[192,256]{1,0:T(8,128)(2,1)S(1)} %get-tuple-element.18), channel_id=1, source_target_pairs={{0,16},{8,24},{16,0},{24,8},{1,17},{9,25},{17,1},{25,9},{2,18},{10... | collective-permute-start | bytes 294920 | tf_op jit(solution)/shard_map/ppermute | solution.py:79
  23.0 0.6 %collective-permute-start.3 = (bf16[192,256]{1,0:T(8,128)(2,1)S(1)}, bf16[192,256]{1,0:T(8,128)(2,1)S(1)}, u32[]{:S(2)}, u32[]{:S(2)}) collective-permute-start(bf16[192,256]{1,0:T(8,128)(2,1)S(1)} %get-tuple-element.19), channel_id=1, source_target_pairs={{0,8},{8,0},{16,24},{24,16},{1,9},{9,1},{17,25},{25,17},{2,10},{10... | collective-permute-start | bytes 294920 | tf_op jit(solution)/shard_map/ppermute | solution.py:79
  23.6 0.9 %collective-permute-done.7 = bf16[128,256]{1,0:T(8,128)(2,1)S(1)} collective-permute-done((bf16[128,256]{1,0:T(8,128)(2,1)S(1)}, bf16[128,256]{1,0:T(8,128)(2,1)S(1)}, u32[]{:S(2)}, u32[]{:S(2)}) %collective-permute-start.7) | collective-permute-done | bytes 65568 | tf_op jit(solution)/shard_map/ppermute | solution.py:79
  24.6 0.2 convolution_convert_fusion.4
  24.9 3.9 %collective-permute-start.11 = (bf16[128,256]{1,0:T(8,128)(2,1)S(1)}, bf16[128,256]{1,0:T(8,128)(2,1)S(1)}, u32[]{:S(2)}, u32[]{:S(2)}) collective-permute-start(bf16[128,256]{1,0:T(8,128)(2,1)S(1)} %convolution_convert_fusion.4), channel_id=1, source_target_pairs={{0,6},{1,7},{2,4},{3,5},{4,2},{5,3},{6,0},{7,1},{8,14},{9,15},{10,... | collective-permute-start | bytes 196616 | tf_op jit(solution)/shard_map/ppermute | solution.py:33
  28.8 0.7 %collective-permute-start.10 = (bf16[128,256]{1,0:T(8,128)(2,1)S(1)}, bf16[128,256]{1,0:T(8,128)(2,1)S(1)}, u32[]{:S(2)}, u32[]{:S(2)}) collective-permute-start(bf16[128,256]{1,0:T(8,128)(2,1)S(1)} %convolution_convert_fusion.4), channel_id=1, source_target_pairs={{0,4},{1,5},{2,6},{3,7},{4,0},{5,1},{6,2},{7,3},{8,12},{9,13},{10,... | collective-permute-start | bytes 196616 | tf_op jit(solution)/shard_map/ppermute | solution.py:33
  29.4 1.6 %collective-permute-start.9 = (bf16[128,256]{1,0:T(8,128)(2,1)S(1)}, bf16[128,256]{1,0:T(8,128)(2,1)S(1)}, u32[]{:S(2)}, u32[]{:S(2)}) collective-permute-start(bf16[128,256]{1,0:T(8,128)(2,1)S(1)} %convolution_convert_fusion.4), channel_id=1, source_target_pairs={{0,2},{1,3},{2,0},{3,1},{4,6},{5,7},{6,4},{7,5},{8,10},{9,11},{10,... | collective-permute-start | bytes 196616 | tf_op jit(solution)/shard_map/ppermute | solution.py:33
  31.1 0.3 convolution_convert_fusion.2
  31.4 0.3 fusion.13
  31.7 0.2 convolution_convert_fusion.3
  32.0 3.0 %collective-permute-done.10 = bf16[128,256]{1,0:T(8,128)(2,1)S(1)} collective-permute-done((bf16[128,256]{1,0:T(8,128)(2,1)S(1)}, bf16[128,256]{1,0:T(8,128)(2,1)S(1)}, u32[]{:S(2)}, u32[]{:S(2)}) %collective-permute-start.10) | collective-permute-done | bytes 65568 | tf_op jit(solution)/shard_map/ppermute | solution.py:33
  35.2 0.5 %collective-permute-start.14 = (bf16[128,256]{1,0:T(8,128)(2,1)S(1)}, bf16[128,256]{1,0:T(8,128)(2,1)S(1)}, u32[]{:S(2)}, u32[]{:S(2)}) collective-permute-start(bf16[128,256]{1,0:T(8,128)(2,1)S(1)} %collective-permute-done.10), channel_id=1, source_target_pairs={{0,1},{1,0},{2,3},{3,2},{4,5},{5,4},{6,7},{7,6},{8,9},{9,8},{10,11... | collective-permute-start | bytes 196616 | tf_op jit(solution)/shard_map/ppermute | solution.py:35
  35.8 0.3 convolution_convert_fusion.1
  36.1 0.4 collective-permute-done.15
  36.6 0.4 collective-permute-done.13
  37.0 0.3 convolution_convert_fusion
  37.4 0.2 copy.16
  37.6 0.2 copy.15
  37.8 1.3 %fusion.5 = bf16[4,64,256]{2,1,0:T(8,128)(2,1)S(1)} fusion(bf16[1024,4,64]{0,2,1:T(8,128)(2,1)S(1)} %bitcast.83, bf16[1024,4,64]{0,2,1:T(8,128)(2,1)S(1)} %bitcast.82, bf16[256,4,64]{0,2,1:T(8,128)(2,1)S(1)} %bitcast.86, pred[1024]{0:T(1024)(128)(4,1)S(1)} %fusion.21, f32[]{:T(128)S(6)} %sqrt.3), kind=kOutput, calls=%fused_computation.13 | convolution fusion | flops 273809408 | bytes 1311748 | tf_op jit(solution)/shard_map/bgo,ogl->bgl/dot_general | solution.py:63
  39.1 2.2 %fusion.8 = f32[1,256]{1,0:T(1,128)} fusion(bf16[1024,1]{0,1:T(2,128)(2,1)S(1)} %reshape.136, f32[256,1024]{1,0:T(8,128)S(1)} %fusion.13, bf16[256,256]{0,1:T(8,128)(2,1)S(1)} %bitcast.105, bf16[512,1024]{1,0:T(8,128)(2,1)} %param.20), kind=kOutput, calls=%fused_computation.17 | convolution fusion | flops 136314880 | bytes 1707008 | tf_op jit(solution)/shard_map/dot_general | solution.py:153
  (51 shorter events, 2.0 us)
Async XLA Ops:
  0.0 31.7 %copy-start = (bf16[256,256]{1,0:T(8,128)(2,1)S(1)}, bf16[256,256]{1,0:T(8,128)(2,1)}, u32[]{:S(2)}) copy-start(bf16[256,256]{1,0:T(8,128)(2,1)} %param.17) | copy-start | bytes 393220
  1.8 8.0 %collective-permute-start = (s32[320]{0:T(512)S(1)}, s32[320]{0:T(512)S(1)}, u32[]{:S(2)}, u32[]{:S(2)}) collective-permute-start(s32[320]{0:T(512)S(1)} %get-tuple-element.5), channel_id=1, source_target_pairs={{0,8},{8,0},{16,24},{24,16},{1,9},{9,1},{17,25},{25,17},{2,10},{10... | collective-permute-start | bytes 3848 | tf_op jit(solution)/shard_map/ppermute | solution.py:79
  4.8 5.0 %collective-permute-start.2 = (s32[320]{0:T(512)S(1)}, s32[320]{0:T(512)S(1)}, u32[]{:S(2)}, u32[]{:S(2)}) collective-permute-start(s32[320]{0:T(512)S(1)} %get-tuple-element.6), channel_id=1, source_target_pairs={{0,24},{8,16},{16,8},{24,0},{1,25},{9,17},{17,9},{25,1},{2,26},{10... | collective-permute-start | bytes 3848 | tf_op jit(solution)/shard_map/ppermute | solution.py:79
  6.3 3.6 %collective-permute-start.1 = (s32[320]{0:T(512)S(1)}, s32[320]{0:T(512)S(1)}, u32[]{:S(2)}, u32[]{:S(2)}) collective-permute-start(s32[320]{0:T(512)S(1)} %get-tuple-element.7), channel_id=1, source_target_pairs={{0,16},{8,24},{16,0},{24,8},{1,17},{9,25},{17,1},{25,9},{2,18},{10... | collective-permute-start | bytes 3848 | tf_op jit(solution)/shard_map/ppermute | solution.py:79
  10.0 21.4 %copy-start.1 = (bf16[512,1024]{1,0:T(8,128)(2,1)S(1)}, bf16[512,1024]{1,0:T(8,128)(2,1)}, u32[]{:S(2)}) copy-start(bf16[512,1024]{1,0:T(8,128)(2,1)} %param.20) | copy-start | bytes 3145732
  16.0 7.1 %collective-permute-start.8 = (bf16[128,256]{1,0:T(8,128)(2,1)S(1)}, bf16[128,256]{1,0:T(8,128)(2,1)S(1)}, u32[]{:S(2)}, u32[]{:S(2)}) collective-permute-start(bf16[128,256]{1,0:T(8,128)(2,1)S(1)} %get-tuple-element.13), channel_id=1, source_target_pairs={{0,24},{8,16},{16,8},{24,0},{1,25},{9,17},{17,9},{25,1},{2,26},{10... | collective-permute-start | bytes 196616 | tf_op jit(solution)/shard_map/ppermute | solution.py:79
  18.9 5.6 %collective-permute-start.7 = (bf16[128,256]{1,0:T(8,128)(2,1)S(1)}, bf16[128,256]{1,0:T(8,128)(2,1)S(1)}, u32[]{:S(2)}, u32[]{:S(2)}) collective-permute-start(bf16[128,256]{1,0:T(8,128)(2,1)S(1)} %get-tuple-element.14), channel_id=1, source_target_pairs={{0,16},{8,24},{16,0},{24,8},{1,17},{9,25},{17,1},{25,9},{2,18},{10... | collective-permute-start | bytes 196616 | tf_op jit(solution)/shard_map/ppermute | solution.py:79
  19.4 5.1 %collective-permute-start.6 = (bf16[128,256]{1,0:T(8,128)(2,1)S(1)}, bf16[128,256]{1,0:T(8,128)(2,1)S(1)}, u32[]{:S(2)}, u32[]{:S(2)}) collective-permute-start(bf16[128,256]{1,0:T(8,128)(2,1)S(1)} %get-tuple-element.15), channel_id=1, source_target_pairs={{0,8},{8,0},{16,24},{24,16},{1,9},{9,1},{17,25},{25,17},{2,10},{10... | collective-permute-start | bytes 196616 | tf_op jit(solution)/shard_map/ppermute | solution.py:79
  19.6 9.2 %collective-permute-start.5 = (bf16[192,256]{1,0:T(8,128)(2,1)S(1)}, bf16[192,256]{1,0:T(8,128)(2,1)S(1)}, u32[]{:S(2)}, u32[]{:S(2)}) collective-permute-start(bf16[192,256]{1,0:T(8,128)(2,1)S(1)} %get-tuple-element.17), channel_id=1, source_target_pairs={{0,24},{8,16},{16,8},{24,0},{1,25},{9,17},{17,9},{25,1},{2,26},{10... | collective-permute-start | bytes 294920 | tf_op jit(solution)/shard_map/ppermute | solution.py:79
  22.5 6.9 %collective-permute-start.4 = (bf16[192,256]{1,0:T(8,128)(2,1)S(1)}, bf16[192,256]{1,0:T(8,128)(2,1)S(1)}, u32[]{:S(2)}, u32[]{:S(2)}) collective-permute-start(bf16[192,256]{1,0:T(8,128)(2,1)S(1)} %get-tuple-element.18), channel_id=1, source_target_pairs={{0,16},{8,24},{16,0},{24,8},{1,17},{9,25},{17,1},{25,9},{2,18},{10... | collective-permute-start | bytes 294920 | tf_op jit(solution)/shard_map/ppermute | solution.py:79
  23.0 8.0 %collective-permute-start.3 = (bf16[192,256]{1,0:T(8,128)(2,1)S(1)}, bf16[192,256]{1,0:T(8,128)(2,1)S(1)}, u32[]{:S(2)}, u32[]{:S(2)}) collective-permute-start(bf16[192,256]{1,0:T(8,128)(2,1)S(1)} %get-tuple-element.19), channel_id=1, source_target_pairs={{0,8},{8,0},{16,24},{24,16},{1,9},{9,1},{17,25},{25,17},{2,10},{10... | collective-permute-start | bytes 294920 | tf_op jit(solution)/shard_map/ppermute | solution.py:79
  24.8 11.3 %collective-permute-start.12 = (bf16[128,256]{1,0:T(8,128)(2,1)S(1)}, bf16[128,256]{1,0:T(8,128)(2,1)S(1)}, u32[]{:S(2)}, u32[]{:S(2)}) collective-permute-start(bf16[128,256]{1,0:T(8,128)(2,1)S(1)} %convolution_convert_fusion.4), channel_id=1, source_target_pairs={{0,1},{1,0},{2,3},{3,2},{4,5},{5,4},{6,7},{7,6},{8,9},{9,8},{10,11... | collective-permute-start | bytes 196616 | tf_op jit(solution)/shard_map/ppermute | solution.py:35
  24.9 7.1 %collective-permute-start.11 = (bf16[128,256]{1,0:T(8,128)(2,1)S(1)}, bf16[128,256]{1,0:T(8,128)(2,1)S(1)}, u32[]{:S(2)}, u32[]{:S(2)}) collective-permute-start(bf16[128,256]{1,0:T(8,128)(2,1)S(1)} %convolution_convert_fusion.4), channel_id=1, source_target_pairs={{0,6},{1,7},{2,4},{3,5},{4,2},{5,3},{6,0},{7,1},{8,14},{9,15},{10,... | collective-permute-start | bytes 196616 | tf_op jit(solution)/shard_map/ppermute | solution.py:33
  28.8 6.2 %collective-permute-start.10 = (bf16[128,256]{1,0:T(8,128)(2,1)S(1)}, bf16[128,256]{1,0:T(8,128)(2,1)S(1)}, u32[]{:S(2)}, u32[]{:S(2)}) collective-permute-start(bf16[128,256]{1,0:T(8,128)(2,1)S(1)} %convolution_convert_fusion.4), channel_id=1, source_target_pairs={{0,4},{1,5},{2,6},{3,7},{4,0},{5,1},{6,2},{7,3},{8,12},{9,13},{10,... | collective-permute-start | bytes 196616 | tf_op jit(solution)/shard_map/ppermute | solution.py:33
  29.4 5.7 %collective-permute-start.9 = (bf16[128,256]{1,0:T(8,128)(2,1)S(1)}, bf16[128,256]{1,0:T(8,128)(2,1)S(1)}, u32[]{:S(2)}, u32[]{:S(2)}) collective-permute-start(bf16[128,256]{1,0:T(8,128)(2,1)S(1)} %convolution_convert_fusion.4), channel_id=1, source_target_pairs={{0,2},{1,3},{2,0},{3,1},{4,6},{5,7},{6,4},{7,5},{8,10},{9,11},{10,... | collective-permute-start | bytes 196616 | tf_op jit(solution)/shard_map/ppermute | solution.py:33
  35.2 1.3 %collective-permute-start.15 = (bf16[128,256]{1,0:T(8,128)(2,1)S(1)}, bf16[128,256]{1,0:T(8,128)(2,1)S(1)}, u32[]{:S(2)}, u32[]{:S(2)}) collective-permute-start(bf16[128,256]{1,0:T(8,128)(2,1)S(1)} %collective-permute-done.11), channel_id=1, source_target_pairs={{0,1},{1,0},{2,3},{3,2},{4,5},{5,4},{6,7},{7,6},{8,9},{9,8},{10,11... | collective-permute-start | bytes 196616 | tf_op jit(solution)/shard_map/ppermute | solution.py:35
  35.2 1.4 %collective-permute-start.14 = (bf16[128,256]{1,0:T(8,128)(2,1)S(1)}, bf16[128,256]{1,0:T(8,128)(2,1)S(1)}, u32[]{:S(2)}, u32[]{:S(2)}) collective-permute-start(bf16[128,256]{1,0:T(8,128)(2,1)S(1)} %collective-permute-done.10), channel_id=1, source_target_pairs={{0,1},{1,0},{2,3},{3,2},{4,5},{5,4},{6,7},{7,6},{8,9},{9,8},{10,11... | collective-permute-start | bytes 196616 | tf_op jit(solution)/shard_map/ppermute | solution.py:35
  35.7 1.3 %collective-permute-start.13 = (bf16[128,256]{1,0:T(8,128)(2,1)S(1)}, bf16[128,256]{1,0:T(8,128)(2,1)S(1)}, u32[]{:S(2)}, u32[]{:S(2)}) collective-permute-start(bf16[128,256]{1,0:T(8,128)(2,1)S(1)} %collective-permute-done.9), channel_id=1, source_target_pairs={{0,1},{1,0},{2,3},{3,2},{4,5},{5,4},{6,7},{7,6},{8,9},{9,8},{10,11... | collective-permute-start | bytes 196616 | tf_op jit(solution)/shard_map/ppermute | solution.py:35

commit v22 on v17

--- a/solution.py
+++ b/solution.py
@@ -107,12 +107,21 @@
     cand_cap = 3 * cand_dev // n_dest
     assert n_dest & (n_dest - 1) == 0
     me = lax.axis_index("req")
-    hist_slot = slot_index(hist_shards ^ me, hist_cap)
-    cand_slot = slot_index(cand_shards ^ me, cand_cap)
+    shards = jnp.concatenate([hist_shards, cand_shards]) ^ me
+    in_hist = jnp.arange(hist_dev + cand_dev, dtype=jnp.int32) < hist_dev
+    earlier = lax.broadcasted_iota(jnp.int32, (shards.shape[0],) * 2, 1) < lax.broadcasted_iota(
+        jnp.int32, (shards.shape[0],) * 2, 0
+    )
+    same = (shards[:, None] == shards[None, :]) & (in_hist[:, None] == in_hist[None, :]) & earlier
+    rank = jnp.sum(same.astype(jnp.int32), axis=1)
+    hist_slot = (shards * hist_cap + rank)[:hist_dev]
+    cand_slot = (shards * cand_cap + rank)[hist_dev:]
     hist_pick = select_rows(hist_slot, n_dest * hist_cap)
     cand_pick = select_rows(cand_slot, n_dest * cand_cap)
-    hist_wanted = wanted_rows(hist_slot, n_dest * hist_cap, hist_rows).reshape(n_dest, hist_cap)
-    cand_wanted = wanted_rows(cand_slot, n_dest * cand_cap, cand_rows).reshape(n_dest, cand_cap)
+    joint_slot = jnp.concatenate([hist_slot, cand_slot + n_dest * hist_cap])
+    joint_wanted = wanted_rows(joint_slot, n_dest * (hist_cap + cand_cap), jnp.concatenate([hist_rows, cand_rows]))
+    hist_wanted = joint_wanted[: n_dest * hist_cap].reshape(n_dest, hist_cap)
+    cand_wanted = joint_wanted[n_dest * hist_cap :].reshape(n_dest, cand_cap)
     asked = swap_over_req(jnp.concatenate([hist_wanted, cand_wanted], axis=1))
     fetched = jnp.take(table, asked.reshape(-1), axis=0, mode="clip").reshape(
         n_dest, hist_cap + cand_cap, d_model

time: 37.7 us -> 37.7 us (level)
  no operation moved by 1% of the time
where the time goes in v22:
time: 37.7 us; the launch traced here: 37.5 us
  starting transfers between devices  17.1 us (45%)
  local copies, waits for them, and re-layouts  7.1 us (19%)
  waiting for transfers between devices  6.47 us (17%)
  matrix products  4.52 us (12%)
  other arithmetic  1.39 us (4%)
  between operations  0.99 us (3%)
    ppermute x9, starting transfers between devices, swap_over_req(): lax.ppermute(blocks[hop], 'req', [(i, i ^ hop) for i in range(n_req)])  12 us
    gather x1, local copies, waits for them, and re-layouts, body(): jnp.take(table, asked.reshape(-1), axis=0, mode='clip')  5.96 us
    ppermute x3, starting transfers between devices, gather_over_cand(): lax.ppermute(rows, 'cand', [(i, i ^ hop) for i in range(n_cand)])  4.52 us
    ppermute x3, waiting for transfers between devices, gather_over_cand(): lax.ppermute(rows, 'cand', [(i, i ^ hop) for i in range(n_cand)])  3.56 us
    ppermute x9, waiting for transfers between devices, swap_over_req(): lax.ppermute(blocks[hop], 'req', [(i, i ^ hop) for i in range(n_req)])  2.05 us
    dot_general x1, matrix products, attend(): jnp.einsum('bgo,ogl->bgl', gates, values, preferred_element_type=jnp.floa...  1.32 us
    dot_general x1, matrix products, body(): jnp.dot(hidden, tower_out, preferred_element_type=jnp.float32)[None, :]  1.2 us
    ppermute x4, waiting for transfers between devices, gather_over_cand(): lax.ppermute(block, 'cand', [(i, i ^ 1) for i in range(n_cand)])  0.86 us
  transfers between devices with their start and end apart: 16, of which 7 were waited for; matrix products, arithmetic and copies ran while one was open for 6% of the time, Pallas kernels for 0%

profile of v22, /device:TPU:0, one launch (start us, length us, event | category | flops | bytes accessed | tf_op | source)
XLA Modules:
  0.0 37.5 jit_solution(12146748177654925797)
XLA Ops:
  0.0 0.7 %pad_add_fusion.1 = s32[768]{0:T(1024)S(1)} fusion(s32[256]{0:T(256)} %bitcast.96, s32[256]{0:T(256)} %bitcast.97, s32[128]{0:T(128)} %bitcast.98, s32[128]{0:T(128)} %bitcast.99), kind=kLoop, calls=%fused_computation.58 | loop fusion | flops 2304 | bytes 6144 | tf_op jit(solution)/shard_map/concatenate | solution.py:98
  0.8 0.3 convert_reduce_fusion
  1.1 0.4 %convolution_convert_fusion = s32[1280,2]{0,1:T(2,128)S(1)} fusion(s32[384]{0:T(512)S(1)} %pad_add_fusion.2, bf16[384,1]{0,1:T(2,128)(2,1)S(1)} %fusion.22, bf16[384,1]{0,1:T(2,128)(2,1)S(1)} %get-tuple-element.8), kind=kOutput, calls=%fused_computation.2 | convolution fusion | flops 2463232 | bytes 13312 | tf_op jit(solution)/shard_map/dot_general | solution.py:68
  1.7 3.0 %collective-permute-start = (s32[320]{0:T(512)S(1)}, s32[320]{0:T(512)S(1)}, u32[]{:S(2)}, u32[]{:S(2)}) collective-permute-start(s32[320]{0:T(512)S(1)} %get-tuple-element.5), channel_id=1, source_target_pairs={{0,8},{8,0},{16,24},{24,16},{1,9},{9,1},{17,25},{25,17},{2,10},{10... | collective-permute-start | bytes 3848 | tf_op jit(solution)/shard_map/ppermute | solution.py:76
  4.8 1.5 %collective-permute-start.2 = (s32[320]{0:T(512)S(1)}, s32[320]{0:T(512)S(1)}, u32[]{:S(2)}, u32[]{:S(2)}) collective-permute-start(s32[320]{0:T(512)S(1)} %get-tuple-element.6), channel_id=1, source_target_pairs={{0,24},{8,16},{16,8},{24,0},{1,25},{9,17},{17,9},{25,1},{2,26},{10... | collective-permute-start | bytes 3848 | tf_op jit(solution)/shard_map/ppermute | solution.py:76
  6.9 0.1 add_xor_fusion.1
  7.0 0.1 concatenate.102
  7.2 0.7 %reshape.370 = bf16[1024,1]{0,1:T(2,128)(2,1)S(1)} reshape(bf16[1024]{0:T(1024)(128)(2,1)} %param.21) | data formatting | bytes 4096 | tf_op args[10]
  7.9 1.3 %collective-permute-done.2 = s32[320]{0:T(512)S(1)} collective-permute-done((s32[320]{0:T(512)S(1)}, s32[320]{0:T(512)S(1)}, u32[]{:S(2)}, u32[]{:S(2)}) %collective-permute-start.2) | collective-permute-done | bytes 1312 | tf_op jit(solution)/shard_map/ppermute | solution.py:76
  9.2 0.6 %collective-permute-done.1 = s32[320]{0:T(512)S(1)} collective-permute-done((s32[320]{0:T(512)S(1)}, s32[320]{0:T(512)S(1)}, u32[]{:S(2)}, u32[]{:S(2)}) %collective-permute-start.1) | collective-permute-done | bytes 1312 | tf_op jit(solution)/shard_map/ppermute | solution.py:76
  9.8 0.1 reshape.363
  9.9 6.0 %gather_fusion = bf16[1280,256]{1,0:T(8,128)(2,1)S(1)} fusion(bf16[8192,256]{1,0:T(8,128)(2,1)} %param.11, s32[2048]{0:T(1024)S(1)} %pad_clamp_fusion), kind=kCustom, calls=%fused_computation | custom fusion | bytes 1315840 | tf_op jit(solution)/shard_map/jit(_take)/gather | solution.py:126
  16.0 1.5 %collective-permute-start.8 = (bf16[128,256]{1,0:T(8,128)(2,1)S(1)}, bf16[128,256]{1,0:T(8,128)(2,1)S(1)}, u32[]{:S(2)}, u32[]{:S(2)}) collective-permute-start(bf16[128,256]{1,0:T(8,128)(2,1)S(1)} %get-tuple-element.13), channel_id=1, source_target_pairs={{0,24},{8,16},{16,8},{24,0},{1,25},{9,17},{17,9},{25,1},{2,26},{10... | collective-permute-start | bytes 196616 | tf_op jit(solution)/shard_map/ppermute | solution.py:76
  17.5 1.5 %collective-permute-start.7 = (bf16[128,256]{1,0:T(8,128)(2,1)S(1)}, bf16[128,256]{1,0:T(8,128)(2,1)S(1)}, u32[]{:S(2)}, u32[]{:S(2)}) collective-permute-start(bf16[128,256]{1,0:T(8,128)(2,1)S(1)} %get-tuple-element.14), channel_id=1, source_target_pairs={{0,16},{8,24},{16,0},{24,8},{1,17},{9,25},{17,1},{25,9},{2,18},{10... | collective-permute-start | bytes 196616 | tf_op jit(solution)/shard_map/ppermute | solution.py:76
  19.0 0.5 %collective-permute-start.6 = (bf16[128,256]{1,0:T(8,128)(2,1)S(1)}, bf16[128,256]{1,0:T(8,128)(2,1)S(1)}, u32[]{:S(2)}, u32[]{:S(2)}) collective-permute-start(bf16[128,256]{1,0:T(8,128)(2,1)S(1)} %get-tuple-element.15), channel_id=1, source_target_pairs={{0,8},{8,0},{16,24},{24,16},{1,9},{9,1},{17,25},{25,17},{2,10},{10... | collective-permute-start | bytes 196616 | tf_op jit(solution)/shard_map/ppermute | solution.py:76
  19.5 1.5 %collective-permute-start.5 = (bf16[192,256]{1,0:T(8,128)(2,1)S(1)}, bf16[192,256]{1,0:T(8,128)(2,1)S(1)}, u32[]{:S(2)}, u32[]{:S(2)}) collective-permute-start(bf16[192,256]{1,0:T(8,128)(2,1)S(1)} %get-tuple-element.17), channel_id=1, source_target_pairs={{0,24},{8,16},{16,8},{24,0},{1,25},{9,17},{17,9},{25,1},{2,26},{10... | collective-permute-start | bytes 294920 | tf_op jit(solution)/shard_map/ppermute | solution.py:76
  21.0 1.5 %collective-permute-start.4 = (bf16[192,256]{1,0:T(8,128)(2,1)S(1)}, bf16[192,256]{1,0:T(8,128)(2,1)S(1)}, u32[]{:S(2)}, u32[]{:S(2)}) collective-permute-start(bf16[192,256]{1,0:T(8,128)(2,1)S(1)} %get-tuple-element.18), channel_id=1, source_target_pairs={{0,16},{8,24},{16,0},{24,8},{1,17},{9,25},{17,1},{25,9},{2,18},{10... | collective-permute-start | bytes 294920 | tf_op jit(solution)/shard_map/ppermute | solution.py:76
  22.6 0.9 %collective-permute-start.3 = (bf16[192,256]{1,0:T(8,128)(2,1)S(1)}, bf16[192,256]{1,0:T(8,128)(2,1)S(1)}, u32[]{:S(2)}, u32[]{:S(2)}) collective-permute-start(bf16[192,256]{1,0:T(8,128)(2,1)S(1)} %get-tuple-element.19), channel_id=1, source_target_pairs={{0,8},{8,0},{16,24},{24,16},{1,9},{9,1},{17,25},{25,17},{2,10},{10... | collective-permute-start | bytes 294920 | tf_op jit(solution)/shard_map/ppermute | solution.py:76
  23.5 0.1 collective-permute-done.6
  23.7 0.2 bitcast_dynamic-update-slice_fusion.7
  23.9 3.9 %collective-permute-start.11 = (bf16[128,256]{1,0:T(8,128)(2,1)S(1)}, bf16[128,256]{1,0:T(8,128)(2,1)S(1)}, u32[]{:S(2)}, u32[]{:S(2)}) collective-permute-start(bf16[128,256]{1,0:T(8,128)(2,1)S(1)} %get-tuple-element.30), channel_id=1, source_target_pairs={{0,6},{1,7},{2,4},{3,5},{4,2},{5,3},{6,0},{7,1},{8,14},{9,15},{10,... | collective-permute-start | bytes 196616 | tf_op jit(solution)/shard_map/ppermute | solution.py:33
  27.8 0.6 %collective-permute-start.9 = (bf16[128,256]{1,0:T(8,128)(2,1)S(1)}, bf16[128,256]{1,0:T(8,128)(2,1)S(1)}, u32[]{:S(2)}, u32[]{:S(2)}) collective-permute-start(bf16[128,256]{1,0:T(8,128)(2,1)S(1)} %get-tuple-element.30), channel_id=1, source_target_pairs={{0,2},{1,3},{2,0},{3,1},{4,6},{5,7},{6,4},{7,5},{8,10},{9,11},{10,... | collective-permute-start | bytes 196616 | tf_op jit(solution)/shard_map/ppermute | solution.py:33
  28.5 0.3 convolution_convert_fusion.2
  28.8 0.3 fusion.14
  29.2 0.2 convolution_convert_fusion.3
  29.4 0.8 %collective-permute-done.11 = bf16[128,256]{1,0:T(8,128)(2,1)S(1)} collective-permute-done((bf16[128,256]{1,0:T(8,128)(2,1)S(1)}, bf16[128,256]{1,0:T(8,128)(2,1)S(1)}, u32[]{:S(2)}, u32[]{:S(2)}) %collective-permute-start.11) | collective-permute-done | bytes 65568 | tf_op jit(solution)/shard_map/ppermute | solution.py:33
  30.2 2.8 %collective-permute-done.10 = bf16[128,256]{1,0:T(8,128)(2,1)S(1)} collective-permute-done((bf16[128,256]{1,0:T(8,128)(2,1)S(1)}, bf16[128,256]{1,0:T(8,128)(2,1)S(1)}, u32[]{:S(2)}, u32[]{:S(2)}) %collective-permute-start.10) | collective-permute-done | bytes 65568 | tf_op jit(solution)/shard_map/ppermute | solution.py:33
  33.0 0.5 %collective-permute-start.13 = (bf16[128,256]{1,0:T(8,128)(2,1)S(1)}, bf16[128,256]{1,0:T(8,128)(2,1)S(1)}, u32[]{:S(2)}, u32[]{:S(2)}) collective-permute-start(bf16[128,256]{1,0:T(8,128)(2,1)S(1)} %collective-permute-done.9), channel_id=1, source_target_pairs={{0,1},{1,0},{2,3},{3,2},{4,5},{5,4},{6,7},{7,6},{8,9},{9,8},{10,11... | collective-permute-start | bytes 196616 | tf_op jit(solution)/shard_map/ppermute | solution.py:35
  33.5 0.8 %collective-permute-done.13 = bf16[128,256]{1,0:T(8,128)(2,1)S(1)} collective-permute-done((bf16[128,256]{1,0:T(8,128)(2,1)S(1)}, bf16[128,256]{1,0:T(8,128)(2,1)S(1)}, u32[]{:S(2)}, u32[]{:S(2)}) %collective-permute-start.13) | collective-permute-done | bytes 65568 | tf_op jit(solution)/shard_map/ppermute | solution.py:35
  34.4 0.5 %convolution_convert_fusion.1 = bf16[1024,512]{0,1:T(8,128)(2,1)S(1)} fusion(bf16[1024,256]{1,0:T(8,128)(2,1)S(1)} %bitcast.83, bf16[256,256]{1,0:T(8,128)(2,1)S(1)} %copy-done.2, bf16[256,256]{1,0:T(8,128)(2,1)S(1)} %copy-done.3), kind=kOutput, calls=%fused_computation.6 | convolution fusion | flops 269484032 | bytes 1835008 | tf_op jit(solution)/shard_map/dot_general | solution.py:48
  35.0 1.3 %fusion.5 = bf16[4,64,256]{2,1,0:T(8,128)(2,1)S(1)} fusion(bf16[1024,4,64]{0,2,1:T(8,128)(2,1)S(1)} %bitcast.85, bf16[1024,4,64]{0,2,1:T(8,128)(2,1)S(1)} %bitcast.84, bf16[256,4,64]{0,2,1:T(8,128)(2,1)S(1)} %bitcast.87, pred[1024]{0:T(1024)(128)(4,1)S(1)} %fusion.21, f32[]{:T(128)S(6)} %sqrt.3), kind=kOutput, calls=%fused_computation.12 | convolution fusion | flops 273809408 | bytes 1311748 | tf_op jit(solution)/shard_map/bgo,ogl->bgl/dot_general | solution.py:60
  36.3 1.2 %fusion.8 = f32[1,256]{1,0:T(1,128)} fusion(bf16[1024,1]{0,1:T(2,128)(2,1)S(1)} %reshape.370, f32[256,1024]{1,0:T(8,128)S(1)} %fusion.14, bf16[256,256]{0,1:T(8,128)(2,1)S(1)} %bitcast.100, bf16[512,1024]{1,0:T(8,128)(2,1)S(1)} %copy-done.1), kind=kOutput, calls=%fused_computation.14 | convolution fusion | flops 136314880 | bytes 1709056 | tf_op jit(solution)/shard_map/dot_general | solution.py:159
  (57 shorter events, 0.7 us)
Async XLA Ops:
  0.0 29.2 %copy-start = (bf16[256,256]{1,0:T(8,128)(2,1)S(1)}, bf16[256,256]{1,0:T(8,128)(2,1)}, u32[]{:S(2)}) copy-start(bf16[256,256]{1,0:T(8,128)(2,1)} %param.17) | copy-start | bytes 393220
  1.7 6.2 %collective-permute-start = (s32[320]{0:T(512)S(1)}, s32[320]{0:T(512)S(1)}, u32[]{:S(2)}, u32[]{:S(2)}) collective-permute-start(s32[320]{0:T(512)S(1)} %get-tuple-element.5), channel_id=1, source_target_pairs={{0,8},{8,0},{16,24},{24,16},{1,9},{9,1},{17,25},{25,17},{2,10},{10... | collective-permute-start | bytes 3848 | tf_op jit(solution)/shard_map/ppermute | solution.py:76
  4.8 4.5 %collective-permute-start.2 = (s32[320]{0:T(512)S(1)}, s32[320]{0:T(512)S(1)}, u32[]{:S(2)}, u32[]{:S(2)}) collective-permute-start(s32[320]{0:T(512)S(1)} %get-tuple-element.6), channel_id=1, source_target_pairs={{0,24},{8,16},{16,8},{24,0},{1,25},{9,17},{17,9},{25,1},{2,26},{10... | collective-permute-start | bytes 3848 | tf_op jit(solution)/shard_map/ppermute | solution.py:76
  6.2 3.6 %collective-permute-start.1 = (s32[320]{0:T(512)S(1)}, s32[320]{0:T(512)S(1)}, u32[]{:S(2)}, u32[]{:S(2)}) collective-permute-start(s32[320]{0:T(512)S(1)} %get-tuple-element.7), channel_id=1, source_target_pairs={{0,16},{8,24},{16,0},{24,8},{1,17},{9,25},{17,1},{25,9},{2,18},{10... | collective-permute-start | bytes 3848 | tf_op jit(solution)/shard_map/ppermute | solution.py:76
  9.9 18.9 %copy-start.1 = (bf16[512,1024]{1,0:T(8,128)(2,1)S(1)}, bf16[512,1024]{1,0:T(8,128)(2,1)}, u32[]{:S(2)}) copy-start(bf16[512,1024]{1,0:T(8,128)(2,1)} %param.20) | copy-start | bytes 3145732
  15.9 18.5 %copy-start.2 = (bf16[256,256]{1,0:T(8,128)(2,1)S(1)}, bf16[256,256]{1,0:T(8,128)(2,1)}, u32[]{:S(2)}) copy-start(bf16[256,256]{1,0:T(8,128)(2,1)} %param.19) | copy-start | bytes 393220
  15.9 18.5 %copy-start.3 = (bf16[256,256]{1,0:T(8,128)(2,1)S(1)}, bf16[256,256]{1,0:T(8,128)(2,1)}, u32[]{:S(2)}) copy-start(bf16[256,256]{1,0:T(8,128)(2,1)} %param.18) | copy-start | bytes 393220
  16.0 6.6 %collective-permute-start.8 = (bf16[128,256]{1,0:T(8,128)(2,1)S(1)}, bf16[128,256]{1,0:T(8,128)(2,1)S(1)}, u32[]{:S(2)}, u32[]{:S(2)}) collective-permute-start(bf16[128,256]{1,0:T(8,128)(2,1)S(1)} %get-tuple-element.13), channel_id=1, source_target_pairs={{0,24},{8,16},{16,8},{24,0},{1,25},{9,17},{17,9},{25,1},{2,26},{10... | collective-permute-start | bytes 196616 | tf_op jit(solution)/shard_map/ppermute | solution.py:76
  17.5 6.1 %collective-permute-start.7 = (bf16[128,256]{1,0:T(8,128)(2,1)S(1)}, bf16[128,256]{1,0:T(8,128)(2,1)S(1)}, u32[]{:S(2)}, u32[]{:S(2)}) collective-permute-start(bf16[128,256]{1,0:T(8,128)(2,1)S(1)} %get-tuple-element.14), channel_id=1, source_target_pairs={{0,16},{8,24},{16,0},{24,8},{1,17},{9,25},{17,1},{25,9},{2,18},{10... | collective-permute-start | bytes 196616 | tf_op jit(solution)/shard_map/ppermute | solution.py:76
  19.0 4.7 %collective-permute-start.6 = (bf16[128,256]{1,0:T(8,128)(2,1)S(1)}, bf16[128,256]{1,0:T(8,128)(2,1)S(1)}, u32[]{:S(2)}, u32[]{:S(2)}) collective-permute-start(bf16[128,256]{1,0:T(8,128)(2,1)S(1)} %get-tuple-element.15), channel_id=1, source_target_pairs={{0,8},{8,0},{16,24},{24,16},{1,9},{9,1},{17,25},{25,17},{2,10},{10... | collective-permute-start | bytes 196616 | tf_op jit(solution)/shard_map/ppermute | solution.py:76
  19.5 8.3 %collective-permute-start.5 = (bf16[192,256]{1,0:T(8,128)(2,1)S(1)}, bf16[192,256]{1,0:T(8,128)(2,1)S(1)}, u32[]{:S(2)}, u32[]{:S(2)}) collective-permute-start(bf16[192,256]{1,0:T(8,128)(2,1)S(1)} %get-tuple-element.17), channel_id=1, source_target_pairs={{0,24},{8,16},{16,8},{24,0},{1,25},{9,17},{17,9},{25,1},{2,26},{10... | collective-permute-start | bytes 294920 | tf_op jit(solution)/shard_map/ppermute | solution.py:76
  21.0 7.4 %collective-permute-start.4 = (bf16[192,256]{1,0:T(8,128)(2,1)S(1)}, bf16[192,256]{1,0:T(8,128)(2,1)S(1)}, u32[]{:S(2)}, u32[]{:S(2)}) collective-permute-start(bf16[192,256]{1,0:T(8,128)(2,1)S(1)} %get-tuple-element.18), channel_id=1, source_target_pairs={{0,16},{8,24},{16,0},{24,8},{1,17},{9,25},{17,1},{25,9},{2,18},{10... | collective-permute-start | bytes 294920 | tf_op jit(solution)/shard_map/ppermute | solution.py:76
  22.6 5.9 %collective-permute-start.3 = (bf16[192,256]{1,0:T(8,128)(2,1)S(1)}, bf16[192,256]{1,0:T(8,128)(2,1)S(1)}, u32[]{:S(2)}, u32[]{:S(2)}) collective-permute-start(bf16[192,256]{1,0:T(8,128)(2,1)S(1)} %get-tuple-element.19), channel_id=1, source_target_pairs={{0,8},{8,0},{16,24},{24,16},{1,9},{9,1},{17,25},{25,17},{2,10},{10... | collective-permute-start | bytes 294920 | tf_op jit(solution)/shard_map/ppermute | solution.py:76
  23.9 6.2 %collective-permute-start.11 = (bf16[128,256]{1,0:T(8,128)(2,1)S(1)}, bf16[128,256]{1,0:T(8,128)(2,1)S(1)}, u32[]{:S(2)}, u32[]{:S(2)}) collective-permute-start(bf16[128,256]{1,0:T(8,128)(2,1)S(1)} %get-tuple-element.30), channel_id=1, source_target_pairs={{0,6},{1,7},{2,4},{3,5},{4,2},{5,3},{6,0},{7,1},{8,14},{9,15},{10,... | collective-permute-start | bytes 196616 | tf_op jit(solution)/shard_map/ppermute | solution.py:33
  27.8 5.2 %collective-permute-start.10 = (bf16[128,256]{1,0:T(8,128)(2,1)S(1)}, bf16[128,256]{1,0:T(8,128)(2,1)S(1)}, u32[]{:S(2)}, u32[]{:S(2)}) collective-permute-start(bf16[128,256]{1,0:T(8,128)(2,1)S(1)} %get-tuple-element.30), channel_id=1, source_target_pairs={{0,4},{1,5},{2,6},{3,7},{4,0},{5,1},{6,2},{7,3},{8,12},{9,13},{10,... | collective-permute-start | bytes 196616 | tf_op jit(solution)/shard_map/ppermute | solution.py:33
  27.8 5.2 %collective-permute-start.9 = (bf16[128,256]{1,0:T(8,128)(2,1)S(1)}, bf16[128,256]{1,0:T(8,128)(2,1)S(1)}, u32[]{:S(2)}, u32[]{:S(2)}) collective-permute-start(bf16[128,256]{1,0:T(8,128)(2,1)S(1)} %get-tuple-element.30), channel_id=1, source_target_pairs={{0,2},{1,3},{2,0},{3,1},{4,6},{5,7},{6,4},{7,5},{8,10},{9,11},{10,... | collective-permute-start | bytes 196616 | tf_op jit(solution)/shard_map/ppermute | solution.py:33
  28.4 5.1 %collective-permute-start.12 = (bf16[128,256]{1,0:T(8,128)(2,1)S(1)}, bf16[128,256]{1,0:T(8,128)(2,1)S(1)}, u32[]{:S(2)}, u32[]{:S(2)}) collective-permute-start(bf16[128,256]{1,0:T(8,128)(2,1)S(1)} %get-tuple-element.30), channel_id=1, source_target_pairs={{0,1},{1,0},{2,3},{3,2},{4,5},{5,4},{6,7},{7,6},{8,9},{9,8},{10,11... | collective-permute-start | bytes 196616 | tf_op jit(solution)/shard_map/ppermute | solution.py:35
  30.2 4.3 %collective-permute-start.15 = (bf16[128,256]{1,0:T(8,128)(2,1)S(1)}, bf16[128,256]{1,0:T(8,128)(2,1)S(1)}, u32[]{:S(2)}, u32[]{:S(2)}) collective-permute-start(bf16[128,256]{1,0:T(8,128)(2,1)S(1)} %collective-permute-done.11), channel_id=1, source_target_pairs={{0,1},{1,0},{2,3},{3,2},{4,5},{5,4},{6,7},{7,6},{8,9},{9,8},{10,11... | collective-permute-start | bytes 196616 | tf_op jit(solution)/shard_map/ppermute | solution.py:35
  33.0 1.4 %collective-permute-start.14 = (bf16[128,256]{1,0:T(8,128)(2,1)S(1)}, bf16[128,256]{1,0:T(8,128)(2,1)S(1)}, u32[]{:S(2)}, u32[]{:S(2)}) collective-permute-start(bf16[128,256]{1,0:T(8,128)(2,1)S(1)} %collective-permute-done.10), channel_id=1, source_target_pairs={{0,1},{1,0},{2,3},{3,2},{4,5},{5,4},{6,7},{7,6},{8,9},{9,8},{10,11... | collective-permute-start | bytes 196616 | tf_op jit(solution)/shard_map/ppermute | solution.py:35
  33.0 1.4 %collective-permute-start.13 = (bf16[128,256]{1,0:T(8,128)(2,1)S(1)}, bf16[128,256]{1,0:T(8,128)(2,1)S(1)}, u32[]{:S(2)}, u32[]{:S(2)}) collective-permute-start(bf16[128,256]{1,0:T(8,128)(2,1)S(1)} %collective-permute-done.9), channel_id=1, source_target_pairs={{0,1},{1,0},{2,3},{3,2},{4,5},{5,4},{6,7},{7,6},{8,9},{9,8},{10,11... | collective-permute-start | bytes 196616 | tf_op jit(solution)/shard_map/ppermute | solution.py:35

commit v23 on v22

--- a/solution.py
+++ b/solution.py
@@ -41,13 +41,11 @@
     return 0.5 + 0.5 * jnp.tanh(0.5 * x)
 
 
-def attend(query, blocks, sources, w_pair, length, scale_factor):
-    n_blocks, block_rows, d_model = blocks.shape
-    count = n_blocks * block_rows
+def attend(query, pair_blocks, sources, length, scale_factor):
+    n_blocks, block_rows, width = pair_blocks.shape
+    count, d_model = n_blocks * block_rows, width // 2
     head_size = d_model // HEADS
-    pair_rows = jnp.dot(
-        blocks.reshape(count, d_model), w_pair, preferred_element_type=jnp.float32
-    ).astype(jnp.bfloat16)
+    pair_rows = pair_blocks.reshape(count, width)
     keys = pair_rows[:, :d_model].reshape(count, HEADS, head_size)
     values = pair_rows[:, d_model:].reshape(count, HEADS, head_size)
     scores = jnp.einsum("zun,aun->zua", query, keys, preferred_element_type=jnp.float32) * scale_factor
@@ -138,12 +136,12 @@
         jnp.bfloat16
     )
     query_row_matrix = query_row_matrix.reshape(cand_dev, HEADS, head_size)
-    (mine, mine_sources), (partner, partner_sources) = gather_over_cand(hist_emb)
+    pair_local = jnp.dot(hist_emb, w_pair, preferred_element_type=jnp.float32).astype(jnp.bfloat16)
+    (mine, mine_sources), (partner, partner_sources) = gather_over_cand(pair_local)
     weighted_sum = attend(
         query_row_matrix,
         jnp.concatenate([mine, partner], axis=0),
         jnp.concatenate([mine_sources, partner_sources]),
-        w_pair,
         length,
         scale_factor,
     )

time: 37.7 us -> 41.2 us (1.093)
  waiting for transfers between devices: 6.47 us -> 9.25 us
  local copies, waits for them, and re-layouts: 7.1 us -> 7.55 us
    ppermute x3, waiting for transfers between devices: 3.56 us -> 6.25 us  [gather_over_cand(): lax.ppermute(rows, 'cand', [(i, i ^ hop) for i in range(n_cand)])]
    dot_general x2 -> x1, matrix products: 0.71 us -> 1.07 us  [body(): jnp.dot(hist_emb, w_pair, preferred_element_type=jnp.float32)]
    unnamed x15 -> x18, local copies, waits for them, and re-layouts: 0.75 us -> 0.98 us
  transfers between devices with their start and end apart: 16 -> 16, of which waited for: 7 -> 7; matrix products, arithmetic and copies ran while one was open for 6% -> 7% of each run, Pallas kernels for 0% -> 0%
where the time goes in v23:
time: 41.2 us; the launch traced here: 41 us
  starting transfers between devices  16.9 us (41%)
  waiting for transfers between devices  9.25 us (22%)
  local copies, waits for them, and re-layouts  7.55 us (18%)
  matrix products  4.87 us (12%)
  other arithmetic  1.39 us (3%)
  between operations  1.02 us (2%)
    ppermute x9, starting transfers between devices, swap_over_req(): lax.ppermute(blocks[hop], 'req', [(i, i ^ hop) for i in range(n_req)])  12 us
    ppermute x3, waiting for transfers between devices, gather_over_cand(): lax.ppermute(rows, 'cand', [(i, i ^ hop) for i in range(n_cand)])  6.25 us
    gather x1, local copies, waits for them, and re-layouts, body(): jnp.take(table, asked.reshape(-1), axis=0, mode='clip')  5.96 us
    ppermute x3, starting transfers between devices, gather_over_cand(): lax.ppermute(rows, 'cand', [(i, i ^ hop) for i in range(n_cand)])  4.39 us
    ppermute x9, waiting for transfers between devices, swap_over_req(): lax.ppermute(blocks[hop], 'req', [(i, i ^ hop) for i in range(n_req)])  2.05 us
    dot_general x1, matrix products, attend(): jnp.einsum('bgo,ogl->bgl', gates, values, preferred_element_type=jnp.floa...  1.32 us
    dot_general x1, matrix products, body(): jnp.dot(hidden, tower_out, preferred_element_type=jnp.float32)[None, :]  1.2 us
    dot_general x1, matrix products, body(): jnp.dot(hist_emb, w_pair, preferred_element_type=jnp.float32)  1.07 us
  transfers between devices with their start and end apart: 16, of which 7 were waited for; matrix products, arithmetic and copies ran while one was open for 7% of the time, Pallas kernels for 0%

profile of v23, /device:TPU:0, one launch (start us, length us, event | category | flops | bytes accessed | tf_op | source)
XLA Modules:
  0.0 41.0 jit_solution(1962867929178540301)
XLA Ops:
  0.0 0.7 %pad_add_fusion.1 = s32[768]{0:T(1024)S(1)} fusion(s32[256]{0:T(256)} %bitcast.95, s32[256]{0:T(256)} %bitcast.96, s32[128]{0:T(128)} %bitcast.97, s32[128]{0:T(128)} %bitcast.98), kind=kLoop, calls=%fused_computation.58 | loop fusion | flops 2304 | bytes 6144 | tf_op jit(solution)/shard_map/concatenate | solution.py:96
  0.8 0.3 convert_reduce_fusion
  1.2 0.4 %convolution_convert_fusion = s32[1280,2]{0,1:T(2,128)S(1)} fusion(s32[384]{0:T(512)S(1)} %pad_add_fusion.2, bf16[384,1]{0,1:T(2,128)(2,1)S(1)} %fusion.23, bf16[384,1]{0,1:T(2,128)(2,1)S(1)} %get-tuple-element.8), kind=kOutput, calls=%fused_computation.2 | convolution fusion | flops 2463232 | bytes 13312 | tf_op jit(solution)/shard_map/dot_general | solution.py:66
  1.8 3.0 %collective-permute-start = (s32[320]{0:T(512)S(1)}, s32[320]{0:T(512)S(1)}, u32[]{:S(2)}, u32[]{:S(2)}) collective-permute-start(s32[320]{0:T(512)S(1)} %get-tuple-element.5), channel_id=1, source_target_pairs={{0,8},{8,0},{16,24},{24,16},{1,9},{9,1},{17,25},{25,17},{2,10},{10... | collective-permute-start | bytes 3848 | tf_op jit(solution)/shard_map/ppermute | solution.py:74
  4.8 1.5 %collective-permute-start.2 = (s32[320]{0:T(512)S(1)}, s32[320]{0:T(512)S(1)}, u32[]{:S(2)}, u32[]{:S(2)}) collective-permute-start(s32[320]{0:T(512)S(1)} %get-tuple-element.6), channel_id=1, source_target_pairs={{0,24},{8,16},{16,8},{24,0},{1,25},{9,17},{17,9},{25,1},{2,26},{10... | collective-permute-start | bytes 3848 | tf_op jit(solution)/shard_map/ppermute | solution.py:74
  7.0 0.1 concatenate.102
  7.3 0.7 %reshape.370 = bf16[1024,1]{0,1:T(2,128)(2,1)S(1)} reshape(bf16[1024]{0:T(1024)(128)(2,1)} %param.21) | data formatting | bytes 4096 | tf_op args[10]
  8.0 1.3 %collective-permute-done.2 = s32[320]{0:T(512)S(1)} collective-permute-done((s32[320]{0:T(512)S(1)}, s32[320]{0:T(512)S(1)}, u32[]{:S(2)}, u32[]{:S(2)}) %collective-permute-start.2) | collective-permute-done | bytes 1312 | tf_op jit(solution)/shard_map/ppermute | solution.py:74
  9.3 0.6 %collective-permute-done.1 = s32[320]{0:T(512)S(1)} collective-permute-done((s32[320]{0:T(512)S(1)}, s32[320]{0:T(512)S(1)}, u32[]{:S(2)}, u32[]{:S(2)}) %collective-permute-start.1) | collective-permute-done | bytes 1312 | tf_op jit(solution)/shard_map/ppermute | solution.py:74
  9.9 0.1 reshape.363
  10.0 6.0 %gather_fusion = bf16[1280,256]{1,0:T(8,128)(2,1)S(1)} fusion(bf16[8192,256]{1,0:T(8,128)(2,1)} %param.11, s32[2048]{0:T(1024)S(1)} %pad_clamp_fusion), kind=kCustom, calls=%fused_computation | custom fusion | bytes 1315840 | tf_op jit(solution)/shard_map/jit(_take)/gather | solution.py:124
  16.0 1.5 %collective-permute-start.8 = (bf16[128,256]{1,0:T(8,128)(2,1)S(1)}, bf16[128,256]{1,0:T(8,128)(2,1)S(1)}, u32[]{:S(2)}, u32[]{:S(2)}) collective-permute-start(bf16[128,256]{1,0:T(8,128)(2,1)S(1)} %get-tuple-element.13), channel_id=1, source_target_pairs={{0,24},{8,16},{16,8},{24,0},{1,25},{9,17},{17,9},{25,1},{2,26},{10... | collective-permute-start | bytes 196616 | tf_op jit(solution)/shard_map/ppermute | solution.py:74
  17.5 1.5 %collective-permute-start.7 = (bf16[128,256]{1,0:T(8,128)(2,1)S(1)}, bf16[128,256]{1,0:T(8,128)(2,1)S(1)}, u32[]{:S(2)}, u32[]{:S(2)}) collective-permute-start(bf16[128,256]{1,0:T(8,128)(2,1)S(1)} %get-tuple-element.14), channel_id=1, source_target_pairs={{0,16},{8,24},{16,0},{24,8},{1,17},{9,25},{17,1},{25,9},{2,18},{10... | collective-permute-start | bytes 196616 | tf_op jit(solution)/shard_map/ppermute | solution.py:74
  19.0 0.5 %collective-permute-start.6 = (bf16[128,256]{1,0:T(8,128)(2,1)S(1)}, bf16[128,256]{1,0:T(8,128)(2,1)S(1)}, u32[]{:S(2)}, u32[]{:S(2)}) collective-permute-start(bf16[128,256]{1,0:T(8,128)(2,1)S(1)} %get-tuple-element.15), channel_id=1, source_target_pairs={{0,8},{8,0},{16,24},{24,16},{1,9},{9,1},{17,25},{25,17},{2,10},{10... | collective-permute-start | bytes 196616 | tf_op jit(solution)/shard_map/ppermute | solution.py:74
  19.5 1.5 %collective-permute-start.5 = (bf16[192,256]{1,0:T(8,128)(2,1)S(1)}, bf16[192,256]{1,0:T(8,128)(2,1)S(1)}, u32[]{:S(2)}, u32[]{:S(2)}) collective-permute-start(bf16[192,256]{1,0:T(8,128)(2,1)S(1)} %get-tuple-element.17), channel_id=1, source_target_pairs={{0,24},{8,16},{16,8},{24,0},{1,25},{9,17},{17,9},{25,1},{2,26},{10... | collective-permute-start | bytes 294920 | tf_op jit(solution)/shard_map/ppermute | solution.py:74
  21.0 1.5 %collective-permute-start.4 = (bf16[192,256]{1,0:T(8,128)(2,1)S(1)}, bf16[192,256]{1,0:T(8,128)(2,1)S(1)}, u32[]{:S(2)}, u32[]{:S(2)}) collective-permute-start(bf16[192,256]{1,0:T(8,128)(2,1)S(1)} %get-tuple-element.18), channel_id=1, source_target_pairs={{0,16},{8,24},{16,0},{24,8},{1,17},{9,25},{17,1},{25,9},{2,18},{10... | collective-permute-start | bytes 294920 | tf_op jit(solution)/shard_map/ppermute | solution.py:74
  22.6 0.9 %collective-permute-start.3 = (bf16[192,256]{1,0:T(8,128)(2,1)S(1)}, bf16[192,256]{1,0:T(8,128)(2,1)S(1)}, u32[]{:S(2)}, u32[]{:S(2)}) collective-permute-start(bf16[192,256]{1,0:T(8,128)(2,1)S(1)} %get-tuple-element.19), channel_id=1, source_target_pairs={{0,8},{8,0},{16,24},{24,16},{1,9},{9,1},{17,25},{25,17},{2,10},{10... | collective-permute-start | bytes 294920 | tf_op jit(solution)/shard_map/ppermute | solution.py:74
  23.5 0.1 collective-permute-done.6
  23.7 1.1 %bitcast_dynamic-update-slice_fusion.7 = (bf16[8,128,512]{2,1,0:T(8,128)(2,1)S(1)}, bf16[128,512]{1,0:T(8,128)(2,1)}) fusion(bf16[256,256]{1,0:T(8,128)(2,1)S(1)} %copy-done.3, bf16[256,256]{1,0:T(8,128)(2,1)S(1)} %copy-done.4, bf16[512,256]{1,0:T(8,128)(2,1)S(1)} %bitcast.85, s32[128]{0:T(128)S(1)} %slice.96), kind=kOutput, calls=%fused_computation.38 | convolution fusion | flops 67796992 | bytes 786944 | tf_op jit(solution)/shard_map/dot_general | solution.py:139
  24.8 3.8 %collective-permute-start.11 = (bf16[128,512]{1,0:T(8,128)(2,1)}, bf16[128,512]{1,0:T(8,128)(2,1)S(1)}, u32[]{:S(2)}, u32[]{:S(2)}) collective-permute-start(bf16[128,512]{1,0:T(8,128)(2,1)} %get-tuple-element.30), channel_id=1, source_target_pairs={{0,6},{1,7},{2,4},{3,5},{4,2},{5,3},{6,0},{7,1},{8,14},{9,15},{10,... | collective-permute-start | bytes 393224 | tf_op jit(solution)/shard_map/ppermute | solution.py:33
  28.6 0.6 %collective-permute-start.9 = (bf16[128,512]{1,0:T(8,128)(2,1)}, bf16[128,512]{1,0:T(8,128)(2,1)S(1)}, u32[]{:S(2)}, u32[]{:S(2)}) collective-permute-start(bf16[128,512]{1,0:T(8,128)(2,1)} %get-tuple-element.30), channel_id=1, source_target_pairs={{0,2},{1,3},{2,0},{3,1},{4,6},{5,7},{6,4},{7,5},{8,10},{9,11},{10,... | collective-permute-start | bytes 393224 | tf_op jit(solution)/shard_map/ppermute | solution.py:33
  29.2 0.3 convolution_convert_fusion.1
  29.6 0.3 fusion.14
  29.9 0.2 convolution_convert_fusion.2
  30.1 2.2 %collective-permute-done.11 = bf16[128,512]{1,0:T(8,128)(2,1)S(1)} collective-permute-done((bf16[128,512]{1,0:T(8,128)(2,1)}, bf16[128,512]{1,0:T(8,128)(2,1)S(1)}, u32[]{:S(2)}, u32[]{:S(2)}) %collective-permute-start.11) | collective-permute-done | bytes 131104 | tf_op jit(solution)/shard_map/ppermute | solution.py:33
  32.3 4.0 %collective-permute-done.10 = bf16[128,512]{1,0:T(8,128)(2,1)S(1)} collective-permute-done((bf16[128,512]{1,0:T(8,128)(2,1)}, bf16[128,512]{1,0:T(8,128)(2,1)S(1)}, u32[]{:S(2)}, u32[]{:S(2)}) %collective-permute-start.10) | collective-permute-done | bytes 131104 | tf_op jit(solution)/shard_map/ppermute | solution.py:33
  36.4 0.5 %collective-permute-start.13 = (bf16[128,512]{1,0:T(8,128)(2,1)S(1)}, bf16[128,512]{1,0:T(8,128)(2,1)S(1)}, u32[]{:S(2)}, u32[]{:S(2)}) collective-permute-start(bf16[128,512]{1,0:T(8,128)(2,1)S(1)} %collective-permute-done.9), channel_id=1, source_target_pairs={{0,1},{1,0},{2,3},{3,2},{4,5},{5,4},{6,7},{7,6},{8,9},{9,8},{10,11... | collective-permute-start | bytes 393224 | tf_op jit(solution)/shard_map/ppermute | solution.py:35
  37.0 0.9 %collective-permute-done.13 = bf16[128,512]{1,0:T(8,128)(2,1)S(1)} collective-permute-done((bf16[128,512]{1,0:T(8,128)(2,1)S(1)}, bf16[128,512]{1,0:T(8,128)(2,1)S(1)}, u32[]{:S(2)}, u32[]{:S(2)}) %collective-permute-start.13) | collective-permute-done | bytes 131104 | tf_op jit(solution)/shard_map/ppermute | solution.py:35
  38.1 0.2 copy.20
  38.3 0.2 copy.16
  38.5 1.3 %fusion.5 = bf16[4,64,256]{2,1,0:T(8,128)(2,1)S(1)} fusion(bf16[1024,4,64]{0,2,1:T(8,128)(2,1)S(1)} %bitcast.83, bf16[1024,4,64]{0,2,1:T(8,128)(2,1)S(1)} %bitcast.82, bf16[256,4,64]{0,2,1:T(8,128)(2,1)S(1)} %bitcast.86, pred[1024]{0:T(1024)(128)(4,1)S(1)} %fusion.22, f32[]{:T(128)S(6)} %sqrt.3), kind=kOutput, calls=%fused_computation.12 | convolution fusion | flops 273809408 | bytes 1311748 | tf_op jit(solution)/shard_map/bgo,ogl->bgl/dot_general | solution.py:58
  39.8 1.2 %fusion.8 = f32[1,256]{1,0:T(1,128)} fusion(bf16[1024,1]{0,1:T(2,128)(2,1)S(1)} %reshape.370, f32[256,1024]{1,0:T(8,128)S(1)} %fusion.14, bf16[256,256]{0,1:T(8,128)(2,1)S(1)} %bitcast.99, bf16[512,1024]{1,0:T(8,128)(2,1)S(1)} %copy-done.2), kind=kOutput, calls=%fused_computation.14 | convolution fusion | flops 136314880 | bytes 1709056 | tf_op jit(solution)/shard_map/dot_general | solution.py:157
  (60 shorter events, 0.9 us)
Async XLA Ops:
  0.0 29.9 %copy-start = (bf16[256,256]{1,0:T(8,128)(2,1)S(1)}, bf16[256,256]{1,0:T(8,128)(2,1)}, u32[]{:S(2)}) copy-start(bf16[256,256]{1,0:T(8,128)(2,1)} %param.17) | copy-start | bytes 393220
  1.1 22.5 %copy-start.3 = (bf16[256,256]{1,0:T(8,128)(2,1)S(1)}, bf16[256,256]{1,0:T(8,128)(2,1)}, u32[]{:S(2)}) copy-start(bf16[256,256]{1,0:T(8,128)(2,1)} %param.19) | copy-start | bytes 393220
  1.2 22.5 %copy-start.4 = (bf16[256,256]{1,0:T(8,128)(2,1)S(1)}, bf16[256,256]{1,0:T(8,128)(2,1)}, u32[]{:S(2)}) copy-start(bf16[256,256]{1,0:T(8,128)(2,1)} %param.18) | copy-start | bytes 393220
  1.8 6.2 %collective-permute-start = (s32[320]{0:T(512)S(1)}, s32[320]{0:T(512)S(1)}, u32[]{:S(2)}, u32[]{:S(2)}) collective-permute-start(s32[320]{0:T(512)S(1)} %get-tuple-element.5), channel_id=1, source_target_pairs={{0,8},{8,0},{16,24},{24,16},{1,9},{9,1},{17,25},{25,17},{2,10},{10... | collective-permute-start | bytes 3848 | tf_op jit(solution)/shard_map/ppermute | solution.py:74
  4.8 4.5 %collective-permute-start.2 = (s32[320]{0:T(512)S(1)}, s32[320]{0:T(512)S(1)}, u32[]{:S(2)}, u32[]{:S(2)}) collective-permute-start(s32[320]{0:T(512)S(1)} %get-tuple-element.6), channel_id=1, source_target_pairs={{0,24},{8,16},{16,8},{24,0},{1,25},{9,17},{17,9},{25,1},{2,26},{10... | collective-permute-start | bytes 3848 | tf_op jit(solution)/shard_map/ppermute | solution.py:74
  6.3 3.6 %collective-permute-start.1 = (s32[320]{0:T(512)S(1)}, s32[320]{0:T(512)S(1)}, u32[]{:S(2)}, u32[]{:S(2)}) collective-permute-start(s32[320]{0:T(512)S(1)} %get-tuple-element.7), channel_id=1, source_target_pairs={{0,16},{8,24},{16,0},{24,8},{1,17},{9,25},{17,1},{25,9},{2,18},{10... | collective-permute-start | bytes 3848 | tf_op jit(solution)/shard_map/ppermute | solution.py:74
  10.0 19.6 %copy-start.1 = (bf16[512,1024]{1,0:T(8,128)(2,1)S(1)}, bf16[512,1024]{1,0:T(8,128)(2,1)}, u32[]{:S(2)}) copy-start(bf16[512,1024]{1,0:T(8,128)(2,1)} %param.20) | copy-start | bytes 3145732
  16.0 6.6 %collective-permute-start.8 = (bf16[128,256]{1,0:T(8,128)(2,1)S(1)}, bf16[128,256]{1,0:T(8,128)(2,1)S(1)}, u32[]{:S(2)}, u32[]{:S(2)}) collective-permute-start(bf16[128,256]{1,0:T(8,128)(2,1)S(1)} %get-tuple-element.13), channel_id=1, source_target_pairs={{0,24},{8,16},{16,8},{24,0},{1,25},{9,17},{17,9},{25,1},{2,26},{10... | collective-permute-start | bytes 196616 | tf_op jit(solution)/shard_map/ppermute | solution.py:74
  17.5 6.1 %collective-permute-start.7 = (bf16[128,256]{1,0:T(8,128)(2,1)S(1)}, bf16[128,256]{1,0:T(8,128)(2,1)S(1)}, u32[]{:S(2)}, u32[]{:S(2)}) collective-permute-start(bf16[128,256]{1,0:T(8,128)(2,1)S(1)} %get-tuple-element.14), channel_id=1, source_target_pairs={{0,16},{8,24},{16,0},{24,8},{1,17},{9,25},{17,1},{25,9},{2,18},{10... | collective-permute-start | bytes 196616 | tf_op jit(solution)/shard_map/ppermute | solution.py:74
  19.0 4.7 %collective-permute-start.6 = (bf16[128,256]{1,0:T(8,128)(2,1)S(1)}, bf16[128,256]{1,0:T(8,128)(2,1)S(1)}, u32[]{:S(2)}, u32[]{:S(2)}) collective-permute-start(bf16[128,256]{1,0:T(8,128)(2,1)S(1)} %get-tuple-element.15), channel_id=1, source_target_pairs={{0,8},{8,0},{16,24},{24,16},{1,9},{9,1},{17,25},{25,17},{2,10},{10... | collective-permute-start | bytes 196616 | tf_op jit(solution)/shard_map/ppermute | solution.py:74
  19.5 9.0 %collective-permute-start.5 = (bf16[192,256]{1,0:T(8,128)(2,1)S(1)}, bf16[192,256]{1,0:T(8,128)(2,1)S(1)}, u32[]{:S(2)}, u32[]{:S(2)}) collective-permute-start(bf16[192,256]{1,0:T(8,128)(2,1)S(1)} %get-tuple-element.17), channel_id=1, source_target_pairs={{0,24},{8,16},{16,8},{24,0},{1,25},{9,17},{17,9},{25,1},{2,26},{10... | collective-permute-start | bytes 294920 | tf_op jit(solution)/shard_map/ppermute | solution.py:74
  21.0 8.1 %collective-permute-start.4 = (bf16[192,256]{1,0:T(8,128)(2,1)S(1)}, bf16[192,256]{1,0:T(8,128)(2,1)S(1)}, u32[]{:S(2)}, u32[]{:S(2)}) collective-permute-start(bf16[192,256]{1,0:T(8,128)(2,1)S(1)} %get-tuple-element.18), channel_id=1, source_target_pairs={{0,16},{8,24},{16,0},{24,8},{1,17},{9,25},{17,1},{25,9},{2,18},{10... | collective-permute-start | bytes 294920 | tf_op jit(solution)/shard_map/ppermute | solution.py:74
  22.6 6.6 %collective-permute-start.3 = (bf16[192,256]{1,0:T(8,128)(2,1)S(1)}, bf16[192,256]{1,0:T(8,128)(2,1)S(1)}, u32[]{:S(2)}, u32[]{:S(2)}) collective-permute-start(bf16[192,256]{1,0:T(8,128)(2,1)S(1)} %get-tuple-element.19), channel_id=1, source_target_pairs={{0,8},{8,0},{16,24},{24,16},{1,9},{9,1},{17,25},{25,17},{2,10},{10... | collective-permute-start | bytes 294920 | tf_op jit(solution)/shard_map/ppermute | solution.py:74
  24.8 7.6 %collective-permute-start.11 = (bf16[128,512]{1,0:T(8,128)(2,1)}, bf16[128,512]{1,0:T(8,128)(2,1)S(1)}, u32[]{:S(2)}, u32[]{:S(2)}) collective-permute-start(bf16[128,512]{1,0:T(8,128)(2,1)} %get-tuple-element.30), channel_id=1, source_target_pairs={{0,6},{1,7},{2,4},{3,5},{4,2},{5,3},{6,0},{7,1},{8,14},{9,15},{10,... | collective-permute-start | bytes 393224 | tf_op jit(solution)/shard_map/ppermute | solution.py:33
  28.6 7.8 %collective-permute-start.10 = (bf16[128,512]{1,0:T(8,128)(2,1)}, bf16[128,512]{1,0:T(8,128)(2,1)S(1)}, u32[]{:S(2)}, u32[]{:S(2)}) collective-permute-start(bf16[128,512]{1,0:T(8,128)(2,1)} %get-tuple-element.30), channel_id=1, source_target_pairs={{0,4},{1,5},{2,6},{3,7},{4,0},{5,1},{6,2},{7,3},{8,12},{9,13},{10,... | collective-permute-start | bytes 393224 | tf_op jit(solution)/shard_map/ppermute | solution.py:33
  28.6 7.8 %collective-permute-start.9 = (bf16[128,512]{1,0:T(8,128)(2,1)}, bf16[128,512]{1,0:T(8,128)(2,1)S(1)}, u32[]{:S(2)}, u32[]{:S(2)}) collective-permute-start(bf16[128,512]{1,0:T(8,128)(2,1)} %get-tuple-element.30), channel_id=1, source_target_pairs={{0,2},{1,3},{2,0},{3,1},{4,6},{5,7},{6,4},{7,5},{8,10},{9,11},{10,... | collective-permute-start | bytes 393224 | tf_op jit(solution)/shard_map/ppermute | solution.py:33
  29.2 7.8 %collective-permute-start.12 = (bf16[128,512]{1,0:T(8,128)(2,1)}, bf16[128,512]{1,0:T(8,128)(2,1)S(1)}, u32[]{:S(2)}, u32[]{:S(2)}) collective-permute-start(bf16[128,512]{1,0:T(8,128)(2,1)} %get-tuple-element.30), channel_id=1, source_target_pairs={{0,1},{1,0},{2,3},{3,2},{4,5},{5,4},{6,7},{7,6},{8,9},{9,8},{10,11... | collective-permute-start | bytes 393224 | tf_op jit(solution)/shard_map/ppermute | solution.py:35
  32.3 5.6 %collective-permute-start.15 = (bf16[128,512]{1,0:T(8,128)(2,1)S(1)}, bf16[128,512]{1,0:T(8,128)(2,1)S(1)}, u32[]{:S(2)}, u32[]{:S(2)}) collective-permute-start(bf16[128,512]{1,0:T(8,128)(2,1)S(1)} %collective-permute-done.11), channel_id=1, source_target_pairs={{0,1},{1,0},{2,3},{3,2},{4,5},{5,4},{6,7},{7,6},{8,9},{9,8},{10,11... | collective-permute-start | bytes 393224 | tf_op jit(solution)/shard_map/ppermute | solution.py:35
  36.4 1.6 %collective-permute-start.14 = (bf16[128,512]{1,0:T(8,128)(2,1)S(1)}, bf16[128,512]{1,0:T(8,128)(2,1)S(1)}, u32[]{:S(2)}, u32[]{:S(2)}) collective-permute-start(bf16[128,512]{1,0:T(8,128)(2,1)S(1)} %collective-permute-done.10), channel_id=1, source_target_pairs={{0,1},{1,0},{2,3},{3,2},{4,5},{5,4},{6,7},{7,6},{8,9},{9,8},{10,11... | collective-permute-start | bytes 393224 | tf_op jit(solution)/shard_map/ppermute | solution.py:35
  36.4 1.5 %collective-permute-start.13 = (bf16[128,512]{1,0:T(8,128)(2,1)S(1)}, bf16[128,512]{1,0:T(8,128)(2,1)S(1)}, u32[]{:S(2)}, u32[]{:S(2)}) collective-permute-start(bf16[128,512]{1,0:T(8,128)(2,1)S(1)} %collective-permute-done.9), channel_id=1, source_target_pairs={{0,1},{1,0},{2,3},{3,2},{4,5},{5,4},{6,7},{7,6},{8,9},{9,8},{10,11... | collective-permute-start | bytes 393224 | tf_op jit(solution)/shard_map/ppermute | solution.py:35
  38.5 1.3 %copy-start.2 = (bf16[512,1024]{1,0:T(8,128)(2,1)S(1)}, bf16[512,1024]{1,0:T(8,128)(2,1)}, u32[]{:S(2)}) copy-start(bf16[512,1024]{1,0:T(8,128)(2,1)} %param.20) | copy-start | bytes 3145732
